TPU v7x, 32 devices: a whole 2x2x4 slice. The times are simulated.
32 devices in a mesh: img: 8 (over z, y), sub: 4 (over x, core).
Axes of the slice: x: 2, y: 2, z: 4, core: 2. Of those that a mesh axis runs over, the one named last changes fastest.
Arguments:
- embeddings: bfloat16 [4096, 768], P('img'), may hold values from -60 to 60
- labels: bfloat16 [4096, 256], P('img', 'sub'), may hold values from -6 to 6
- image_lists: int32 [4096, 2], P('img'), may hold values from 0 to 7, all different within a row; in each aligned block of 512 rows (0 to 511, 512 to 1023, ...) at most 256 rows name the same one
- rank_keys: int32 [4096, 2], P('img'), may hold values from 0 to 255
Outputs:
- propagated: bfloat16 [4096, 256], P('img', 'sub')
Inputs may be any that keep to these rules, and one draw needn't show every extreme that they name: `image_lists`: the two lists of an image differ. On the rows of one index of img no list is named more than 256 times, a bound that some block reaches.
All inputs are finite; a program needn't handle non-finite values.
Results may differ from a plain program's by a relative error of at most 0.0034.
Values may be sent and summed in bfloat16 or wider, within the bound.
No kernel may reach another device: no remote copies, remote signals or barrier semaphores. Data moves between devices by JAX's collectives and lax.ppermute only.
A program may use at most 64 MiB of HBM per device.

v0:
```python
import jax
import jax.numpy as jnp
from jax import lax
from jax.sharding import PartitionSpec as P

SLOTS = 2048
BAND = 64
LIST_DEV = 1


def affinity(gram, row_keys, col_keys):
    keep = jnp.abs(row_keys[:, :, None] - col_keys[:, None, :]) <= BAND
    positive = jnp.maximum(gram, 0.0)
    return jnp.where(keep, positive * positive * positive, 0.0).astype(jnp.bfloat16)


def list_major(bucket):
    moved = jnp.moveaxis(bucket, 1, 0)
    return moved.reshape((moved.shape[0], moved.shape[1] * moved.shape[2]) + moved.shape[3:])


def blocked_affinity(rows, key_rows):
    lists_here = rows.shape[0]
    slot_count = rows.shape[1]
    block_rows = min(512, slot_count)
    block_count = slot_count // block_rows
    row_blocks = jnp.moveaxis(
        rows.reshape(lists_here, block_count, block_rows, rows.shape[2]), 1, 0
    )
    key_blocks = jnp.moveaxis(key_rows.reshape(lists_here, block_count, block_rows), 1, 0)

    def one_block(packed):
        picked, picked_keys = packed
        gram = jnp.einsum("ajf,akf->ajk", picked, rows, preferred_element_type=jnp.float32)
        return affinity(gram, picked_keys, key_rows)

    blocks = lax.map(one_block, (row_blocks, key_blocks))
    return jnp.moveaxis(blocks, 0, 1).reshape(lists_here, slot_count, slot_count)


def on_device(embeddings, labels, image_lists, rank_keys):
    img_count = lax.axis_size("img")
    per_list = SLOTS // img_count
    rows_here = image_lists.shape[0]
    pair_count = rows_here * 2
    lists_flat = image_lists.reshape(-1)
    order = jnp.arange(pair_count, dtype=jnp.int32)
    same = (lists_flat[:, None] == lists_flat[None, :]) & (order[None, :] < order[:, None])
    within = jnp.sum(same.astype(jnp.int32), axis=1)
    slot_of_pair = lists_flat * per_list + within
    slot_total = LIST_DEV * img_count * per_list
    filler = jnp.full((slot_total,), pair_count, jnp.int32).at[slot_of_pair].set(order)
    image_of_slot = filler // 2

    def to_bucket(rows):
        padded = jnp.concatenate([rows, jnp.zeros((1, rows.shape[1]), rows.dtype)], axis=0)
        return padded[image_of_slot].reshape(img_count, LIST_DEV, per_list, rows.shape[1])

    def bucket_major(listed):
        shaped = listed.reshape((listed.shape[0], img_count, per_list) + listed.shape[2:])
        return jnp.moveaxis(shaped, 0, 1)

    def from_bucket(returned):
        flat = returned.reshape(slot_total, -1)
        return jnp.sum(flat[slot_of_pair].reshape(rows_here, 2, -1), axis=1)

    values = embeddings.astype(jnp.float32)
    unit = (values * lax.rsqrt(jnp.sum(values * values, axis=1, keepdims=True) + 1e-06)).astype(
        jnp.bfloat16
    )
    key_pad = jnp.concatenate(
        [rank_keys.reshape(-1).astype(jnp.float32), jnp.full((1,), -4096.0, jnp.float32)]
    )
    slot_keys = key_pad[filler].astype(jnp.bfloat16).reshape(img_count, LIST_DEV, per_list)
    feats = lax.all_to_all(to_bucket(unit), "img", split_axis=0, concat_axis=0, tiled=True)
    got_keys = lax.all_to_all(slot_keys, "img", split_axis=0, concat_axis=0, tiled=True)
    rows = list_major(feats)
    key_rows = list_major(got_keys).astype(jnp.float32)
    weights = blocked_affinity(rows, key_rows)
    row_sums = jnp.sum(weights, axis=2, dtype=jnp.float32)
    degree_slots = lax.all_to_all(
        bucket_major(row_sums), "img", split_axis=0, concat_axis=0, tiled=True
    )
    degree = from_bucket(degree_slots)[:, 0]
    inv = lax.rsqrt(degree)
    starting = labels.astype(jnp.float32)
    current = starting
    for step in range(2):
        scaled = (inv[:, None] * current).astype(jnp.bfloat16)
        arrived = lax.all_to_all(to_bucket(scaled), "img", split_axis=0, concat_axis=0, tiled=True)
        product = jnp.einsum(
            "ajk,akc->ajc", weights, list_major(arrived), preferred_element_type=jnp.float32
        )
        returned = lax.all_to_all(
            bucket_major(product), "img", split_axis=0, concat_axis=0, tiled=True
        )
        spread = from_bucket(returned)
        current = 0.8 * inv[:, None] * spread + 0.2 * starting
    return current.astype(jnp.bfloat16)


def solution(mesh):
    return jax.shard_map(
        on_device,
        mesh=mesh,
        in_specs=(P("img", None), P("img", "sub"), P("img", None), P("img", None)),
        out_specs=P("img", "sub"),
        check_vma=False,
    )
```

profile of v0, /device:TPU:0, one launch (start us, length us, event | category | flops | bytes accessed | tf_op | source)
XLA Modules:
  0.0 242.4 jit_solution(18362139141305591906)
XLA Ops:
  0.0 0.0 copy-start
  0.0 0.9 copy.97
  0.9 0.7 broadcast_multiply_fusion
  1.6 0.2 eq.15
  1.8 0.5 convert_reduce_fusion.1
  2.3 0.1 copy.96
  2.5 0.2 mul.78
  2.7 4.3 %scatter_custom_fusion = s32[2048]{0:T(1024)S(1)} fusion(s32[1024]{0:T(1024)S(1)} %bitcast.85, s32[1024]{0:T(1024)S(1)} %iota.9, s32[]{:T(128)} %constant.13.clone.1), kind=kCustom, calls=%fused_computation.50 | custom fusion | bytes 8196 | tf_op jit(solution)/shard_map/scatter | solution.py:52
  7.0 0.7 convert_element_type.76
  7.7 0.2 copy.95
  7.9 0.2 convert_element_type.77
  8.1 13.1 %gather_fusion = bf16[2048]{0:T(1024)(128)(2,1)S(1)} fusion(bf16[1025]{0:T(1024)(128)(2,1)S(1)} %pad_maximum_fusion, s32[2048]{0:T(1024)S(1)} %get-tuple-element.81), kind=kCustom, calls=%fused_computation | custom fusion | bytes 16384 | tf_op jit(solution)/shard_map/gather | solution.py:74
  21.2 0.5 broadcast.112
  21.7 0.7 reduce.3
  22.4 0.6 reshape.261
  23.0 7.3 %all-to-all-start = ((bf16[8,2,128]{2,1,0:T(2,128)(2,1)}), bf16[8,2,128]{2,1,0:T(2,128)(2,1)S(1)}, u32[]{:S(2)}, u32[]{:S(2)}) async-start(bf16[8,2,128]{2,1,0:T(2,128)(2,1)} %reshape.261), calls=%async_computation | async-start | bytes 8192 | tf_op jit(solution)/shard_map/all_to_all | solution.py:76
  30.3 0.0 copy-done
  30.3 0.2 fusion.13
  30.5 0.2 fusion.14
  30.7 0.1 concatenate.13
  30.8 9.4 %gather_fusion.1 = bf16[2048,768]{1,0:T(8,128)(2,1)} fusion(bf16[513,768]{1,0:T(8,128)(2,1)S(1)} %concatenate.13, s32[2048]{0:T(1024)S(1)} %get-tuple-element.80), kind=kCustom, calls=%fused_computation.1 | custom fusion | bytes 6299648 | tf_op jit(solution)/shard_map/gather | solution.py:57
  40.2 0.0 all-to-all-done
  40.2 6.0 %all-to-all-start.1 = ((bf16[8,1,256,768]{3,2,1,0:T(8,128)(2,1)}), bf16[8,1,256,768]{3,2,1,0:T(8,128)(2,1)S(1)}, u32[]{:S(2)}, u32[]{:S(2)}) async-start(bf16[8,1,256,768]{3,2,1,0:T(8,128)(2,1)} %bitcast.70), calls=%async_computation.1 | async-start | bytes 6291456 | tf_op jit(solution)/shard_map/all_to_all | solution.py:75
  46.2 70.1 %all-to-all-done.1 = bf16[8,1,256,768]{3,2,1,0:T(8,128)(2,1)S(1)} async-done(((bf16[8,1,256,768]{3,2,1,0:T(8,128)(2,1)}), bf16[8,1,256,768]{3,2,1,0:T(8,128)(2,1)S(1)}, u32[]{:S(2)}, u32[]{:S(2)}) %all-to-all-start.1) | async-done | bytes 3145760 | tf_op jit(solution)/shard_map/all_to_all | solution.py:75
  116.3 13.2 %while.10 = (s32[]{:T(128)}, bf16[4,1,512,2048]{3,2,1,0:T(8,128)(2,1)}, f32[4,1,512]{2,1,0:T(1,128)S(1)}, f32[1,2048]{1,0:T(1,128)S(1)}, bf16[4,1,512,768]{3,2,1...) while((s32[]{:T(128)}, bf16[4,1,512,2048]{3,2,1,0:T(8,128)(2,1)}, ...), condition=%wide.region_4.5_spmd, body=%wide.region_3.4_spmd.sunk | while | flops 1619001344 | bytes 6044753 | solution.py:37
  116.3 3.3 %fusion.36 = bf16[4,1,512,2048]{3,2,1,0:T(8,128)(2,1)} fusion(bf16[4,1,512,2048]{3,2,1,0:T(8,128)(2,1)} %get-tuple-element.129, s32[]{:T(128)} %get-tuple-element.128, bf16[1,2048,768]{2,1,0:T(8,128)(2,1)S(1)} %get-tuple-element.140, f32[2048]{0:T(1024)S(1)} %bitcast.83, f32[512]{0:T(512)S(1)} %bitcast.79, bf16[4,1,512,768]{3,2,1,0:T(8,128)(2,1)S(1)} %bitcast.73), kind=kOutput, calls=%fused_computation.14.clone.1 | convolution fusion | flops 1619001344 | bytes 6040576 | tf_op jit(solution)/shard_map/while/body/eval_jaxpr/ajf,akf->ajk/dot_general | solution.py:34
  119.7 3.3 %fusion.36 = bf16[4,1,512,2048]{3,2,1,0:T(8,128)(2,1)} fusion(bf16[4,1,512,2048]{3,2,1,0:T(8,128)(2,1)} %get-tuple-element.129, s32[]{:T(128)} %get-tuple-element.128, bf16[1,2048,768]{2,1,0:T(8,128)(2,1)S(1)} %get-tuple-element.140, f32[2048]{0:T(1024)S(1)} %bitcast.83, f32[512]{0:T(512)S(1)} %bitcast.79, bf16[4,1,512,768]{3,2,1,0:T(8,128)(2,1)S(1)} %bitcast.73), kind=kOutput, calls=%fused_computation.14.clone.1 | convolution fusion | flops 1619001344 | bytes 6040576 | tf_op jit(solution)/shard_map/while/body/eval_jaxpr/ajf,akf->ajk/dot_general | solution.py:34
  122.9 3.3 %fusion.36 = bf16[4,1,512,2048]{3,2,1,0:T(8,128)(2,1)} fusion(bf16[4,1,512,2048]{3,2,1,0:T(8,128)(2,1)} %get-tuple-element.129, s32[]{:T(128)} %get-tuple-element.128, bf16[1,2048,768]{2,1,0:T(8,128)(2,1)S(1)} %get-tuple-element.140, f32[2048]{0:T(1024)S(1)} %bitcast.83, f32[512]{0:T(512)S(1)} %bitcast.79, bf16[4,1,512,768]{3,2,1,0:T(8,128)(2,1)S(1)} %bitcast.73), kind=kOutput, calls=%fused_computation.14.clone.1 | convolution fusion | flops 1619001344 | bytes 6040576 | tf_op jit(solution)/shard_map/while/body/eval_jaxpr/ajf,akf->ajk/dot_general | solution.py:34
  126.2 3.3 %fusion.36 = bf16[4,1,512,2048]{3,2,1,0:T(8,128)(2,1)} fusion(bf16[4,1,512,2048]{3,2,1,0:T(8,128)(2,1)} %get-tuple-element.129, s32[]{:T(128)} %get-tuple-element.128, bf16[1,2048,768]{2,1,0:T(8,128)(2,1)S(1)} %get-tuple-element.140, f32[2048]{0:T(1024)S(1)} %bitcast.83, f32[512]{0:T(512)S(1)} %bitcast.79, bf16[4,1,512,768]{3,2,1,0:T(8,128)(2,1)S(1)} %bitcast.73), kind=kOutput, calls=%fused_computation.14.clone.1 | convolution fusion | flops 1619001344 | bytes 6040576 | tf_op jit(solution)/shard_map/while/body/eval_jaxpr/ajf,akf->ajk/dot_general | solution.py:34
  129.5 4.5 %convert_reduce_fusion = f32[4,512]{1,0:T(4,128)S(1)} fusion(bf16[4,1,512,2048]{3,2,1,0:T(8,128)(2,1)} %get-tuple-element.37), kind=kLoop, calls=%fused_computation.19 | loop fusion | flops 8386560 | bytes 8396800 | tf_op jit(solution)/shard_map/reduce_sum | solution.py:80
  134.1 0.0 copy-start.1
  134.1 0.6 transpose_reshape.2
  134.7 3.6 %all-to-all-start.2 = ((f32[8,1,256]{2,1,0:T(1,128)}), f32[8,1,256]{2,1,0:T(1,128)S(1)}, u32[]{:S(2)}, u32[]{:S(2)}) async-start(f32[8,1,256]{2,1,0:T(1,128)} %transpose_reshape.2), calls=%async_computation.2 | async-start | bytes 16384 | tf_op jit(solution)/shard_map/all_to_all | solution.py:81
  138.3 6.5 %all-to-all-done.2 = f32[8,1,256]{2,1,0:T(1,128)S(1)} async-done(((f32[8,1,256]{2,1,0:T(1,128)}), f32[8,1,256]{2,1,0:T(1,128)S(1)}, u32[]{:S(2)}, u32[]{:S(2)}) %all-to-all-start.2) | async-done | bytes 8224 | tf_op jit(solution)/shard_map/all_to_all | solution.py:81
  144.9 6.1 %gather_fusion.2 = f32[1024]{0:T(1024)S(1)} fusion(f32[2048]{0:T(1024)S(1)} %bitcast.65, s32[1024]{0:T(1024)S(1)} %broadcast_clamp_fusion), kind=kCustom, calls=%fused_computation.2 | custom fusion | bytes 12288 | tf_op jit(solution)/shard_map/gather | solution.py:65
  151.0 0.2 reshape.171
  151.2 0.1 reduce_sum.60
  151.4 0.0 copy-done.1
  151.4 0.1 copy.120
  151.6 6.2 %gather_fusion.3 = bf16[2048,64]{1,0:T(8,128)(2,1)S(1)} fusion(bf16[513,64]{1,0:T(8,128)(2,1)S(1)} %concatenate.14.clone, s32[2048]{0:T(1024)S(1)} %get-tuple-element.80), kind=kCustom, calls=%fused_computation.3 | custom fusion | bytes 532480 | tf_op jit(solution)/shard_map/gather | solution.py:57
  157.8 0.2 copy.103
  158.0 10.6 %all_to_all.35 = bf16[8,1,256,64]{2,3,1,0:T(8,128)(2,1)S(1)} all-to-all(bf16[8,1,256,64]{2,3,1,0:T(8,128)(2,1)S(1)} %copy.103), channel_id=1, replica_groups=mesh['img'=8,'sub'=4] {'img'}, dimensions={0} | all-to-all | bytes 524288 | tf_op jit(solution)/shard_map/all_to_all | solution.py:90
  168.6 0.1 copy.104
  168.8 0.1 reshape.255
  168.9 6.0 %convolution_bitcast_fusion.1 = f32[8,1,256,64]{2,3,1,0:T(8,128)S(1)} fusion(bf16[8,256,2048]{2,1,0:T(8,128)(2,1)} %bitcast.66, bf16[2048,64,1]{0,1,2:T(8,128)(2,1)S(1)} %reshape.255), kind=kOutput, calls=%fused_computation.28 | convolution fusion | flops 536870912 | bytes 9175040 | tf_op jit(solution)/shard_map/ajk,akc->ajc/dot_general | solution.py:91
  174.9 16.8 %all_to_all.36 = f32[8,1,256,64]{2,3,1,0:T(8,128)S(1)} all-to-all(f32[8,1,256,64]{2,3,1,0:T(8,128)S(1)} %convolution_bitcast_fusion.1), channel_id=1, replica_groups=mesh['img'=8,'sub'=4] {'img'}, dimensions={0} | all-to-all | bytes 1048576 | tf_op jit(solution)/shard_map/all_to_all | solution.py:94
  191.7 0.3 copy.116
  192.1 2.8 %gather_fusion.4 = f32[1024,64]{1,0:T(8,128)S(1)} fusion(f32[2048,64]{1,0:T(8,128)S(1)} %bitcast.69, s32[1024]{0:T(1024)S(1)} %broadcast_clamp_fusion), kind=kCustom, calls=%fused_computation.4 | custom fusion | bytes 528384 | tf_op jit(solution)/shard_map/gather | solution.py:65
  194.9 0.6 reduce_sum.61
  195.6 0.1 copy.108
  195.7 0.1 copy.121
  195.9 6.2 %gather_fusion.5 = bf16[2048,64]{1,0:T(8,128)(2,1)S(1)} fusion(bf16[513,64]{1,0:T(8,128)(2,1)S(1)} %concatenate.15.clone, s32[2048]{0:T(1024)S(1)} %get-tuple-element.80), kind=kCustom, calls=%fused_computation.5 | custom fusion | bytes 532480 | tf_op jit(solution)/shard_map/gather | solution.py:57
  202.1 0.2 copy.110
  202.3 12.0 %all_to_all.37 = bf16[8,1,256,64]{2,3,1,0:T(8,128)(2,1)S(1)} all-to-all(bf16[8,1,256,64]{2,3,1,0:T(8,128)(2,1)S(1)} %copy.110), channel_id=1, replica_groups=mesh['img'=8,'sub'=4] {'img'}, dimensions={0} | all-to-all | bytes 524288 | tf_op jit(solution)/shard_map/all_to_all | solution.py:90
  214.2 0.1 copy.111
  214.4 0.1 reshape.256
  214.5 6.0 %convolution_bitcast_fusion = f32[8,1,256,64]{2,3,1,0:T(8,128)S(1)} fusion(bf16[8,256,2048]{2,1,0:T(8,128)(2,1)} %bitcast.67, bf16[2048,64,1]{0,1,2:T(8,128)(2,1)S(1)} %reshape.256), kind=kOutput, calls=%fused_computation.27 | convolution fusion | flops 536870912 | bytes 9175040 | tf_op jit(solution)/shard_map/ajk,akc->ajc/dot_general | solution.py:91
  220.6 17.3 %all_to_all.38 = f32[8,1,256,64]{2,3,1,0:T(8,128)S(1)} all-to-all(f32[8,1,256,64]{2,3,1,0:T(8,128)S(1)} %convolution_bitcast_fusion), channel_id=1, replica_groups=mesh['img'=8,'sub'=4] {'img'}, dimensions={0} | all-to-all | bytes 1048576 | tf_op jit(solution)/shard_map/all_to_all | solution.py:94
  237.8 0.3 copy.117
  238.2 2.8 %gather_fusion.6 = f32[1024,64]{1,0:T(8,128)S(1)} fusion(f32[2048,64]{1,0:T(8,128)S(1)} %bitcast.68, s32[1024]{0:T(1024)S(1)} %broadcast_clamp_fusion), kind=kCustom, calls=%fused_computation.6 | custom fusion | bytes 528384 | tf_op jit(solution)/shard_map/gather | solution.py:65
  241.0 0.6 reduce_sum.62
  241.6 0.1 copy.115
  241.8 0.7 fusion.19
  (19 shorter events, 0.2 us)
Async XLA Ops:
  0.0 30.3 %copy-start = (bf16[512,768]{1,0:T(8,128)(2,1)S(1)}, bf16[512,768]{1,0:T(8,128)(2,1)}, u32[]{:S(2)}) copy-start(bf16[512,768]{1,0:T(8,128)(2,1)} %param.6) | copy-start | bytes 2359300
  23.0 17.2 %all-to-all-start = ((bf16[8,2,128]{2,1,0:T(2,128)(2,1)}), bf16[8,2,128]{2,1,0:T(2,128)(2,1)S(1)}, u32[]{:S(2)}, u32[]{:S(2)}) async-start(bf16[8,2,128]{2,1,0:T(2,128)(2,1)} %reshape.261), calls=%async_computation | async-start | bytes 8192 | tf_op jit(solution)/shard_map/all_to_all | solution.py:76
  40.2 76.1 %all-to-all-start.1 = ((bf16[8,1,256,768]{3,2,1,0:T(8,128)(2,1)}), bf16[8,1,256,768]{3,2,1,0:T(8,128)(2,1)S(1)}, u32[]{:S(2)}, u32[]{:S(2)}) async-start(bf16[8,1,256,768]{3,2,1,0:T(8,128)(2,1)} %bitcast.70), calls=%async_computation.1 | async-start | bytes 6291456 | tf_op jit(solution)/shard_map/all_to_all | solution.py:75
  134.1 17.3 %copy-start.1 = (bf16[512,64]{0,1:T(8,128)(2,1)S(1)}, bf16[512,64]{0,1:T(8,128)(2,1)}, u32[]{:S(2)}) copy-start(bf16[512,64]{0,1:T(8,128)(2,1)} %param.7) | copy-start | bytes 196612
  134.7 10.2 %all-to-all-start.2 = ((f32[8,1,256]{2,1,0:T(1,128)}), f32[8,1,256]{2,1,0:T(1,128)S(1)}, u32[]{:S(2)}, u32[]{:S(2)}) async-start(f32[8,1,256]{2,1,0:T(1,128)} %transpose_reshape.2), calls=%async_computation.2 | async-start | bytes 16384 | tf_op jit(solution)/shard_map/all_to_all | solution.py:81
where the time goes:
time: 243 us; the launch traced here: 242 us
  waiting for transfers between devices  76.6 us (32%)
  local copies, waits for them, and re-layouts  56.9 us (23%)
  blocking collectives  56.7 us (23%)
  matrix products  25.2 us (10%)
  starting transfers between devices  16.9 us (7%)
  other arithmetic  9.76 us (4%)
    all_to_all x1, waiting for transfers between devices, on_device(): lax.all_to_all(to_bucket(unit), 'img', split_axis=0, concat_axis=0, tiled...  70.1 us
    all_to_all x2, blocking collectives, on_device(): lax.all_to_all(bucket_major(product), 'img', split_axis=0, concat_axis=0,...  34.1 us
    all_to_all x2, blocking collectives, on_device(): lax.all_to_all(to_bucket(scaled), 'img', split_axis=0, concat_axis=0, til...  22.6 us
    gather x3, local copies, waits for them, and re-layouts, to_bucket(): padded[image_of_slot].reshape(img_count, LIST_DEV, per_list, rows.shape[1])  21.8 us
    dot_general x4, matrix products, one_block(): jnp.einsum('ajf,akf->ajk', picked, rows, preferred_element_type=jnp.float32)  13.2 us
    gather x1, local copies, waits for them, and re-layouts, on_device(): key_pad[filler].astype(jnp.bfloat16).reshape(img_count, LIST_DEV, per_list)  13.1 us
    dot_general x2, matrix products, on_device(): jnp.einsum('ajk,akc->ajc', weights, list_major(arrived), preferred_elemen...  12.1 us
    gather x3, local copies, waits for them, and re-layouts, from_bucket(): return jnp.sum(flat[slot_of_pair].reshape(rows_here, 2, -1), axis=1)  11.8 us
  transfers between devices with their start and end apart: 3, of which 2 were waited for; matrix products, arithmetic and copies ran while one was open for 4% of the time, Pallas kernels for 0%

commit v1 on v0

--- a/solution.py
+++ b/solution.py
@@ -72,7 +72,17 @@
         [rank_keys.reshape(-1).astype(jnp.float32), jnp.full((1,), -4096.0, jnp.float32)]
     )
     slot_keys = key_pad[filler].astype(jnp.bfloat16).reshape(img_count, LIST_DEV, per_list)
-    feats = lax.all_to_all(to_bucket(unit), "img", split_axis=0, concat_axis=0, tiled=True)
+    sub_count = lax.axis_size("sub")
+    part = per_list // sub_count
+    mine = lax.dynamic_index_in_dim(
+        image_of_slot.reshape(img_count, sub_count, part), lax.axis_index("sub"), axis=1,
+        keepdims=False,
+    )
+    unit_pad = jnp.concatenate([unit, jnp.zeros((1, unit.shape[1]), unit.dtype)], axis=0)
+    sent = lax.all_to_all(unit_pad[mine], "img", split_axis=0, concat_axis=0, tiled=True)
+    feats = lax.all_gather(sent, "sub", axis=1, tiled=False).reshape(
+        img_count, LIST_DEV, per_list, unit.shape[1]
+    )
     got_keys = lax.all_to_all(slot_keys, "img", split_axis=0, concat_axis=0, tiled=True)
     rows = list_major(feats)
     key_rows = list_major(got_keys).astype(jnp.float32)

time: 243 us -> 218 us (0.90)
  waiting for transfers between devices: 76.6 us -> 15.3 us
  blocking collectives: 56.7 us -> 84.5 us
  between operations: 0.31 us -> 13.7 us
  matrix products: 25.2 us -> 33.9 us
  starting transfers between devices: 16.9 us -> 9.12 us
  local copies, waits for them, and re-layouts: 56.9 us -> 49.6 us
    all_to_all x1 -> x0, waiting for transfers between devices: 70.1 us -> none  [on_device(): lax.all_to_all(to_bucket(unit), 'img', split_axis=0, concat_axis=0, tiled...]
    all_to_all x0 -> x1, blocking collectives: none -> 27.3 us  [on_device(): lax.all_to_all(unit_pad[mine], 'img', split_axis=0, concat_axis=0, tiled=...]
    gather x3 -> x2, local copies, waits for them, and re-layouts: 21.8 us -> 12.4 us  [to_bucket(): padded[image_of_slot].reshape(img_count, LIST_DEV, per_list, rows.shape[1])]
    dot_general x4, matrix products: 13.2 us -> 21.8 us  [one_block(): jnp.einsum('ajf,akf->ajk', picked, rows, preferred_element_type=jnp.float32)]
    all_to_all x1, waiting for transfers between devices: 0.01 us -> 6.39 us  [on_device(): lax.all_to_all(slot_keys, 'img', split_axis=0, concat_axis=0, tiled=True)]
    all_to_all x1 -> x0, starting transfers between devices: 5.99 us -> none  [on_device(): lax.all_to_all(to_bucket(unit), 'img', split_axis=0, concat_axis=0, tiled...]
    all_to_all x1, starting transfers between devices: 7.28 us -> 3.59 us  [on_device(): lax.all_to_all(slot_keys, 'img', split_axis=0, concat_axis=0, tiled=True)]
  transfers between devices with their start and end apart: 3 -> 3, of which waited for: 2 -> 3; matrix products, arithmetic and copies ran while one was open for 4% -> 7% of each run, Pallas kernels for 0% -> 0%
where the time goes in v1:
time: 218 us; the launch traced here: 217 us
  blocking collectives  84.5 us (39%)
  local copies, waits for them, and re-layouts  49.6 us (23%)
  matrix products  33.9 us (16%)
  waiting for transfers between devices  15.3 us (7%)
  between operations  13.7 us (6%)
  other arithmetic  11.4 us (5%)
  starting transfers between devices  9.12 us (4%)
    all_to_all x2, blocking collectives, on_device(): lax.all_to_all(bucket_major(product), 'img', split_axis=0, concat_axis=0,...  34.4 us
    all_to_all x1, blocking collectives, on_device(): lax.all_to_all(unit_pad[mine], 'img', split_axis=0, concat_axis=0, tiled=...  27.3 us
    all_to_all x2, blocking collectives, on_device(): lax.all_to_all(to_bucket(scaled), 'img', split_axis=0, concat_axis=0, til...  22.7 us
    dot_general x4, matrix products, one_block(): jnp.einsum('ajf,akf->ajk', picked, rows, preferred_element_type=jnp.float32)  21.8 us
    gather x1, local copies, waits for them, and re-layouts, on_device(): key_pad[filler].astype(jnp.bfloat16).reshape(img_count, LIST_DEV, per_list)  13.1 us
    gather x2, local copies, waits for them, and re-layouts, to_bucket(): padded[image_of_slot].reshape(img_count, LIST_DEV, per_list, rows.shape[1])  12.4 us
    dot_general x2, matrix products, on_device(): jnp.einsum('ajk,akc->ajc', weights, list_major(arrived), preferred_elemen...  12.1 us
    gather x3, local copies, waits for them, and re-layouts, from_bucket(): return jnp.sum(flat[slot_of_pair].reshape(rows_here, 2, -1), axis=1)  11.8 us
  transfers between devices with their start and end apart: 3, of which 3 were waited for; matrix products, arithmetic and copies ran while one was open for 7% of the time, Pallas kernels for 0%

profile of v1, /device:TPU:0, one launch (start us, length us, event | category | flops | bytes accessed | tf_op | source)
XLA Modules:
  0.0 217.4 jit_solution(4173252699219720566)
XLA Ops:
  6.5 0.8 copy.89
  7.4 0.7 broadcast_multiply_fusion
  8.1 0.2 eq.15
  8.2 0.5 convert_reduce_fusion.1
  8.8 0.1 copy.88
  8.9 0.2 mul.78
  9.1 4.3 %scatter_custom_fusion = s32[2048]{0:T(1024)S(1)} fusion(s32[1024]{0:T(1024)S(1)} %bitcast.80, s32[1024]{0:T(1024)S(1)} %iota.9, s32[]{:T(128)} %constant.30.clone.1), kind=kCustom, calls=%fused_computation.52 | custom fusion | bytes 8196 | tf_op jit(solution)/shard_map/scatter | solution.py:52
  13.5 0.1 reshape.197
  13.6 0.1 reshape.221
  13.7 1.4 fusion.13
  15.0 1.3 fusion.14
  16.4 0.1 concatenate.13
  16.4 0.0 copy-start.1
  16.4 2.0 gather_fusion.1
  18.5 27.3 %all_to_all.35 = bf16[8,64,768]{2,1,0:T(8,128)(2,1)} all-to-all(bf16[8,64,768]{2,1,0:T(8,128)(2,1)S(1)} %bitcast.69), channel_id=1, replica_groups=mesh['img'=8,'sub'=4] {'img'}, dimensions={0} | all-to-all | bytes 1572864 | tf_op jit(solution)/shard_map/all_to_all | solution.py:82
  45.8 0.0 all-gather.3.cloned.1.call-update
  45.9 0.2 copy.87
  46.1 0.2 convert_element_type.77
  46.3 13.1 %gather_fusion = bf16[2048]{0:T(1024)(128)(2,1)S(1)} fusion(bf16[1025]{0:T(1024)(128)(2,1)S(1)} %pad_maximum_fusion, s32[2048]{0:T(1024)S(1)} %get-tuple-element.81), kind=kCustom, calls=%fused_computation | custom fusion | bytes 16384 | tf_op jit(solution)/shard_map/gather | solution.py:74
  59.4 0.5 broadcast.131
  59.9 0.7 reduce.3
  60.5 0.6 reshape.292
  61.2 3.6 %all-to-all-start = ((bf16[8,2,128]{2,1,0:T(2,128)(2,1)}), bf16[8,2,128]{2,1,0:T(2,128)(2,1)S(1)}, u32[]{:S(2)}, u32[]{:S(2)}) async-start(bf16[8,2,128]{2,1,0:T(2,128)(2,1)} %reshape.292), calls=%async_computation | async-start | bytes 8192 | tf_op jit(solution)/shard_map/all_to_all | solution.py:86
  64.7 6.4 %all-to-all-done = bf16[8,2,128]{2,1,0:T(2,128)(2,1)S(1)} async-done(((bf16[8,2,128]{2,1,0:T(2,128)(2,1)}), bf16[8,2,128]{2,1,0:T(2,128)(2,1)S(1)}, u32[]{:S(2)}, u32[]{:S(2)}) %all-to-all-start) | async-done | bytes 4128 | tf_op jit(solution)/shard_map/all_to_all | solution.py:86
  71.2 2.4 %all-gather.3.cloned.1.call-done = bf16[8,256,768]{2,1,0:T(8,128)(2,1)} async-done(((bf16[8,64,768]{2,1,0:T(8,128)(2,1)}), bf16[8,256,768]{2,1,0:T(8,128)(2,1)}) %all-gather.3.cloned.1.call-update) | async-done | bytes 3145744 | tf_op jit(solution)/shard_map/all_gather | solution.py:83
  73.5 21.8 %while.10 = (s32[]{:T(128)}, bf16[4,1,512,2048]{3,2,1,0:T(8,128)(2,1)}, f32[4,1,512]{2,1,0:T(1,128)S(1)}, f32[1,2048]{1,0:T(1,128)S(1)}, bf16[4,1,512,768]{3,2,1...) while((s32[]{:T(128)}, bf16[4,1,512,2048]{3,2,1,0:T(8,128)(2,1)}, f32[4,1,512]{2,1,0:T(1,128)S(1)}, ...), condition=%wide.region_4.5_spmd, body=%wide.region_3.4_spmd.sunk | while | flops 1619001344 | bytes 6044753 | solution.py:37
  73.5 5.5 %fusion.36 = bf16[4,1,512,2048]{3,2,1,0:T(8,128)(2,1)} fusion(bf16[4,1,512,2048]{3,2,1,0:T(8,128)(2,1)} %get-tuple-element.130, s32[]{:T(128)} %get-tuple-element.129, bf16[1,2048,768]{2,1,0:T(8,128)(2,1)} %get-tuple-element.141, f32[2048]{0:T(1024)S(1)} %bitcast.78, f32[512]{0:T(512)S(1)} %bitcast.74, bf16[4,1,512,768]{3,2,1,0:T(8,128)(2,1)} %bitcast.86), kind=kOutput, calls=%fused_computation.14.clone.1 | convolution fusion | flops 1619001344 | bytes 6040576 | tf_op jit(solution)/shard_map/while/body/eval_jaxpr/ajf,akf->ajk/dot_general | solution.py:34
  79.0 5.4 %fusion.36 = bf16[4,1,512,2048]{3,2,1,0:T(8,128)(2,1)} fusion(bf16[4,1,512,2048]{3,2,1,0:T(8,128)(2,1)} %get-tuple-element.130, s32[]{:T(128)} %get-tuple-element.129, bf16[1,2048,768]{2,1,0:T(8,128)(2,1)} %get-tuple-element.141, f32[2048]{0:T(1024)S(1)} %bitcast.78, f32[512]{0:T(512)S(1)} %bitcast.74, bf16[4,1,512,768]{3,2,1,0:T(8,128)(2,1)} %bitcast.86), kind=kOutput, calls=%fused_computation.14.clone.1 | convolution fusion | flops 1619001344 | bytes 6040576 | tf_op jit(solution)/shard_map/while/body/eval_jaxpr/ajf,akf->ajk/dot_general | solution.py:34
  84.4 5.4 %fusion.36 = bf16[4,1,512,2048]{3,2,1,0:T(8,128)(2,1)} fusion(bf16[4,1,512,2048]{3,2,1,0:T(8,128)(2,1)} %get-tuple-element.130, s32[]{:T(128)} %get-tuple-element.129, bf16[1,2048,768]{2,1,0:T(8,128)(2,1)} %get-tuple-element.141, f32[2048]{0:T(1024)S(1)} %bitcast.78, f32[512]{0:T(512)S(1)} %bitcast.74, bf16[4,1,512,768]{3,2,1,0:T(8,128)(2,1)} %bitcast.86), kind=kOutput, calls=%fused_computation.14.clone.1 | convolution fusion | flops 1619001344 | bytes 6040576 | tf_op jit(solution)/shard_map/while/body/eval_jaxpr/ajf,akf->ajk/dot_general | solution.py:34
  89.9 5.4 %fusion.36 = bf16[4,1,512,2048]{3,2,1,0:T(8,128)(2,1)} fusion(bf16[4,1,512,2048]{3,2,1,0:T(8,128)(2,1)} %get-tuple-element.130, s32[]{:T(128)} %get-tuple-element.129, bf16[1,2048,768]{2,1,0:T(8,128)(2,1)} %get-tuple-element.141, f32[2048]{0:T(1024)S(1)} %bitcast.78, f32[512]{0:T(512)S(1)} %bitcast.74, bf16[4,1,512,768]{3,2,1,0:T(8,128)(2,1)} %bitcast.86), kind=kOutput, calls=%fused_computation.14.clone.1 | convolution fusion | flops 1619001344 | bytes 6040576 | tf_op jit(solution)/shard_map/while/body/eval_jaxpr/ajf,akf->ajk/dot_general | solution.py:34
  95.3 4.5 %convert_reduce_fusion = f32[4,512]{1,0:T(4,128)S(1)} fusion(bf16[4,1,512,2048]{3,2,1,0:T(8,128)(2,1)} %get-tuple-element.37), kind=kLoop, calls=%fused_computation.19 | loop fusion | flops 8386560 | bytes 8396800 | tf_op jit(solution)/shard_map/reduce_sum | solution.py:90
  99.9 0.0 copy-start
  99.9 0.6 transpose_reshape.2
  100.5 5.5 %all-to-all-start.2 = ((f32[8,1,256]{2,1,0:T(1,128)}), f32[8,1,256]{2,1,0:T(1,128)S(1)}, u32[]{:S(2)}, u32[]{:S(2)}) async-start(f32[8,1,256]{2,1,0:T(1,128)} %transpose_reshape.2), calls=%async_computation.2 | async-start | bytes 16384 | tf_op jit(solution)/shard_map/all_to_all | solution.py:91
  106.0 6.5 %all-to-all-done.2 = f32[8,1,256]{2,1,0:T(1,128)S(1)} async-done(((f32[8,1,256]{2,1,0:T(1,128)}), f32[8,1,256]{2,1,0:T(1,128)S(1)}, u32[]{:S(2)}, u32[]{:S(2)}) %all-to-all-start.2) | async-done | bytes 8224 | tf_op jit(solution)/shard_map/all_to_all | solution.py:91
  112.5 6.1 %gather_fusion.2 = f32[1024]{0:T(1024)S(1)} fusion(f32[2048]{0:T(1024)S(1)} %bitcast.64, s32[1024]{0:T(1024)S(1)} %broadcast_clamp_fusion), kind=kCustom, calls=%fused_computation.2 | custom fusion | bytes 12288 | tf_op jit(solution)/shard_map/gather | solution.py:65
  118.7 0.2 reshape.199
  118.9 0.1 reduce_sum.60
  119.1 0.0 copy-done
  119.1 0.1 copy.110
  119.3 6.2 %gather_fusion.3 = bf16[2048,64]{1,0:T(8,128)(2,1)S(1)} fusion(bf16[513,64]{1,0:T(8,128)(2,1)S(1)} %concatenate.14.clone, s32[2048]{0:T(1024)S(1)} %get-tuple-element.80), kind=kCustom, calls=%fused_computation.3 | custom fusion | bytes 532480 | tf_op jit(solution)/shard_map/gather | solution.py:57
  125.5 0.2 copy.93
  125.7 10.7 %all_to_all.36 = bf16[8,1,256,64]{2,3,1,0:T(8,128)(2,1)S(1)} all-to-all(bf16[8,1,256,64]{2,3,1,0:T(8,128)(2,1)S(1)} %copy.93), channel_id=1, replica_groups=mesh['img'=8,'sub'=4] {'img'}, dimensions={0} | all-to-all | bytes 524288 | tf_op jit(solution)/shard_map/all_to_all | solution.py:100
  136.4 0.1 copy.94
  136.5 0.1 reshape.286
  136.7 6.0 %convolution_bitcast_fusion.1 = f32[8,1,256,64]{2,3,1,0:T(8,128)S(1)} fusion(bf16[8,256,2048]{2,1,0:T(8,128)(2,1)} %bitcast.65, bf16[2048,64,1]{0,1,2:T(8,128)(2,1)S(1)} %reshape.286), kind=kOutput, calls=%fused_computation.28 | convolution fusion | flops 536870912 | bytes 9175040 | tf_op jit(solution)/shard_map/ajk,akc->ajc/dot_general | solution.py:101
  142.7 17.2 %all_to_all.37 = f32[8,1,256,64]{2,3,1,0:T(8,128)S(1)} all-to-all(f32[8,1,256,64]{2,3,1,0:T(8,128)S(1)} %convolution_bitcast_fusion.1), channel_id=1, replica_groups=mesh['img'=8,'sub'=4] {'img'}, dimensions={0} | all-to-all | bytes 1048576 | tf_op jit(solution)/shard_map/all_to_all | solution.py:104
  159.9 0.3 copy.106
  160.2 2.8 %gather_fusion.4 = f32[1024,64]{1,0:T(8,128)S(1)} fusion(f32[2048,64]{1,0:T(8,128)S(1)} %bitcast.68, s32[1024]{0:T(1024)S(1)} %broadcast_clamp_fusion), kind=kCustom, calls=%fused_computation.4 | custom fusion | bytes 528384 | tf_op jit(solution)/shard_map/gather | solution.py:65
  163.0 0.6 reduce_sum.61
  163.7 0.1 copy.98
  163.9 0.1 copy.111
  164.0 6.2 %gather_fusion.5 = bf16[2048,64]{1,0:T(8,128)(2,1)S(1)} fusion(bf16[513,64]{1,0:T(8,128)(2,1)S(1)} %concatenate.15.clone, s32[2048]{0:T(1024)S(1)} %get-tuple-element.80), kind=kCustom, calls=%fused_computation.5 | custom fusion | bytes 532480 | tf_op jit(solution)/shard_map/gather | solution.py:57
  170.2 0.2 copy.100
  170.4 12.0 %all_to_all.38 = bf16[8,1,256,64]{2,3,1,0:T(8,128)(2,1)S(1)} all-to-all(bf16[8,1,256,64]{2,3,1,0:T(8,128)(2,1)S(1)} %copy.100), channel_id=1, replica_groups=mesh['img'=8,'sub'=4] {'img'}, dimensions={0} | all-to-all | bytes 524288 | tf_op jit(solution)/shard_map/all_to_all | solution.py:100
  182.4 0.1 copy.101
  182.5 0.1 reshape.287
  182.7 6.0 %convolution_bitcast_fusion = f32[8,1,256,64]{2,3,1,0:T(8,128)S(1)} fusion(bf16[8,256,2048]{2,1,0:T(8,128)(2,1)} %bitcast.66, bf16[2048,64,1]{0,1,2:T(8,128)(2,1)S(1)} %reshape.287), kind=kOutput, calls=%fused_computation.27 | convolution fusion | flops 536870912 | bytes 9175040 | tf_op jit(solution)/shard_map/ajk,akc->ajc/dot_general | solution.py:101
  188.7 17.3 %all_to_all.39 = f32[8,1,256,64]{2,3,1,0:T(8,128)S(1)} all-to-all(f32[8,1,256,64]{2,3,1,0:T(8,128)S(1)} %convolution_bitcast_fusion), channel_id=1, replica_groups=mesh['img'=8,'sub'=4] {'img'}, dimensions={0} | all-to-all | bytes 1048576 | tf_op jit(solution)/shard_map/all_to_all | solution.py:104
  206.0 0.3 copy.107
  206.3 2.8 %gather_fusion.6 = f32[1024,64]{1,0:T(8,128)S(1)} fusion(f32[2048,64]{1,0:T(8,128)S(1)} %bitcast.67, s32[1024]{0:T(1024)S(1)} %broadcast_clamp_fusion), kind=kCustom, calls=%fused_computation.6 | custom fusion | bytes 528384 | tf_op jit(solution)/shard_map/gather | solution.py:65
  209.1 0.6 reduce_sum.62
  209.8 0.1 copy.105
  209.9 0.7 fusion.19
  (25 shorter events, 0.2 us)
Async XLA Ops:
  6.5 67.0 %all-gather.3.cloned.1.call-start = ((), (), s32[]{:S(2)}) async-start(), calls=%async_computation.7 | async-start | bytes 3932160 | tf_op jit(solution)/shard_map/all_gather | solution.py:83
  16.4 29.4 %copy-start.1 = (s32[512,2]{0,1:T(2,128)S(1)}, s32[512,2]{0,1:T(2,128)}, u32[]{:S(2)}) copy-start(s32[512,2]{0,1:T(2,128)} %param.9) | copy-start | bytes 12292
  61.2 10.0 %all-to-all-start = ((bf16[8,2,128]{2,1,0:T(2,128)(2,1)}), bf16[8,2,128]{2,1,0:T(2,128)(2,1)S(1)}, u32[]{:S(2)}, u32[]{:S(2)}) async-start(bf16[8,2,128]{2,1,0:T(2,128)(2,1)} %reshape.292), calls=%async_computation | async-start | bytes 8192 | tf_op jit(solution)/shard_map/all_to_all | solution.py:86
  99.9 19.2 %copy-start = (bf16[512,64]{0,1:T(8,128)(2,1)S(1)}, bf16[512,64]{0,1:T(8,128)(2,1)}, u32[]{:S(2)}) copy-start(bf16[512,64]{0,1:T(8,128)(2,1)} %param.7) | copy-start | bytes 196612
  100.5 12.0 %all-to-all-start.2 = ((f32[8,1,256]{2,1,0:T(1,128)}), f32[8,1,256]{2,1,0:T(1,128)S(1)}, u32[]{:S(2)}, u32[]{:S(2)}) async-start(f32[8,1,256]{2,1,0:T(1,128)} %transpose_reshape.2), calls=%async_computation.2 | async-start | bytes 16384 | tf_op jit(solution)/shard_map/all_to_all | solution.py:91
Sparse Core Ops, SparseCore 0:
  46.0 27.5 all-gather.2

commit v2 on v0

--- a/solution.py
+++ b/solution.py
@@ -40,21 +40,27 @@
 
 def on_device(embeddings, labels, image_lists, rank_keys):
     img_count = lax.axis_size("img")
+    sub_count = lax.axis_size("sub")
     per_list = SLOTS // img_count
+    part = per_list // sub_count
     rows_here = image_lists.shape[0]
     pair_count = rows_here * 2
     lists_flat = image_lists.reshape(-1)
     order = jnp.arange(pair_count, dtype=jnp.int32)
     same = (lists_flat[:, None] == lists_flat[None, :]) & (order[None, :] < order[:, None])
     within = jnp.sum(same.astype(jnp.int32), axis=1)
-    slot_of_pair = lists_flat * per_list + within
+    slot_of_pair = (lists_flat * per_list + within).reshape(rows_here, 2)
     slot_total = LIST_DEV * img_count * per_list
-    filler = jnp.full((slot_total,), pair_count, jnp.int32).at[slot_of_pair].set(order)
-    image_of_slot = filler // 2
+
+    slot_ids = jnp.arange(slot_total, dtype=jnp.int32)[:, None]
+    hit_a = slot_of_pair[None, :, 0] == slot_ids
+    hit_b = slot_of_pair[None, :, 1] == slot_ids
+    hit = hit_a | hit_b
+    pick = hit.astype(jnp.bfloat16)
 
     def to_bucket(rows):
-        padded = jnp.concatenate([rows, jnp.zeros((1, rows.shape[1]), rows.dtype)], axis=0)
-        return padded[image_of_slot].reshape(img_count, LIST_DEV, per_list, rows.shape[1])
+        picked = jnp.dot(pick, rows, preferred_element_type=jnp.float32).astype(rows.dtype)
+        return picked.reshape(img_count, LIST_DEV, per_list, rows.shape[1])
 
     def bucket_major(listed):
         shaped = listed.reshape((listed.shape[0], img_count, per_list) + listed.shape[2:])
@@ -62,17 +68,40 @@
 
     def from_bucket(returned):
         flat = returned.reshape(slot_total, -1)
-        return jnp.sum(flat[slot_of_pair].reshape(rows_here, 2, -1), axis=1)
+        return jnp.einsum(
+            "kg,kc->gc", pick.astype(jnp.float32), flat,
+            precision=lax.Precision.HIGHEST, preferred_element_type=jnp.float32,
+        )
 
     values = embeddings.astype(jnp.float32)
     unit = (values * lax.rsqrt(jnp.sum(values * values, axis=1, keepdims=True) + 1e-06)).astype(
         jnp.bfloat16
     )
-    key_pad = jnp.concatenate(
-        [rank_keys.reshape(-1).astype(jnp.float32), jnp.full((1,), -4096.0, jnp.float32)]
+    keys_f = rank_keys.astype(jnp.float32)
+    key_sum = jnp.sum(
+        jnp.where(hit_a, keys_f[None, :, 0], 0.0) + jnp.where(hit_b, keys_f[None, :, 1], 0.0),
+        axis=1,
     )
-    slot_keys = key_pad[filler].astype(jnp.bfloat16).reshape(img_count, LIST_DEV, per_list)
-    feats = lax.all_to_all(to_bucket(unit), "img", split_axis=0, concat_axis=0, tiled=True)
+    key_of_slot = jnp.where(jnp.any(hit, axis=1), key_sum, -4096.0)
+    slot_keys = key_of_slot.astype(jnp.bfloat16).reshape(img_count, LIST_DEV, per_list)
+
+    me_sub = lax.axis_index("sub")
+    mine = (
+        jnp.arange(img_count, dtype=jnp.int32)[:, None] * per_list
+        + me_sub * part
+        + jnp.arange(part, dtype=jnp.int32)[None, :]
+    ).reshape(-1, 1)
+    pick_mine = (
+        (slot_of_pair[None, :, 0] == mine) | (slot_of_pair[None, :, 1] == mine)
+    ).astype(jnp.bfloat16)
+    quarter = jnp.dot(pick_mine, unit, preferred_element_type=jnp.float32).astype(jnp.bfloat16)
+    sent = lax.all_to_all(
+        quarter.reshape(img_count, part, unit.shape[1]), "img", split_axis=0, concat_axis=0,
+        tiled=True,
+    )
+    feats = lax.all_gather(sent, "sub", axis=1, tiled=False).reshape(
+        img_count, LIST_DEV, per_list, unit.shape[1]
+    )
     got_keys = lax.all_to_all(slot_keys, "img", split_axis=0, concat_axis=0, tiled=True)
     rows = list_major(feats)
     key_rows = list_major(got_keys).astype(jnp.float32)
@@ -81,7 +110,7 @@
     degree_slots = lax.all_to_all(
         bucket_major(row_sums), "img", split_axis=0, concat_axis=0, tiled=True
     )
-    degree = from_bucket(degree_slots)[:, 0]
+    degree = jnp.sum(jnp.where(hit, degree_slots.reshape(slot_total, 1), 0.0), axis=0)
     inv = lax.rsqrt(degree)
     starting = labels.astype(jnp.float32)
     current = starting

time: 243 us -> 191 us (0.79)
  waiting for transfers between devices: 76.6 us -> 20.3 us
  local copies, waits for them, and re-layouts: 56.9 us -> 3.41 us
  blocking collectives: 56.7 us -> 96.3 us
  matrix products: 25.2 us -> 42 us
  starting transfers between devices: 16.9 us -> 3.59 us
  between operations: 0.31 us -> 13.6 us
    all_to_all x2 -> x0, waiting for transfers between devices: 76.6 us -> none  [the longest x1 70.1 us: on_device(): lax.all_to_all(to_bucket(unit), 'img', split_axis=0, concat_axis=0, tiled...]
    gather x7 -> x0, local copies, waits for them, and re-layouts: 46.6 us -> none  [the longest x3 21.8 us: to_bucket(): padded[image_of_slot].reshape(img_count, LIST_DEV, per_list, rows.shape[1])]
    all_to_all x0 -> x2, blocking collectives: none -> 39.2 us  [the longest x1 27.3 us: on_device(): lax.all_to_all(quarter.reshape(img_count, part, unit.shape[1]), 'img', sp...]
    all_gather x0 -> x1, waiting for transfers between devices: none -> 13.9 us  [on_device(): lax.all_gather(sent, 'sub', axis=1, tiled=False)]
    all_to_all x2 -> x0, starting transfers between devices: 9.63 us -> none  [the longest x1 5.99 us: on_device(): lax.all_to_all(to_bucket(unit), 'img', split_axis=0, concat_axis=0, tiled...]
    dot_general x4, matrix products: 13.2 us -> 21.8 us  [one_block(): jnp.einsum('ajf,akf->ajk', picked, rows, preferred_element_type=jnp.float32)]
    dot_general x0 -> x5, matrix products: none -> 8.15 us  [the longest x2 4.12 us: from_bucket(): jnp.einsum('kg,kc->gc', pick.astype(jnp.float32), flat, precision=lax.Pre...]
    all_to_all x1, waiting for transfers between devices: 0.01 us -> 6.39 us  [on_device(): lax.all_to_all(slot_keys, 'img', split_axis=0, concat_axis=0, tiled=True)]
  transfers between devices with their start and end apart: 3 -> 2, of which waited for: 2 -> 2; matrix products, arithmetic and copies ran while one was open for 4% -> 2% of each run, Pallas kernels for 0% -> 0%
where the time goes in v2:
time: 191 us; the launch traced here: 190 us
  blocking collectives  96.3 us (50%)
  matrix products  42 us (22%)
  waiting for transfers between devices  20.3 us (11%)
  between operations  13.6 us (7%)
  other arithmetic  11 us (6%)
  starting transfers between devices  3.59 us (2%)
  local copies, waits for them, and re-layouts  3.41 us (2%)
    all_to_all x2, blocking collectives, on_device(): lax.all_to_all(bucket_major(product), 'img', split_axis=0, concat_axis=0,...  34.4 us
    all_to_all x1, blocking collectives, on_device(): lax.all_to_all(quarter.reshape(img_count, part, unit.shape[1]), 'img', sp...  27.3 us
    all_to_all x2, blocking collectives, on_device(): lax.all_to_all(to_bucket(scaled), 'img', split_axis=0, concat_axis=0, til...  22.7 us
    dot_general x4, matrix products, one_block(): jnp.einsum('ajf,akf->ajk', picked, rows, preferred_element_type=jnp.float32)  21.8 us
    all_gather x1, waiting for transfers between devices, on_device(): lax.all_gather(sent, 'sub', axis=1, tiled=False)  13.9 us
    dot_general x2, matrix products, on_device(): jnp.einsum('ajk,akc->ajc', weights, list_major(arrived), preferred_elemen...  12.1 us
    all_to_all x1, blocking collectives, on_device(): lax.all_to_all(bucket_major(row_sums), 'img', split_axis=0, concat_axis=0...  11.8 us
    all_to_all x1, waiting for transfers between devices, on_device(): lax.all_to_all(slot_keys, 'img', split_axis=0, concat_axis=0, tiled=True)  6.39 us
  transfers between devices with their start and end apart: 2, of which 2 were waited for; matrix products, arithmetic and copies ran while one was open for 2% of the time, Pallas kernels for 0%

profile of v2, /device:TPU:0, one launch (start us, length us, event | category | flops | bytes accessed | tf_op | source)
XLA Modules:
  0.0 190.2 jit_solution(15388162317028311887)
XLA Ops:
  6.5 0.0 copy-start
  6.5 0.0 all-gather.3.cloned.1.call-start
  6.5 0.8 copy.53
  7.4 0.2 eq.34
  7.6 0.5 convert_reduce_fusion.1
  8.1 0.2 reduce_sum.48
  8.3 0.1 copy.54
  8.4 0.7 multiply_add_fusion
  9.1 0.1 iota_add_fusion
  9.2 0.1 add.65
  9.3 1.4 fusion.14
  10.7 1.9 convolution_convert_fusion.2
  12.5 27.3 %all_to_all.35 = bf16[8,64,768]{2,1,0:T(8,128)(2,1)} all-to-all(bf16[8,64,768]{2,1,0:T(8,128)(2,1)S(1)} %bitcast.88), channel_id=1, replica_groups=mesh['img'=8,'sub'=4] {'img'}, dimensions={0} | all-to-all | bytes 1572864 | tf_op jit(solution)/shard_map/all_to_all | solution.py:98
  39.9 0.0 all-gather.3.cloned.1.call-update
  39.9 0.0 copy-done
  39.9 1.0 fusion.36
  41.0 0.9 add_reduce_fusion
  41.9 0.5 broadcast.65
  42.4 0.7 reduce.2
  43.1 0.6 reshape.187
  43.7 3.6 %all-to-all-start = ((bf16[8,2,128]{2,1,0:T(2,128)(2,1)}), bf16[8,2,128]{2,1,0:T(2,128)(2,1)S(1)}, u32[]{:S(2)}, u32[]{:S(2)}) async-start(bf16[8,2,128]{2,1,0:T(2,128)(2,1)} %reshape.187), calls=%async_computation | async-start | bytes 8192 | tf_op jit(solution)/shard_map/all_to_all | solution.py:105
  47.3 6.4 %all-to-all-done = bf16[8,2,128]{2,1,0:T(2,128)(2,1)S(1)} async-done(((bf16[8,2,128]{2,1,0:T(2,128)(2,1)}), bf16[8,2,128]{2,1,0:T(2,128)(2,1)S(1)}, u32[]{:S(2)}, u32[]{:S(2)}) %all-to-all-start) | async-done | bytes 4128 | tf_op jit(solution)/shard_map/all_to_all | solution.py:105
  53.7 13.9 %all-gather.3.cloned.1.call-done = bf16[8,256,768]{2,1,0:T(8,128)(2,1)} async-done(((bf16[8,64,768]{2,1,0:T(8,128)(2,1)}), bf16[8,256,768]{2,1,0:T(8,128)(2,1)}) %all-gather.3.cloned.1.call-update) | async-done | bytes 3145744 | tf_op jit(solution)/shard_map/all_gather | solution.py:102
  67.6 21.8 %while.10 = (s32[]{:T(128)}, bf16[4,1,512,2048]{3,2,1,0:T(8,128)(2,1)}, f32[4,1,512]{2,1,0:T(1,128)S(1)}, f32[1,2048]{1,0:T(1,128)S(1)}, bf16[4,1,512,768]{3,2,1...) while((s32[]{:T(128)}, bf16[4,1,512,2048]{3,2,1,0:T(8,128)(2,1)}, f32[4,1,512]{2,1,0:T(1,128)S(1)}, ...), condition=%wide.region_5.6_spmd, body=%wide.region_4.5_spmd.sunk | while | flops 1619001344 | bytes 6044753 | solution.py:37
  67.6 5.5 %fusion.51 = bf16[4,1,512,2048]{3,2,1,0:T(8,128)(2,1)} fusion(bf16[4,1,512,2048]{3,2,1,0:T(8,128)(2,1)} %get-tuple-element.125, s32[]{:T(128)} %get-tuple-element.124, bf16[1,2048,768]{2,1,0:T(8,128)(2,1)} %get-tuple-element.136, f32[2048]{0:T(1024)S(1)} %bitcast.97, f32[512]{0:T(512)S(1)} %bitcast.93, bf16[4,1,512,768]{3,2,1,0:T(8,128)(2,1)} %bitcast.120), kind=kOutput, calls=%fused_computation.6.clone.1 | convolution fusion | flops 1619001344 | bytes 6040576 | tf_op jit(solution)/shard_map/while/body/eval_jaxpr/ajf,akf->ajk/dot_general | solution.py:34
  73.1 5.4 %fusion.51 = bf16[4,1,512,2048]{3,2,1,0:T(8,128)(2,1)} fusion(bf16[4,1,512,2048]{3,2,1,0:T(8,128)(2,1)} %get-tuple-element.125, s32[]{:T(128)} %get-tuple-element.124, bf16[1,2048,768]{2,1,0:T(8,128)(2,1)} %get-tuple-element.136, f32[2048]{0:T(1024)S(1)} %bitcast.97, f32[512]{0:T(512)S(1)} %bitcast.93, bf16[4,1,512,768]{3,2,1,0:T(8,128)(2,1)} %bitcast.120), kind=kOutput, calls=%fused_computation.6.clone.1 | convolution fusion | flops 1619001344 | bytes 6040576 | tf_op jit(solution)/shard_map/while/body/eval_jaxpr/ajf,akf->ajk/dot_general | solution.py:34
  78.5 5.4 %fusion.51 = bf16[4,1,512,2048]{3,2,1,0:T(8,128)(2,1)} fusion(bf16[4,1,512,2048]{3,2,1,0:T(8,128)(2,1)} %get-tuple-element.125, s32[]{:T(128)} %get-tuple-element.124, bf16[1,2048,768]{2,1,0:T(8,128)(2,1)} %get-tuple-element.136, f32[2048]{0:T(1024)S(1)} %bitcast.97, f32[512]{0:T(512)S(1)} %bitcast.93, bf16[4,1,512,768]{3,2,1,0:T(8,128)(2,1)} %bitcast.120), kind=kOutput, calls=%fused_computation.6.clone.1 | convolution fusion | flops 1619001344 | bytes 6040576 | tf_op jit(solution)/shard_map/while/body/eval_jaxpr/ajf,akf->ajk/dot_general | solution.py:34
  83.9 5.4 %fusion.51 = bf16[4,1,512,2048]{3,2,1,0:T(8,128)(2,1)} fusion(bf16[4,1,512,2048]{3,2,1,0:T(8,128)(2,1)} %get-tuple-element.125, s32[]{:T(128)} %get-tuple-element.124, bf16[1,2048,768]{2,1,0:T(8,128)(2,1)} %get-tuple-element.136, f32[2048]{0:T(1024)S(1)} %bitcast.97, f32[512]{0:T(512)S(1)} %bitcast.93, bf16[4,1,512,768]{3,2,1,0:T(8,128)(2,1)} %bitcast.120), kind=kOutput, calls=%fused_computation.6.clone.1 | convolution fusion | flops 1619001344 | bytes 6040576 | tf_op jit(solution)/shard_map/while/body/eval_jaxpr/ajf,akf->ajk/dot_general | solution.py:34
  89.4 0.0 copy-start.1
  89.4 4.6 %convert_reduce_fusion = f32[4,512]{1,0:T(4,128)S(1)} fusion(bf16[4,1,512,2048]{3,2,1,0:T(8,128)(2,1)} %get-tuple-element.37), kind=kLoop, calls=%fused_computation.11 | loop fusion | flops 8386560 | bytes 8396800 | tf_op jit(solution)/shard_map/reduce_sum | solution.py:109
  94.0 11.8 %all_to_all.36 = f32[8,1,256]{2,1,0:T(1,128)S(1)} all-to-all(f32[8,1,256]{2,1,0:T(1,128)S(1)} %transpose_reshape.2), channel_id=1, replica_groups=mesh['img'=8,'sub'=4] {'img'}, dimensions={0} | all-to-all | bytes 16384 | tf_op jit(solution)/shard_map/all_to_all | solution.py:110
  105.8 1.1 select_reduce_fusion
  106.9 0.0 copy-done.1
  106.9 1.1 convolution_convert_fusion.1
  108.0 0.1 copy.65
  108.1 10.7 %all_to_all.37 = bf16[8,1,256,64]{2,3,1,0:T(8,128)(2,1)S(1)} all-to-all(bf16[8,1,256,64]{2,3,1,0:T(8,128)(2,1)S(1)} %copy.57), channel_id=1, replica_groups=mesh['img'=8,'sub'=4] {'img'}, dimensions={0} | all-to-all | bytes 524288 | tf_op jit(solution)/shard_map/all_to_all | solution.py:119
  118.9 0.1 copy.58
  119.0 0.1 reshape.183
  119.2 6.0 %convolution_bitcast_fusion.1 = f32[8,1,256,64]{2,3,1,0:T(8,128)S(1)} fusion(bf16[8,256,2048]{2,1,0:T(8,128)(2,1)} %bitcast.82, bf16[2048,64,1]{0,1,2:T(8,128)(2,1)S(1)} %reshape.183), kind=kOutput, calls=%fused_computation.28 | convolution fusion | flops 536870912 | bytes 9175040 | tf_op jit(solution)/shard_map/ajk,akc->ajc/dot_general | solution.py:120
  125.2 17.2 %all_to_all.38 = f32[8,1,256,64]{2,3,1,0:T(8,128)S(1)} all-to-all(f32[8,1,256,64]{2,3,1,0:T(8,128)S(1)} %convolution_bitcast_fusion.1), channel_id=1, replica_groups=mesh['img'=8,'sub'=4] {'img'}, dimensions={0} | all-to-all | bytes 1048576 | tf_op jit(solution)/shard_map/all_to_all | solution.py:123
  142.4 1.7 fusion.19
  144.2 1.1 convolution_convert_fusion
  145.2 0.1 copy.67
  145.4 12.0 %all_to_all.39 = bf16[8,1,256,64]{2,3,1,0:T(8,128)(2,1)S(1)} all-to-all(bf16[8,1,256,64]{2,3,1,0:T(8,128)(2,1)S(1)} %copy.61), channel_id=1, replica_groups=mesh['img'=8,'sub'=4] {'img'}, dimensions={0} | all-to-all | bytes 524288 | tf_op jit(solution)/shard_map/all_to_all | solution.py:119
  157.3 0.1 copy.62
  157.5 0.1 reshape.184
  157.6 6.0 %convolution_bitcast_fusion = f32[8,1,256,64]{2,3,1,0:T(8,128)S(1)} fusion(bf16[8,256,2048]{2,1,0:T(8,128)(2,1)} %bitcast.83, bf16[2048,64,1]{0,1,2:T(8,128)(2,1)S(1)} %reshape.184), kind=kOutput, calls=%fused_computation.27 | convolution fusion | flops 536870912 | bytes 9175040 | tf_op jit(solution)/shard_map/ajk,akc->ajc/dot_general | solution.py:120
  163.7 17.3 %all_to_all.40 = f32[8,1,256,64]{2,3,1,0:T(8,128)S(1)} all-to-all(f32[8,1,256,64]{2,3,1,0:T(8,128)S(1)} %convolution_bitcast_fusion), channel_id=1, replica_groups=mesh['img'=8,'sub'=4] {'img'}, dimensions={0} | all-to-all | bytes 1048576 | tf_op jit(solution)/shard_map/all_to_all | solution.py:123
  181.0 2.4 %fusion.20 = bf16[512,64]{0,1:T(8,128)(2,1)} fusion(f32[2048,64]{0,1:T(8,128)S(1)} %bitcast.89, bf16[512,64]{0,1:T(8,128)(2,1)S(1)} %copy-done.1, f32[512]{0:T(512)S(1)} %get-tuple-element.78, s32[512]{0:T(512)S(1)} %bitcast.115, s32[512]{0:T(512)S(1)} %bitcast.107), kind=kOutput, calls=%fused_computation.35 | convolution fusion | flops 808615936 | bytes 661504 | tf_op jit(solution)/shard_map/kg,kc->gc/dot_general | solution.py:71
  (20 shorter events, 0.3 us)
Async XLA Ops:
  6.5 33.4 %copy-start = (s32[512,2]{0,1:T(2,128)S(1)}, s32[512,2]{0,1:T(2,128)}, u32[]{:S(2)}) copy-start(s32[512,2]{0,1:T(2,128)} %param.9) | copy-start | bytes 12292
  6.5 61.1 %all-gather.3.cloned.1.call-start = ((), (), s32[]{:S(2)}) async-start(), calls=%async_computation.7 | async-start | bytes 3932160 | tf_op jit(solution)/shard_map/all_gather | solution.py:102
  43.7 10.0 %all-to-all-start = ((bf16[8,2,128]{2,1,0:T(2,128)(2,1)}), bf16[8,2,128]{2,1,0:T(2,128)(2,1)S(1)}, u32[]{:S(2)}, u32[]{:S(2)}) async-start(bf16[8,2,128]{2,1,0:T(2,128)(2,1)} %reshape.187), calls=%async_computation | async-start | bytes 8192 | tf_op jit(solution)/shard_map/all_to_all | solution.py:105
  89.4 17.5 %copy-start.1 = (bf16[512,64]{0,1:T(8,128)(2,1)S(1)}, bf16[512,64]{0,1:T(8,128)(2,1)}, u32[]{:S(2)}) copy-start(bf16[512,64]{0,1:T(8,128)(2,1)} %param.7) | copy-start | bytes 196612
Sparse Core Ops, SparseCore 0:
  40.0 27.5 all-gather.2

commit v3 on v0

v3 whole, which is shorter than its diff:
```python
import jax
import jax.numpy as jnp
from jax import lax
from jax.sharding import PartitionSpec as P

SLOTS = 2048
BAND = 64
RING_MOST = 16


def affinity(gram, row_keys, col_keys):
    keep = jnp.abs(row_keys[:, :, None] - col_keys[:, None, :]) <= BAND
    positive = jnp.maximum(gram, 0.0)
    return jnp.where(keep, positive * positive * positive, 0.0).astype(jnp.bfloat16)


def blocked_affinity(rows, key_rows):
    lists_here = rows.shape[0]
    slot_count = rows.shape[1]
    block_rows = min(512, slot_count)
    block_count = slot_count // block_rows
    row_blocks = jnp.moveaxis(
        rows.reshape(lists_here, block_count, block_rows, rows.shape[2]), 1, 0
    )
    key_blocks = jnp.moveaxis(key_rows.reshape(lists_here, block_count, block_rows), 1, 0)

    def one_block(packed):
        picked, picked_keys = packed
        gram = jnp.einsum("ajf,akf->ajk", picked, rows, preferred_element_type=jnp.float32)
        return affinity(gram, picked_keys, key_rows)

    blocks = lax.map(one_block, (row_blocks, key_blocks))
    return jnp.moveaxis(blocks, 0, 1).reshape(lists_here, slot_count, slot_count)


def on_device(embeddings, labels, image_lists, rank_keys):
    img_count = lax.axis_size("img")
    sub_count = lax.axis_size("sub")
    per_list = SLOTS // img_count
    part = per_list // sub_count
    width = embeddings.shape[1]
    rows_here = image_lists.shape[0]
    pair_count = rows_here * 2
    me_img = lax.axis_index("img")
    me_sub = lax.axis_index("sub")
    lists_flat = image_lists.reshape(-1)
    order = jnp.arange(pair_count, dtype=jnp.int32)
    same = (lists_flat[:, None] == lists_flat[None, :]) & (order[None, :] < order[:, None])
    within = jnp.sum(same.astype(jnp.int32), axis=1)
    slot_of_pair = (lists_flat * per_list + within).reshape(rows_here, 2)

    def picker(ids):
        ids = ids.reshape(-1, 1)
        return slot_of_pair[None, :, 0] == ids, slot_of_pair[None, :, 1] == ids

    shifts = jnp.arange(img_count, dtype=jnp.int32)
    ring = img_count <= RING_MOST
    dest = (me_img + shifts) % img_count if ring else shifts
    quarters = (me_sub - jnp.arange(sub_count, dtype=jnp.int32)) % sub_count
    within_part = jnp.arange(part, dtype=jnp.int32)
    bucket_ids = (
        dest[:, None, None] * per_list + quarters[None, :, None] * part + within_part[None, None, :]
    )
    hit_a, hit_b = picker(bucket_ids)
    hit = hit_a | hit_b
    pick = hit.astype(jnp.bfloat16)
    pick_f32 = hit.astype(jnp.float32)

    def over_img(blocks, back=False):
        if not ring:
            return lax.all_to_all(blocks, "img", split_axis=0, concat_axis=0, tiled=True)
        out = [blocks[0]]
        for k in range(1, img_count):
            shift = img_count - k if back else k
            pairs = [(i, (i + shift) % img_count) for i in range(img_count)]
            out.append(lax.ppermute(blocks[k], "img", pairs))
        return jnp.stack(out)

    values = embeddings.astype(jnp.float32)
    unit = (values * lax.rsqrt(jnp.sum(values * values, axis=1, keepdims=True) + 1e-06)).astype(
        jnp.bfloat16
    )
    quarter_ids = dest[:, None] * per_list + me_sub * part + within_part[None, :]
    q_a, q_b = picker(quarter_ids)
    q_hit = q_a | q_b
    keys_f = rank_keys.astype(jnp.float32)
    key_sum = jnp.sum(
        jnp.where(q_a, keys_f[None, :, 0], 0.0) + jnp.where(q_b, keys_f[None, :, 1], 0.0), axis=1
    )
    q_keys = jnp.where(jnp.any(q_hit, axis=1), key_sum, -4096.0).astype(jnp.bfloat16)
    quarter = jnp.dot(q_hit.astype(jnp.bfloat16), unit, preferred_element_type=jnp.float32)
    payload = jnp.concatenate(
        [
            quarter.astype(jnp.bfloat16).reshape(img_count, part, width),
            jnp.pad(q_keys.reshape(img_count, 1, part), ((0, 0), (0, 0), (0, width - part))),
        ],
        axis=1,
    )
    got = over_img(payload)
    gathered = [got]
    for m in range(1, sub_count):
        pairs = [(t, (t + m) % sub_count) for t in range(sub_count)]
        gathered.append(lax.ppermute(got, "sub", pairs))
    every = jnp.stack(gathered, axis=1)
    slot_count = img_count * per_list
    rows = every[:, :, :part, :].reshape(1, slot_count, width)
    key_rows = every[:, :, part, :part].reshape(1, slot_count).astype(jnp.float32)
    weights = blocked_affinity(rows, key_rows)
    row_sums = jnp.sum(weights, axis=2, dtype=jnp.float32)
    degree_slots = over_img(row_sums.reshape(img_count, per_list), back=True)
    degree = jnp.sum(jnp.where(hit, degree_slots.reshape(slot_count, 1), 0.0), axis=0)
    inv = lax.rsqrt(degree)
    starting = labels.astype(jnp.float32)
    current = starting
    channels = labels.shape[1]
    for step in range(2):
        scaled = (inv[:, None] * current).astype(jnp.bfloat16)
        bucket = jnp.dot(pick, scaled, preferred_element_type=jnp.float32).astype(jnp.bfloat16)
        arrived = over_img(bucket.reshape(img_count, per_list, channels))
        product = jnp.dot(
            weights[0], arrived.reshape(slot_count, channels), preferred_element_type=jnp.float32
        )
        returned = over_img(product.reshape(img_count, per_list, channels), back=True)
        spread = jnp.einsum(
            "kg,kc->gc", pick_f32, returned.reshape(slot_count, channels),
            precision=lax.Precision.HIGHEST, preferred_element_type=jnp.float32,
        )
        current = 0.8 * inv[:, None] * spread + 0.2 * starting
    return current.astype(jnp.bfloat16)


def solution(mesh):
    return jax.shard_map(
        on_device,
        mesh=mesh,
        in_specs=(P("img", None), P("img", "sub"), P("img", None), P("img", None)),
        out_specs=P("img", "sub"),
        check_vma=False,
    )
```

time: 243 us -> 203 us (0.84)
  starting transfers between devices: 16.9 us -> 74.5 us
  blocking collectives: 56.7 us -> 0 us
  local copies, waits for them, and re-layouts: 56.9 us -> 12.5 us
  matrix products: 25.2 us -> 39.2 us
  waiting for transfers between devices: 76.6 us -> 62.7 us
  other arithmetic: 9.76 us -> 12.8 us
    all_to_all x3 -> x0, waiting for transfers between devices: 76.6 us -> none  [the longest x1 70.1 us: on_device(): lax.all_to_all(to_bucket(unit), 'img', split_axis=0, concat_axis=0, tiled...]
    ppermute x0 -> x45, starting transfers between devices: none -> 74.5 us  [the longest x42 71.5 us: over_img(): out.append(lax.ppermute(blocks[k], 'img', pairs))]
    ppermute x0 -> x45, waiting for transfers between devices: none -> 62.7 us  [the longest x3 33.3 us: on_device(): gathered.append(lax.ppermute(got, 'sub', pairs))]
    all_to_all x4 -> x0, blocking collectives: 56.7 us -> none  [the longest x2 34.1 us: on_device(): lax.all_to_all(bucket_major(product), 'img', split_axis=0, concat_axis=0,...]
    gather x7 -> x0, local copies, waits for them, and re-layouts: 46.6 us -> none  [the longest x3 21.8 us: to_bucket(): padded[image_of_slot].reshape(img_count, LIST_DEV, per_list, rows.shape[1])]
    all_to_all x3 -> x0, starting transfers between devices: 16.9 us -> none  [the longest x1 7.28 us: on_device(): lax.all_to_all(slot_keys, 'img', split_axis=0, concat_axis=0, tiled=True)]
    dot_general x4, matrix products: 13.2 us -> 21.8 us  [one_block(): jnp.einsum('ajf,akf->ajk', picked, rows, preferred_element_type=jnp.float32)]
    dot_general x2 -> x7, matrix products: 12.1 us -> 17.4 us  [the longest x2 8.83 us: on_device(): jnp.dot(weights[0], arrived.reshape(slot_count, channels), preferred_elem...]
  transfers between devices with their start and end apart: 3 -> 45, of which waited for: 2 -> 21; matrix products, arithmetic and copies ran while one was open for 4% -> 1% of each run, Pallas kernels for 0% -> 0%
where the time goes in v3:
time: 203 us; the launch traced here: 202 us
  starting transfers between devices  74.5 us (37%)
  waiting for transfers between devices  62.7 us (31%)
  matrix products  39.2 us (19%)
  other arithmetic  12.8 us (6%)
  local copies, waits for them, and re-layouts  12.5 us (6%)
    ppermute x42, starting transfers between devices, over_img(): out.append(lax.ppermute(blocks[k], 'img', pairs))  71.5 us
    ppermute x3, waiting for transfers between devices, on_device(): gathered.append(lax.ppermute(got, 'sub', pairs))  33.3 us
    ppermute x42, waiting for transfers between devices, over_img(): out.append(lax.ppermute(blocks[k], 'img', pairs))  29.4 us
    dot_general x4, matrix products, one_block(): jnp.einsum('ajf,akf->ajk', picked, rows, preferred_element_type=jnp.float32)  21.8 us
    dot_general x2, matrix products, on_device(): jnp.dot(weights[0], arrived.reshape(slot_count, channels), preferred_elem...  8.83 us
    another operation x13, local copies, waits for them, and re-layouts, over_img(): return jnp.stack(out)  5.28 us
    reduce_sum x1, other arithmetic, on_device(): row_sums = jnp.sum(weights, axis=2, dtype=jnp.float32)  4.58 us
    dot_general x2, matrix products, on_device(): jnp.einsum('kg,kc->gc', pick_f32, returned.reshape(slot_count, channels),...  4.12 us
  transfers between devices with their start and end apart: 45, of which 21 were waited for; matrix products, arithmetic and copies ran while one was open for 1% of the time, Pallas kernels for 0%

profile of v3, /device:TPU:0, one launch (start us, length us, event | category | flops | bytes accessed | tf_op | source)
XLA Modules:
  0.0 202.3 jit_solution(3636892495385973051)
XLA Ops:
  0.0 0.8 copy.227
  4.3 1.4 fusion.14
  5.6 1.9 convolution_convert_fusion.2
  8.0 1.3 fusion.37
  9.4 3.0 %collective-permute-start = (bf16[65,768]{1,0:T(8,128)(2,1)S(1)}, bf16[65,768]{1,0:T(8,128)(2,1)S(1)}, u32[]{:S(2)}, u32[]{:S(2)}) collective-permute-start(bf16[65,768]{1,0:T(8,128)(2,1)S(1)} %bitcast.215), channel_id=1, source_target_pairs={{0,4},{4,8},{8,12},{12,16},{16,20},{20,24},{24,28},{28,0},{1,5},{5... | collective-permute-start | bytes 299528 | tf_op jit(solution)/shard_map/ppermute | solution.py:76
  12.4 1.6 collective-permute-start.1
  14.1 2.6 %collective-permute-start.2 = (bf16[65,768]{1,0:T(8,128)(2,1)S(1)}, bf16[65,768]{1,0:T(8,128)(2,1)S(1)}, u32[]{:S(2)}, u32[]{:S(2)}) collective-permute-start(bf16[65,768]{1,0:T(8,128)(2,1)S(1)} %bitcast.206), channel_id=1, source_target_pairs={{0,12},{4,16},{8,20},{12,24},{16,28},{20,0},{24,4},{28,8},{1,13},{... | collective-permute-start | bytes 299528 | tf_op jit(solution)/shard_map/ppermute | solution.py:76
  16.7 1.3 collective-permute-start.3
  18.0 2.7 %collective-permute-start.4 = (bf16[65,768]{1,0:T(8,128)(2,1)S(1)}, bf16[65,768]{1,0:T(8,128)(2,1)S(1)}, u32[]{:S(2)}, u32[]{:S(2)}) collective-permute-start(bf16[65,768]{1,0:T(8,128)(2,1)S(1)} %bitcast.210), channel_id=1, source_target_pairs={{0,20},{4,24},{8,28},{12,0},{16,4},{20,8},{24,12},{28,16},{1,21},{... | collective-permute-start | bytes 299528 | tf_op jit(solution)/shard_map/ppermute | solution.py:76
  20.7 1.4 collective-permute-start.5
  22.1 1.4 collective-permute-start.6
  23.9 4.3 %collective-permute-done.2 = bf16[65,768]{1,0:T(8,128)(2,1)S(1)} collective-permute-done((bf16[65,768]{1,0:T(8,128)(2,1)S(1)}, bf16[65,768]{1,0:T(8,128)(2,1)S(1)}, u32[]{:S(2)}, u32[]{:S(2)}) %collective-permute-start.2) | collective-permute-done | bytes 99872 | tf_op jit(solution)/shard_map/ppermute | solution.py:76
  29.4 4.1 %stack.166 = bf16[8,65,768]{2,0,1:T(8,128)(2,1)S(1)} concatenate(bf16[1,65,768]{2,0,1:T(2,128)(2,1)S(1)} %get-tuple-element.117, bf16[1,65,768]{2,0,1:T(2,128)(2,1)S(1)} %copy.230, bf16[1,65,768]{2,0,1:T(2,128)(2,1)S(1)} %copy.231, bf16[1,65,768]{2,0,1:T(2,128)(2,1)S(1)} %copy.232, bf16[1,65,768]{2,0,1:T(2,128)(2,1)S(1)} %copy.233, bf16[1,65,768]{2,0,1:T(2,128)(2,1)S(1)} %copy.234, ...), dimensions={0} | concatenate | bytes 1597440 | tf_op jit(solution)/shard_map/stack | solution.py:77
  33.6 1.6 collective-permute-start.8
  35.1 1.4 collective-permute-start.9
  36.5 16.5 %collective-permute-done.7 = bf16[8,65,768]{2,0,1:T(8,128)(2,1)S(1)} collective-permute-done((bf16[8,65,768]{2,0,1:T(8,128)(2,1)S(1)}, bf16[8,65,768]{2,0,1:T(8,128)(2,1)S(1)}, u32[]{:S(2)}, u32[]{:S(2)}) %collective-permute-start.7) | collective-permute-done | bytes 798752 | tf_op jit(solution)/shard_map/ppermute | solution.py:103
  53.1 1.2 collective-permute-done.8
  54.3 15.5 %collective-permute-done.9 = bf16[8,65,768]{2,0,1:T(8,128)(2,1)S(1)} collective-permute-done((bf16[8,65,768]{2,0,1:T(8,128)(2,1)S(1)}, bf16[8,65,768]{2,0,1:T(8,128)(2,1)S(1)}, u32[]{:S(2)}, u32[]{:S(2)}) %collective-permute-start.9) | collective-permute-done | bytes 798752 | tf_op jit(solution)/shard_map/ppermute | solution.py:103
  69.8 0.9 copy-done.6
  70.7 3.2 %pad_maximum_fusion = bf16[8,4,64,768]{3,0,2,1:T(8,128)(2,1)S(1)} fusion(bf16[8,1,65,768]{3,0,2,1:T(8,128)(2,1)} %bitcast.188, bf16[8,1,65,768]{3,0,2,1:T(8,128)(2,1)} %bitcast.186, bf16[8,1,65,768]{3,0,2,1:T(8,128)(2,1)} %bitcast.184, bf16[8,1,65,768]{3,0,2,1:T(8,128)(2,1)} %bitcast.182), kind=kLoop, calls=%fused_computation.17 | loop fusion | flops 4718592 | bytes 6340608 | tf_op jit(solution)/shard_map/stack | solution.py:104
  74.1 2.3 %copy.239 = bf16[8,4,64,768]{3,2,1,0:T(8,128)(2,1)} copy(bf16[8,4,64,768]{3,0,2,1:T(8,128)(2,1)S(1)} %pad_maximum_fusion) | data formatting | bytes 6291456 | tf_op jit(solution)/shard_map/slice | solution.py:106
  76.5 21.9 %while.10 = (s32[]{:T(128)}, bf16[4,1,512,2048]{3,2,1,0:T(8,128)(2,1)}, f32[4,1,512]{2,1,0:T(1,128)S(1)}, f32[1,2048]{1,0:T(1,128)S(1)}, bf16[4,1,512,768]{3,2,1...) while((s32[]{:T(128)}, bf16[4,1,512,2048]{3,2,1,0:T(8,128)(2,1)}, f32[4,1,512]{2,1,0:T(1,128)S(1)}, ...), condition=%wide.region_5.6_spmd, body=%wide.region_4.5_spmd.sunk | while | flops 1619001344 | bytes 6044753 | solution.py:32
  76.5 5.4 %fusion.59 = bf16[4,1,512,2048]{3,2,1,0:T(8,128)(2,1)} fusion(bf16[4,1,512,2048]{3,2,1,0:T(8,128)(2,1)} %get-tuple-element.207, s32[]{:T(128)} %get-tuple-element.206, bf16[1,2048,768]{2,1,0:T(8,128)(2,1)} %get-tuple-element.218, f32[2048]{0:T(1024)S(1)} %bitcast.238, f32[512]{0:T(512)S(1)} %bitcast.217, bf16[4,1,512,768]{3,2,1,0:T(8,128)(2,1)} %bitcast.192), kind=kOutput, calls=%fused_computation.6.clone.1 | convolution fusion | flops 1619001344 | bytes 6040576 | tf_op jit(solution)/shard_map/while/body/eval_jaxpr/ajf,akf->ajk/dot_general | solution.py:29
  81.9 5.4 %fusion.59 = bf16[4,1,512,2048]{3,2,1,0:T(8,128)(2,1)} fusion(bf16[4,1,512,2048]{3,2,1,0:T(8,128)(2,1)} %get-tuple-element.207, s32[]{:T(128)} %get-tuple-element.206, bf16[1,2048,768]{2,1,0:T(8,128)(2,1)} %get-tuple-element.218, f32[2048]{0:T(1024)S(1)} %bitcast.238, f32[512]{0:T(512)S(1)} %bitcast.217, bf16[4,1,512,768]{3,2,1,0:T(8,128)(2,1)} %bitcast.192), kind=kOutput, calls=%fused_computation.6.clone.1 | convolution fusion | flops 1619001344 | bytes 6040576 | tf_op jit(solution)/shard_map/while/body/eval_jaxpr/ajf,akf->ajk/dot_general | solution.py:29
  87.3 5.5 %fusion.59 = bf16[4,1,512,2048]{3,2,1,0:T(8,128)(2,1)} fusion(bf16[4,1,512,2048]{3,2,1,0:T(8,128)(2,1)} %get-tuple-element.207, s32[]{:T(128)} %get-tuple-element.206, bf16[1,2048,768]{2,1,0:T(8,128)(2,1)} %get-tuple-element.218, f32[2048]{0:T(1024)S(1)} %bitcast.238, f32[512]{0:T(512)S(1)} %bitcast.217, bf16[4,1,512,768]{3,2,1,0:T(8,128)(2,1)} %bitcast.192), kind=kOutput, calls=%fused_computation.6.clone.1 | convolution fusion | flops 1619001344 | bytes 6040576 | tf_op jit(solution)/shard_map/while/body/eval_jaxpr/ajf,akf->ajk/dot_general | solution.py:29
  92.8 5.5 %fusion.59 = bf16[4,1,512,2048]{3,2,1,0:T(8,128)(2,1)} fusion(bf16[4,1,512,2048]{3,2,1,0:T(8,128)(2,1)} %get-tuple-element.207, s32[]{:T(128)} %get-tuple-element.206, bf16[1,2048,768]{2,1,0:T(8,128)(2,1)} %get-tuple-element.218, f32[2048]{0:T(1024)S(1)} %bitcast.238, f32[512]{0:T(512)S(1)} %bitcast.217, bf16[4,1,512,768]{3,2,1,0:T(8,128)(2,1)} %bitcast.192), kind=kOutput, calls=%fused_computation.6.clone.1 | convolution fusion | flops 1619001344 | bytes 6040576 | tf_op jit(solution)/shard_map/while/body/eval_jaxpr/ajf,akf->ajk/dot_general | solution.py:29
  98.3 4.6 %convert_reduce_fusion = f32[4,512]{1,0:T(4,128)S(1)} fusion(bf16[4,1,512,2048]{3,2,1,0:T(8,128)(2,1)} %get-tuple-element.37), kind=kLoop, calls=%fused_computation.11 | loop fusion | flops 8386560 | bytes 8396800 | tf_op jit(solution)/shard_map/reduce_sum | solution.py:109
  102.9 9.3 %collective-permute-start.10 = (f32[256]{0:T(256)S(1)}, f32[256]{0:T(256)S(1)}, u32[]{:S(2)}, u32[]{:S(2)}) collective-permute-start(f32[256]{0:T(256)S(1)} %bitcast.253), channel_id=1, source_target_pairs={{0,28},{4,0},{8,4},{12,8},{16,12},{20,16},{24,20},{28,24},{1,29},{... | collective-permute-start | bytes 3080 | tf_op jit(solution)/shard_map/ppermute | solution.py:76
  112.3 0.8 collective-permute-start.11
  113.2 2.2 %collective-permute-start.13 = (f32[256]{0:T(256)S(1)}, f32[256]{0:T(256)S(1)}, u32[]{:S(2)}, u32[]{:S(2)}) collective-permute-start(f32[256]{0:T(256)S(1)} %bitcast.246), channel_id=1, source_target_pairs={{0,16},{4,20},{8,24},{12,28},{16,0},{20,4},{24,8},{28,12},{1,17},{... | collective-permute-start | bytes 3080 | tf_op jit(solution)/shard_map/ppermute | solution.py:76
  116.1 2.4 %collective-permute-start.15 = (f32[256]{0:T(256)S(1)}, f32[256]{0:T(256)S(1)}, u32[]{:S(2)}, u32[]{:S(2)}) collective-permute-start(f32[256]{0:T(256)S(1)} %bitcast.243), channel_id=1, source_target_pairs={{0,8},{4,12},{8,16},{12,20},{16,24},{20,28},{24,0},{28,4},{1,9},{5... | collective-permute-start | bytes 3080 | tf_op jit(solution)/shard_map/ppermute | solution.py:76
  118.9 1.8 collective-permute-done.14
  120.7 1.4 collective-permute-done.15
  122.1 2.6 %collective-permute-done.16 = f32[256]{0:T(256)S(1)} collective-permute-done((f32[256]{0:T(256)S(1)}, f32[256]{0:T(256)S(1)}, u32[]{:S(2)}, u32[]{:S(2)}) %collective-permute-start.16) | collective-permute-done | bytes 1056 | tf_op jit(solution)/shard_map/ppermute | solution.py:76
  125.5 1.3 convolution_convert_fusion.1
  127.0 2.3 %collective-permute-start.19 = (bf16[256,64]{0,1:T(8,128)(2,1)S(1)}, bf16[256,64]{0,1:T(8,128)(2,1)S(1)}, u32[]{:S(2)}, u32[]{:S(2)}) collective-permute-start(bf16[256,64]{0,1:T(8,128)(2,1)S(1)} %get-tuple-element.143), channel_id=1, source_target_pairs={{0,12},{4,16},{8,20},{12,24},{16,28},{20,0},{24,4},{28,8},{1,13},{... | collective-permute-start | bytes 98312 | tf_op jit(solution)/shard_map/ppermute | solution.py:76
  129.3 3.0 %collective-permute-start.20 = (bf16[256,64]{0,1:T(8,128)(2,1)S(1)}, bf16[256,64]{0,1:T(8,128)(2,1)S(1)}, u32[]{:S(2)}, u32[]{:S(2)}) collective-permute-start(bf16[256,64]{0,1:T(8,128)(2,1)S(1)} %get-tuple-element.142), channel_id=1, source_target_pairs={{0,16},{4,20},{8,24},{12,28},{16,0},{20,4},{24,8},{28,12},{1,17},{... | collective-permute-start | bytes 98312 | tf_op jit(solution)/shard_map/ppermute | solution.py:76
  132.2 1.5 collective-permute-done.17
  133.7 1.4 collective-permute-start.22
  135.1 2.3 %collective-permute-start.23 = (bf16[256,64]{0,1:T(8,128)(2,1)S(1)}, bf16[256,64]{0,1:T(8,128)(2,1)S(1)}, u32[]{:S(2)}, u32[]{:S(2)}) collective-permute-start(bf16[256,64]{0,1:T(8,128)(2,1)S(1)} %get-tuple-element.139), channel_id=1, source_target_pairs={{0,28},{4,0},{8,4},{12,8},{16,12},{20,16},{24,20},{28,24},{1,29},{... | collective-permute-start | bytes 98312 | tf_op jit(solution)/shard_map/ppermute | solution.py:76
  137.9 1.1 collective-permute-done.23
  139.1 6.2 %fusion.45 = f32[2048,64]{0,1:T(8,128)S(1)} fusion(bf16[2048,2048]{1,0:T(8,128)(2,1)} %bitcast.178, bf16[2048,64]{0,1:T(8,128)(2,1)S(1)} %bitcast.195), kind=kOutput, calls=%fused_computation.121 | convolution fusion | flops 536870912 | bytes 9175040 | tf_op jit(solution)/shard_map/dot_general | solution.py:120
  145.3 5.1 %collective-permute-start.24 = (f32[256,64]{0,1:T(8,128)S(1)}, f32[256,64]{0,1:T(8,128)S(1)}, u32[]{:S(2)}, u32[]{:S(2)}) collective-permute-start(f32[256,64]{0,1:T(8,128)S(1)} %get-tuple-element.131), channel_id=1, source_target_pairs={{0,28},{4,0},{8,4},{12,8},{16,12},{20,16},{24,20},{28,24},{1,29},{... | collective-permute-start | bytes 196616 | tf_op jit(solution)/shard_map/ppermute | solution.py:76
  150.7 2.7 %collective-permute-start.27 = (f32[256,64]{0,1:T(8,128)S(1)}, f32[256,64]{0,1:T(8,128)S(1)}, u32[]{:S(2)}, u32[]{:S(2)}) collective-permute-start(f32[256,64]{0,1:T(8,128)S(1)} %get-tuple-element.128), channel_id=1, source_target_pairs={{0,16},{4,20},{8,24},{12,28},{16,0},{20,4},{24,8},{28,12},{1,17},{... | collective-permute-start | bytes 196616 | tf_op jit(solution)/shard_map/ppermute | solution.py:76
  153.6 2.9 %collective-permute-start.29 = (f32[256,64]{0,1:T(8,128)S(1)}, f32[256,64]{0,1:T(8,128)S(1)}, u32[]{:S(2)}, u32[]{:S(2)}) collective-permute-start(f32[256,64]{0,1:T(8,128)S(1)} %get-tuple-element.126), channel_id=1, source_target_pairs={{0,8},{4,12},{8,16},{12,20},{16,24},{20,28},{24,0},{28,4},{1,9},{5... | collective-permute-start | bytes 196616 | tf_op jit(solution)/shard_map/ppermute | solution.py:76
  156.9 1.4 collective-permute-done.27
  158.3 2.8 %collective-permute-done.28 = f32[256,64]{0,1:T(8,128)S(1)} collective-permute-done((f32[256,64]{0,1:T(8,128)S(1)}, f32[256,64]{0,1:T(8,128)S(1)}, u32[]{:S(2)}, u32[]{:S(2)}) %collective-permute-start.28) | collective-permute-done | bytes 65568 | tf_op jit(solution)/shard_map/ppermute | solution.py:76
  161.5 2.0 collective-permute-done.30
  163.6 1.7 fusion.19
  165.3 1.3 convolution_convert_fusion
  166.8 2.3 %collective-permute-start.33 = (bf16[256,64]{0,1:T(8,128)(2,1)S(1)}, bf16[256,64]{0,1:T(8,128)(2,1)S(1)}, u32[]{:S(2)}, u32[]{:S(2)}) collective-permute-start(bf16[256,64]{0,1:T(8,128)(2,1)S(1)} %get-tuple-element.136), channel_id=1, source_target_pairs={{0,12},{4,16},{8,20},{12,24},{16,28},{20,0},{24,4},{28,8},{1,13},{... | collective-permute-start | bytes 98312 | tf_op jit(solution)/shard_map/ppermute | solution.py:76
  169.1 3.0 %collective-permute-start.34 = (bf16[256,64]{0,1:T(8,128)(2,1)S(1)}, bf16[256,64]{0,1:T(8,128)(2,1)S(1)}, u32[]{:S(2)}, u32[]{:S(2)}) collective-permute-start(bf16[256,64]{0,1:T(8,128)(2,1)S(1)} %get-tuple-element.135), channel_id=1, source_target_pairs={{0,16},{4,20},{8,24},{12,28},{16,0},{20,4},{24,8},{28,12},{1,17},{... | collective-permute-start | bytes 98312 | tf_op jit(solution)/shard_map/ppermute | solution.py:76
  172.0 1.3 collective-permute-done.31
  173.3 1.6 collective-permute-start.36
  174.9 2.3 %collective-permute-start.37 = (bf16[256,64]{0,1:T(8,128)(2,1)S(1)}, bf16[256,64]{0,1:T(8,128)(2,1)S(1)}, u32[]{:S(2)}, u32[]{:S(2)}) collective-permute-start(bf16[256,64]{0,1:T(8,128)(2,1)S(1)} %get-tuple-element.132), channel_id=1, source_target_pairs={{0,28},{4,0},{8,4},{12,8},{16,12},{20,16},{24,20},{28,24},{1,29},{... | collective-permute-start | bytes 98312 | tf_op jit(solution)/shard_map/ppermute | solution.py:76
  177.9 1.1 collective-permute-done.37
  179.1 2.7 %fusion.46 = f32[2048,64]{0,1:T(8,128)S(1)} fusion(bf16[2048,2048]{1,0:T(8,128)(2,1)S(1)} %bitcast.181, bf16[2048,64]{0,1:T(8,128)(2,1)S(1)} %bitcast.194), kind=kOutput, calls=%fused_computation.122 | convolution fusion | flops 536870912 | bytes 9175040 | tf_op jit(solution)/shard_map/dot_general | solution.py:120
  181.8 5.3 %collective-permute-start.38 = (f32[256,64]{0,1:T(8,128)S(1)}, f32[256,64]{0,1:T(8,128)S(1)}, u32[]{:S(2)}, u32[]{:S(2)}) collective-permute-start(f32[256,64]{0,1:T(8,128)S(1)} %get-tuple-element.124), channel_id=1, source_target_pairs={{0,28},{4,0},{8,4},{12,8},{16,12},{20,16},{24,20},{28,24},{1,29},{... | collective-permute-start | bytes 196616 | tf_op jit(solution)/shard_map/ppermute | solution.py:76
  187.1 2.9 %collective-permute-start.41 = (f32[256,64]{0,1:T(8,128)S(1)}, f32[256,64]{0,1:T(8,128)S(1)}, u32[]{:S(2)}, u32[]{:S(2)}) collective-permute-start(f32[256,64]{0,1:T(8,128)S(1)} %get-tuple-element.121), channel_id=1, source_target_pairs={{0,16},{4,20},{8,24},{12,28},{16,0},{20,4},{24,8},{28,12},{1,17},{... | collective-permute-start | bytes 196616 | tf_op jit(solution)/shard_map/ppermute | solution.py:76
  190.1 2.8 %collective-permute-start.43 = (f32[256,64]{0,1:T(8,128)S(1)}, f32[256,64]{0,1:T(8,128)S(1)}, u32[]{:S(2)}, u32[]{:S(2)}) collective-permute-start(f32[256,64]{0,1:T(8,128)S(1)} %get-tuple-element.119), channel_id=1, source_target_pairs={{0,8},{4,12},{8,16},{12,20},{16,24},{20,28},{24,0},{28,4},{1,9},{5... | collective-permute-start | bytes 196616 | tf_op jit(solution)/shard_map/ppermute | solution.py:76
  193.6 3.0 %collective-permute-done.42 = f32[256,64]{0,1:T(8,128)S(1)} collective-permute-done((f32[256,64]{0,1:T(8,128)S(1)}, f32[256,64]{0,1:T(8,128)S(1)}, u32[]{:S(2)}, u32[]{:S(2)}) %collective-permute-start.42) | collective-permute-done | bytes 65568 | tf_op jit(solution)/shard_map/ppermute | solution.py:76
  196.6 1.6 collective-permute-done.43
  198.2 1.7 collective-permute-done.44
  199.9 2.4 %fusion.20 = bf16[512,64]{0,1:T(8,128)(2,1)} fusion(f32[2048,64]{0,1:T(8,128)S(1)} %bitcast.199, bf16[512,64]{0,1:T(8,128)(2,1)S(1)} %copy-done.8, f32[512]{0:T(512)S(1)} %get-tuple-element.158, s32[512]{0:T(512)S(1)} %bitcast.237, s32[512]{0:T(512)S(1)} %bitcast.229, s32[2048]{0:T(1024)S(1)} %add.147), kind=kOutput, calls=%fused_computation.38 | convolution fusion | flops 808615936 | bytes 669696 | tf_op jit(solution)/shard_map/kg,kc->gc/dot_general | solution.py:124
  (159 shorter events, 11.6 us)
Async XLA Ops:
  9.4 11.4 %collective-permute-start = (bf16[65,768]{1,0:T(8,128)(2,1)S(1)}, bf16[65,768]{1,0:T(8,128)(2,1)S(1)}, u32[]{:S(2)}, u32[]{:S(2)}) collective-permute-start(bf16[65,768]{1,0:T(8,128)(2,1)S(1)} %bitcast.215), channel_id=1, source_target_pairs={{0,4},{4,8},{8,12},{12,16},{16,20},{20,24},{24,28},{28,0},{1,5},{5... | collective-permute-start | bytes 299528 | tf_op jit(solution)/shard_map/ppermute | solution.py:76
  12.4 9.7 %collective-permute-start.1 = (bf16[65,768]{1,0:T(8,128)(2,1)S(1)}, bf16[65,768]{1,0:T(8,128)(2,1)S(1)}, u32[]{:S(2)}, u32[]{:S(2)}) collective-permute-start(bf16[65,768]{1,0:T(8,128)(2,1)S(1)} %bitcast.213), channel_id=1, source_target_pairs={{0,8},{4,12},{8,16},{12,20},{16,24},{20,28},{24,0},{28,4},{1,9},{5... | collective-permute-start | bytes 299528 | tf_op jit(solution)/shard_map/ppermute | solution.py:76
  14.1 14.1 %collective-permute-start.2 = (bf16[65,768]{1,0:T(8,128)(2,1)S(1)}, bf16[65,768]{1,0:T(8,128)(2,1)S(1)}, u32[]{:S(2)}, u32[]{:S(2)}) collective-permute-start(bf16[65,768]{1,0:T(8,128)(2,1)S(1)} %bitcast.206), channel_id=1, source_target_pairs={{0,12},{4,16},{8,20},{12,24},{16,28},{20,0},{24,4},{28,8},{1,13},{... | collective-permute-start | bytes 299528 | tf_op jit(solution)/shard_map/ppermute | solution.py:76
  16.7 12.0 %collective-permute-start.3 = (bf16[65,768]{1,0:T(8,128)(2,1)S(1)}, bf16[65,768]{1,0:T(8,128)(2,1)S(1)}, u32[]{:S(2)}, u32[]{:S(2)}) collective-permute-start(bf16[65,768]{1,0:T(8,128)(2,1)S(1)} %bitcast.208), channel_id=1, source_target_pairs={{0,16},{4,20},{8,24},{12,28},{16,0},{20,4},{24,8},{28,12},{1,17},{... | collective-permute-start | bytes 299528 | tf_op jit(solution)/shard_map/ppermute | solution.py:76
  18.0 10.9 %collective-permute-start.4 = (bf16[65,768]{1,0:T(8,128)(2,1)S(1)}, bf16[65,768]{1,0:T(8,128)(2,1)S(1)}, u32[]{:S(2)}, u32[]{:S(2)}) collective-permute-start(bf16[65,768]{1,0:T(8,128)(2,1)S(1)} %bitcast.210), channel_id=1, source_target_pairs={{0,20},{4,24},{8,28},{12,0},{16,4},{20,8},{24,12},{28,16},{1,21},{... | collective-permute-start | bytes 299528 | tf_op jit(solution)/shard_map/ppermute | solution.py:76
  20.7 8.3 %collective-permute-start.5 = (bf16[65,768]{1,0:T(8,128)(2,1)S(1)}, bf16[65,768]{1,0:T(8,128)(2,1)S(1)}, u32[]{:S(2)}, u32[]{:S(2)}) collective-permute-start(bf16[65,768]{1,0:T(8,128)(2,1)S(1)} %bitcast.212), channel_id=1, source_target_pairs={{0,24},{4,28},{8,0},{12,4},{16,8},{20,12},{24,16},{28,20},{1,25},{... | collective-permute-start | bytes 299528 | tf_op jit(solution)/shard_map/ppermute | solution.py:76
  22.1 7.1 %collective-permute-start.6 = (bf16[65,768]{1,0:T(8,128)(2,1)S(1)}, bf16[65,768]{1,0:T(8,128)(2,1)S(1)}, u32[]{:S(2)}, u32[]{:S(2)}) collective-permute-start(bf16[65,768]{1,0:T(8,128)(2,1)S(1)} %bitcast.204), channel_id=1, source_target_pairs={{0,28},{4,0},{8,4},{12,8},{16,12},{20,16},{24,20},{28,24},{1,29},{... | collective-permute-start | bytes 299528 | tf_op jit(solution)/shard_map/ppermute | solution.py:76
  33.5 36.3 %copy-start = (bf16[8,65,768]{2,0,1:T(8,128)(2,1)}, bf16[8,65,768]{2,0,1:T(8,128)(2,1)S(1)}, u32[]{:S(2)}) copy-start(bf16[8,65,768]{2,0,1:T(8,128)(2,1)S(1)} %stack.166) | copy-start | bytes 2396164
  33.5 19.5 %collective-permute-start.7 = (bf16[8,65,768]{2,0,1:T(8,128)(2,1)S(1)}, bf16[8,65,768]{2,0,1:T(8,128)(2,1)S(1)}, u32[]{:S(2)}, u32[]{:S(2)}) collective-permute-start(bf16[8,65,768]{2,0,1:T(8,128)(2,1)S(1)} %stack.166), channel_id=1, source_target_pairs={{0,1},{1,2},{2,3},{3,0},{4,5},{5,6},{6,7},{7,4},{8,9},{9,10},{10,1... | collective-permute-start | bytes 2396168 | tf_op jit(solution)/shard_map/ppermute | solution.py:103
  33.6 20.7 %collective-permute-start.8 = (bf16[8,65,768]{2,0,1:T(8,128)(2,1)S(1)}, bf16[8,65,768]{2,0,1:T(8,128)(2,1)S(1)}, u32[]{:S(2)}, u32[]{:S(2)}) collective-permute-start(bf16[8,65,768]{2,0,1:T(8,128)(2,1)S(1)} %stack.166), channel_id=1, source_target_pairs={{0,2},{1,3},{2,0},{3,1},{4,6},{5,7},{6,4},{7,5},{8,10},{9,11},{10,... | collective-permute-start | bytes 2396168 | tf_op jit(solution)/shard_map/ppermute | solution.py:103
  35.1 34.7 %collective-permute-start.9 = (bf16[8,65,768]{2,0,1:T(8,128)(2,1)S(1)}, bf16[8,65,768]{2,0,1:T(8,128)(2,1)S(1)}, u32[]{:S(2)}, u32[]{:S(2)}) collective-permute-start(bf16[8,65,768]{2,0,1:T(8,128)(2,1)S(1)} %stack.166), channel_id=1, source_target_pairs={{0,3},{1,0},{2,1},{3,2},{4,7},{5,4},{6,5},{7,6},{8,11},{9,8},{10,9... | collective-permute-start | bytes 2396168 | tf_op jit(solution)/shard_map/ppermute | solution.py:103
  53.1 16.7 %copy-start.2 = (bf16[8,65,768]{2,0,1:T(8,128)(2,1)}, bf16[8,65,768]{2,0,1:T(8,128)(2,1)S(1)}, u32[]{:S(2)}) copy-start(bf16[8,65,768]{2,0,1:T(8,128)(2,1)S(1)} %collective-permute-done.7) | copy-start | bytes 2396164
  54.3 15.5 %copy-start.4 = (bf16[8,65,768]{2,0,1:T(8,128)(2,1)}, bf16[8,65,768]{2,0,1:T(8,128)(2,1)S(1)}, u32[]{:S(2)}) copy-start(bf16[8,65,768]{2,0,1:T(8,128)(2,1)S(1)} %collective-permute-done.8) | copy-start | bytes 2396164
  69.8 0.9 copy-start.6
  70.7 3.2 %copy-start.1 = (bf16[8,65,768]{2,0,1:T(8,128)(2,1)S(1)}, bf16[8,65,768]{2,0,1:T(8,128)(2,1)}, u32[]{:S(2)}) copy-start(bf16[8,65,768]{2,0,1:T(8,128)(2,1)} %copy-done) | copy-start | bytes 2396164
  70.7 3.2 %copy-start.3 = (bf16[8,65,768]{2,0,1:T(8,128)(2,1)S(1)}, bf16[8,65,768]{2,0,1:T(8,128)(2,1)}, u32[]{:S(2)}) copy-start(bf16[8,65,768]{2,0,1:T(8,128)(2,1)} %copy-done.2) | copy-start | bytes 2396164
  70.7 3.2 %copy-start.5 = (bf16[8,65,768]{2,0,1:T(8,128)(2,1)S(1)}, bf16[8,65,768]{2,0,1:T(8,128)(2,1)}, u32[]{:S(2)}) copy-start(bf16[8,65,768]{2,0,1:T(8,128)(2,1)} %copy-done.4) | copy-start | bytes 2396164
  70.7 3.2 %copy-start.7 = (bf16[8,65,768]{2,0,1:T(8,128)(2,1)S(1)}, bf16[8,65,768]{2,0,1:T(8,128)(2,1)}, u32[]{:S(2)}) copy-start(bf16[8,65,768]{2,0,1:T(8,128)(2,1)} %copy-done.6) | copy-start | bytes 2396164
  98.3 27.2 %copy-start.8 = (bf16[512,64]{0,1:T(8,128)(2,1)S(1)}, bf16[512,64]{0,1:T(8,128)(2,1)}, u32[]{:S(2)}) copy-start(bf16[512,64]{0,1:T(8,128)(2,1)} %param.7) | copy-start | bytes 196612
  102.9 13.2 %collective-permute-start.10 = (f32[256]{0:T(256)S(1)}, f32[256]{0:T(256)S(1)}, u32[]{:S(2)}, u32[]{:S(2)}) collective-permute-start(f32[256]{0:T(256)S(1)} %bitcast.253), channel_id=1, source_target_pairs={{0,28},{4,0},{8,4},{12,8},{16,12},{20,16},{24,20},{28,24},{1,29},{... | collective-permute-start | bytes 3080 | tf_op jit(solution)/shard_map/ppermute | solution.py:76
  112.3 6.2 %collective-permute-start.11 = (f32[256]{0:T(256)S(1)}, f32[256]{0:T(256)S(1)}, u32[]{:S(2)}, u32[]{:S(2)}) collective-permute-start(f32[256]{0:T(256)S(1)} %bitcast.251), channel_id=1, source_target_pairs={{0,24},{4,28},{8,0},{12,4},{16,8},{20,12},{24,16},{28,20},{1,25},{... | collective-permute-start | bytes 3080 | tf_op jit(solution)/shard_map/ppermute | solution.py:76
  113.1 5.8 %collective-permute-start.12 = (f32[256]{0:T(256)S(1)}, f32[256]{0:T(256)S(1)}, u32[]{:S(2)}, u32[]{:S(2)}) collective-permute-start(f32[256]{0:T(256)S(1)} %bitcast.248), channel_id=1, source_target_pairs={{0,20},{4,24},{8,28},{12,0},{16,4},{20,8},{24,12},{28,16},{1,21},{... | collective-permute-start | bytes 3080 | tf_op jit(solution)/shard_map/ppermute | solution.py:76
  113.2 5.8 %collective-permute-start.13 = (f32[256]{0:T(256)S(1)}, f32[256]{0:T(256)S(1)}, u32[]{:S(2)}, u32[]{:S(2)}) collective-permute-start(f32[256]{0:T(256)S(1)} %bitcast.246), channel_id=1, source_target_pairs={{0,16},{4,20},{8,24},{12,28},{16,0},{20,4},{24,8},{28,12},{1,17},{... | collective-permute-start | bytes 3080 | tf_op jit(solution)/shard_map/ppermute | solution.py:76
  115.3 5.4 %collective-permute-start.14 = (f32[256]{0:T(256)S(1)}, f32[256]{0:T(256)S(1)}, u32[]{:S(2)}, u32[]{:S(2)}) collective-permute-start(f32[256]{0:T(256)S(1)} %bitcast.245), channel_id=1, source_target_pairs={{0,12},{4,16},{8,20},{12,24},{16,28},{20,0},{24,4},{28,8},{1,13},{... | collective-permute-start | bytes 3080 | tf_op jit(solution)/shard_map/ppermute | solution.py:76
  116.1 6.0 %collective-permute-start.15 = (f32[256]{0:T(256)S(1)}, f32[256]{0:T(256)S(1)}, u32[]{:S(2)}, u32[]{:S(2)}) collective-permute-start(f32[256]{0:T(256)S(1)} %bitcast.243), channel_id=1, source_target_pairs={{0,8},{4,12},{8,16},{12,20},{16,24},{20,28},{24,0},{28,4},{1,9},{5... | collective-permute-start | bytes 3080 | tf_op jit(solution)/shard_map/ppermute | solution.py:76
  118.5 6.3 %collective-permute-start.16 = (f32[256]{0:T(256)S(1)}, f32[256]{0:T(256)S(1)}, u32[]{:S(2)}, u32[]{:S(2)}) collective-permute-start(f32[256]{0:T(256)S(1)} %bitcast.241), channel_id=1, source_target_pairs={{0,4},{4,8},{8,12},{12,16},{16,20},{20,24},{24,28},{28,0},{1,5},{5... | collective-permute-start | bytes 3080 | tf_op jit(solution)/shard_map/ppermute | solution.py:76
  126.8 6.9 %collective-permute-start.17 = (bf16[256,64]{0,1:T(8,128)(2,1)S(1)}, bf16[256,64]{0,1:T(8,128)(2,1)S(1)}, u32[]{:S(2)}, u32[]{:S(2)}) collective-permute-start(bf16[256,64]{0,1:T(8,128)(2,1)S(1)} %get-tuple-element.145), channel_id=1, source_target_pairs={{0,4},{4,8},{8,12},{12,16},{16,20},{20,24},{24,28},{28,0},{1,5},{5... | collective-permute-start | bytes 98312 | tf_op jit(solution)/shard_map/ppermute | solution.py:76
  126.9 8.2 %collective-permute-start.18 = (bf16[256,64]{0,1:T(8,128)(2,1)S(1)}, bf16[256,64]{0,1:T(8,128)(2,1)S(1)}, u32[]{:S(2)}, u32[]{:S(2)}) collective-permute-start(bf16[256,64]{0,1:T(8,128)(2,1)S(1)} %get-tuple-element.144), channel_id=1, source_target_pairs={{0,8},{4,12},{8,16},{12,20},{16,24},{20,28},{24,0},{28,4},{1,9},{5... | collective-permute-start | bytes 98312 | tf_op jit(solution)/shard_map/ppermute | solution.py:76
  127.0 10.5 %collective-permute-start.19 = (bf16[256,64]{0,1:T(8,128)(2,1)S(1)}, bf16[256,64]{0,1:T(8,128)(2,1)S(1)}, u32[]{:S(2)}, u32[]{:S(2)}) collective-permute-start(bf16[256,64]{0,1:T(8,128)(2,1)S(1)} %get-tuple-element.143), channel_id=1, source_target_pairs={{0,12},{4,16},{8,20},{12,24},{16,28},{20,0},{24,4},{28,8},{1,13},{... | collective-permute-start | bytes 98312 | tf_op jit(solution)/shard_map/ppermute | solution.py:76
  129.3 8.2 %collective-permute-start.20 = (bf16[256,64]{0,1:T(8,128)(2,1)S(1)}, bf16[256,64]{0,1:T(8,128)(2,1)S(1)}, u32[]{:S(2)}, u32[]{:S(2)}) collective-permute-start(bf16[256,64]{0,1:T(8,128)(2,1)S(1)} %get-tuple-element.142), channel_id=1, source_target_pairs={{0,16},{4,20},{8,24},{12,28},{16,0},{20,4},{24,8},{28,12},{1,17},{... | collective-permute-start | bytes 98312 | tf_op jit(solution)/shard_map/ppermute | solution.py:76
  132.2 5.2 %collective-permute-start.21 = (bf16[256,64]{0,1:T(8,128)(2,1)S(1)}, bf16[256,64]{0,1:T(8,128)(2,1)S(1)}, u32[]{:S(2)}, u32[]{:S(2)}) collective-permute-start(bf16[256,64]{0,1:T(8,128)(2,1)S(1)} %get-tuple-element.141), channel_id=1, source_target_pairs={{0,20},{4,24},{8,28},{12,0},{16,4},{20,8},{24,12},{28,16},{1,21},{... | collective-permute-start | bytes 98312 | tf_op jit(solution)/shard_map/ppermute | solution.py:76
  133.7 4.2 %collective-permute-start.22 = (bf16[256,64]{0,1:T(8,128)(2,1)S(1)}, bf16[256,64]{0,1:T(8,128)(2,1)S(1)}, u32[]{:S(2)}, u32[]{:S(2)}) collective-permute-start(bf16[256,64]{0,1:T(8,128)(2,1)S(1)} %get-tuple-element.140), channel_id=1, source_target_pairs={{0,24},{4,28},{8,0},{12,4},{16,8},{20,12},{24,16},{28,20},{1,25},{... | collective-permute-start | bytes 98312 | tf_op jit(solution)/shard_map/ppermute | solution.py:76
  135.1 3.9 %collective-permute-start.23 = (bf16[256,64]{0,1:T(8,128)(2,1)S(1)}, bf16[256,64]{0,1:T(8,128)(2,1)S(1)}, u32[]{:S(2)}, u32[]{:S(2)}) collective-permute-start(bf16[256,64]{0,1:T(8,128)(2,1)S(1)} %get-tuple-element.139), channel_id=1, source_target_pairs={{0,28},{4,0},{8,4},{12,8},{16,12},{20,16},{24,20},{28,24},{1,29},{... | collective-permute-start | bytes 98312 | tf_op jit(solution)/shard_map/ppermute | solution.py:76
  139.0 40.0 %slice-start = ((s8[8388608]{0:T(1024)(128)(4,1)}), s8[4194304]{0:T(1024)(128)(4,1)S(1)}, s32[]{:S(2)}) async-start(s8[8388608]{0:T(1024)(128)(4,1)} %bitcast.179), calls=%async_computation | async-start | bytes 8388608
  139.0 40.0 %slice-start.1 = ((s8[8388608]{0:T(1024)(128)(4,1)}), s8[4194304]{0:T(1024)(128)(4,1)S(1)}, s32[]{:S(2)}) async-start(s8[8388608]{0:T(1024)(128)(4,1)} %bitcast.179), calls=%async_computation.1 | async-start | bytes 8388608
  145.3 8.3 %collective-permute-start.24 = (f32[256,64]{0,1:T(8,128)S(1)}, f32[256,64]{0,1:T(8,128)S(1)}, u32[]{:S(2)}, u32[]{:S(2)}) collective-permute-start(f32[256,64]{0,1:T(8,128)S(1)} %get-tuple-element.131), channel_id=1, source_target_pairs={{0,28},{4,0},{8,4},{12,8},{16,12},{20,16},{24,20},{28,24},{1,29},{... | collective-permute-start | bytes 196616 | tf_op jit(solution)/shard_map/ppermute | solution.py:76
  150.4 6.1 %collective-permute-start.25 = (f32[256,64]{0,1:T(8,128)S(1)}, f32[256,64]{0,1:T(8,128)S(1)}, u32[]{:S(2)}, u32[]{:S(2)}) collective-permute-start(f32[256,64]{0,1:T(8,128)S(1)} %get-tuple-element.130), channel_id=1, source_target_pairs={{0,24},{4,28},{8,0},{12,4},{16,8},{20,12},{24,16},{28,20},{1,25},{... | collective-permute-start | bytes 196616 | tf_op jit(solution)/shard_map/ppermute | solution.py:76
  150.4 6.5 %collective-permute-start.26 = (f32[256,64]{0,1:T(8,128)S(1)}, f32[256,64]{0,1:T(8,128)S(1)}, u32[]{:S(2)}, u32[]{:S(2)}) collective-permute-start(f32[256,64]{0,1:T(8,128)S(1)} %get-tuple-element.129), channel_id=1, source_target_pairs={{0,20},{4,24},{8,28},{12,0},{16,4},{20,8},{24,12},{28,16},{1,21},{... | collective-permute-start | bytes 196616 | tf_op jit(solution)/shard_map/ppermute | solution.py:76
  150.7 7.6 %collective-permute-start.27 = (f32[256,64]{0,1:T(8,128)S(1)}, f32[256,64]{0,1:T(8,128)S(1)}, u32[]{:S(2)}, u32[]{:S(2)}) collective-permute-start(f32[256,64]{0,1:T(8,128)S(1)} %get-tuple-element.128), channel_id=1, source_target_pairs={{0,16},{4,20},{8,24},{12,28},{16,0},{20,4},{24,8},{28,12},{1,17},{... | collective-permute-start | bytes 196616 | tf_op jit(solution)/shard_map/ppermute | solution.py:76
  153.4 7.8 %collective-permute-start.28 = (f32[256,64]{0,1:T(8,128)S(1)}, f32[256,64]{0,1:T(8,128)S(1)}, u32[]{:S(2)}, u32[]{:S(2)}) collective-permute-start(f32[256,64]{0,1:T(8,128)S(1)} %get-tuple-element.127), channel_id=1, source_target_pairs={{0,12},{4,16},{8,20},{12,24},{16,28},{20,0},{24,4},{28,8},{1,13},{... | collective-permute-start | bytes 196616 | tf_op jit(solution)/shard_map/ppermute | solution.py:76
  153.6 7.9 %collective-permute-start.29 = (f32[256,64]{0,1:T(8,128)S(1)}, f32[256,64]{0,1:T(8,128)S(1)}, u32[]{:S(2)}, u32[]{:S(2)}) collective-permute-start(f32[256,64]{0,1:T(8,128)S(1)} %get-tuple-element.126), channel_id=1, source_target_pairs={{0,8},{4,12},{8,16},{12,20},{16,24},{20,28},{24,0},{28,4},{1,9},{5... | collective-permute-start | bytes 196616 | tf_op jit(solution)/shard_map/ppermute | solution.py:76
  156.5 7.0 %collective-permute-start.30 = (f32[256,64]{0,1:T(8,128)S(1)}, f32[256,64]{0,1:T(8,128)S(1)}, u32[]{:S(2)}, u32[]{:S(2)}) collective-permute-start(f32[256,64]{0,1:T(8,128)S(1)} %get-tuple-element.125), channel_id=1, source_target_pairs={{0,4},{4,8},{8,12},{12,16},{16,20},{20,24},{24,28},{28,0},{1,5},{5... | collective-permute-start | bytes 196616 | tf_op jit(solution)/shard_map/ppermute | solution.py:76
  166.6 6.7 %collective-permute-start.31 = (bf16[256,64]{0,1:T(8,128)(2,1)S(1)}, bf16[256,64]{0,1:T(8,128)(2,1)S(1)}, u32[]{:S(2)}, u32[]{:S(2)}) collective-permute-start(bf16[256,64]{0,1:T(8,128)(2,1)S(1)} %get-tuple-element.138), channel_id=1, source_target_pairs={{0,4},{4,8},{8,12},{12,16},{16,20},{20,24},{24,28},{28,0},{1,5},{5... | collective-permute-start | bytes 98312 | tf_op jit(solution)/shard_map/ppermute | solution.py:76
  166.7 8.2 %collective-permute-start.32 = (bf16[256,64]{0,1:T(8,128)(2,1)S(1)}, bf16[256,64]{0,1:T(8,128)(2,1)S(1)}, u32[]{:S(2)}, u32[]{:S(2)}) collective-permute-start(bf16[256,64]{0,1:T(8,128)(2,1)S(1)} %get-tuple-element.137), channel_id=1, source_target_pairs={{0,8},{4,12},{8,16},{12,20},{16,24},{20,28},{24,0},{28,4},{1,9},{5... | collective-permute-start | bytes 98312 | tf_op jit(solution)/shard_map/ppermute | solution.py:76
  166.8 10.5 %collective-permute-start.33 = (bf16[256,64]{0,1:T(8,128)(2,1)S(1)}, bf16[256,64]{0,1:T(8,128)(2,1)S(1)}, u32[]{:S(2)}, u32[]{:S(2)}) collective-permute-start(bf16[256,64]{0,1:T(8,128)(2,1)S(1)} %get-tuple-element.136), channel_id=1, source_target_pairs={{0,12},{4,16},{8,20},{12,24},{16,28},{20,0},{24,4},{28,8},{1,13},{... | collective-permute-start | bytes 98312 | tf_op jit(solution)/shard_map/ppermute | solution.py:76
  169.1 8.2 %collective-permute-start.34 = (bf16[256,64]{0,1:T(8,128)(2,1)S(1)}, bf16[256,64]{0,1:T(8,128)(2,1)S(1)}, u32[]{:S(2)}, u32[]{:S(2)}) collective-permute-start(bf16[256,64]{0,1:T(8,128)(2,1)S(1)} %get-tuple-element.135), channel_id=1, source_target_pairs={{0,16},{4,20},{8,24},{12,28},{16,0},{20,4},{24,8},{28,12},{1,17},{... | collective-permute-start | bytes 98312 | tf_op jit(solution)/shard_map/ppermute | solution.py:76
  172.0 5.2 %collective-permute-start.35 = (bf16[256,64]{0,1:T(8,128)(2,1)S(1)}, bf16[256,64]{0,1:T(8,128)(2,1)S(1)}, u32[]{:S(2)}, u32[]{:S(2)}) collective-permute-start(bf16[256,64]{0,1:T(8,128)(2,1)S(1)} %get-tuple-element.134), channel_id=1, source_target_pairs={{0,20},{4,24},{8,28},{12,0},{16,4},{20,8},{24,12},{28,16},{1,21},{... | collective-permute-start | bytes 98312 | tf_op jit(solution)/shard_map/ppermute | solution.py:76
  173.3 4.6 %collective-permute-start.36 = (bf16[256,64]{0,1:T(8,128)(2,1)S(1)}, bf16[256,64]{0,1:T(8,128)(2,1)S(1)}, u32[]{:S(2)}, u32[]{:S(2)}) collective-permute-start(bf16[256,64]{0,1:T(8,128)(2,1)S(1)} %get-tuple-element.133), channel_id=1, source_target_pairs={{0,24},{4,28},{8,0},{12,4},{16,8},{20,12},{24,16},{28,20},{1,25},{... | collective-permute-start | bytes 98312 | tf_op jit(solution)/shard_map/ppermute | solution.py:76
  174.9 4.1 %collective-permute-start.37 = (bf16[256,64]{0,1:T(8,128)(2,1)S(1)}, bf16[256,64]{0,1:T(8,128)(2,1)S(1)}, u32[]{:S(2)}, u32[]{:S(2)}) collective-permute-start(bf16[256,64]{0,1:T(8,128)(2,1)S(1)} %get-tuple-element.132), channel_id=1, source_target_pairs={{0,28},{4,0},{8,4},{12,8},{16,12},{20,16},{24,20},{28,24},{1,29},{... | collective-permute-start | bytes 98312 | tf_op jit(solution)/shard_map/ppermute | solution.py:76
  181.8 8.3 %collective-permute-start.38 = (f32[256,64]{0,1:T(8,128)S(1)}, f32[256,64]{0,1:T(8,128)S(1)}, u32[]{:S(2)}, u32[]{:S(2)}) collective-permute-start(f32[256,64]{0,1:T(8,128)S(1)} %get-tuple-element.124), channel_id=1, source_target_pairs={{0,28},{4,0},{8,4},{12,8},{16,12},{20,16},{24,20},{28,24},{1,29},{... | collective-permute-start | bytes 196616 | tf_op jit(solution)/shard_map/ppermute | solution.py:76
  187.1 5.8 %collective-permute-start.39 = (f32[256,64]{0,1:T(8,128)S(1)}, f32[256,64]{0,1:T(8,128)S(1)}, u32[]{:S(2)}, u32[]{:S(2)}) collective-permute-start(f32[256,64]{0,1:T(8,128)S(1)} %get-tuple-element.123), channel_id=1, source_target_pairs={{0,24},{4,28},{8,0},{12,4},{16,8},{20,12},{24,16},{28,20},{1,25},{... | collective-permute-start | bytes 196616 | tf_op jit(solution)/shard_map/ppermute | solution.py:76
  187.1 6.5 %collective-permute-start.40 = (f32[256,64]{0,1:T(8,128)S(1)}, f32[256,64]{0,1:T(8,128)S(1)}, u32[]{:S(2)}, u32[]{:S(2)}) collective-permute-start(f32[256,64]{0,1:T(8,128)S(1)} %get-tuple-element.122), channel_id=1, source_target_pairs={{0,20},{4,24},{8,28},{12,0},{16,4},{20,8},{24,12},{28,16},{1,21},{... | collective-permute-start | bytes 196616 | tf_op jit(solution)/shard_map/ppermute | solution.py:76
  187.1 6.4 %collective-permute-start.41 = (f32[256,64]{0,1:T(8,128)S(1)}, f32[256,64]{0,1:T(8,128)S(1)}, u32[]{:S(2)}, u32[]{:S(2)}) collective-permute-start(f32[256,64]{0,1:T(8,128)S(1)} %get-tuple-element.121), channel_id=1, source_target_pairs={{0,16},{4,20},{8,24},{12,28},{16,0},{20,4},{24,8},{28,12},{1,17},{... | collective-permute-start | bytes 196616 | tf_op jit(solution)/shard_map/ppermute | solution.py:76
  190.1 6.6 %collective-permute-start.42 = (f32[256,64]{0,1:T(8,128)S(1)}, f32[256,64]{0,1:T(8,128)S(1)}, u32[]{:S(2)}, u32[]{:S(2)}) collective-permute-start(f32[256,64]{0,1:T(8,128)S(1)} %get-tuple-element.120), channel_id=1, source_target_pairs={{0,12},{4,16},{8,20},{12,24},{16,28},{20,0},{24,4},{28,8},{1,13},{... | collective-permute-start | bytes 196616 | tf_op jit(solution)/shard_map/ppermute | solution.py:76
  190.1 8.1 %collective-permute-start.43 = (f32[256,64]{0,1:T(8,128)S(1)}, f32[256,64]{0,1:T(8,128)S(1)}, u32[]{:S(2)}, u32[]{:S(2)}) collective-permute-start(f32[256,64]{0,1:T(8,128)S(1)} %get-tuple-element.119), channel_id=1, source_target_pairs={{0,8},{4,12},{8,16},{12,20},{16,24},{20,28},{24,0},{28,4},{1,9},{5... | collective-permute-start | bytes 196616 | tf_op jit(solution)/shard_map/ppermute | solution.py:76
  192.9 7.0 %collective-permute-start.44 = (f32[256,64]{0,1:T(8,128)S(1)}, f32[256,64]{0,1:T(8,128)S(1)}, u32[]{:S(2)}, u32[]{:S(2)}) collective-permute-start(f32[256,64]{0,1:T(8,128)S(1)} %get-tuple-element.118), channel_id=1, source_target_pairs={{0,4},{4,8},{8,12},{12,16},{16,20},{20,24},{24,28},{28,0},{1,5},{5... | collective-permute-start | bytes 196616 | tf_op jit(solution)/shard_map/ppermute | solution.py:76

commit v4 on v2

--- a/solution.py
+++ b/solution.py
@@ -1,6 +1,8 @@
 import jax
 import jax.numpy as jnp
 from jax import lax
+from jax.experimental import pallas as pl
+from jax.experimental.pallas import tpu as pltpu
 from jax.sharding import PartitionSpec as P
 
 SLOTS = 2048
@@ -8,34 +10,49 @@
 LIST_DEV = 1
 
 
-def affinity(gram, row_keys, col_keys):
-    keep = jnp.abs(row_keys[:, :, None] - col_keys[:, None, :]) <= BAND
-    positive = jnp.maximum(gram, 0.0)
-    return jnp.where(keep, positive * positive * positive, 0.0).astype(jnp.bfloat16)
-
-
 def list_major(bucket):
     moved = jnp.moveaxis(bucket, 1, 0)
     return moved.reshape((moved.shape[0], moved.shape[1] * moved.shape[2]) + moved.shape[3:])
 
 
-def blocked_affinity(rows, key_rows):
-    lists_here = rows.shape[0]
-    slot_count = rows.shape[1]
-    block_rows = min(512, slot_count)
-    block_count = slot_count // block_rows
-    row_blocks = jnp.moveaxis(
-        rows.reshape(lists_here, block_count, block_rows, rows.shape[2]), 1, 0
+def affinity_kernel(row_keys, col_keys, picked, rows, weights, row_sums):
+    gram = lax.dot_general(
+        picked[...], rows[...], (((1,), (1,)), ((), ())), preferred_element_type=jnp.float32
     )
-    key_blocks = jnp.moveaxis(key_rows.reshape(lists_here, block_count, block_rows), 1, 0)
+    keep = jnp.abs(row_keys[...] - col_keys[...]) <= BAND
+    positive = jnp.maximum(gram, 0.0)
+    cubed = jnp.where(keep, positive * positive * positive, 0.0).astype(jnp.bfloat16)
+    weights[...] = cubed
+    row_sums[...] = jnp.sum(cubed.astype(jnp.float32), axis=1, keepdims=True)
 
-    def one_block(packed):
-        picked, picked_keys = packed
-        gram = jnp.einsum("ajf,akf->ajk", picked, rows, preferred_element_type=jnp.float32)
-        return affinity(gram, picked_keys, key_rows)
 
-    blocks = lax.map(one_block, (row_blocks, key_blocks))
-    return jnp.moveaxis(blocks, 0, 1).reshape(lists_here, slot_count, slot_count)
+def fused_affinity(rows, keys):
+    slot_count, width = rows.shape
+    block_rows = min(256, slot_count)
+    return pl.pallas_call(
+        affinity_kernel,
+        grid=(slot_count // block_rows,),
+        in_specs=[
+            pl.BlockSpec((block_rows, 1), lambda i: (i, 0)),
+            pl.BlockSpec((1, slot_count), lambda i: (0, 0)),
+            pl.BlockSpec((block_rows, width), lambda i: (i, 0)),
+            pl.BlockSpec((slot_count, width), lambda i: (0, 0)),
+        ],
+        out_specs=[
+            pl.BlockSpec((block_rows, slot_count), lambda i: (i, 0)),
+            pl.BlockSpec((block_rows, 1), lambda i: (i, 0)),
+        ],
+        out_shape=[
+            jax.ShapeDtypeStruct((slot_count, slot_count), jnp.bfloat16),
+            jax.ShapeDtypeStruct((slot_count, 1), jnp.float32),
+        ],
+        compiler_params=pltpu.CompilerParams(dimension_semantics=("arbitrary",)),
+        cost_estimate=pl.CostEstimate(
+            flops=2 * slot_count * slot_count * width + 6 * slot_count * slot_count,
+            transcendentals=0,
+            bytes_accessed=2 * slot_count * width * 2 + 2 * slot_count * slot_count,
+        ),
+    )(keys.reshape(slot_count, 1), keys.reshape(1, slot_count), rows, rows)
 
 
 def on_device(embeddings, labels, image_lists, rank_keys):
@@ -105,8 +122,10 @@
     got_keys = lax.all_to_all(slot_keys, "img", split_axis=0, concat_axis=0, tiled=True)
     rows = list_major(feats)
     key_rows = list_major(got_keys).astype(jnp.float32)
-    weights = blocked_affinity(rows, key_rows)
-    row_sums = jnp.sum(weights, axis=2, dtype=jnp.float32)
+    lists_here, slot_count = key_rows.shape
+    weight_mat, row_sum_col = fused_affinity(rows.reshape(slot_count, -1), key_rows.reshape(-1))
+    weights = weight_mat.reshape(lists_here, slot_count, slot_count)
+    row_sums = row_sum_col.reshape(lists_here, slot_count)
     degree_slots = lax.all_to_all(
         bucket_major(row_sums), "img", split_axis=0, concat_axis=0, tiled=True
     )

time: 191 us -> 180 us (0.942)
  matrix products: 42 us -> 20.2 us
  Pallas kernels: 0 us -> 13.5 us
  blocking collectives: 96.3 us -> 106 us
  waiting for transfers between devices: 20.3 us -> 13.3 us
  starting transfers between devices: 3.59 us -> 0.01 us
  other arithmetic: 11 us -> 8 us
    dot_general x4 -> x0, matrix products: 21.8 us -> none  [one_block(): jnp.einsum('ajf,akf->ajk', picked, rows, preferred_element_type=jnp.float32)]
    pallas_call x0 -> x1, Pallas kernels: none -> 13.5 us  [fused_affinity(): pl.pallas_call(affinity_kernel, grid=(slot_count // block_rows,), in_spec...]
    all_to_all x0 -> x1, blocking collectives: none -> 9.85 us  [on_device(): lax.all_to_all(slot_keys, 'img', split_axis=0, concat_axis=0, tiled=True)]
    all_to_all x1 -> x0, waiting for transfers between devices: 6.39 us -> none  [on_device(): lax.all_to_all(slot_keys, 'img', split_axis=0, concat_axis=0, tiled=True)]
    reduce_sum x1 -> x0, other arithmetic: 4.58 us -> none  [on_device(): row_sums = jnp.sum(weights, axis=2, dtype=jnp.float32)]
    all_to_all x1 -> x0, starting transfers between devices: 3.59 us -> none  [on_device(): lax.all_to_all(slot_keys, 'img', split_axis=0, concat_axis=0, tiled=True)]
  transfers between devices with their start and end apart: 2 -> 1, of which waited for: 2 -> 1; matrix products, arithmetic and copies ran while one was open for 2% -> 3% of each run, Pallas kernels for 0% -> 0%
where the time goes in v4:
time: 180 us; the launch traced here: 179 us
  blocking collectives  106 us (59%)
  matrix products  20.2 us (11%)
  between operations  13.6 us (8%)
  Pallas kernels  13.5 us (8%)
  waiting for transfers between devices  13.3 us (7%)
  other arithmetic  8 us (4%)
  local copies, waits for them, and re-layouts  4.13 us (2%)
    all_to_all x2, blocking collectives, on_device(): lax.all_to_all(bucket_major(product), 'img', split_axis=0, concat_axis=0,...  34.5 us
    all_to_all x1, blocking collectives, on_device(): lax.all_to_all(quarter.reshape(img_count, part, unit.shape[1]), 'img', sp...  27.3 us
    all_to_all x2, blocking collectives, on_device(): lax.all_to_all(to_bucket(scaled), 'img', split_axis=0, concat_axis=0, til...  22.7 us
    pallas_call x1, Pallas kernels, fused_affinity(): pl.pallas_call(affinity_kernel, grid=(slot_count // block_rows,), in_spec...  13.5 us
    all_gather x1, waiting for transfers between devices, on_device(): lax.all_gather(sent, 'sub', axis=1, tiled=False)  13.2 us
    dot_general x2, matrix products, on_device(): jnp.einsum('ajk,akc->ajc', weights, list_major(arrived), preferred_elemen...  12.1 us
    all_to_all x1, blocking collectives, on_device(): lax.all_to_all(bucket_major(row_sums), 'img', split_axis=0, concat_axis=0...  11.8 us
    all_to_all x1, blocking collectives, on_device(): lax.all_to_all(slot_keys, 'img', split_axis=0, concat_axis=0, tiled=True)  9.85 us
  transfers between devices with their start and end apart: 1, of which 1 were waited for; matrix products, arithmetic and copies ran while one was open for 3% of the time, Pallas kernels for 0%

profile of v4, /device:TPU:0, one launch (start us, length us, event | category | flops | bytes accessed | tf_op | source)
XLA Modules:
  0.0 178.8 jit_solution(12286416780378904161)
XLA Ops:
  6.5 0.0 copy-start.1
  6.5 0.0 all-gather.3.cloned.1.call-start
  6.5 1.4 fusion.2
  7.9 0.1 iota_add_fusion
  8.0 0.1 add.62
  8.1 0.8 copy.58
  8.9 0.2 eq.34
  9.1 0.5 convert_reduce_fusion
  9.6 0.2 reduce_sum.39
  9.8 0.1 copy.59
  9.9 0.7 multiply_add_fusion
  10.6 1.9 %convolution_convert_fusion.2 = bf16[512,768]{1,0:T(8,128)(2,1)S(1)} fusion(bf16[512,768]{1,0:T(8,128)(2,1)} %param.4, f32[512]{0:T(512)S(1)} %add_rsqrt_fusion, s32[512]{0:T(512)S(1)} %bitcast.79, s32[512]{0:T(512)S(1)} %bitcast.71, s32[512]{0:T(512)S(1)} %add.62), kind=kOutput, calls=%fused_computation.14 | convolution fusion | flops 405012480 | bytes 1581056 | tf_op jit(solution)/shard_map/dot_general | solution.py:114
  12.5 27.3 %all_to_all.35 = bf16[8,64,768]{2,1,0:T(8,128)(2,1)} all-to-all(bf16[8,64,768]{2,1,0:T(8,128)(2,1)S(1)} %bitcast.62), channel_id=1, replica_groups=mesh['img'=8,'sub'=4] {'img'}, dimensions={0} | all-to-all | bytes 1572864 | tf_op jit(solution)/shard_map/all_to_all | solution.py:115
  39.9 0.0 all-gather.3.cloned.1.call-update
  39.9 0.0 copy-done.1
  39.9 1.0 fusion.24
  40.9 0.9 add_reduce_fusion
  41.9 0.5 broadcast.51
  42.4 0.7 reduce.1
  43.1 9.8 %all_to_all.36 = bf16[8,2,128]{2,1,0:T(2,128)(2,1)S(1)} all-to-all(bf16[8,2,128]{2,1,0:T(2,128)(2,1)S(1)} %reshape.157), channel_id=1, replica_groups=mesh['img'=8,'sub'=4] {'img'}, dimensions={0} | all-to-all | bytes 8192 | tf_op jit(solution)/shard_map/all_to_all | solution.py:122
  53.0 0.0 copy-start
  53.0 1.3 copy.61.row_keys
  54.3 13.2 %all-gather.3.cloned.1.call-done = bf16[8,256,768]{2,1,0:T(8,128)(2,1)} async-done(((bf16[8,64,768]{2,1,0:T(8,128)(2,1)}), bf16[8,256,768]{2,1,0:T(8,128)(2,1)}) %all-gather.3.cloned.1.call-update) | async-done | bytes 3145744 | tf_op jit(solution)/shard_map/all_gather | solution.py:119
  67.6 0.0 copy-done
  67.6 0.0 copy-start.2
  67.6 13.5 %shard_map.46 = (bf16[2048,2048]{1,0:T(8,128)(2,1)}, f32[2048,1]{1,0:T(8,128)}) custom-call(f32[2048,1]{1,0:T(8,128)} %copy.61.row_keys, f32[1,2048]{1,0:T(1,128)} %bitcast.68, bf16[2048,768]{1,0:T(8,128)(2,1)} %bitcast.89, bf16[2048,768]{1,0:T(8,128)(2,1)} %bitcast.90), custom_call_target="tpu_custom_call" | custom-call | flops 6467616768 | bytes 14680064 | tf_op jit(solution)/shard_map/pallas_call | solution.py:32
  81.1 1.6 reduce
  82.6 11.8 %all_to_all.37 = f32[8,1,256]{2,1,0:T(1,128)S(1)} all-to-all(f32[8,1,256]{2,1,0:T(1,128)S(1)} %bitcast.69), channel_id=1, replica_groups=mesh['img'=8,'sub'=4] {'img'}, dimensions={0} | all-to-all | bytes 16384 | tf_op jit(solution)/shard_map/all_to_all | solution.py:129
  94.5 1.1 select_reduce_fusion
  95.6 0.0 copy-done.2
  95.6 1.1 convolution_convert_fusion.1
  96.7 0.1 copy.71
  96.8 10.7 %all_to_all.38 = bf16[8,1,256,64]{2,3,1,0:T(8,128)(2,1)S(1)} all-to-all(bf16[8,1,256,64]{2,3,1,0:T(8,128)(2,1)S(1)} %copy.63), channel_id=1, replica_groups=mesh['img'=8,'sub'=4] {'img'}, dimensions={0} | all-to-all | bytes 524288 | tf_op jit(solution)/shard_map/all_to_all | solution.py:138
  107.5 0.1 copy.64
  107.7 0.1 reshape.152
  107.8 6.0 %convolution_bitcast_fusion.1 = f32[8,1,256,64]{2,3,1,0:T(8,128)S(1)} fusion(bf16[8,256,2048]{2,1,0:T(8,128)(2,1)} %bitcast.56, bf16[2048,64,1]{0,1,2:T(8,128)(2,1)S(1)} %reshape.152), kind=kOutput, calls=%fused_computation.16 | convolution fusion | flops 536870912 | bytes 9175040 | tf_op jit(solution)/shard_map/ajk,akc->ajc/dot_general | solution.py:139
  113.8 17.2 %all_to_all.39 = f32[8,1,256,64]{2,3,1,0:T(8,128)S(1)} all-to-all(f32[8,1,256,64]{2,3,1,0:T(8,128)S(1)} %convolution_bitcast_fusion.1), channel_id=1, replica_groups=mesh['img'=8,'sub'=4] {'img'}, dimensions={0} | all-to-all | bytes 1048576 | tf_op jit(solution)/shard_map/all_to_all | solution.py:142
  131.1 1.7 fusion.7
  132.8 1.1 convolution_convert_fusion
  133.9 0.1 copy.73
  134.0 12.0 %all_to_all.40 = bf16[8,1,256,64]{2,3,1,0:T(8,128)(2,1)S(1)} all-to-all(bf16[8,1,256,64]{2,3,1,0:T(8,128)(2,1)S(1)} %copy.67), channel_id=1, replica_groups=mesh['img'=8,'sub'=4] {'img'}, dimensions={0} | all-to-all | bytes 524288 | tf_op jit(solution)/shard_map/all_to_all | solution.py:138
  146.0 0.1 copy.68
  146.1 0.1 reshape.153
  146.2 6.0 %convolution_bitcast_fusion = f32[8,1,256,64]{2,3,1,0:T(8,128)S(1)} fusion(bf16[8,256,2048]{2,1,0:T(8,128)(2,1)} %bitcast.57, bf16[2048,64,1]{0,1,2:T(8,128)(2,1)S(1)} %reshape.153), kind=kOutput, calls=%fused_computation.15 | convolution fusion | flops 536870912 | bytes 9175040 | tf_op jit(solution)/shard_map/ajk,akc->ajc/dot_general | solution.py:139
  152.3 17.3 %all_to_all.41 = f32[8,1,256,64]{2,3,1,0:T(8,128)S(1)} all-to-all(f32[8,1,256,64]{2,3,1,0:T(8,128)S(1)} %convolution_bitcast_fusion), channel_id=1, replica_groups=mesh['img'=8,'sub'=4] {'img'}, dimensions={0} | all-to-all | bytes 1048576 | tf_op jit(solution)/shard_map/all_to_all | solution.py:142
  169.6 2.4 %fusion.8 = bf16[512,64]{0,1:T(8,128)(2,1)} fusion(f32[2048,64]{0,1:T(8,128)S(1)} %bitcast.63, bf16[512,64]{0,1:T(8,128)(2,1)S(1)} %copy-done.2, f32[512]{0:T(512)S(1)} %get-tuple-element.13, s32[512]{0:T(512)S(1)} %bitcast.86, s32[512]{0:T(512)S(1)} %bitcast.78), kind=kOutput, calls=%fused_computation.23 | convolution fusion | flops 808615936 | bytes 661504 | tf_op jit(solution)/shard_map/kg,kc->gc/dot_general | solution.py:88
  (15 shorter events, 0.3 us)
Async XLA Ops:
  6.5 33.3 %copy-start.1 = (s32[512,2]{0,1:T(2,128)S(1)}, s32[512,2]{0,1:T(2,128)}, u32[]{:S(2)}) copy-start(s32[512,2]{0,1:T(2,128)} %param.7) | copy-start | bytes 12292
  6.5 61.0 %all-gather.3.cloned.1.call-start = ((), (), s32[]{:S(2)}) async-start(), calls=%async_computation.7 | async-start | bytes 3932160 | tf_op jit(solution)/shard_map/all_gather | solution.py:119
  53.0 14.6 %copy-start = (f32[8,1,256]{2,1,0:T(1,128)}, f32[8,1,256]{2,1,0:T(1,128)S(1)}, u32[]{:S(2)}) copy-start(f32[8,1,256]{2,1,0:T(1,128)S(1)} %convert_element_type.76) | copy-start | bytes 24580
  67.6 28.0 %copy-start.2 = (bf16[512,64]{0,1:T(8,128)(2,1)S(1)}, bf16[512,64]{0,1:T(8,128)(2,1)}, u32[]{:S(2)}) copy-start(bf16[512,64]{0,1:T(8,128)(2,1)} %param.5) | copy-start | bytes 196612
Sparse Core Ops, SparseCore 0:
  40.0 27.5 all-gather.2

commit v5 on v4

--- a/solution.py
+++ b/solution.py
@@ -69,7 +69,13 @@
     slot_of_pair = (lists_flat * per_list + within).reshape(rows_here, 2)
     slot_total = LIST_DEV * img_count * per_list
 
-    slot_ids = jnp.arange(slot_total, dtype=jnp.int32)[:, None]
+    me_sub = lax.axis_index("sub")
+    quarters = (me_sub - jnp.arange(sub_count, dtype=jnp.int32)) % sub_count
+    slot_ids = (
+        jnp.arange(img_count, dtype=jnp.int32)[:, None, None] * per_list
+        + quarters[None, :, None] * part
+        + jnp.arange(part, dtype=jnp.int32)[None, None, :]
+    ).reshape(-1, 1)
     hit_a = slot_of_pair[None, :, 0] == slot_ids
     hit_b = slot_of_pair[None, :, 1] == slot_ids
     hit = hit_a | hit_b
@@ -94,34 +100,37 @@
     unit = (values * lax.rsqrt(jnp.sum(values * values, axis=1, keepdims=True) + 1e-06)).astype(
         jnp.bfloat16
     )
-    keys_f = rank_keys.astype(jnp.float32)
-    key_sum = jnp.sum(
-        jnp.where(hit_a, keys_f[None, :, 0], 0.0) + jnp.where(hit_b, keys_f[None, :, 1], 0.0),
-        axis=1,
-    )
-    key_of_slot = jnp.where(jnp.any(hit, axis=1), key_sum, -4096.0)
-    slot_keys = key_of_slot.astype(jnp.bfloat16).reshape(img_count, LIST_DEV, per_list)
-
-    me_sub = lax.axis_index("sub")
     mine = (
         jnp.arange(img_count, dtype=jnp.int32)[:, None] * per_list
         + me_sub * part
         + jnp.arange(part, dtype=jnp.int32)[None, :]
     ).reshape(-1, 1)
-    pick_mine = (
-        (slot_of_pair[None, :, 0] == mine) | (slot_of_pair[None, :, 1] == mine)
-    ).astype(jnp.bfloat16)
-    quarter = jnp.dot(pick_mine, unit, preferred_element_type=jnp.float32).astype(jnp.bfloat16)
-    sent = lax.all_to_all(
-        quarter.reshape(img_count, part, unit.shape[1]), "img", split_axis=0, concat_axis=0,
-        tiled=True,
+    mine_a = slot_of_pair[None, :, 0] == mine
+    mine_b = slot_of_pair[None, :, 1] == mine
+    mine_hit = mine_a | mine_b
+    keys_f = rank_keys.astype(jnp.float32)
+    key_sum = jnp.sum(
+        jnp.where(mine_a, keys_f[None, :, 0], 0.0) + jnp.where(mine_b, keys_f[None, :, 1], 0.0),
+        axis=1,
     )
-    feats = lax.all_gather(sent, "sub", axis=1, tiled=False).reshape(
-        img_count, LIST_DEV, per_list, unit.shape[1]
+    mine_keys = jnp.where(jnp.any(mine_hit, axis=1), key_sum, -4096.0).astype(jnp.bfloat16)
+    width = unit.shape[1]
+    quarter = jnp.dot(mine_hit.astype(jnp.bfloat16), unit, preferred_element_type=jnp.float32)
+    payload = jnp.concatenate(
+        [
+            quarter.astype(jnp.bfloat16).reshape(img_count, part, width),
+            jnp.pad(mine_keys.reshape(img_count, 1, part), ((0, 0), (0, 0), (0, width - part))),
+        ],
+        axis=1,
     )
-    got_keys = lax.all_to_all(slot_keys, "img", split_axis=0, concat_axis=0, tiled=True)
-    rows = list_major(feats)
-    key_rows = list_major(got_keys).astype(jnp.float32)
+    got = lax.all_to_all(payload, "img", split_axis=0, concat_axis=0, tiled=True)
+    gathered = [got]
+    for m in range(1, sub_count):
+        pairs = [(t, (t + m) % sub_count) for t in range(sub_count)]
+        gathered.append(lax.ppermute(got, "sub", pairs))
+    every = jnp.stack(gathered, axis=1)
+    rows = every[:, :, :part, :].reshape(1, slot_total, width)
+    key_rows = every[:, :, part, :part].reshape(1, slot_total).astype(jnp.float32)
     lists_here, slot_count = key_rows.shape
     weight_mat, row_sum_col = fused_affinity(rows.reshape(slot_count, -1), key_rows.reshape(-1))
     weights = weight_mat.reshape(lists_here, slot_count, slot_count)

time: 180 us -> 186 us (1.033)
  waiting for transfers between devices: 13.3 us -> 39.3 us
  blocking collectives: 106 us -> 88.1 us
  between operations: 13.6 us -> 0.22 us
  starting transfers between devices: 0.01 us -> 6.33 us
  local copies, waits for them, and re-layouts: 4.13 us -> 7.8 us
    ppermute x0 -> x3, waiting for transfers between devices: none -> 33 us  [on_device(): gathered.append(lax.ppermute(got, 'sub', pairs))]
    all_to_all x3 -> x1, blocking collectives: 49 us -> 29.8 us  [on_device(): lax.all_to_all(payload, 'img', split_axis=0, concat_axis=0, tiled=True)]
    all_gather x1 -> x0, waiting for transfers between devices: 13.2 us -> none  [on_device(): lax.all_gather(sent, 'sub', axis=1, tiled=False)]
    all_to_all x0 -> x1, waiting for transfers between devices: none -> 6.3 us  [on_device(): lax.all_to_all(bucket_major(row_sums), 'img', split_axis=0, concat_axis=0...]
    all_to_all x0 -> x1, starting transfers between devices: none -> 3.33 us  [on_device(): lax.all_to_all(bucket_major(row_sums), 'img', split_axis=0, concat_axis=0...]
    ppermute x0 -> x3, starting transfers between devices: none -> 3 us  [on_device(): gathered.append(lax.ppermute(got, 'sub', pairs))]
    slice x0 -> x1, local copies, waits for them, and re-layouts: none -> 2.45 us  [on_device(): rows = every[:, :, :part, :].reshape(1, slot_total, width)]
  transfers between devices with their start and end apart: 1 -> 4, of which waited for: 1 -> 4; matrix products, arithmetic and copies ran while one was open for 3% -> 0% of each run, Pallas kernels for 0% -> 0%
where the time goes in v5:
time: 186 us; the launch traced here: 185 us
  blocking collectives  88.1 us (47%)
  waiting for transfers between devices  39.3 us (21%)
  matrix products  20.6 us (11%)
  Pallas kernels  13.5 us (7%)
  other arithmetic  8.97 us (5%)
  local copies, waits for them, and re-layouts  7.8 us (4%)
  starting transfers between devices  6.33 us (3%)
    all_to_all x2, blocking collectives, on_device(): lax.all_to_all(bucket_major(product), 'img', split_axis=0, concat_axis=0,...  34.8 us
    ppermute x3, waiting for transfers between devices, on_device(): gathered.append(lax.ppermute(got, 'sub', pairs))  33 us
    all_to_all x1, blocking collectives, on_device(): lax.all_to_all(payload, 'img', split_axis=0, concat_axis=0, tiled=True)  29.8 us
    all_to_all x2, blocking collectives, on_device(): lax.all_to_all(to_bucket(scaled), 'img', split_axis=0, concat_axis=0, til...  23.4 us
    pallas_call x1, Pallas kernels, fused_affinity(): pl.pallas_call(affinity_kernel, grid=(slot_count // block_rows,), in_spec...  13.5 us
    dot_general x2, matrix products, on_device(): jnp.einsum('ajk,akc->ajc', weights, list_major(arrived), preferred_elemen...  12.1 us
    all_to_all x1, waiting for transfers between devices, on_device(): lax.all_to_all(bucket_major(row_sums), 'img', split_axis=0, concat_axis=0...  6.3 us
    dot_general x2, matrix products, from_bucket(): jnp.einsum('kg,kc->gc', pick.astype(jnp.float32), flat, precision=lax.Pre...  4.12 us
  transfers between devices with their start and end apart: 4, of which 4 were waited for; matrix products, arithmetic and copies ran while one was open for 0% of the time, Pallas kernels for 0%

profile of v5, /device:TPU:0, one launch (start us, length us, event | category | flops | bytes accessed | tf_op | source)
XLA Modules:
  0.0 184.8 jit_solution(14047213625342935938)
XLA Ops:
  0.0 0.8 copy.71
  0.8 0.2 eq.34
  1.0 0.5 convert_reduce_fusion
  1.5 0.2 reduce_sum.39
  1.7 0.1 copy.72
  1.9 0.7 multiply_add_fusion
  2.6 0.1 iota_add_fusion.1
  2.6 0.1 add.119
  2.7 0.7 convert_element_type.65
  3.4 0.4 fusion.12
  3.8 0.3 fusion.10
  4.2 0.1 convert_element_type.80
  4.2 1.4 fusion.2
  5.6 1.9 %convolution_convert_fusion.2 = bf16[512,768]{1,0:T(8,128)(2,1)S(1)} fusion(bf16[512,768]{1,0:T(8,128)(2,1)} %param.4, f32[512]{0:T(512)S(1)} %add_rsqrt_fusion, s32[512]{0:T(512)S(1)} %bitcast.96, s32[512]{0:T(512)S(1)} %bitcast.88, s32[512]{0:T(512)S(1)} %add.119), kind=kOutput, calls=%fused_computation.16 | convolution fusion | flops 405012480 | bytes 1581056 | tf_op jit(solution)/shard_map/dot_general | solution.py:118
  7.5 0.1 fusion.11
  7.6 29.8 %all_to_all.30 = bf16[8,65,768]{2,1,0:T(8,128)(2,1)S(1)} all-to-all(bf16[8,65,768]{2,1,0:T(8,128)(2,1)S(1)} %fusion.11), channel_id=1, replica_groups=mesh['img'=8,'sub'=4] {'img'}, dimensions={0} | all-to-all | bytes 1597440 | tf_op jit(solution)/shard_map/all_to_all | solution.py:126
  37.4 0.1 copy.74
  37.6 0.1 collective-permute-start
  37.6 1.6 collective-permute-start.1
  39.2 1.4 collective-permute-start.2
  40.6 0.1 broadcast_add_fusion
  40.7 0.1 copy.99
  40.8 16.3 %collective-permute-done = bf16[8,65,768]{2,0,1:T(8,128)(2,1)S(1)} collective-permute-done((bf16[8,65,768]{2,0,1:T(8,128)(2,1)S(1)}, bf16[8,65,768]{2,0,1:T(8,128)(2,1)S(1)}, u32[]{:S(2)}, u32[]{:S(2)}) %collective-permute-start) | collective-permute-done | bytes 798752 | tf_op jit(solution)/shard_map/ppermute | solution.py:130
  57.1 1.2 collective-permute-done.1
  58.3 15.5 %collective-permute-done.2 = bf16[8,65,768]{2,0,1:T(8,128)(2,1)S(1)} collective-permute-done((bf16[8,65,768]{2,0,1:T(8,128)(2,1)S(1)}, bf16[8,65,768]{2,0,1:T(8,128)(2,1)S(1)}, u32[]{:S(2)}, u32[]{:S(2)}) %collective-permute-start.2) | collective-permute-done | bytes 798752 | tf_op jit(solution)/shard_map/ppermute | solution.py:130
  73.8 1.8 pad_maximum_fusion
  75.6 2.0 %reshape.221.row_keys = f32[2048,1]{1,0:T(8,128)} reshape(f32[8,4,1,64]{3,1,0,2:T(4,128)S(1)} %copy.78) | data formatting | bytes 16384 | tf_op jit(solution)/shard_map/convert_element_type | solution.py:133
  77.6 0.7 reshape.218.col_keys
  78.3 2.4 %copy.80 = bf16[8,4,64,768]{3,2,1,0:T(8,128)(2,1)} copy(bf16[8,4,64,768]{3,0,2,1:T(8,128)(2,1)S(1)} %pad_maximum_fusion) | data formatting | bytes 6291456 | tf_op jit(solution)/shard_map/slice | solution.py:132
  80.8 0.0 copy-start
  80.8 13.5 %shard_map.46 = (bf16[2048,2048]{1,0:T(8,128)(2,1)}, f32[2048,1]{1,0:T(8,128)}) custom-call(f32[2048,1]{1,0:T(8,128)} %reshape.221.row_keys, f32[1,2048]{1,0:T(1,128)} %reshape.218.col_keys, bf16[2048,768]{1,0:T(8,128)(2,1)} %bitcast.74, bf16[2048,768]{1,0:T(8,128)(2,1)} %bitcast.75), custom_call_target="tpu_custom_call" | custom-call | flops 6467616768 | bytes 14680064 | tf_op jit(solution)/shard_map/pallas_call | solution.py:32
  94.2 2.2 %reduce = f32[2048]{0:T(1024)} reduce(f32[2048,1]{1,0:T(8,128)} %get-tuple-element.7, f32[]{:T(128)} %constant.43), dimensions={1}, to_apply=%get-tuple-element.7.reduce_sub_computation | reduce | bytes 16388 | tf_op jit(solution)/shard_map/pallas_call | solution.py:32
  96.4 3.3 %all-to-all-start.1 = ((f32[8,1,256]{2,1,0:T(1,128)}), f32[8,1,256]{2,1,0:T(1,128)S(1)}, u32[]{:S(2)}, u32[]{:S(2)}) async-start(f32[8,1,256]{2,1,0:T(1,128)} %bitcast.18), calls=%async_computation.1 | async-start | bytes 16384 | tf_op jit(solution)/shard_map/all_to_all | solution.py:138
  99.7 0.1 iota_add_fusion
  99.8 0.1 add.113
  99.9 6.3 %all-to-all-done.1 = f32[8,1,256]{2,1,0:T(1,128)S(1)} async-done(((f32[8,1,256]{2,1,0:T(1,128)}), f32[8,1,256]{2,1,0:T(1,128)S(1)}, u32[]{:S(2)}, u32[]{:S(2)}) %all-to-all-start.1) | async-done | bytes 8224 | tf_op jit(solution)/shard_map/all_to_all | solution.py:138
  106.2 0.7 select_reduce_fusion
  106.9 0.0 copy-done
  106.9 1.3 convolution_convert_fusion.1
  108.2 0.1 copy.92
  108.3 11.4 %all_to_all.31 = bf16[8,1,256,64]{2,3,1,0:T(8,128)(2,1)S(1)} all-to-all(bf16[8,1,256,64]{2,3,1,0:T(8,128)(2,1)S(1)} %copy.83), channel_id=1, replica_groups=mesh['img'=8,'sub'=4] {'img'}, dimensions={0} | all-to-all | bytes 524288 | tf_op jit(solution)/shard_map/all_to_all | solution.py:147
  119.8 0.1 copy.84
  119.9 0.1 reshape.219
  120.0 6.0 %convolution_bitcast_fusion.1 = f32[8,1,256,64]{2,3,1,0:T(8,128)S(1)} fusion(bf16[8,256,2048]{2,1,0:T(8,128)(2,1)} %bitcast.64, bf16[2048,64,1]{0,1,2:T(8,128)(2,1)S(1)} %reshape.219), kind=kOutput, calls=%fused_computation.21 | convolution fusion | flops 536870912 | bytes 9175040 | tf_op jit(solution)/shard_map/ajk,akc->ajc/dot_general | solution.py:148
  126.1 17.5 %all_to_all.32 = f32[8,1,256,64]{2,3,1,0:T(8,128)S(1)} all-to-all(f32[8,1,256,64]{2,3,1,0:T(8,128)S(1)} %convolution_bitcast_fusion.1), channel_id=1, replica_groups=mesh['img'=8,'sub'=4] {'img'}, dimensions={0} | all-to-all | bytes 1048576 | tf_op jit(solution)/shard_map/all_to_all | solution.py:151
  143.7 1.7 fusion.7
  145.4 1.3 convolution_convert_fusion
  146.7 0.1 copy.94
  146.8 12.0 %all_to_all.33 = bf16[8,1,256,64]{2,3,1,0:T(8,128)(2,1)S(1)} all-to-all(bf16[8,1,256,64]{2,3,1,0:T(8,128)(2,1)S(1)} %copy.87), channel_id=1, replica_groups=mesh['img'=8,'sub'=4] {'img'}, dimensions={0} | all-to-all | bytes 524288 | tf_op jit(solution)/shard_map/all_to_all | solution.py:147
  158.8 0.1 copy.88
  158.9 0.1 reshape.220
  159.1 6.0 %convolution_bitcast_fusion = f32[8,1,256,64]{2,3,1,0:T(8,128)S(1)} fusion(bf16[8,256,2048]{2,1,0:T(8,128)(2,1)} %bitcast.65, bf16[2048,64,1]{0,1,2:T(8,128)(2,1)S(1)} %reshape.220), kind=kOutput, calls=%fused_computation.20 | convolution fusion | flops 536870912 | bytes 9175040 | tf_op jit(solution)/shard_map/ajk,akc->ajc/dot_general | solution.py:148
  165.1 17.3 %all_to_all.34 = f32[8,1,256,64]{2,3,1,0:T(8,128)S(1)} all-to-all(f32[8,1,256,64]{2,3,1,0:T(8,128)S(1)} %convolution_bitcast_fusion), channel_id=1, replica_groups=mesh['img'=8,'sub'=4] {'img'}, dimensions={0} | all-to-all | bytes 1048576 | tf_op jit(solution)/shard_map/all_to_all | solution.py:151
  182.4 2.4 %fusion.8 = bf16[512,64]{0,1:T(8,128)(2,1)} fusion(f32[2048,64]{0,1:T(8,128)S(1)} %bitcast.81, bf16[512,64]{0,1:T(8,128)(2,1)S(1)} %copy-done, f32[512]{0:T(512)S(1)} %get-tuple-element.13, s32[512]{0:T(512)S(1)} %bitcast.101, s32[512]{0:T(512)S(1)} %bitcast.93, s32[2048]{0:T(1024)S(1)} %add.113), kind=kOutput, calls=%fused_computation.28 | convolution fusion | flops 808615936 | bytes 669696 | tf_op jit(solution)/shard_map/kg,kc->gc/dot_general | solution.py:94
  (14 shorter events, 0.2 us)
Async XLA Ops:
  37.6 19.5 %collective-permute-start = (bf16[8,65,768]{2,0,1:T(8,128)(2,1)S(1)}, bf16[8,65,768]{2,0,1:T(8,128)(2,1)S(1)}, u32[]{:S(2)}, u32[]{:S(2)}) collective-permute-start(bf16[8,65,768]{2,0,1:T(8,128)(2,1)S(1)} %copy.74), channel_id=1, source_target_pairs={{0,1},{1,2},{2,3},{3,0},{4,5},{5,6},{6,7},{7,4},{8,9},{9,10},{10,1... | collective-permute-start | bytes 2396168 | tf_op jit(solution)/shard_map/ppermute | solution.py:130
  37.6 20.7 %collective-permute-start.1 = (bf16[8,65,768]{2,0,1:T(8,128)(2,1)S(1)}, bf16[8,65,768]{2,0,1:T(8,128)(2,1)S(1)}, u32[]{:S(2)}, u32[]{:S(2)}) collective-permute-start(bf16[8,65,768]{2,0,1:T(8,128)(2,1)S(1)} %copy.74), channel_id=1, source_target_pairs={{0,2},{1,3},{2,0},{3,1},{4,6},{5,7},{6,4},{7,5},{8,10},{9,11},{10,... | collective-permute-start | bytes 2396168 | tf_op jit(solution)/shard_map/ppermute | solution.py:130
  39.2 34.7 %collective-permute-start.2 = (bf16[8,65,768]{2,0,1:T(8,128)(2,1)S(1)}, bf16[8,65,768]{2,0,1:T(8,128)(2,1)S(1)}, u32[]{:S(2)}, u32[]{:S(2)}) collective-permute-start(bf16[8,65,768]{2,0,1:T(8,128)(2,1)S(1)} %copy.74), channel_id=1, source_target_pairs={{0,3},{1,0},{2,1},{3,2},{4,7},{5,4},{6,5},{7,6},{8,11},{9,8},{10,9... | collective-permute-start | bytes 2396168 | tf_op jit(solution)/shard_map/ppermute | solution.py:130
  80.8 26.2 %copy-start = (bf16[512,64]{0,1:T(8,128)(2,1)S(1)}, bf16[512,64]{0,1:T(8,128)(2,1)}, u32[]{:S(2)}) copy-start(bf16[512,64]{0,1:T(8,128)(2,1)} %param.5) | copy-start | bytes 196612
  96.4 9.8 %all-to-all-start.1 = ((f32[8,1,256]{2,1,0:T(1,128)}), f32[8,1,256]{2,1,0:T(1,128)S(1)}, u32[]{:S(2)}, u32[]{:S(2)}) async-start(f32[8,1,256]{2,1,0:T(1,128)} %bitcast.18), calls=%async_computation.1 | async-start | bytes 16384 | tf_op jit(solution)/shard_map/all_to_all | solution.py:138

commit v6 on v5

--- a/solution.py
+++ b/solution.py
@@ -69,8 +69,13 @@
     slot_of_pair = (lists_flat * per_list + within).reshape(rows_here, 2)
     slot_total = LIST_DEV * img_count * per_list
 
+    arrival = [0]
+    bit = sub_count // 2
+    while bit >= 1:
+        arrival = arrival + [d ^ bit for d in arrival]
+        bit //= 2
     me_sub = lax.axis_index("sub")
-    quarters = (me_sub - jnp.arange(sub_count, dtype=jnp.int32)) % sub_count
+    quarters = jnp.bitwise_xor(me_sub, jnp.array(arrival, dtype=jnp.int32))
     slot_ids = (
         jnp.arange(img_count, dtype=jnp.int32)[:, None, None] * per_list
         + quarters[None, :, None] * part
@@ -123,14 +128,14 @@
         ],
         axis=1,
     )
-    got = lax.all_to_all(payload, "img", split_axis=0, concat_axis=0, tiled=True)
-    gathered = [got]
-    for m in range(1, sub_count):
-        pairs = [(t, (t + m) % sub_count) for t in range(sub_count)]
-        gathered.append(lax.ppermute(got, "sub", pairs))
-    every = jnp.stack(gathered, axis=1)
-    rows = every[:, :, :part, :].reshape(1, slot_total, width)
-    key_rows = every[:, :, part, :part].reshape(1, slot_total).astype(jnp.float32)
+    got = lax.all_to_all(payload, "img", split_axis=0, concat_axis=0, tiled=True)[:, None]
+    bit = sub_count // 2
+    while bit >= 1:
+        pairs = [(t, t ^ bit) for t in range(sub_count)]
+        got = jnp.concatenate([got, lax.ppermute(got, "sub", pairs)], axis=1)
+        bit //= 2
+    rows = got[:, :, :part, :].reshape(1, slot_total, width)
+    key_rows = got[:, :, part, :part].reshape(1, slot_total).astype(jnp.float32)
     lists_here, slot_count = key_rows.shape
     weight_mat, row_sum_col = fused_affinity(rows.reshape(slot_count, -1), key_rows.reshape(-1))
     weights = weight_mat.reshape(lists_here, slot_count, slot_count)

time: 186 us -> 170 us (0.914)
  waiting for transfers between devices: 39.3 us -> 26.4 us
    ppermute x3 -> x2, waiting for transfers between devices: 33 us -> 20 us  [on_device(): got = jnp.concatenate([got, lax.ppermute(got, 'sub', pairs)], axis=1)]
  transfers between devices with their start and end apart: 4 -> 3, of which waited for: 4 -> 3; matrix products, arithmetic and copies ran while one was open for 0% -> 0% of each run, Pallas kernels for 0% -> 0%
where the time goes in v6:
time: 170 us; the launch traced here: 169 us
  blocking collectives  86.8 us (51%)
  waiting for transfers between devices  26.4 us (16%)
  matrix products  20.6 us (12%)
  Pallas kernels  13.5 us (8%)
  local copies, waits for them, and re-layouts  7.67 us (5%)
  other arithmetic  7.66 us (5%)
  starting transfers between devices  5.91 us (3%)
    all_to_all x2, blocking collectives, on_device(): lax.all_to_all(bucket_major(product), 'img', split_axis=0, concat_axis=0,...  34.3 us
    all_to_all x1, blocking collectives, on_device(): lax.all_to_all(payload, 'img', split_axis=0, concat_axis=0, tiled=True)  29.8 us
    all_to_all x2, blocking collectives, on_device(): lax.all_to_all(to_bucket(scaled), 'img', split_axis=0, concat_axis=0, til...  22.6 us
    ppermute x2, waiting for transfers between devices, on_device(): got = jnp.concatenate([got, lax.ppermute(got, 'sub', pairs)], axis=1)  20 us
    pallas_call x1, Pallas kernels, fused_affinity(): pl.pallas_call(affinity_kernel, grid=(slot_count // block_rows,), in_spec...  13.5 us
    dot_general x2, matrix products, on_device(): jnp.einsum('ajk,akc->ajc', weights, list_major(arrived), preferred_elemen...  12.1 us
    all_to_all x1, waiting for transfers between devices, on_device(): lax.all_to_all(bucket_major(row_sums), 'img', split_axis=0, concat_axis=0...  6.36 us
    all_to_all x1, starting transfers between devices, on_device(): lax.all_to_all(bucket_major(row_sums), 'img', split_axis=0, concat_axis=0...  4.29 us
  transfers between devices with their start and end apart: 3, of which 3 were waited for; matrix products, arithmetic and copies ran while one was open for 0% of the time, Pallas kernels for 0%

profile of v6, /device:TPU:0, one launch (start us, length us, event | category | flops | bytes accessed | tf_op | source)
XLA Modules:
  0.0 168.7 jit_solution(2378793577017022273)
XLA Ops:
  0.0 0.8 copy.60
  0.8 0.2 eq.32
  1.0 0.5 convert_reduce_fusion
  1.5 0.2 reduce_sum.39
  1.7 0.1 copy.61
  1.9 0.7 multiply_add_fusion
  2.6 0.1 iota_add_fusion.1
  2.6 0.1 add.108
  2.7 0.7 convert_element_type.65
  3.4 0.4 fusion.12
  3.8 0.3 fusion.10
  4.2 0.1 convert_element_type.80
  4.2 1.4 fusion.2
  5.6 1.9 %convolution_convert_fusion.2 = bf16[512,768]{1,0:T(8,128)(2,1)S(1)} fusion(bf16[512,768]{1,0:T(8,128)(2,1)} %param.5, f32[512]{0:T(512)S(1)} %add_rsqrt_fusion, s32[512]{0:T(512)S(1)} %bitcast.89, s32[512]{0:T(512)S(1)} %bitcast.81, s32[512]{0:T(512)S(1)} %add.108), kind=kOutput, calls=%fused_computation.16 | convolution fusion | flops 405012480 | bytes 1581056 | tf_op jit(solution)/shard_map/dot_general | solution.py:123
  7.5 0.0 copy-start.1
  7.5 0.1 fusion.11
  7.6 29.8 %all_to_all.30 = bf16[8,65,768]{2,1,0:T(8,128)(2,1)S(1)} all-to-all(bf16[8,65,768]{2,1,0:T(8,128)(2,1)S(1)} %fusion.11), channel_id=1, replica_groups=mesh['img'=8,'sub'=4] {'img'}, dimensions={0} | all-to-all | bytes 1597440 | tf_op jit(solution)/shard_map/all_to_all | solution.py:131
  37.4 0.1 copy.85
  37.6 1.6 collective-permute-start
  39.1 16.7 %collective-permute-done = bf16[8,1,65,768]{3,0,2,1:T(8,128)(2,1)S(1)} collective-permute-done((bf16[8,1,65,768]{3,0,2,1:T(8,128)(2,1)S(1)}, bf16[8,1,65,768]{3,0,2,1:T(8,128)(2,1)S(1)}, u32[]{:S(2)}, u32[]{:S(2)}) %collective-permute-start) | collective-permute-done | bytes 798752 | tf_op jit(solution)/shard_map/ppermute | solution.py:135
  55.8 0.1 pad_maximum_fusion.2
  56.0 0.1 collective-permute-start.1
  56.1 0.0 copy-done.1
  56.1 0.1 broadcast_add_fusion
  56.1 3.3 %collective-permute-done.1 = bf16[8,2,65,768]{3,0,2,1:T(8,128)(2,1)S(1)} collective-permute-done((bf16[8,2,65,768]{3,0,2,1:T(8,128)(2,1)S(1)}, bf16[8,2,65,768]{3,0,2,1:T(8,128)(2,1)S(1)}, u32[]{:S(2)}, u32[]{:S(2)}) %collective-permute-start.1) | collective-permute-done | bytes 1597472 | tf_op jit(solution)/shard_map/ppermute | solution.py:135
  59.5 2.0 %reshape.204.row_keys = f32[2048,1]{1,0:T(8,128)} reshape(f32[8,4,1,64]{3,1,0,2:T(4,128)S(1)} %copy.64) | data formatting | bytes 16384 | tf_op jit(solution)/shard_map/convert_element_type | solution.py:138
  61.5 0.7 reshape.201.col_keys
  62.2 0.3 pad_maximum_fusion
  62.5 2.4 %copy.66 = bf16[8,4,64,768]{3,2,1,0:T(8,128)(2,1)} copy(bf16[8,4,64,768]{3,0,2,1:T(8,128)(2,1)S(1)} %pad_maximum_fusion) | data formatting | bytes 6291456 | tf_op jit(solution)/shard_map/slice | solution.py:137
  64.9 0.0 copy-start
  64.9 13.5 %shard_map.55 = (bf16[2048,2048]{1,0:T(8,128)(2,1)}, f32[2048,1]{1,0:T(8,128)}) custom-call(f32[2048,1]{1,0:T(8,128)} %reshape.204.row_keys, f32[1,2048]{1,0:T(1,128)} %reshape.201.col_keys, bf16[2048,768]{1,0:T(8,128)(2,1)} %bitcast.67, bf16[2048,768]{1,0:T(8,128)(2,1)} %bitcast.68), custom_call_target="tpu_custom_call" | custom-call | flops 6467616768 | bytes 14680064 | tf_op jit(solution)/shard_map/pallas_call | solution.py:32
  78.4 2.2 %reduce = f32[2048]{0:T(1024)} reduce(f32[2048,1]{1,0:T(8,128)} %get-tuple-element.7, f32[]{:T(128)} %constant.32), dimensions={1}, to_apply=%get-tuple-element.7.reduce_sub_computation | reduce | bytes 16388 | tf_op jit(solution)/shard_map/pallas_call | solution.py:32
  80.6 4.3 %all-to-all-start.1 = ((f32[8,1,256]{2,1,0:T(1,128)}), f32[8,1,256]{2,1,0:T(1,128)S(1)}, u32[]{:S(2)}, u32[]{:S(2)}) async-start(f32[8,1,256]{2,1,0:T(1,128)} %bitcast.15), calls=%async_computation.1 | async-start | bytes 16384 | tf_op jit(solution)/shard_map/all_to_all | solution.py:143
  84.8 0.1 iota_add_fusion
  84.9 0.1 add.102
  85.0 6.4 %all-to-all-done.1 = f32[8,1,256]{2,1,0:T(1,128)S(1)} async-done(((f32[8,1,256]{2,1,0:T(1,128)}), f32[8,1,256]{2,1,0:T(1,128)S(1)}, u32[]{:S(2)}, u32[]{:S(2)}) %all-to-all-start.1) | async-done | bytes 8224 | tf_op jit(solution)/shard_map/all_to_all | solution.py:143
  91.4 0.7 select_reduce_fusion
  92.1 0.0 copy-done
  92.1 1.3 convolution_convert_fusion.1
  93.4 0.1 copy.78
  93.5 10.6 %all_to_all.31 = bf16[8,1,256,64]{2,3,1,0:T(8,128)(2,1)S(1)} all-to-all(bf16[8,1,256,64]{2,3,1,0:T(8,128)(2,1)S(1)} %copy.69), channel_id=1, replica_groups=mesh['img'=8,'sub'=4] {'img'}, dimensions={0} | all-to-all | bytes 524288 | tf_op jit(solution)/shard_map/all_to_all | solution.py:152
  104.1 0.1 copy.70
  104.3 0.1 reshape.202
  104.4 6.0 %convolution_bitcast_fusion.1 = f32[8,1,256,64]{2,3,1,0:T(8,128)S(1)} fusion(bf16[8,256,2048]{2,1,0:T(8,128)(2,1)} %bitcast.61, bf16[2048,64,1]{0,1,2:T(8,128)(2,1)S(1)} %reshape.202), kind=kOutput, calls=%fused_computation.21 | convolution fusion | flops 536870912 | bytes 9175040 | tf_op jit(solution)/shard_map/ajk,akc->ajc/dot_general | solution.py:153
  110.5 17.0 %all_to_all.32 = f32[8,1,256,64]{2,3,1,0:T(8,128)S(1)} all-to-all(f32[8,1,256,64]{2,3,1,0:T(8,128)S(1)} %convolution_bitcast_fusion.1), channel_id=1, replica_groups=mesh['img'=8,'sub'=4] {'img'}, dimensions={0} | all-to-all | bytes 1048576 | tf_op jit(solution)/shard_map/all_to_all | solution.py:156
  127.5 1.7 %fusion.7 = bf16[512,64]{0,1:T(8,128)(2,1)S(1)} fusion(f32[2048,64]{0,1:T(8,128)S(1)} %bitcast.75, bf16[512,64]{0,1:T(8,128)(2,1)S(1)} %copy-done, f32[512]{0:T(512)S(1)} %get-tuple-element.14, f32[512]{0:T(512)S(1)} %get-tuple-element.13, s32[512]{0:T(512)S(1)} %bitcast.92, s32[512]{0:T(512)S(1)} %bitcast.84, s32[2048]{0:T(1024)S(1)} %add.102), kind=kOutput, calls=%fused_computation.27 | convolution fusion | flops 808648704 | bytes 671744 | tf_op jit(solution)/shard_map/kg,kc->gc/dot_general | solution.py:99
  129.3 1.3 convolution_convert_fusion
  130.6 0.1 copy.80
  130.7 12.0 %all_to_all.33 = bf16[8,1,256,64]{2,3,1,0:T(8,128)(2,1)S(1)} all-to-all(bf16[8,1,256,64]{2,3,1,0:T(8,128)(2,1)S(1)} %copy.73), channel_id=1, replica_groups=mesh['img'=8,'sub'=4] {'img'}, dimensions={0} | all-to-all | bytes 524288 | tf_op jit(solution)/shard_map/all_to_all | solution.py:152
  142.6 0.1 copy.74
  142.8 0.1 reshape.203
  142.9 6.0 %convolution_bitcast_fusion = f32[8,1,256,64]{2,3,1,0:T(8,128)S(1)} fusion(bf16[8,256,2048]{2,1,0:T(8,128)(2,1)} %bitcast.62, bf16[2048,64,1]{0,1,2:T(8,128)(2,1)S(1)} %reshape.203), kind=kOutput, calls=%fused_computation.20 | convolution fusion | flops 536870912 | bytes 9175040 | tf_op jit(solution)/shard_map/ajk,akc->ajc/dot_general | solution.py:153
  149.0 17.3 %all_to_all.34 = f32[8,1,256,64]{2,3,1,0:T(8,128)S(1)} all-to-all(f32[8,1,256,64]{2,3,1,0:T(8,128)S(1)} %convolution_bitcast_fusion), channel_id=1, replica_groups=mesh['img'=8,'sub'=4] {'img'}, dimensions={0} | all-to-all | bytes 1048576 | tf_op jit(solution)/shard_map/all_to_all | solution.py:156
  166.3 2.4 %fusion.8 = bf16[512,64]{0,1:T(8,128)(2,1)} fusion(f32[2048,64]{0,1:T(8,128)S(1)} %bitcast.74, bf16[512,64]{0,1:T(8,128)(2,1)S(1)} %copy-done, f32[512]{0:T(512)S(1)} %get-tuple-element.13, s32[512]{0:T(512)S(1)} %bitcast.94, s32[512]{0:T(512)S(1)} %bitcast.86, s32[2048]{0:T(1024)S(1)} %add.102), kind=kOutput, calls=%fused_computation.28 | convolution fusion | flops 808615936 | bytes 669696 | tf_op jit(solution)/shard_map/kg,kc->gc/dot_general | solution.py:99
  (14 shorter events, 0.2 us)
Async XLA Ops:
  7.5 48.5 %copy-start.1 = (s32[4]{0:T(128)S(1)}, s32[4]{0:T(128)}, u32[]{:S(2)}) copy-start(s32[4]{0:T(128)} %constant.11.clone) | copy-start | bytes 52
  37.6 18.2 %collective-permute-start = (bf16[8,1,65,768]{3,0,2,1:T(8,128)(2,1)S(1)}, bf16[8,1,65,768]{3,0,2,1:T(8,128)(2,1)S(1)}, u32[]{:S(2)}, u32[]{:S(2)}) collective-permute-start(bf16[8,1,65,768]{3,0,2,1:T(8,128)(2,1)S(1)} %bitcast.63), channel_id=1, source_target_pairs={{0,2},{1,3},{2,0},{3,1},{4,6},{5,7},{6,4},{7,5},{8,10},{9,11},{10,... | collective-permute-start | bytes 2396168 | tf_op jit(solution)/shard_map/ppermute | solution.py:135
  56.0 3.5 %collective-permute-start.1 = (bf16[8,2,65,768]{3,0,2,1:T(8,128)(2,1)S(1)}, bf16[8,2,65,768]{3,0,2,1:T(8,128)(2,1)S(1)}, u32[]{:S(2)}, u32[]{:S(2)}) collective-permute-start(bf16[8,2,65,768]{3,0,2,1:T(8,128)(2,1)S(1)} %pad_maximum_fusion.2), channel_id=1, source_target_pairs={{0,1},{1,0},{2,3},{3,2},{4,5},{5,4},{6,7},{7,6},{8,9},{9,8},{10,11... | collective-permute-start | bytes 4792328 | tf_op jit(solution)/shard_map/ppermute | solution.py:135
  64.9 27.2 %copy-start = (bf16[512,64]{0,1:T(8,128)(2,1)S(1)}, bf16[512,64]{0,1:T(8,128)(2,1)}, u32[]{:S(2)}) copy-start(bf16[512,64]{0,1:T(8,128)(2,1)} %param.6) | copy-start | bytes 196612
  80.6 10.8 %all-to-all-start.1 = ((f32[8,1,256]{2,1,0:T(1,128)}), f32[8,1,256]{2,1,0:T(1,128)S(1)}, u32[]{:S(2)}, u32[]{:S(2)}) async-start(f32[8,1,256]{2,1,0:T(1,128)} %bitcast.15), calls=%async_computation.1 | async-start | bytes 16384 | tf_op jit(solution)/shard_map/all_to_all | solution.py:143

commit v7 on v6

--- a/solution.py
+++ b/solution.py
@@ -15,44 +15,50 @@
     return moved.reshape((moved.shape[0], moved.shape[1] * moved.shape[2]) + moved.shape[3:])
 
 
-def affinity_kernel(row_keys, col_keys, picked, rows, weights, row_sums):
+def affinity_kernel(row_keys, col_keys, low_picked, high_picked, low_rows, high_rows, weights, row_sums):
+    contract = (((1,), (1,)), ((), ()))
     gram = lax.dot_general(
-        picked[...], rows[...], (((1,), (1,)), ((), ())), preferred_element_type=jnp.float32
-    )
+        low_picked[...], low_rows[...], contract, preferred_element_type=jnp.float32
+    ) + lax.dot_general(high_picked[...], high_rows[...], contract, preferred_element_type=jnp.float32)
     keep = jnp.abs(row_keys[...] - col_keys[...]) <= BAND
     positive = jnp.maximum(gram, 0.0)
     cubed = jnp.where(keep, positive * positive * positive, 0.0).astype(jnp.bfloat16)
     weights[...] = cubed
-    row_sums[...] = jnp.sum(cubed.astype(jnp.float32), axis=1, keepdims=True)
+    ones = jnp.ones((8, cubed.shape[1]), jnp.bfloat16)
+    summed = lax.dot_general(ones, cubed, contract, preferred_element_type=jnp.float32)
+    row_sums[...] = summed[0:1, :]
 
 
-def fused_affinity(rows, keys):
-    slot_count, width = rows.shape
+def fused_affinity(low, high, keys):
+    slot_count = low.shape[0]
     block_rows = min(256, slot_count)
+    width = low.shape[1] + high.shape[1]
     return pl.pallas_call(
         affinity_kernel,
         grid=(slot_count // block_rows,),
         in_specs=[
             pl.BlockSpec((block_rows, 1), lambda i: (i, 0)),
             pl.BlockSpec((1, slot_count), lambda i: (0, 0)),
-            pl.BlockSpec((block_rows, width), lambda i: (i, 0)),
-            pl.BlockSpec((slot_count, width), lambda i: (0, 0)),
+            pl.BlockSpec((block_rows, low.shape[1]), lambda i: (i, 0)),
+            pl.BlockSpec((block_rows, high.shape[1]), lambda i: (i, 0)),
+            pl.BlockSpec((slot_count, low.shape[1]), lambda i: (0, 0)),
+            pl.BlockSpec((slot_count, high.shape[1]), lambda i: (0, 0)),
         ],
         out_specs=[
             pl.BlockSpec((block_rows, slot_count), lambda i: (i, 0)),
-            pl.BlockSpec((block_rows, 1), lambda i: (i, 0)),
+            pl.BlockSpec((1, block_rows), lambda i: (0, i)),
         ],
         out_shape=[
             jax.ShapeDtypeStruct((slot_count, slot_count), jnp.bfloat16),
-            jax.ShapeDtypeStruct((slot_count, 1), jnp.float32),
+            jax.ShapeDtypeStruct((1, slot_count), jnp.float32),
         ],
         compiler_params=pltpu.CompilerParams(dimension_semantics=("arbitrary",)),
         cost_estimate=pl.CostEstimate(
-            flops=2 * slot_count * slot_count * width + 6 * slot_count * slot_count,
+            flops=2 * slot_count * slot_count * width + 22 * slot_count * slot_count,
             transcendentals=0,
             bytes_accessed=2 * slot_count * width * 2 + 2 * slot_count * slot_count,
         ),
-    )(keys.reshape(slot_count, 1), keys.reshape(1, slot_count), rows, rows)
+    )(keys.reshape(slot_count, 1), keys.reshape(1, slot_count), low, high, low, high)
 
 
 def on_device(embeddings, labels, image_lists, rank_keys):
@@ -121,25 +127,34 @@
     mine_keys = jnp.where(jnp.any(mine_hit, axis=1), key_sum, -4096.0).astype(jnp.bfloat16)
     width = unit.shape[1]
     quarter = jnp.dot(mine_hit.astype(jnp.bfloat16), unit, preferred_element_type=jnp.float32)
-    payload = jnp.concatenate(
+    half = width // 2
+    quarter = quarter.astype(jnp.bfloat16).reshape(img_count, part, width)
+    low_payload = jnp.concatenate(
         [
-            quarter.astype(jnp.bfloat16).reshape(img_count, part, width),
-            jnp.pad(mine_keys.reshape(img_count, 1, part), ((0, 0), (0, 0), (0, width - part))),
+            quarter[:, :, :half],
+            jnp.pad(mine_keys.reshape(img_count, 1, part), ((0, 0), (0, 0), (0, half - part))),
         ],
         axis=1,
     )
-    got = lax.all_to_all(payload, "img", split_axis=0, concat_axis=0, tiled=True)[:, None]
+    high_payload = quarter[:, :, half:]
+
+    def exchange_stage(got, bit):
+        pairs = [(t, t ^ bit) for t in range(sub_count)]
+        return jnp.concatenate([got, lax.ppermute(got, "sub", pairs)], axis=1)
+
+    low_got = lax.all_to_all(low_payload, "img", split_axis=0, concat_axis=0, tiled=True)[:, None]
+    high_got = lax.all_to_all(high_payload, "img", split_axis=0, concat_axis=0, tiled=True)[:, None]
     bit = sub_count // 2
     while bit >= 1:
-        pairs = [(t, t ^ bit) for t in range(sub_count)]
-        got = jnp.concatenate([got, lax.ppermute(got, "sub", pairs)], axis=1)
+        low_got = exchange_stage(low_got, bit)
+        high_got = exchange_stage(high_got, bit)
         bit //= 2
-    rows = got[:, :, :part, :].reshape(1, slot_total, width)
-    key_rows = got[:, :, part, :part].reshape(1, slot_total).astype(jnp.float32)
-    lists_here, slot_count = key_rows.shape
-    weight_mat, row_sum_col = fused_affinity(rows.reshape(slot_count, -1), key_rows.reshape(-1))
-    weights = weight_mat.reshape(lists_here, slot_count, slot_count)
-    row_sums = row_sum_col.reshape(lists_here, slot_count)
+    slot_count = slot_total
+    low_rows = low_got[:, :, :part, :].reshape(slot_count, half)
+    high_rows = high_got.reshape(slot_count, width - half)
+    key_rows = low_got[:, :, part, :part].reshape(slot_count).astype(jnp.float32)
+    weight_mat, row_sums = fused_affinity(low_rows, high_rows, key_rows)
+    weights = weight_mat.reshape(1, slot_count, slot_count)
     degree_slots = lax.all_to_all(
         bucket_major(row_sums), "img", split_axis=0, concat_axis=0, tiled=True
     )

time: 170 us -> 165 us (0.971)
  blocking collectives: 86.8 us -> 57.1 us
  starting transfers between devices: 5.91 us -> 20.7 us
  waiting for transfers between devices: 26.4 us -> 34.3 us
  Pallas kernels: 13.5 us -> 16.3 us
  other arithmetic: 7.66 us -> 5.68 us
    all_to_all x1 -> x0, blocking collectives: 29.8 us -> none  [on_device(): lax.all_to_all(payload, 'img', split_axis=0, concat_axis=0, tiled=True)]
    all_to_all x0 -> x2, waiting for transfers between devices: none -> 21.1 us  [the longest x1 11.1 us: on_device(): lax.all_to_all(low_payload, 'img', split_axis=0, concat_axis=0, tiled=True)]
    ppermute x2 -> x4, waiting for transfers between devices: 20 us -> 6.84 us  [exchange_stage(): return jnp.concatenate([got, lax.ppermute(got, 'sub', pairs)], axis=1)]
    all_to_all x0 -> x2, starting transfers between devices: none -> 10.9 us  [the longest x1 7.28 us: on_device(): lax.all_to_all(high_payload, 'img', split_axis=0, concat_axis=0, tiled=True)]
    pallas_call x1, Pallas kernels: 13.5 us -> 16.3 us  [fused_affinity(): pl.pallas_call(affinity_kernel, grid=(slot_count // block_rows,), in_spec...]
    all_to_all x1, starting transfers between devices: 4.29 us -> 6.57 us  [on_device(): lax.all_to_all(bucket_major(row_sums), 'img', split_axis=0, concat_axis=0...]
    pallas_call x1 -> x0, other arithmetic: 2.17 us -> none  [fused_affinity(): pl.pallas_call(affinity_kernel, grid=(slot_count // block_rows,), in_spec...]
  transfers between devices with their start and end apart: 3 -> 7, of which waited for: 3 -> 5; matrix products, arithmetic and copies ran while one was open for 0% -> 2% of each run, Pallas kernels for 0% -> 0%
where the time goes in v7:
time: 165 us; the launch traced here: 164 us
  blocking collectives  57.1 us (35%)
  waiting for transfers between devices  34.3 us (21%)
  starting transfers between devices  20.7 us (13%)
  matrix products  20.6 us (12%)
  Pallas kernels  16.3 us (10%)
  local copies, waits for them, and re-layouts  8.86 us (5%)
  other arithmetic  5.68 us (3%)
    all_to_all x2, blocking collectives, on_device(): lax.all_to_all(bucket_major(product), 'img', split_axis=0, concat_axis=0,...  34.4 us
    all_to_all x2, blocking collectives, on_device(): lax.all_to_all(to_bucket(scaled), 'img', split_axis=0, concat_axis=0, til...  22.8 us
    pallas_call x1, Pallas kernels, fused_affinity(): pl.pallas_call(affinity_kernel, grid=(slot_count // block_rows,), in_spec...  16.3 us
    dot_general x2, matrix products, on_device(): jnp.einsum('ajk,akc->ajc', weights, list_major(arrived), preferred_elemen...  12.1 us
    all_to_all x1, waiting for transfers between devices, on_device(): lax.all_to_all(low_payload, 'img', split_axis=0, concat_axis=0, tiled=True)  11.1 us
    all_to_all x1, waiting for transfers between devices, on_device(): lax.all_to_all(high_payload, 'img', split_axis=0, concat_axis=0, tiled=True)  10 us
    all_to_all x1, starting transfers between devices, on_device(): lax.all_to_all(high_payload, 'img', split_axis=0, concat_axis=0, tiled=True)  7.28 us
    ppermute x4, waiting for transfers between devices, exchange_stage(): return jnp.concatenate([got, lax.ppermute(got, 'sub', pairs)], axis=1)  6.84 us
  transfers between devices with their start and end apart: 7, of which 5 were waited for; matrix products, arithmetic and copies ran while one was open for 2% of the time, Pallas kernels for 0%

profile of v7, /device:TPU:0, one launch (start us, length us, event | category | flops | bytes accessed | tf_op | source)
XLA Modules:
  0.0 163.8 jit_solution(4895722877640438850)
XLA Ops:
  0.0 0.0 copy-start
  0.0 0.8 copy.65
  0.8 0.2 eq.32
  1.0 0.5 convert_reduce_fusion
  1.5 0.2 reduce_sum.39
  1.8 0.1 copy.66
  1.9 0.7 multiply_add_fusion
  2.6 0.1 iota_add_fusion.1
  2.7 0.1 add.108
  2.7 1.4 fusion.1
  4.1 1.9 %convolution_convert_fusion.2 = bf16[512,768]{1,0:T(8,128)(2,1)S(1)} fusion(bf16[512,768]{1,0:T(8,128)(2,1)} %param.5, f32[512]{0:T(512)S(1)} %add_rsqrt_fusion, s32[512]{0:T(512)S(1)} %bitcast.94, s32[512]{0:T(512)S(1)} %bitcast.86, s32[512]{0:T(512)S(1)} %add.108), kind=kOutput, calls=%fused_computation.14 | convolution fusion | flops 405012480 | bytes 1581056 | tf_op jit(solution)/shard_map/dot_general | solution.py:129
  6.0 0.0 copy-start.2
  6.0 0.8 fusion.21
  6.9 7.3 %all-to-all-start.1 = ((bf16[8,64,384]{2,1,0:T(8,128)(2,1)}), bf16[8,64,384]{2,1,0:T(8,128)(2,1)S(1)}, u32[]{:S(2)}, u32[]{:S(2)}) async-start(bf16[8,64,384]{2,1,0:T(8,128)(2,1)} %get-tuple-element.9), calls=%async_computation.1 | async-start | bytes 786432 | tf_op jit(solution)/shard_map/all_to_all | solution.py:146
  14.1 0.0 copy-done
  14.2 0.4 fusion.11
  14.6 0.3 fusion.9
  14.9 0.1 convert_element_type.96
  15.0 0.8 fusion.17
  15.8 10.0 %all-to-all-done.1 = bf16[8,64,384]{2,1,0:T(8,128)(2,1)S(1)} async-done(((bf16[8,64,384]{2,1,0:T(8,128)(2,1)}), bf16[8,64,384]{2,1,0:T(8,128)(2,1)S(1)}, u32[]{:S(2)}, u32[]{:S(2)}) %all-to-all-start.1) | async-done | bytes 393248 | tf_op jit(solution)/shard_map/all_to_all | solution.py:146
  25.8 3.6 %all-to-all-start = ((bf16[8,65,384]{2,1,0:T(8,128)(2,1)}), bf16[8,65,384]{2,1,0:T(8,128)(2,1)S(1)}, u32[]{:S(2)}, u32[]{:S(2)}) async-start(bf16[8,65,384]{2,1,0:T(8,128)(2,1)} %fusion.17), calls=%async_computation | async-start | bytes 884736 | tf_op jit(solution)/shard_map/all_to_all | solution.py:145
  29.5 1.5 collective-permute-start.2
  31.0 11.1 %all-to-all-done = bf16[8,65,384]{2,1,0:T(8,128)(2,1)S(1)} async-done(((bf16[8,65,384]{2,1,0:T(8,128)(2,1)}), bf16[8,65,384]{2,1,0:T(8,128)(2,1)S(1)}, u32[]{:S(2)}, u32[]{:S(2)}) %all-to-all-start) | async-done | bytes 399392 | tf_op jit(solution)/shard_map/all_to_all | solution.py:145
  42.2 1.6 collective-permute-start
  43.7 0.0 collective-permute-done.2
  43.7 0.1 pad_maximum_fusion.4
  43.8 0.1 collective-permute-start.3
  43.9 6.2 %collective-permute-done = bf16[8,1,65,384]{3,0,2,1:T(8,128)(2,1)S(1)} collective-permute-done((bf16[8,1,65,384]{3,0,2,1:T(8,128)(2,1)S(1)}, bf16[8,1,65,384]{3,0,2,1:T(8,128)(2,1)S(1)}, u32[]{:S(2)}, u32[]{:S(2)}) %collective-permute-start) | collective-permute-done | bytes 399392 | tf_op jit(solution)/shard_map/ppermute | solution.py:143
  50.1 0.1 pad_maximum_fusion.3
  50.2 0.1 collective-permute-start.1
  50.2 0.0 copy-done.2
  50.3 0.1 broadcast_add_fusion
  50.3 0.0 collective-permute-done.3
  50.3 0.2 pad_maximum_fusion.2
  50.5 1.3 copy.72
  51.9 0.7 collective-permute-done.1
  52.5 2.0 %reshape.212.row_keys = f32[2048,1]{1,0:T(8,128)} reshape(f32[8,4,1,64]{3,1,0,2:T(4,128)S(1)} %copy.69) | data formatting | bytes 16384 | tf_op jit(solution)/shard_map/convert_element_type | solution.py:155
  54.5 0.7 reshape.209.col_keys
  55.2 0.2 pad_maximum_fusion
  55.4 1.5 copy.71
  56.9 0.0 copy-start.1
  56.9 16.3 %shard_map.55 = (bf16[2048,2048]{1,0:T(8,128)(2,1)}, f32[1,2048]{1,0:T(1,128)}) custom-call(f32[2048,1]{1,0:T(8,128)} %reshape.212.row_keys, f32[1,2048]{1,0:T(1,128)} %reshape.209.col_keys, bf16[2048,384]{1,0:T(8,128)(2,1)} %bitcast.76, bf16[2048,384]{1,0:T(8,128)(2,1)} %bitcast.74, bf16[2048,384]{1,0:T(8,128)(2,1)} %bitcast.77, bf16[2048,384]{1,0:T(8,128)(2,1)} %bitcast.75), custom_call_target="tpu_custom_call" | custom-call | flops 6534725632 | bytes 14680064 | tf_op jit(solution)/shard_map/pallas_call | solution.py:36
  73.2 6.6 %all-to-all-start.2 = ((f32[8,1,256]{2,1,0:T(1,128)}), f32[8,1,256]{2,1,0:T(1,128)S(1)}, u32[]{:S(2)}, u32[]{:S(2)}) async-start(f32[8,1,256]{2,1,0:T(1,128)} %bitcast.102), calls=%async_computation.2 | async-start | bytes 16384 | tf_op jit(solution)/shard_map/all_to_all | solution.py:158
  79.8 0.1 iota_add_fusion
  79.9 0.1 add.102
  80.0 6.4 %all-to-all-done.2 = f32[8,1,256]{2,1,0:T(1,128)S(1)} async-done(((f32[8,1,256]{2,1,0:T(1,128)}), f32[8,1,256]{2,1,0:T(1,128)S(1)}, u32[]{:S(2)}, u32[]{:S(2)}) %all-to-all-start.2) | async-done | bytes 8224 | tf_op jit(solution)/shard_map/all_to_all | solution.py:158
  86.3 0.7 select_reduce_fusion
  87.0 0.0 copy-done.1
  87.0 1.3 convolution_convert_fusion.1
  88.3 0.1 copy.84
  88.4 10.6 %all_to_all.35 = bf16[8,1,256,64]{2,3,1,0:T(8,128)(2,1)S(1)} all-to-all(bf16[8,1,256,64]{2,3,1,0:T(8,128)(2,1)S(1)} %copy.75), channel_id=1, replica_groups=mesh['img'=8,'sub'=4] {'img'}, dimensions={0} | all-to-all | bytes 524288 | tf_op jit(solution)/shard_map/all_to_all | solution.py:167
  99.1 0.1 copy.76
  99.2 0.1 reshape.210
  99.4 6.0 %convolution_bitcast_fusion.1 = f32[8,1,256,64]{2,3,1,0:T(8,128)S(1)} fusion(bf16[8,256,2048]{2,1,0:T(8,128)(2,1)} %bitcast.63, bf16[2048,64,1]{0,1,2:T(8,128)(2,1)S(1)} %reshape.210), kind=kOutput, calls=%fused_computation.19 | convolution fusion | flops 536870912 | bytes 9175040 | tf_op jit(solution)/shard_map/ajk,akc->ajc/dot_general | solution.py:168
  105.4 17.1 %all_to_all.36 = f32[8,1,256,64]{2,3,1,0:T(8,128)S(1)} all-to-all(f32[8,1,256,64]{2,3,1,0:T(8,128)S(1)} %convolution_bitcast_fusion.1), channel_id=1, replica_groups=mesh['img'=8,'sub'=4] {'img'}, dimensions={0} | all-to-all | bytes 1048576 | tf_op jit(solution)/shard_map/all_to_all | solution.py:171
  122.5 1.7 %fusion.6 = bf16[512,64]{0,1:T(8,128)(2,1)S(1)} fusion(f32[2048,64]{0,1:T(8,128)S(1)} %bitcast.82, bf16[512,64]{0,1:T(8,128)(2,1)S(1)} %copy-done.1, f32[512]{0:T(512)S(1)} %get-tuple-element.16, f32[512]{0:T(512)S(1)} %get-tuple-element.15, s32[512]{0:T(512)S(1)} %bitcast.99, s32[512]{0:T(512)S(1)} %bitcast.91, s32[2048]{0:T(1024)S(1)} %add.102), kind=kOutput, calls=%fused_computation.25 | convolution fusion | flops 808648704 | bytes 671744 | tf_op jit(solution)/shard_map/kg,kc->gc/dot_general | solution.py:105
  124.3 1.3 convolution_convert_fusion
  125.5 0.1 copy.86
  125.7 12.1 %all_to_all.37 = bf16[8,1,256,64]{2,3,1,0:T(8,128)(2,1)S(1)} all-to-all(bf16[8,1,256,64]{2,3,1,0:T(8,128)(2,1)S(1)} %copy.79), channel_id=1, replica_groups=mesh['img'=8,'sub'=4] {'img'}, dimensions={0} | all-to-all | bytes 524288 | tf_op jit(solution)/shard_map/all_to_all | solution.py:167
  137.8 0.1 copy.80
  138.0 0.1 reshape.211
  138.1 6.0 %convolution_bitcast_fusion = f32[8,1,256,64]{2,3,1,0:T(8,128)S(1)} fusion(bf16[8,256,2048]{2,1,0:T(8,128)(2,1)} %bitcast.64, bf16[2048,64,1]{0,1,2:T(8,128)(2,1)S(1)} %reshape.211), kind=kOutput, calls=%fused_computation.18 | convolution fusion | flops 536870912 | bytes 9175040 | tf_op jit(solution)/shard_map/ajk,akc->ajc/dot_general | solution.py:168
  144.1 17.3 %all_to_all.38 = f32[8,1,256,64]{2,3,1,0:T(8,128)S(1)} all-to-all(f32[8,1,256,64]{2,3,1,0:T(8,128)S(1)} %convolution_bitcast_fusion), channel_id=1, replica_groups=mesh['img'=8,'sub'=4] {'img'}, dimensions={0} | all-to-all | bytes 1048576 | tf_op jit(solution)/shard_map/all_to_all | solution.py:171
  161.5 2.4 %fusion.7 = bf16[512,64]{0,1:T(8,128)(2,1)} fusion(f32[2048,64]{0,1:T(8,128)S(1)} %bitcast.81, bf16[512,64]{0,1:T(8,128)(2,1)S(1)} %copy-done.1, f32[512]{0:T(512)S(1)} %get-tuple-element.15, s32[512]{0:T(512)S(1)} %bitcast.101, s32[512]{0:T(512)S(1)} %bitcast.93, s32[2048]{0:T(1024)S(1)} %add.102), kind=kOutput, calls=%fused_computation.26 | convolution fusion | flops 808615936 | bytes 669696 | tf_op jit(solution)/shard_map/kg,kc->gc/dot_general | solution.py:105
  (16 shorter events, 0.3 us)
Async XLA Ops:
  0.0 14.1 %copy-start = (s32[512,2]{0,1:T(2,128)S(1)}, s32[512,2]{0,1:T(2,128)}, u32[]{:S(2)}) copy-start(s32[512,2]{0,1:T(2,128)} %param.8) | copy-start | bytes 12292
  6.0 44.2 %copy-start.2 = (s32[4]{0:T(128)S(1)}, s32[4]{0:T(128)}, u32[]{:S(2)}) copy-start(s32[4]{0:T(128)} %constant.11.clone) | copy-start | bytes 52
  6.9 19.0 %all-to-all-start.1 = ((bf16[8,64,384]{2,1,0:T(8,128)(2,1)}), bf16[8,64,384]{2,1,0:T(8,128)(2,1)S(1)}, u32[]{:S(2)}, u32[]{:S(2)}) async-start(bf16[8,64,384]{2,1,0:T(8,128)(2,1)} %get-tuple-element.9), calls=%async_computation.1 | async-start | bytes 786432 | tf_op jit(solution)/shard_map/all_to_all | solution.py:146
  25.8 16.3 %all-to-all-start = ((bf16[8,65,384]{2,1,0:T(8,128)(2,1)}), bf16[8,65,384]{2,1,0:T(8,128)(2,1)S(1)}, u32[]{:S(2)}, u32[]{:S(2)}) async-start(bf16[8,65,384]{2,1,0:T(8,128)(2,1)} %fusion.17), calls=%async_computation | async-start | bytes 884736 | tf_op jit(solution)/shard_map/all_to_all | solution.py:145
  29.5 14.2 %collective-permute-start.2 = (bf16[8,1,64,384]{3,2,0,1:T(8,128)(2,1)S(1)}, bf16[8,1,64,384]{3,2,0,1:T(8,128)(2,1)S(1)}, u32[]{:S(2)}, u32[]{:S(2)}) collective-permute-start(bf16[8,1,64,384]{3,2,0,1:T(8,128)(2,1)S(1)} %bitcast.69), channel_id=1, source_target_pairs={{0,2},{1,3},{2,0},{3,1},{4,6},{5,7},{6,4},{7,5},{8,10},{9,11},{10,... | collective-permute-start | bytes 1179656 | tf_op jit(solution)/shard_map/ppermute | solution.py:143
  42.2 7.9 %collective-permute-start = (bf16[8,1,65,384]{3,0,2,1:T(8,128)(2,1)S(1)}, bf16[8,1,65,384]{3,0,2,1:T(8,128)(2,1)S(1)}, u32[]{:S(2)}, u32[]{:S(2)}) collective-permute-start(bf16[8,1,65,384]{3,0,2,1:T(8,128)(2,1)S(1)} %bitcast.65), channel_id=1, source_target_pairs={{0,2},{1,3},{2,0},{3,1},{4,6},{5,7},{6,4},{7,5},{8,10},{9,11},{10,... | collective-permute-start | bytes 1198088 | tf_op jit(solution)/shard_map/ppermute | solution.py:143
  43.8 6.5 %collective-permute-start.3 = (bf16[8,2,64,384]{3,2,0,1:T(8,128)(2,1)S(1)}, bf16[8,2,64,384]{3,2,0,1:T(8,128)(2,1)S(1)}, u32[]{:S(2)}, u32[]{:S(2)}) collective-permute-start(bf16[8,2,64,384]{3,2,0,1:T(8,128)(2,1)S(1)} %pad_maximum_fusion.4), channel_id=1, source_target_pairs={{0,1},{1,0},{2,3},{3,2},{4,5},{5,4},{6,7},{7,6},{8,9},{9,8},{10,11... | collective-permute-start | bytes 2359304 | tf_op jit(solution)/shard_map/ppermute | solution.py:143
  50.2 2.4 %collective-permute-start.1 = (bf16[8,2,65,384]{3,0,2,1:T(8,128)(2,1)S(1)}, bf16[8,2,65,384]{3,0,2,1:T(8,128)(2,1)S(1)}, u32[]{:S(2)}, u32[]{:S(2)}) collective-permute-start(bf16[8,2,65,384]{3,0,2,1:T(8,128)(2,1)S(1)} %pad_maximum_fusion.3), channel_id=1, source_target_pairs={{0,1},{1,0},{2,3},{3,2},{4,5},{5,4},{6,7},{7,6},{8,9},{9,8},{10,11... | collective-permute-start | bytes 2396168 | tf_op jit(solution)/shard_map/ppermute | solution.py:143
  56.9 30.1 %copy-start.1 = (bf16[512,64]{0,1:T(8,128)(2,1)S(1)}, bf16[512,64]{0,1:T(8,128)(2,1)}, u32[]{:S(2)}) copy-start(bf16[512,64]{0,1:T(8,128)(2,1)} %param.6) | copy-start | bytes 196612
  73.2 13.1 %all-to-all-start.2 = ((f32[8,1,256]{2,1,0:T(1,128)}), f32[8,1,256]{2,1,0:T(1,128)S(1)}, u32[]{:S(2)}, u32[]{:S(2)}) async-start(f32[8,1,256]{2,1,0:T(1,128)} %bitcast.102), calls=%async_computation.2 | async-start | bytes 16384 | tf_op jit(solution)/shard_map/all_to_all | solution.py:158

commit v8 on v7

--- a/solution.py
+++ b/solution.py
@@ -15,11 +15,9 @@
     return moved.reshape((moved.shape[0], moved.shape[1] * moved.shape[2]) + moved.shape[3:])
 
 
-def affinity_kernel(row_keys, col_keys, low_picked, high_picked, low_rows, high_rows, weights, row_sums):
+def affinity_kernel(row_keys, col_keys, picked, rows, weights, row_sums):
     contract = (((1,), (1,)), ((), ()))
-    gram = lax.dot_general(
-        low_picked[...], low_rows[...], contract, preferred_element_type=jnp.float32
-    ) + lax.dot_general(high_picked[...], high_rows[...], contract, preferred_element_type=jnp.float32)
+    gram = lax.dot_general(picked[...], rows[...], contract, preferred_element_type=jnp.float32)
     keep = jnp.abs(row_keys[...] - col_keys[...]) <= BAND
     positive = jnp.maximum(gram, 0.0)
     cubed = jnp.where(keep, positive * positive * positive, 0.0).astype(jnp.bfloat16)
@@ -29,20 +27,17 @@
     row_sums[...] = summed[0:1, :]
 
 
-def fused_affinity(low, high, keys):
-    slot_count = low.shape[0]
+def fused_affinity(rows, keys):
+    slot_count, width = rows.shape
     block_rows = min(256, slot_count)
-    width = low.shape[1] + high.shape[1]
     return pl.pallas_call(
         affinity_kernel,
         grid=(slot_count // block_rows,),
         in_specs=[
             pl.BlockSpec((block_rows, 1), lambda i: (i, 0)),
             pl.BlockSpec((1, slot_count), lambda i: (0, 0)),
-            pl.BlockSpec((block_rows, low.shape[1]), lambda i: (i, 0)),
-            pl.BlockSpec((block_rows, high.shape[1]), lambda i: (i, 0)),
-            pl.BlockSpec((slot_count, low.shape[1]), lambda i: (0, 0)),
-            pl.BlockSpec((slot_count, high.shape[1]), lambda i: (0, 0)),
+            pl.BlockSpec((block_rows, width), lambda i: (i, 0)),
+            pl.BlockSpec((slot_count, width), lambda i: (0, 0)),
         ],
         out_specs=[
             pl.BlockSpec((block_rows, slot_count), lambda i: (i, 0)),
@@ -58,7 +53,7 @@
             transcendentals=0,
             bytes_accessed=2 * slot_count * width * 2 + 2 * slot_count * slot_count,
         ),
-    )(keys.reshape(slot_count, 1), keys.reshape(1, slot_count), low, high, low, high)
+    )(keys.reshape(slot_count, 1), keys.reshape(1, slot_count), rows, rows)
 
 
 def on_device(embeddings, labels, image_lists, rank_keys):
@@ -150,10 +145,11 @@
         high_got = exchange_stage(high_got, bit)
         bit //= 2
     slot_count = slot_total
-    low_rows = low_got[:, :, :part, :].reshape(slot_count, half)
-    high_rows = high_got.reshape(slot_count, width - half)
+    rows = jnp.concatenate(
+        [low_got[:, :, :part, :], high_got], axis=3
+    ).reshape(slot_count, width)
     key_rows = low_got[:, :, part, :part].reshape(slot_count).astype(jnp.float32)
-    weight_mat, row_sums = fused_affinity(low_rows, high_rows, key_rows)
+    weight_mat, row_sums = fused_affinity(rows, key_rows)
     weights = weight_mat.reshape(1, slot_count, slot_count)
     degree_slots = lax.all_to_all(
         bucket_major(row_sums), "img", split_axis=0, concat_axis=0, tiled=True

time: 165 us -> 165 us (level)
  blocking collectives: 57.1 us -> 77.5 us
  waiting for transfers between devices: 34.3 us -> 22.3 us
  starting transfers between devices: 20.7 us -> 12.8 us
  other arithmetic: 5.68 us -> 7.76 us
  Pallas kernels: 16.3 us -> 14.4 us
    all_to_all x0 -> x1, blocking collectives: none -> 20 us  [on_device(): lax.all_to_all(low_payload, 'img', split_axis=0, concat_axis=0, tiled=True)]
    all_to_all x1 -> x0, waiting for transfers between devices: 11.1 us -> none  [on_device(): lax.all_to_all(low_payload, 'img', split_axis=0, concat_axis=0, tiled=True)]
    all_to_all x1, starting transfers between devices: 7.28 us -> 3.45 us  [on_device(): lax.all_to_all(high_payload, 'img', split_axis=0, concat_axis=0, tiled=True)]
    all_to_all x1 -> x0, starting transfers between devices: 3.63 us -> none  [on_device(): lax.all_to_all(low_payload, 'img', split_axis=0, concat_axis=0, tiled=True)]
    pallas_call x1, Pallas kernels: 16.3 us -> 14.4 us  [fused_affinity(): pl.pallas_call(affinity_kernel, grid=(slot_count // block_rows,), in_spec...]
    concatenate x0 -> x1, other arithmetic: none -> 1.67 us  [on_device(): jnp.concatenate([low_got[:, :, :part, :], high_got], axis=3)]
  transfers between devices with their start and end apart: 7 -> 6, of which waited for: 5 -> 3; matrix products, arithmetic and copies ran while one was open for 2% -> 3% of each run, Pallas kernels for 0% -> 0%
where the time goes in v8:
time: 165 us; the launch traced here: 164 us
  blocking collectives  77.5 us (47%)
  waiting for transfers between devices  22.3 us (14%)
  matrix products  20.6 us (12%)
  Pallas kernels  14.4 us (9%)
  starting transfers between devices  12.8 us (8%)
  local copies, waits for them, and re-layouts  8.7 us (5%)
  other arithmetic  7.76 us (5%)
    all_to_all x2, blocking collectives, on_device(): lax.all_to_all(bucket_major(product), 'img', split_axis=0, concat_axis=0,...  34.6 us
    all_to_all x2, blocking collectives, on_device(): lax.all_to_all(to_bucket(scaled), 'img', split_axis=0, concat_axis=0, til...  22.9 us
    all_to_all x1, blocking collectives, on_device(): lax.all_to_all(low_payload, 'img', split_axis=0, concat_axis=0, tiled=True)  20 us
    pallas_call x1, Pallas kernels, fused_affinity(): pl.pallas_call(affinity_kernel, grid=(slot_count // block_rows,), in_spec...  14.4 us
    dot_general x2, matrix products, on_device(): jnp.einsum('ajk,akc->ajc', weights, list_major(arrived), preferred_elemen...  12.1 us
    all_to_all x1, waiting for transfers between devices, on_device(): lax.all_to_all(high_payload, 'img', split_axis=0, concat_axis=0, tiled=True)  9.83 us
    all_to_all x1, waiting for transfers between devices, on_device(): lax.all_to_all(bucket_major(row_sums), 'img', split_axis=0, concat_axis=0...  6.36 us
    all_to_all x1, starting transfers between devices, on_device(): lax.all_to_all(bucket_major(row_sums), 'img', split_axis=0, concat_axis=0...  6.15 us
  transfers between devices with their start and end apart: 6, of which 3 were waited for; matrix products, arithmetic and copies ran while one was open for 3% of the time, Pallas kernels for 0%

profile of v8, /device:TPU:0, one launch (start us, length us, event | category | flops | bytes accessed | tf_op | source)
XLA Modules:
  0.0 164.3 jit_solution(5757020055293582011)
XLA Ops:
  0.0 0.8 copy.73
  0.8 0.2 eq.32
  1.0 0.5 convert_reduce_fusion
  1.5 0.2 reduce_sum.39
  1.7 0.1 copy.74
  1.9 0.7 multiply_add_fusion
  2.6 0.1 iota_add_fusion.1
  2.7 0.1 add.108
  2.7 0.7 convert_element_type.81
  3.4 0.4 fusion.12
  3.8 0.3 fusion.10
  4.2 0.1 convert_element_type.96
  4.3 1.4 fusion.2
  5.6 1.9 %convolution_convert_fusion.2 = bf16[512,768]{1,0:T(8,128)(2,1)S(1)} fusion(bf16[512,768]{1,0:T(8,128)(2,1)} %param.5, f32[512]{0:T(512)S(1)} %add_rsqrt_fusion, s32[512]{0:T(512)S(1)} %bitcast.91, s32[512]{0:T(512)S(1)} %bitcast.83, s32[512]{0:T(512)S(1)} %add.108), kind=kOutput, calls=%fused_computation.14 | convolution fusion | flops 405012480 | bytes 1581056 | tf_op jit(solution)/shard_map/dot_general | solution.py:124
  7.5 0.0 copy-start.1
  7.5 0.9 fusion.22
  8.4 20.0 %all_to_all.35 = bf16[8,65,384]{2,1,0:T(8,128)(2,1)S(1)} all-to-all(bf16[8,65,384]{2,1,0:T(8,128)(2,1)S(1)} %fusion.18), channel_id=1, replica_groups=mesh['img'=8,'sub'=4] {'img'}, dimensions={0} | all-to-all | bytes 798720 | tf_op jit(solution)/shard_map/all_to_all | solution.py:140
  28.5 3.5 %all-to-all-start.1 = ((bf16[8,64,384]{2,1,0:T(8,128)(2,1)}), bf16[8,64,384]{2,1,0:T(8,128)(2,1)S(1)}, u32[]{:S(2)}, u32[]{:S(2)}) async-start(bf16[8,64,384]{2,1,0:T(8,128)(2,1)} %get-tuple-element.9), calls=%async_computation.1 | async-start | bytes 786432 | tf_op jit(solution)/shard_map/all_to_all | solution.py:141
  32.0 1.6 collective-permute-start
  33.5 9.8 %all-to-all-done.1 = bf16[8,64,384]{2,1,0:T(8,128)(2,1)S(1)} async-done(((bf16[8,64,384]{2,1,0:T(8,128)(2,1)}), bf16[8,64,384]{2,1,0:T(8,128)(2,1)S(1)}, u32[]{:S(2)}, u32[]{:S(2)}) %all-to-all-start.1) | async-done | bytes 393248 | tf_op jit(solution)/shard_map/all_to_all | solution.py:141
  43.4 0.2 copy.81
  43.6 1.6 collective-permute-start.2
  45.2 0.0 collective-permute-done
  45.2 0.1 pad_maximum_fusion.2
  45.3 0.1 collective-permute-start.1
  45.3 6.1 %collective-permute-done.2 = bf16[8,1,64,384]{3,0,2,1:T(8,128)(2,1)S(1)} collective-permute-done((bf16[8,1,64,384]{3,0,2,1:T(8,128)(2,1)S(1)}, bf16[8,1,64,384]{3,0,2,1:T(8,128)(2,1)S(1)}, u32[]{:S(2)}, u32[]{:S(2)}) %collective-permute-start.2) | collective-permute-done | bytes 393248 | tf_op jit(solution)/shard_map/ppermute | solution.py:138
  51.5 1.0 pad_maximum_fusion.3
  52.4 0.0 collective-permute-start.3
  52.4 0.0 copy-done.1
  52.5 0.1 broadcast_add_fusion
  52.5 0.0 collective-permute-done.1
  52.5 2.0 %reshape.208.row_keys = f32[2048,1]{1,0:T(8,128)} reshape(f32[8,4,1,64]{3,1,0,2:T(4,128)S(1)} %copy.77) | data formatting | bytes 16384 | tf_op jit(solution)/shard_map/convert_element_type | solution.py:151
  54.5 0.7 reshape.205.col_keys
  55.2 0.0 collective-permute-done.3
  55.2 1.7 %fusion.1 = bf16[8,4,64,768]{3,0,2,1:T(8,128)(2,1)S(1)} fusion(bf16[8,2,65,384]{3,0,2,1:T(8,128)(2,1)S(1)} %collective-permute-done.1, bf16[8,1,65,384]{3,0,2,1:T(8,128)(2,1)S(1)} %collective-permute-done, bf16[8,1,65,384]{3,0,2,1:T(8,128)(2,1)S(1)} %bitcast.67, bf16[8,2,64,384]{3,0,2,1:T(8,128)(2,1)S(1)} %collective-permute-done.3, ...), kind=kLoop, calls=%fused_computation.6 | loop fusion | flops 18874368 | bytes 6316032 | tf_op jit(solution)/shard_map/concatenate | solution.py:148
  56.9 2.5 %copy.82 = bf16[8,4,64,768]{3,2,1,0:T(8,128)(2,1)} copy(bf16[8,4,64,768]{3,0,2,1:T(8,128)(2,1)S(1)} %fusion.1) | data formatting | bytes 6291456 | tf_op jit(solution)/shard_map/concatenate | solution.py:148
  59.4 0.0 copy-start
  59.4 14.4 %shard_map.55 = (bf16[2048,2048]{1,0:T(8,128)(2,1)}, f32[1,2048]{1,0:T(1,128)}) custom-call(f32[2048,1]{1,0:T(8,128)} %reshape.208.row_keys, f32[1,2048]{1,0:T(1,128)} %reshape.205.col_keys, bf16[2048,768]{1,0:T(8,128)(2,1)} %bitcast.68, bf16[2048,768]{1,0:T(8,128)(2,1)} %bitcast.69), custom_call_target="tpu_custom_call" | custom-call | flops 6534725632 | bytes 14680064 | tf_op jit(solution)/shard_map/pallas_call | solution.py:33
  73.8 6.1 %all-to-all-start.2 = ((f32[8,1,256]{2,1,0:T(1,128)}), f32[8,1,256]{2,1,0:T(1,128)S(1)}, u32[]{:S(2)}, u32[]{:S(2)}) async-start(f32[8,1,256]{2,1,0:T(1,128)} %bitcast.97), calls=%async_computation.2 | async-start | bytes 16384 | tf_op jit(solution)/shard_map/all_to_all | solution.py:154
  79.9 0.1 iota_add_fusion
  80.0 0.1 add.102
  80.1 6.4 %all-to-all-done.2 = f32[8,1,256]{2,1,0:T(1,128)S(1)} async-done(((f32[8,1,256]{2,1,0:T(1,128)}), f32[8,1,256]{2,1,0:T(1,128)S(1)}, u32[]{:S(2)}, u32[]{:S(2)}) %all-to-all-start.2) | async-done | bytes 8224 | tf_op jit(solution)/shard_map/all_to_all | solution.py:154
  86.4 0.7 select_reduce_fusion
  87.2 0.0 copy-done
  87.2 1.3 convolution_convert_fusion.1
  88.5 0.1 copy.94
  88.6 10.9 %all_to_all.36 = bf16[8,1,256,64]{2,3,1,0:T(8,128)(2,1)S(1)} all-to-all(bf16[8,1,256,64]{2,3,1,0:T(8,128)(2,1)S(1)} %copy.85), channel_id=1, replica_groups=mesh['img'=8,'sub'=4] {'img'}, dimensions={0} | all-to-all | bytes 524288 | tf_op jit(solution)/shard_map/all_to_all | solution.py:163
  99.5 0.1 copy.86
  99.7 0.1 reshape.206
  99.8 6.0 %convolution_bitcast_fusion.1 = f32[8,1,256,64]{2,3,1,0:T(8,128)S(1)} fusion(bf16[8,256,2048]{2,1,0:T(8,128)(2,1)} %bitcast.62, bf16[2048,64,1]{0,1,2:T(8,128)(2,1)S(1)} %reshape.206), kind=kOutput, calls=%fused_computation.19 | convolution fusion | flops 536870912 | bytes 9175040 | tf_op jit(solution)/shard_map/ajk,akc->ajc/dot_general | solution.py:164
  105.8 17.3 %all_to_all.37 = f32[8,1,256,64]{2,3,1,0:T(8,128)S(1)} all-to-all(f32[8,1,256,64]{2,3,1,0:T(8,128)S(1)} %convolution_bitcast_fusion.1), channel_id=1, replica_groups=mesh['img'=8,'sub'=4] {'img'}, dimensions={0} | all-to-all | bytes 1048576 | tf_op jit(solution)/shard_map/all_to_all | solution.py:167
  123.1 1.7 %fusion.7 = bf16[512,64]{0,1:T(8,128)(2,1)S(1)} fusion(f32[2048,64]{0,1:T(8,128)S(1)} %bitcast.77, bf16[512,64]{0,1:T(8,128)(2,1)S(1)} %copy-done, f32[512]{0:T(512)S(1)} %get-tuple-element.16, f32[512]{0:T(512)S(1)} %get-tuple-element.15, s32[512]{0:T(512)S(1)} %bitcast.94, s32[512]{0:T(512)S(1)} %bitcast.86, s32[2048]{0:T(1024)S(1)} %add.102), kind=kOutput, calls=%fused_computation.25 | convolution fusion | flops 808648704 | bytes 671744 | tf_op jit(solution)/shard_map/kg,kc->gc/dot_general | solution.py:100
  124.9 1.3 convolution_convert_fusion
  126.2 0.1 copy.96
  126.3 12.0 %all_to_all.38 = bf16[8,1,256,64]{2,3,1,0:T(8,128)(2,1)S(1)} all-to-all(bf16[8,1,256,64]{2,3,1,0:T(8,128)(2,1)S(1)} %copy.89), channel_id=1, replica_groups=mesh['img'=8,'sub'=4] {'img'}, dimensions={0} | all-to-all | bytes 524288 | tf_op jit(solution)/shard_map/all_to_all | solution.py:163
  138.2 0.1 copy.90
  138.4 0.1 reshape.207
  138.5 6.0 %convolution_bitcast_fusion = f32[8,1,256,64]{2,3,1,0:T(8,128)S(1)} fusion(bf16[8,256,2048]{2,1,0:T(8,128)(2,1)} %bitcast.63, bf16[2048,64,1]{0,1,2:T(8,128)(2,1)S(1)} %reshape.207), kind=kOutput, calls=%fused_computation.18 | convolution fusion | flops 536870912 | bytes 9175040 | tf_op jit(solution)/shard_map/ajk,akc->ajc/dot_general | solution.py:164
  144.6 17.3 %all_to_all.39 = f32[8,1,256,64]{2,3,1,0:T(8,128)S(1)} all-to-all(f32[8,1,256,64]{2,3,1,0:T(8,128)S(1)} %convolution_bitcast_fusion), channel_id=1, replica_groups=mesh['img'=8,'sub'=4] {'img'}, dimensions={0} | all-to-all | bytes 1048576 | tf_op jit(solution)/shard_map/all_to_all | solution.py:167
  161.9 2.4 %fusion.8 = bf16[512,64]{0,1:T(8,128)(2,1)} fusion(f32[2048,64]{0,1:T(8,128)S(1)} %bitcast.76, bf16[512,64]{0,1:T(8,128)(2,1)S(1)} %copy-done, f32[512]{0:T(512)S(1)} %get-tuple-element.15, s32[512]{0:T(512)S(1)} %bitcast.96, s32[512]{0:T(512)S(1)} %bitcast.88, s32[2048]{0:T(1024)S(1)} %add.102), kind=kOutput, calls=%fused_computation.26 | convolution fusion | flops 808615936 | bytes 669696 | tf_op jit(solution)/shard_map/kg,kc->gc/dot_general | solution.py:100
  (16 shorter events, 0.3 us)
Async XLA Ops:
  7.5 44.9 %copy-start.1 = (s32[4]{0:T(128)S(1)}, s32[4]{0:T(128)}, u32[]{:S(2)}) copy-start(s32[4]{0:T(128)} %constant.11.clone) | copy-start | bytes 52
  28.5 14.9 %all-to-all-start.1 = ((bf16[8,64,384]{2,1,0:T(8,128)(2,1)}), bf16[8,64,384]{2,1,0:T(8,128)(2,1)S(1)}, u32[]{:S(2)}, u32[]{:S(2)}) async-start(bf16[8,64,384]{2,1,0:T(8,128)(2,1)} %get-tuple-element.9), calls=%async_computation.1 | async-start | bytes 786432 | tf_op jit(solution)/shard_map/all_to_all | solution.py:141
  32.0 13.2 %collective-permute-start = (bf16[8,1,65,384]{3,0,2,1:T(8,128)(2,1)S(1)}, bf16[8,1,65,384]{3,0,2,1:T(8,128)(2,1)S(1)}, u32[]{:S(2)}, u32[]{:S(2)}) collective-permute-start(bf16[8,1,65,384]{3,0,2,1:T(8,128)(2,1)S(1)} %bitcast.64), channel_id=1, source_target_pairs={{0,2},{1,3},{2,0},{3,1},{4,6},{5,7},{6,4},{7,5},{8,10},{9,11},{10,... | collective-permute-start | bytes 1198088 | tf_op jit(solution)/shard_map/ppermute | solution.py:138
  43.6 7.8 %collective-permute-start.2 = (bf16[8,1,64,384]{3,0,2,1:T(8,128)(2,1)S(1)}, bf16[8,1,64,384]{3,0,2,1:T(8,128)(2,1)S(1)}, u32[]{:S(2)}, u32[]{:S(2)}) collective-permute-start(bf16[8,1,64,384]{3,0,2,1:T(8,128)(2,1)S(1)} %copy.81), channel_id=1, source_target_pairs={{0,2},{1,3},{2,0},{3,1},{4,6},{5,7},{6,4},{7,5},{8,10},{9,11},{10,... | collective-permute-start | bytes 1179656 | tf_op jit(solution)/shard_map/ppermute | solution.py:138
  45.3 7.3 %collective-permute-start.1 = (bf16[8,2,65,384]{3,0,2,1:T(8,128)(2,1)S(1)}, bf16[8,2,65,384]{3,0,2,1:T(8,128)(2,1)S(1)}, u32[]{:S(2)}, u32[]{:S(2)}) collective-permute-start(bf16[8,2,65,384]{3,0,2,1:T(8,128)(2,1)S(1)} %pad_maximum_fusion.2), channel_id=1, source_target_pairs={{0,1},{1,0},{2,3},{3,2},{4,5},{5,4},{6,7},{7,6},{8,9},{9,8},{10,11... | collective-permute-start | bytes 2396168 | tf_op jit(solution)/shard_map/ppermute | solution.py:138
  52.4 2.8 %collective-permute-start.3 = (bf16[8,2,64,384]{3,0,2,1:T(8,128)(2,1)}, bf16[8,2,64,384]{3,0,2,1:T(8,128)(2,1)S(1)}, u32[]{:S(2)}, u32[]{:S(2)}) collective-permute-start(bf16[8,2,64,384]{3,0,2,1:T(8,128)(2,1)} %pad_maximum_fusion.3), channel_id=1, source_target_pairs={{0,1},{1,0},{2,3},{3,2},{4,5},{5,4},{6,7},{7,6},{8,9},{9,8},{10,11... | collective-permute-start | bytes 2359304 | tf_op jit(solution)/shard_map/ppermute | solution.py:138
  59.4 27.8 %copy-start = (bf16[512,64]{0,1:T(8,128)(2,1)S(1)}, bf16[512,64]{0,1:T(8,128)(2,1)}, u32[]{:S(2)}) copy-start(bf16[512,64]{0,1:T(8,128)(2,1)} %param.6) | copy-start | bytes 196612
  73.8 12.7 %all-to-all-start.2 = ((f32[8,1,256]{2,1,0:T(1,128)}), f32[8,1,256]{2,1,0:T(1,128)S(1)}, u32[]{:S(2)}, u32[]{:S(2)}) async-start(f32[8,1,256]{2,1,0:T(1,128)} %bitcast.97), calls=%async_computation.2 | async-start | bytes 16384 | tf_op jit(solution)/shard_map/all_to_all | solution.py:154

commit v9 on v8

--- a/solution.py
+++ b/solution.py
@@ -29,7 +29,7 @@
 
 def fused_affinity(rows, keys):
     slot_count, width = rows.shape
-    block_rows = min(256, slot_count)
+    block_rows = min(512, slot_count)
     return pl.pallas_call(
         affinity_kernel,
         grid=(slot_count // block_rows,),
@@ -54,6 +54,31 @@
             bytes_accessed=2 * slot_count * width * 2 + 2 * slot_count * slot_count,
         ),
     )(keys.reshape(slot_count, 1), keys.reshape(1, slot_count), rows, rows)
+
+
+def product_kernel(weights, scaled_rows, product):
+    product[...] = jnp.dot(weights[...], scaled_rows[...], preferred_element_type=jnp.float32)
+
+
+def weighted_sum(weights, scaled_rows):
+    slot_count, channels = scaled_rows.shape
+    block_rows = min(512, slot_count)
+    return pl.pallas_call(
+        product_kernel,
+        grid=(slot_count // block_rows,),
+        in_specs=[
+            pl.BlockSpec((block_rows, slot_count), lambda i: (i, 0)),
+            pl.BlockSpec((slot_count, channels), lambda i: (0, 0)),
+        ],
+        out_specs=pl.BlockSpec((block_rows, channels), lambda i: (i, 0)),
+        out_shape=jax.ShapeDtypeStruct((slot_count, channels), jnp.float32),
+        compiler_params=pltpu.CompilerParams(dimension_semantics=("arbitrary",)),
+        cost_estimate=pl.CostEstimate(
+            flops=2 * slot_count * slot_count * channels,
+            transcendentals=0,
+            bytes_accessed=2 * slot_count * slot_count + 6 * slot_count * channels,
+        ),
+    )(weights, scaled_rows)
 
 
 def on_device(embeddings, labels, image_lists, rank_keys):
@@ -150,7 +175,6 @@
     ).reshape(slot_count, width)
     key_rows = low_got[:, :, part, :part].reshape(slot_count).astype(jnp.float32)
     weight_mat, row_sums = fused_affinity(rows, key_rows)
-    weights = weight_mat.reshape(1, slot_count, slot_count)
     degree_slots = lax.all_to_all(
         bucket_major(row_sums), "img", split_axis=0, concat_axis=0, tiled=True
     )
@@ -161,9 +185,7 @@
     for step in range(2):
         scaled = (inv[:, None] * current).astype(jnp.bfloat16)
         arrived = lax.all_to_all(to_bucket(scaled), "img", split_axis=0, concat_axis=0, tiled=True)
-        product = jnp.einsum(
-            "ajk,akc->ajc", weights, list_major(arrived), preferred_element_type=jnp.float32
-        )
+        product = weighted_sum(weight_mat, list_major(arrived)[0])[None]
         returned = lax.all_to_all(
             bucket_major(product), "img", split_axis=0, concat_axis=0, tiled=True
         )

time: 165 us -> 170 us (1.030)
  matrix products: 20.6 us -> 8.54 us
  Pallas kernels: 14.4 us -> 26.4 us
  local copies, waits for them, and re-layouts: 8.7 us -> 13.3 us
    pallas_call x0 -> x2, Pallas kernels: none -> 12.8 us  [weighted_sum(): pl.pallas_call(product_kernel, grid=(slot_count // block_rows,), in_specs...]
    dot_general x2 -> x0, matrix products: 12.1 us -> none  [on_device(): jnp.einsum('ajk,akc->ajc', weights, list_major(arrived), preferred_elemen...]
    another operation x2, local copies, waits for them, and re-layouts: 0.25 us -> 3.07 us  [bucket_major(): return jnp.moveaxis(shaped, 0, 1)]
    all_to_all x2, local copies, waits for them, and re-layouts: 0.3 us -> 2.02 us  [on_device(): lax.all_to_all(to_bucket(scaled), 'img', split_axis=0, concat_axis=0, til...]
where the time goes in v9:
time: 170 us; the launch traced here: 169 us
  blocking collectives  77.5 us (46%)
  Pallas kernels  26.4 us (16%)
  waiting for transfers between devices  22.3 us (13%)
  local copies, waits for them, and re-layouts  13.3 us (8%)
  starting transfers between devices  12.8 us (8%)
  matrix products  8.54 us (5%)
  other arithmetic  7.76 us (5%)
    all_to_all x2, blocking collectives, on_device(): lax.all_to_all(bucket_major(product), 'img', split_axis=0, concat_axis=0,...  34.6 us
    all_to_all x2, blocking collectives, on_device(): lax.all_to_all(to_bucket(scaled), 'img', split_axis=0, concat_axis=0, til...  22.9 us
    all_to_all x1, blocking collectives, on_device(): lax.all_to_all(low_payload, 'img', split_axis=0, concat_axis=0, tiled=True)  20 us
    pallas_call x1, Pallas kernels, fused_affinity(): pl.pallas_call(affinity_kernel, grid=(slot_count // block_rows,), in_spec...  13.7 us
    pallas_call x2, Pallas kernels, weighted_sum(): pl.pallas_call(product_kernel, grid=(slot_count // block_rows,), in_specs...  12.8 us
    all_to_all x1, waiting for transfers between devices, on_device(): lax.all_to_all(high_payload, 'img', split_axis=0, concat_axis=0, tiled=True)  9.83 us
    all_to_all x1, waiting for transfers between devices, on_device(): lax.all_to_all(bucket_major(row_sums), 'img', split_axis=0, concat_axis=0...  6.36 us
    all_to_all x1, starting transfers between devices, on_device(): lax.all_to_all(bucket_major(row_sums), 'img', split_axis=0, concat_axis=0...  6.14 us
  transfers between devices with their start and end apart: 6, of which 3 were waited for; matrix products, arithmetic and copies ran while one was open for 3% of the time, Pallas kernels for 0%

profile of v9, /device:TPU:0, one launch (start us, length us, event | category | flops | bytes accessed | tf_op | source)
XLA Modules:
  0.0 168.8 jit_solution(14680872417383897283)
XLA Ops:
  0.0 0.8 copy.94
  0.8 0.2 eq.32
  1.0 0.5 convert_reduce_fusion
  1.5 0.2 reduce_sum.39
  1.7 0.1 copy.95
  1.9 0.7 multiply_add_fusion
  2.6 0.1 iota_add_fusion.1
  2.7 0.1 add.108
  2.7 0.7 convert_element_type.81
  3.4 0.4 fusion.12
  3.8 0.3 fusion.10
  4.2 0.1 convert_element_type.96
  4.3 1.4 fusion.2
  5.6 1.9 %convolution_convert_fusion.2 = bf16[512,768]{1,0:T(8,128)(2,1)S(1)} fusion(bf16[512,768]{1,0:T(8,128)(2,1)} %param.5, f32[512]{0:T(512)S(1)} %add_rsqrt_fusion, s32[512]{0:T(512)S(1)} %bitcast.76, s32[512]{0:T(512)S(1)} %bitcast.68, s32[512]{0:T(512)S(1)} %add.108), kind=kOutput, calls=%fused_computation.14 | convolution fusion | flops 405012480 | bytes 1581056 | tf_op jit(solution)/shard_map/dot_general | solution.py:149
  7.5 0.0 copy-start.1
  7.5 0.9 fusion.22
  8.4 20.0 %all_to_all.35 = bf16[8,65,384]{2,1,0:T(8,128)(2,1)S(1)} all-to-all(bf16[8,65,384]{2,1,0:T(8,128)(2,1)S(1)} %fusion.18), channel_id=1, replica_groups=mesh['img'=8,'sub'=4] {'img'}, dimensions={0} | all-to-all | bytes 798720 | tf_op jit(solution)/shard_map/all_to_all | solution.py:165
  28.5 3.5 %all-to-all-start.1 = ((bf16[8,64,384]{2,1,0:T(8,128)(2,1)}), bf16[8,64,384]{2,1,0:T(8,128)(2,1)S(1)}, u32[]{:S(2)}, u32[]{:S(2)}) async-start(bf16[8,64,384]{2,1,0:T(8,128)(2,1)} %get-tuple-element.9), calls=%async_computation.1 | async-start | bytes 786432 | tf_op jit(solution)/shard_map/all_to_all | solution.py:166
  32.0 1.6 collective-permute-start
  33.5 9.8 %all-to-all-done.1 = bf16[8,64,384]{2,1,0:T(8,128)(2,1)S(1)} async-done(((bf16[8,64,384]{2,1,0:T(8,128)(2,1)}), bf16[8,64,384]{2,1,0:T(8,128)(2,1)S(1)}, u32[]{:S(2)}, u32[]{:S(2)}) %all-to-all-start.1) | async-done | bytes 393248 | tf_op jit(solution)/shard_map/all_to_all | solution.py:166
  43.4 0.2 copy.102
  43.6 1.6 collective-permute-start.2
  45.2 0.0 collective-permute-done
  45.2 0.1 pad_maximum_fusion.2
  45.3 0.1 collective-permute-start.1
  45.3 6.1 %collective-permute-done.2 = bf16[8,1,64,384]{3,0,2,1:T(8,128)(2,1)S(1)} collective-permute-done((bf16[8,1,64,384]{3,0,2,1:T(8,128)(2,1)S(1)}, bf16[8,1,64,384]{3,0,2,1:T(8,128)(2,1)S(1)}, u32[]{:S(2)}, u32[]{:S(2)}) %collective-permute-start.2) | collective-permute-done | bytes 393248 | tf_op jit(solution)/shard_map/ppermute | solution.py:163
  51.5 1.0 pad_maximum_fusion.3
  52.4 0.0 collective-permute-start.3
  52.4 0.0 copy-done.1
  52.5 0.1 broadcast_add_fusion
  52.5 0.0 collective-permute-done.1
  52.5 2.0 %reshape.174.row_keys = f32[2048,1]{1,0:T(8,128)} reshape(f32[8,4,1,64]{3,1,0,2:T(4,128)S(1)} %copy.98) | data formatting | bytes 16384 | tf_op jit(solution)/shard_map/convert_element_type | solution.py:176
  54.5 0.7 reshape.173.col_keys
  55.2 0.0 collective-permute-done.3
  55.2 1.7 fusion.1
  56.9 2.5 %copy.103 = bf16[8,4,64,768]{3,2,1,0:T(8,128)(2,1)} copy(bf16[8,4,64,768]{3,0,2,1:T(8,128)(2,1)S(1)} %fusion.1) | data formatting | bytes 6291456 | tf_op jit(solution)/shard_map/concatenate | solution.py:173
  59.4 0.0 copy-start
  59.4 13.7 %shard_map.55 = (bf16[2048,2048]{1,0:T(8,128)(2,1)}, f32[1,2048]{1,0:T(1,128)}) custom-call(f32[2048,1]{1,0:T(8,128)} %reshape.174.row_keys, f32[1,2048]{1,0:T(1,128)} %reshape.173.col_keys, bf16[2048,768]{1,0:T(8,128)(2,1)} %bitcast.51, bf16[2048,768]{1,0:T(8,128)(2,1)} %bitcast.52), custom_call_target="tpu_custom_call" | custom-call | flops 6534725632 | bytes 14680064 | tf_op jit(solution)/shard_map/pallas_call | solution.py:33
  73.0 6.1 %all-to-all-start.2 = ((f32[8,1,256]{2,1,0:T(1,128)}), f32[8,1,256]{2,1,0:T(1,128)S(1)}, u32[]{:S(2)}, u32[]{:S(2)}) async-start(f32[8,1,256]{2,1,0:T(1,128)} %bitcast.82), calls=%async_computation.2 | async-start | bytes 16384 | tf_op jit(solution)/shard_map/all_to_all | solution.py:178
  79.2 0.1 iota_add_fusion
  79.2 0.1 add.102
  79.3 6.4 %all-to-all-done.2 = f32[8,1,256]{2,1,0:T(1,128)S(1)} async-done(((f32[8,1,256]{2,1,0:T(1,128)}), f32[8,1,256]{2,1,0:T(1,128)S(1)}, u32[]{:S(2)}, u32[]{:S(2)}) %all-to-all-start.2) | async-done | bytes 8224 | tf_op jit(solution)/shard_map/all_to_all | solution.py:178
  85.7 0.7 select_reduce_fusion
  86.4 0.0 copy-done
  86.4 1.3 convolution_convert_fusion.1
  87.7 0.1 copy.115
  87.8 10.9 %all_to_all.36 = bf16[8,1,256,64]{2,3,1,0:T(8,128)(2,1)S(1)} all-to-all(bf16[8,1,256,64]{2,3,1,0:T(8,128)(2,1)S(1)} %copy.106), channel_id=1, replica_groups=mesh['img'=8,'sub'=4] {'img'}, dimensions={0} | all-to-all | bytes 524288 | tf_op jit(solution)/shard_map/all_to_all | solution.py:187
  98.7 1.0 copy.107
  99.8 6.4 %shard_map.56 = f32[2048,64]{1,0:T(8,128)} custom-call(bf16[2048,2048]{1,0:T(8,128)(2,1)} %get-tuple-element.8.weights, bf16[2048,64]{1,0:T(8,128)(2,1)} %bitcast.53), custom_call_target="tpu_custom_call" | custom-call | flops 536870912 | bytes 9175040 | tf_op jit(solution)/shard_map/pallas_call | solution.py:66
  106.1 1.5 copy.108
  107.7 17.3 %all_to_all.37 = f32[8,1,256,64]{2,3,1,0:T(8,128)S(1)} all-to-all(f32[8,1,256,64]{2,3,1,0:T(8,128)S(1)} %copy.108), channel_id=1, replica_groups=mesh['img'=8,'sub'=4] {'img'}, dimensions={0} | all-to-all | bytes 1048576 | tf_op jit(solution)/shard_map/all_to_all | solution.py:189
  125.0 1.7 %fusion.7 = bf16[512,64]{0,1:T(8,128)(2,1)S(1)} fusion(f32[2048,64]{0,1:T(8,128)S(1)} %bitcast.62, bf16[512,64]{0,1:T(8,128)(2,1)S(1)} %copy-done, f32[512]{0:T(512)S(1)} %get-tuple-element.16, f32[512]{0:T(512)S(1)} %get-tuple-element.15, s32[512]{0:T(512)S(1)} %bitcast.79, s32[512]{0:T(512)S(1)} %bitcast.71, s32[2048]{0:T(1024)S(1)} %add.102), kind=kOutput, calls=%fused_computation.23 | convolution fusion | flops 808648704 | bytes 671744 | tf_op jit(solution)/shard_map/kg,kc->gc/dot_general | solution.py:125
  126.8 1.3 convolution_convert_fusion
  128.1 0.1 copy.117
  128.2 12.0 %all_to_all.38 = bf16[8,1,256,64]{2,3,1,0:T(8,128)(2,1)S(1)} all-to-all(bf16[8,1,256,64]{2,3,1,0:T(8,128)(2,1)S(1)} %copy.110), channel_id=1, replica_groups=mesh['img'=8,'sub'=4] {'img'}, dimensions={0} | all-to-all | bytes 524288 | tf_op jit(solution)/shard_map/all_to_all | solution.py:187
  140.1 1.0 copy.111
  141.1 6.4 %shard_map.57 = f32[2048,64]{1,0:T(8,128)} custom-call(bf16[2048,2048]{1,0:T(8,128)(2,1)} %get-tuple-element.8.weights, bf16[2048,64]{1,0:T(8,128)(2,1)} %bitcast.54), custom_call_target="tpu_custom_call" | custom-call | flops 536870912 | bytes 9175040 | tf_op jit(solution)/shard_map/pallas_call | solution.py:66
  147.5 1.5 copy.112
  149.1 17.3 %all_to_all.39 = f32[8,1,256,64]{2,3,1,0:T(8,128)S(1)} all-to-all(f32[8,1,256,64]{2,3,1,0:T(8,128)S(1)} %copy.112), channel_id=1, replica_groups=mesh['img'=8,'sub'=4] {'img'}, dimensions={0} | all-to-all | bytes 1048576 | tf_op jit(solution)/shard_map/all_to_all | solution.py:189
  166.4 2.4 %fusion.8 = bf16[512,64]{0,1:T(8,128)(2,1)} fusion(f32[2048,64]{0,1:T(8,128)S(1)} %bitcast.61, bf16[512,64]{0,1:T(8,128)(2,1)S(1)} %copy-done, f32[512]{0:T(512)S(1)} %get-tuple-element.15, s32[512]{0:T(512)S(1)} %bitcast.81, s32[512]{0:T(512)S(1)} %bitcast.73, s32[2048]{0:T(1024)S(1)} %add.102), kind=kOutput, calls=%fused_computation.24 | convolution fusion | flops 808615936 | bytes 669696 | tf_op jit(solution)/shard_map/kg,kc->gc/dot_general | solution.py:125
  (16 shorter events, 0.3 us)
Async XLA Ops:
  7.5 44.9 %copy-start.1 = (s32[4]{0:T(128)S(1)}, s32[4]{0:T(128)}, u32[]{:S(2)}) copy-start(s32[4]{0:T(128)} %constant.11.clone) | copy-start | bytes 52
  28.5 14.9 %all-to-all-start.1 = ((bf16[8,64,384]{2,1,0:T(8,128)(2,1)}), bf16[8,64,384]{2,1,0:T(8,128)(2,1)S(1)}, u32[]{:S(2)}, u32[]{:S(2)}) async-start(bf16[8,64,384]{2,1,0:T(8,128)(2,1)} %get-tuple-element.9), calls=%async_computation.1 | async-start | bytes 786432 | tf_op jit(solution)/shard_map/all_to_all | solution.py:166
  32.0 13.2 %collective-permute-start = (bf16[8,1,65,384]{3,0,2,1:T(8,128)(2,1)S(1)}, bf16[8,1,65,384]{3,0,2,1:T(8,128)(2,1)S(1)}, u32[]{:S(2)}, u32[]{:S(2)}) collective-permute-start(bf16[8,1,65,384]{3,0,2,1:T(8,128)(2,1)S(1)} %bitcast.45), channel_id=1, source_target_pairs={{0,2},{1,3},{2,0},{3,1},{4,6},{5,7},{6,4},{7,5},{8,10},{9,11},{10,... | collective-permute-start | bytes 1198088 | tf_op jit(solution)/shard_map/ppermute | solution.py:163
  43.6 7.8 %collective-permute-start.2 = (bf16[8,1,64,384]{3,0,2,1:T(8,128)(2,1)S(1)}, bf16[8,1,64,384]{3,0,2,1:T(8,128)(2,1)S(1)}, u32[]{:S(2)}, u32[]{:S(2)}) collective-permute-start(bf16[8,1,64,384]{3,0,2,1:T(8,128)(2,1)S(1)} %copy.102), channel_id=1, source_target_pairs={{0,2},{1,3},{2,0},{3,1},{4,6},{5,7},{6,4},{7,5},{8,10},{9,11},{10,... | collective-permute-start | bytes 1179656 | tf_op jit(solution)/shard_map/ppermute | solution.py:163
  45.3 7.3 %collective-permute-start.1 = (bf16[8,2,65,384]{3,0,2,1:T(8,128)(2,1)S(1)}, bf16[8,2,65,384]{3,0,2,1:T(8,128)(2,1)S(1)}, u32[]{:S(2)}, u32[]{:S(2)}) collective-permute-start(bf16[8,2,65,384]{3,0,2,1:T(8,128)(2,1)S(1)} %pad_maximum_fusion.2), channel_id=1, source_target_pairs={{0,1},{1,0},{2,3},{3,2},{4,5},{5,4},{6,7},{7,6},{8,9},{9,8},{10,11... | collective-permute-start | bytes 2396168 | tf_op jit(solution)/shard_map/ppermute | solution.py:163
  52.4 2.8 %collective-permute-start.3 = (bf16[8,2,64,384]{3,0,2,1:T(8,128)(2,1)}, bf16[8,2,64,384]{3,0,2,1:T(8,128)(2,1)S(1)}, u32[]{:S(2)}, u32[]{:S(2)}) collective-permute-start(bf16[8,2,64,384]{3,0,2,1:T(8,128)(2,1)} %pad_maximum_fusion.3), channel_id=1, source_target_pairs={{0,1},{1,0},{2,3},{3,2},{4,5},{5,4},{6,7},{7,6},{8,9},{9,8},{10,11... | collective-permute-start | bytes 2359304 | tf_op jit(solution)/shard_map/ppermute | solution.py:163
  59.4 27.0 %copy-start = (bf16[512,64]{0,1:T(8,128)(2,1)S(1)}, bf16[512,64]{0,1:T(8,128)(2,1)}, u32[]{:S(2)}) copy-start(bf16[512,64]{0,1:T(8,128)(2,1)} %param.6) | copy-start | bytes 196612
  73.0 12.7 %all-to-all-start.2 = ((f32[8,1,256]{2,1,0:T(1,128)}), f32[8,1,256]{2,1,0:T(1,128)S(1)}, u32[]{:S(2)}, u32[]{:S(2)}) async-start(f32[8,1,256]{2,1,0:T(1,128)} %bitcast.82), calls=%async_computation.2 | async-start | bytes 16384 | tf_op jit(solution)/shard_map/all_to_all | solution.py:178

commit v10 on v8

--- a/solution.py
+++ b/solution.py
@@ -29,7 +29,7 @@
 
 def fused_affinity(rows, keys):
     slot_count, width = rows.shape
-    block_rows = min(256, slot_count)
+    block_rows = min(512, slot_count)
     return pl.pallas_call(
         affinity_kernel,
         grid=(slot_count // block_rows,),
@@ -97,10 +97,15 @@
 
     def from_bucket(returned):
         flat = returned.reshape(slot_total, -1)
-        return jnp.einsum(
-            "kg,kc->gc", pick.astype(jnp.float32), flat,
-            precision=lax.Precision.HIGHEST, preferred_element_type=jnp.float32,
-        )
+        top = flat.astype(jnp.bfloat16)
+        rest = flat - top.astype(jnp.float32)
+        middle = rest.astype(jnp.bfloat16)
+        bottom = (rest - middle.astype(jnp.float32)).astype(jnp.bfloat16)
+
+        def select(piece):
+            return jnp.einsum("kg,kc->gc", pick, piece, preferred_element_type=jnp.float32)
+
+        return select(top) + select(middle) + select(bottom)
 
     values = embeddings.astype(jnp.float32)
     unit = (values * lax.rsqrt(jnp.sum(values * values, axis=1, keepdims=True) + 1e-06)).astype(

time: 165 us -> 166 us (level)
  matrix products: 20.6 us -> 22.6 us
    dot_general x2 -> x5, matrix products: 4.12 us -> 5.59 us  [select(): jnp.einsum('kg,kc->gc', pick, piece, preferred_element_type=jnp.float32)]
where the time goes in v10:
time: 166 us
  blocking collectives  77.5 us (47%)
  matrix products  22.6 us (14%)
  waiting for transfers between devices  22.3 us (13%)
  Pallas kernels  13.7 us (8%)
  starting transfers between devices  12.8 us (8%)
  local copies, waits for them, and re-layouts  8.7 us (5%)
  other arithmetic  7.76 us (5%)
    all_to_all x2, blocking collectives, on_device(): lax.all_to_all(bucket_major(product), 'img', split_axis=0, concat_axis=0,...  34.6 us
    all_to_all x2, blocking collectives, on_device(): lax.all_to_all(to_bucket(scaled), 'img', split_axis=0, concat_axis=0, til...  22.9 us
    all_to_all x1, blocking collectives, on_device(): lax.all_to_all(low_payload, 'img', split_axis=0, concat_axis=0, tiled=True)  20 us
    pallas_call x1, Pallas kernels, fused_affinity(): pl.pallas_call(affinity_kernel, grid=(slot_count // block_rows,), in_spec...  13.7 us
    dot_general x2, matrix products, on_device(): jnp.einsum('ajk,akc->ajc', weights, list_major(arrived), preferred_elemen...  12.1 us
    all_to_all x1, waiting for transfers between devices, on_device(): lax.all_to_all(high_payload, 'img', split_axis=0, concat_axis=0, tiled=True)  9.83 us
    all_to_all x1, waiting for transfers between devices, on_device(): lax.all_to_all(bucket_major(row_sums), 'img', split_axis=0, concat_axis=0...  6.36 us
    all_to_all x1, starting transfers between devices, on_device(): lax.all_to_all(bucket_major(row_sums), 'img', split_axis=0, concat_axis=0...  6.14 us
  transfers between devices with their start and end apart: 6, of which 3 were waited for; matrix products, arithmetic and copies ran while one was open for 3% of the time, Pallas kernels for 0%

profile of v10, /device:TPU:0, one launch (start us, length us, event | category | flops | bytes accessed | tf_op | source)
XLA Modules:
  0.0 165.6 jit_solution(12009538032138155522)
XLA Ops:
  0.0 0.8 copy.73
  0.8 0.2 eq.32
  1.0 0.5 convert_reduce_fusion
  1.5 0.2 reduce_sum.39
  1.7 0.1 copy.74
  1.9 0.7 multiply_add_fusion
  2.6 0.1 iota_add_fusion.1
  2.7 0.1 add.120
  2.7 0.7 convert_element_type.109
  3.4 0.4 fusion.14
  3.8 0.3 fusion.12
  4.2 0.1 convert_element_type.134
  4.3 1.4 fusion.2
  5.6 1.9 %convolution_convert_fusion.2 = bf16[512,768]{1,0:T(8,128)(2,1)S(1)} fusion(bf16[512,768]{1,0:T(8,128)(2,1)} %param.5, f32[512]{0:T(512)S(1)} %add_rsqrt_fusion, s32[512]{0:T(512)S(1)} %bitcast.95, s32[512]{0:T(512)S(1)} %bitcast.84, s32[512]{0:T(512)S(1)} %add.120), kind=kOutput, calls=%fused_computation.14 | convolution fusion | flops 405012480 | bytes 1581056 | tf_op jit(solution)/shard_map/dot_general | solution.py:129
  7.5 0.0 copy-start.1
  7.5 0.9 fusion.36
  8.4 20.0 %all_to_all.35 = bf16[8,65,384]{2,1,0:T(8,128)(2,1)S(1)} all-to-all(bf16[8,65,384]{2,1,0:T(8,128)(2,1)S(1)} %fusion.20), channel_id=1, replica_groups=mesh['img'=8,'sub'=4] {'img'}, dimensions={0} | all-to-all | bytes 798720 | tf_op jit(solution)/shard_map/all_to_all | solution.py:145
  28.5 3.5 %all-to-all-start.1 = ((bf16[8,64,384]{2,1,0:T(8,128)(2,1)}), bf16[8,64,384]{2,1,0:T(8,128)(2,1)S(1)}, u32[]{:S(2)}, u32[]{:S(2)}) async-start(bf16[8,64,384]{2,1,0:T(8,128)(2,1)} %get-tuple-element.9), calls=%async_computation.1 | async-start | bytes 786432 | tf_op jit(solution)/shard_map/all_to_all | solution.py:146
  32.0 1.6 collective-permute-start
  33.5 9.8 %all-to-all-done.1 = bf16[8,64,384]{2,1,0:T(8,128)(2,1)S(1)} async-done(((bf16[8,64,384]{2,1,0:T(8,128)(2,1)}), bf16[8,64,384]{2,1,0:T(8,128)(2,1)S(1)}, u32[]{:S(2)}, u32[]{:S(2)}) %all-to-all-start.1) | async-done | bytes 393248 | tf_op jit(solution)/shard_map/all_to_all | solution.py:146
  43.4 0.2 copy.81
  43.6 1.6 collective-permute-start.2
  45.2 0.0 collective-permute-done
  45.2 0.1 pad_maximum_fusion.2
  45.3 0.1 collective-permute-start.1
  45.3 6.1 %collective-permute-done.2 = bf16[8,1,64,384]{3,0,2,1:T(8,128)(2,1)S(1)} collective-permute-done((bf16[8,1,64,384]{3,0,2,1:T(8,128)(2,1)S(1)}, bf16[8,1,64,384]{3,0,2,1:T(8,128)(2,1)S(1)}, u32[]{:S(2)}, u32[]{:S(2)}) %collective-permute-start.2) | collective-permute-done | bytes 393248 | tf_op jit(solution)/shard_map/ppermute | solution.py:143
  51.5 1.0 pad_maximum_fusion.3
  52.4 0.0 collective-permute-start.3
  52.4 0.0 copy-done.1
  52.5 0.1 broadcast_add_fusion
  52.5 0.0 collective-permute-done.1
  52.5 2.0 %reshape.208.row_keys = f32[2048,1]{1,0:T(8,128)} reshape(f32[8,4,1,64]{3,1,0,2:T(4,128)S(1)} %copy.77) | data formatting | bytes 16384 | tf_op jit(solution)/shard_map/convert_element_type | solution.py:156
  54.5 0.7 reshape.205.col_keys
  55.2 0.0 collective-permute-done.3
  55.2 1.7 %fusion.1 = bf16[8,4,64,768]{3,0,2,1:T(8,128)(2,1)S(1)} fusion(bf16[8,2,65,384]{3,0,2,1:T(8,128)(2,1)S(1)} %collective-permute-done.1, bf16[8,1,65,384]{3,0,2,1:T(8,128)(2,1)S(1)} %collective-permute-done, bf16[8,1,65,384]{3,0,2,1:T(8,128)(2,1)S(1)} %bitcast.64, bf16[8,2,64,384]{3,0,2,1:T(8,128)(2,1)S(1)} %collective-permute-done.3, ...), kind=kLoop, calls=%fused_computation.6 | loop fusion | flops 18874368 | bytes 6316032 | tf_op jit(solution)/shard_map/concatenate | solution.py:153
  56.9 2.5 %copy.82 = bf16[8,4,64,768]{3,2,1,0:T(8,128)(2,1)} copy(bf16[8,4,64,768]{3,0,2,1:T(8,128)(2,1)S(1)} %fusion.1) | data formatting | bytes 6291456 | tf_op jit(solution)/shard_map/concatenate | solution.py:153
  59.4 0.0 copy-start
  59.4 13.7 %shard_map.55 = (bf16[2048,2048]{1,0:T(8,128)(2,1)}, f32[1,2048]{1,0:T(1,128)}) custom-call(f32[2048,1]{1,0:T(8,128)} %reshape.208.row_keys, f32[1,2048]{1,0:T(1,128)} %reshape.205.col_keys, bf16[2048,768]{1,0:T(8,128)(2,1)} %bitcast.65, bf16[2048,768]{1,0:T(8,128)(2,1)} %bitcast.66), custom_call_target="tpu_custom_call" | custom-call | flops 6534725632 | bytes 14680064 | tf_op jit(solution)/shard_map/pallas_call | solution.py:33
  73.0 6.1 %all-to-all-start.2 = ((f32[8,1,256]{2,1,0:T(1,128)}), f32[8,1,256]{2,1,0:T(1,128)S(1)}, u32[]{:S(2)}, u32[]{:S(2)}) async-start(f32[8,1,256]{2,1,0:T(1,128)} %bitcast.104), calls=%async_computation.2 | async-start | bytes 16384 | tf_op jit(solution)/shard_map/all_to_all | solution.py:159
  79.2 0.1 iota_add_fusion
  79.2 0.1 add.114
  79.3 6.4 %all-to-all-done.2 = f32[8,1,256]{2,1,0:T(1,128)S(1)} async-done(((f32[8,1,256]{2,1,0:T(1,128)}), f32[8,1,256]{2,1,0:T(1,128)S(1)}, u32[]{:S(2)}, u32[]{:S(2)}) %all-to-all-start.2) | async-done | bytes 8224 | tf_op jit(solution)/shard_map/all_to_all | solution.py:159
  85.7 0.7 select_reduce_fusion
  86.4 0.0 copy-done
  86.4 1.3 convolution_convert_fusion.1
  87.7 0.1 copy.94
  87.8 10.9 %all_to_all.36 = bf16[8,1,256,64]{2,3,1,0:T(8,128)(2,1)S(1)} all-to-all(bf16[8,1,256,64]{2,3,1,0:T(8,128)(2,1)S(1)} %copy.85), channel_id=1, replica_groups=mesh['img'=8,'sub'=4] {'img'}, dimensions={0} | all-to-all | bytes 524288 | tf_op jit(solution)/shard_map/all_to_all | solution.py:168
  98.7 0.1 copy.86
  98.9 0.1 reshape.206
  99.0 6.0 %convolution_bitcast_fusion.1 = f32[8,1,256,64]{2,3,1,0:T(8,128)S(1)} fusion(bf16[8,256,2048]{2,1,0:T(8,128)(2,1)} %bitcast.59, bf16[2048,64,1]{0,1,2:T(8,128)(2,1)S(1)} %reshape.206), kind=kOutput, calls=%fused_computation.19 | convolution fusion | flops 536870912 | bytes 9175040 | tf_op jit(solution)/shard_map/ajk,akc->ajc/dot_general | solution.py:169
  105.1 17.3 %all_to_all.37 = f32[8,1,256,64]{2,3,1,0:T(8,128)S(1)} all-to-all(f32[8,1,256,64]{2,3,1,0:T(8,128)S(1)} %convolution_bitcast_fusion.1), channel_id=1, replica_groups=mesh['img'=8,'sub'=4] {'img'}, dimensions={0} | all-to-all | bytes 1048576 | tf_op jit(solution)/shard_map/all_to_all | solution.py:172
  122.4 1.0 fusion.22
  123.4 1.0 convolution_add_fusion.3
  124.4 1.8 %convolution_convert_fusion = bf16[2048,64]{0,1:T(8,128)(2,1)S(1)} fusion(f32[512,64]{0,1:T(8,128)S(1)} %convolution_add_fusion.3, f32[2048,64]{0,1:T(8,128)S(1)} %bitcast.78, bf16[512,64]{0,1:T(8,128)(2,1)S(1)} %copy-done, f32[512]{0:T(512)S(1)} %get-tuple-element.16, f32[512]{0:T(512)S(1)} %get-tuple-element.15, s32[512]{0:T(512)S(1)} %bitcast.100, ...), kind=kOutput, calls=%fused_computation.8 | convolution fusion | flops 276004864 | bytes 999424 | tf_op jit(solution)/shard_map/dot_general | solution.py:91
  126.2 0.1 copy.96
  126.4 12.0 %all_to_all.38 = bf16[8,1,256,64]{2,3,1,0:T(8,128)(2,1)S(1)} all-to-all(bf16[8,1,256,64]{2,3,1,0:T(8,128)(2,1)S(1)} %copy.89), channel_id=1, replica_groups=mesh['img'=8,'sub'=4] {'img'}, dimensions={0} | all-to-all | bytes 524288 | tf_op jit(solution)/shard_map/all_to_all | solution.py:168
  138.3 0.1 copy.90
  138.5 0.1 reshape.207
  138.6 6.0 %convolution_bitcast_fusion = f32[8,1,256,64]{2,3,1,0:T(8,128)S(1)} fusion(bf16[8,256,2048]{2,1,0:T(8,128)(2,1)} %bitcast.60, bf16[2048,64,1]{0,1,2:T(8,128)(2,1)S(1)} %reshape.207), kind=kOutput, calls=%fused_computation.18 | convolution fusion | flops 536870912 | bytes 9175040 | tf_op jit(solution)/shard_map/ajk,akc->ajc/dot_general | solution.py:169
  144.6 17.3 %all_to_all.39 = f32[8,1,256,64]{2,3,1,0:T(8,128)S(1)} all-to-all(f32[8,1,256,64]{2,3,1,0:T(8,128)S(1)} %convolution_bitcast_fusion), channel_id=1, replica_groups=mesh['img'=8,'sub'=4] {'img'}, dimensions={0} | all-to-all | bytes 1048576 | tf_op jit(solution)/shard_map/all_to_all | solution.py:172
  162.0 1.0 fusion.26
  163.0 1.0 convolution_add_fusion.1
  164.0 1.6 fusion.10
  (16 shorter events, 0.3 us)
Async XLA Ops:
  7.5 44.9 %copy-start.1 = (s32[4]{0:T(128)S(1)}, s32[4]{0:T(128)}, u32[]{:S(2)}) copy-start(s32[4]{0:T(128)} %constant.11.clone) | copy-start | bytes 52
  28.5 14.9 %all-to-all-start.1 = ((bf16[8,64,384]{2,1,0:T(8,128)(2,1)}), bf16[8,64,384]{2,1,0:T(8,128)(2,1)S(1)}, u32[]{:S(2)}, u32[]{:S(2)}) async-start(bf16[8,64,384]{2,1,0:T(8,128)(2,1)} %get-tuple-element.9), calls=%async_computation.1 | async-start | bytes 786432 | tf_op jit(solution)/shard_map/all_to_all | solution.py:146
  32.0 13.2 %collective-permute-start = (bf16[8,1,65,384]{3,0,2,1:T(8,128)(2,1)S(1)}, bf16[8,1,65,384]{3,0,2,1:T(8,128)(2,1)S(1)}, u32[]{:S(2)}, u32[]{:S(2)}) collective-permute-start(bf16[8,1,65,384]{3,0,2,1:T(8,128)(2,1)S(1)} %bitcast.61), channel_id=1, source_target_pairs={{0,2},{1,3},{2,0},{3,1},{4,6},{5,7},{6,4},{7,5},{8,10},{9,11},{10,... | collective-permute-start | bytes 1198088 | tf_op jit(solution)/shard_map/ppermute | solution.py:143
  43.6 7.8 %collective-permute-start.2 = (bf16[8,1,64,384]{3,0,2,1:T(8,128)(2,1)S(1)}, bf16[8,1,64,384]{3,0,2,1:T(8,128)(2,1)S(1)}, u32[]{:S(2)}, u32[]{:S(2)}) collective-permute-start(bf16[8,1,64,384]{3,0,2,1:T(8,128)(2,1)S(1)} %copy.81), channel_id=1, source_target_pairs={{0,2},{1,3},{2,0},{3,1},{4,6},{5,7},{6,4},{7,5},{8,10},{9,11},{10,... | collective-permute-start | bytes 1179656 | tf_op jit(solution)/shard_map/ppermute | solution.py:143
  45.3 7.3 %collective-permute-start.1 = (bf16[8,2,65,384]{3,0,2,1:T(8,128)(2,1)S(1)}, bf16[8,2,65,384]{3,0,2,1:T(8,128)(2,1)S(1)}, u32[]{:S(2)}, u32[]{:S(2)}) collective-permute-start(bf16[8,2,65,384]{3,0,2,1:T(8,128)(2,1)S(1)} %pad_maximum_fusion.2), channel_id=1, source_target_pairs={{0,1},{1,0},{2,3},{3,2},{4,5},{5,4},{6,7},{7,6},{8,9},{9,8},{10,11... | collective-permute-start | bytes 2396168 | tf_op jit(solution)/shard_map/ppermute | solution.py:143
  52.4 2.8 %collective-permute-start.3 = (bf16[8,2,64,384]{3,0,2,1:T(8,128)(2,1)}, bf16[8,2,64,384]{3,0,2,1:T(8,128)(2,1)S(1)}, u32[]{:S(2)}, u32[]{:S(2)}) collective-permute-start(bf16[8,2,64,384]{3,0,2,1:T(8,128)(2,1)} %pad_maximum_fusion.3), channel_id=1, source_target_pairs={{0,1},{1,0},{2,3},{3,2},{4,5},{5,4},{6,7},{7,6},{8,9},{9,8},{10,11... | collective-permute-start | bytes 2359304 | tf_op jit(solution)/shard_map/ppermute | solution.py:143
  59.4 27.0 %copy-start = (bf16[512,64]{0,1:T(8,128)(2,1)S(1)}, bf16[512,64]{0,1:T(8,128)(2,1)}, u32[]{:S(2)}) copy-start(bf16[512,64]{0,1:T(8,128)(2,1)} %param.6) | copy-start | bytes 196612
  73.0 12.7 %all-to-all-start.2 = ((f32[8,1,256]{2,1,0:T(1,128)}), f32[8,1,256]{2,1,0:T(1,128)S(1)}, u32[]{:S(2)}, u32[]{:S(2)}) async-start(f32[8,1,256]{2,1,0:T(1,128)} %bitcast.104), calls=%async_computation.2 | async-start | bytes 16384 | tf_op jit(solution)/shard_map/all_to_all | solution.py:159

commit v11 on v8

--- a/solution.py
+++ b/solution.py
@@ -15,30 +15,63 @@
     return moved.reshape((moved.shape[0], moved.shape[1] * moved.shape[2]) + moved.shape[3:])
 
 
-def affinity_kernel(row_keys, col_keys, picked, rows, weights, row_sums):
+def affinity_kernel(col_keys, low_picked, high_picked, low_rows, high_rows, weights, row_sums):
+    block_rows = weights.shape[0]
+    slot_count = weights.shape[1]
+
+    def flat(ref):
+        value = ref[...]
+        return value.reshape(-1, value.shape[-1])
+
     contract = (((1,), (1,)), ((), ()))
-    gram = lax.dot_general(picked[...], rows[...], contract, preferred_element_type=jnp.float32)
-    keep = jnp.abs(row_keys[...] - col_keys[...]) <= BAND
+    gram = lax.dot_general(
+        flat(low_picked), flat(low_rows), contract, preferred_element_type=jnp.float32
+    ) + lax.dot_general(
+        flat(high_picked), flat(high_rows), contract, preferred_element_type=jnp.float32
+    )
+    start = pl.multiple_of(pl.program_id(0) * block_rows, block_rows)
+    own_keys = col_keys[:, pl.ds(start, block_rows)]
+    diagonal = (
+        lax.broadcasted_iota(jnp.int32, (block_rows, block_rows), 0)
+        == lax.broadcasted_iota(jnp.int32, (block_rows, block_rows), 1)
+    )
+    row_keys = jnp.sum(jnp.where(diagonal, own_keys, 0.0), axis=1, keepdims=True)
+    keep = jnp.abs(row_keys - col_keys[...]) <= BAND
     positive = jnp.maximum(gram, 0.0)
     cubed = jnp.where(keep, positive * positive * positive, 0.0).astype(jnp.bfloat16)
     weights[...] = cubed
-    ones = jnp.ones((8, cubed.shape[1]), jnp.bfloat16)
+    ones = jnp.ones((8, slot_count), jnp.bfloat16)
     summed = lax.dot_general(ones, cubed, contract, preferred_element_type=jnp.float32)
     row_sums[...] = summed[0:1, :]
 
 
-def fused_affinity(rows, keys):
-    slot_count, width = rows.shape
-    block_rows = min(256, slot_count)
+def fused_affinity(low, high, keys, part):
+    sources, quarters = high.shape[0], high.shape[1]
+    slot_count = sources * quarters * part
+    block_rows = quarters * part
+    aligned = part % 16 == 0 and block_rows % 128 == 0
+    if aligned:
+        def spec(array, count):
+            shape = (count, quarters, part, array.shape[3])
+            return pl.BlockSpec(shape, (lambda i: (i, 0, 0, 0)) if count == 1 else (lambda i: (0, 0, 0, 0)))
+        operands = (low, high, low, high)
+        in_specs = [spec(low, 1), spec(high, 1), spec(low, sources), spec(high, sources)]
+    else:
+        low = low[:, :, :part, :].reshape(slot_count, -1)
+        high = high.reshape(slot_count, -1)
+        block_rows = min(256, slot_count)
+        operands = (low, high, low, high)
+        in_specs = [
+            pl.BlockSpec((block_rows, low.shape[1]), lambda i: (i, 0)),
+            pl.BlockSpec((block_rows, high.shape[1]), lambda i: (i, 0)),
+            pl.BlockSpec((slot_count, low.shape[1]), lambda i: (0, 0)),
+            pl.BlockSpec((slot_count, high.shape[1]), lambda i: (0, 0)),
+        ]
+    width = low.shape[-1] + high.shape[-1]
     return pl.pallas_call(
         affinity_kernel,
         grid=(slot_count // block_rows,),
-        in_specs=[
-            pl.BlockSpec((block_rows, 1), lambda i: (i, 0)),
-            pl.BlockSpec((1, slot_count), lambda i: (0, 0)),
-            pl.BlockSpec((block_rows, width), lambda i: (i, 0)),
-            pl.BlockSpec((slot_count, width), lambda i: (0, 0)),
-        ],
+        in_specs=[pl.BlockSpec((1, slot_count), lambda i: (0, 0))] + in_specs,
         out_specs=[
             pl.BlockSpec((block_rows, slot_count), lambda i: (i, 0)),
             pl.BlockSpec((1, block_rows), lambda i: (0, i)),
@@ -53,7 +86,7 @@
             transcendentals=0,
             bytes_accessed=2 * slot_count * width * 2 + 2 * slot_count * slot_count,
         ),
-    )(keys.reshape(slot_count, 1), keys.reshape(1, slot_count), rows, rows)
+    )(keys.reshape(1, slot_count), *operands)
 
 
 def on_device(embeddings, labels, image_lists, rank_keys):
@@ -145,11 +178,8 @@
         high_got = exchange_stage(high_got, bit)
         bit //= 2
     slot_count = slot_total
-    rows = jnp.concatenate(
-        [low_got[:, :, :part, :], high_got], axis=3
-    ).reshape(slot_count, width)
     key_rows = low_got[:, :, part, :part].reshape(slot_count).astype(jnp.float32)
-    weight_mat, row_sums = fused_affinity(rows, key_rows)
+    weight_mat, row_sums = fused_affinity(low_got, high_got, key_rows, part)
     weights = weight_mat.reshape(1, slot_count, slot_count)
     degree_slots = lax.all_to_all(
         bucket_major(row_sums), "img", split_axis=0, concat_axis=0, tiled=True

time: 165 us -> 162 us (0.982)
  blocking collectives: 77.5 us -> 56.9 us
  waiting for transfers between devices: 22.3 us -> 35.2 us
  starting transfers between devices: 12.8 us -> 20.9 us
  local copies, waits for them, and re-layouts: 8.7 us -> 4.68 us
  Pallas kernels: 14.4 us -> 16.2 us
    all_to_all x1 -> x0, blocking collectives: 20 us -> none  [on_device(): lax.all_to_all(low_payload, 'img', split_axis=0, concat_axis=0, tiled=True)]
    all_to_all x0 -> x1, waiting for transfers between devices: none -> 11.1 us  [on_device(): lax.all_to_all(low_payload, 'img', split_axis=0, concat_axis=0, tiled=True)]
    all_to_all x1, starting transfers between devices: 3.45 us -> 7.28 us  [on_device(): lax.all_to_all(high_payload, 'img', split_axis=0, concat_axis=0, tiled=True)]
    all_to_all x0 -> x1, starting transfers between devices: none -> 3.63 us  [on_device(): lax.all_to_all(low_payload, 'img', split_axis=0, concat_axis=0, tiled=True)]
    concatenate x1, local copies, waits for them, and re-layouts: 2.46 us -> 0.1 us  [exchange_stage(): return jnp.concatenate([got, lax.ppermute(got, 'sub', pairs)], axis=1)]
    convert_element_type x3 -> x1, local copies, waits for them, and re-layouts: 2.69 us -> 0.84 us  [on_device(): low_got[:, :, part, :part].reshape(slot_count).astype(jnp.float32)]
    pallas_call x1, Pallas kernels: 14.4 us -> 16.2 us  [fused_affinity(): pl.pallas_call(affinity_kernel, grid=(slot_count // block_rows,), in_spec...]
    concatenate x1 -> x0, other arithmetic: 1.67 us -> none  [on_device(): jnp.concatenate([low_got[:, :, :part, :], high_got], axis=3)]
  transfers between devices with their start and end apart: 6 -> 7, of which waited for: 3 -> 5; matrix products, arithmetic and copies ran while one was open for 3% -> 2% of each run, Pallas kernels for 0% -> 0%
where the time goes in v11:
time: 162 us
  blocking collectives  56.9 us (35%)
  waiting for transfers between devices  35.2 us (22%)
  starting transfers between devices  20.9 us (13%)
  matrix products  20.6 us (13%)
  Pallas kernels  16.2 us (10%)
  other arithmetic  6.94 us (4%)
  local copies, waits for them, and re-layouts  4.68 us (3%)
    all_to_all x2, blocking collectives, on_device(): lax.all_to_all(bucket_major(product), 'img', split_axis=0, concat_axis=0,...  34.3 us
    all_to_all x2, blocking collectives, on_device(): lax.all_to_all(to_bucket(scaled), 'img', split_axis=0, concat_axis=0, til...  22.6 us
    pallas_call x1, Pallas kernels, fused_affinity(): pl.pallas_call(affinity_kernel, grid=(slot_count // block_rows,), in_spec...  16.2 us
    dot_general x2, matrix products, on_device(): jnp.einsum('ajk,akc->ajc', weights, list_major(arrived), preferred_elemen...  12.1 us
    all_to_all x1, waiting for transfers between devices, on_device(): lax.all_to_all(low_payload, 'img', split_axis=0, concat_axis=0, tiled=True)  11.1 us
    all_to_all x1, waiting for transfers between devices, on_device(): lax.all_to_all(high_payload, 'img', split_axis=0, concat_axis=0, tiled=True)  10 us
    ppermute x4, waiting for transfers between devices, exchange_stage(): return jnp.concatenate([got, lax.ppermute(got, 'sub', pairs)], axis=1)  7.65 us
    all_to_all x1, starting transfers between devices, on_device(): lax.all_to_all(high_payload, 'img', split_axis=0, concat_axis=0, tiled=True)  7.28 us
  transfers between devices with their start and end apart: 7, of which 5 were waited for; matrix products, arithmetic and copies ran while one was open for 2% of the time, Pallas kernels for 0%

profile of v11, /device:TPU:0, one launch (start us, length us, event | category | flops | bytes accessed | tf_op | source)
XLA Modules:
  0.0 161.7 jit_solution(760001999443383787)
XLA Ops:
  0.0 0.8 copy.60
  0.8 0.2 eq.32
  1.0 0.5 convert_reduce_fusion
  1.5 0.2 reduce_sum.39
  1.8 0.1 copy.61
  1.9 0.7 multiply_add_fusion
  2.6 0.1 iota_add_fusion.1
  2.7 0.1 add.108
  2.7 1.4 fusion.1
  4.1 1.9 %convolution_convert_fusion.2 = bf16[512,768]{1,0:T(8,128)(2,1)S(1)} fusion(bf16[512,768]{1,0:T(8,128)(2,1)} %param.5, f32[512]{0:T(512)S(1)} %add_rsqrt_fusion, s32[512]{0:T(512)S(1)} %bitcast.85, s32[512]{0:T(512)S(1)} %bitcast.77, s32[512]{0:T(512)S(1)} %add.108), kind=kOutput, calls=%fused_computation.13 | convolution fusion | flops 405012480 | bytes 1581056 | tf_op jit(solution)/shard_map/dot_general | solution.py:157
  6.0 0.0 copy-start.3
  6.0 0.8 fusion.22
  6.9 7.3 %all-to-all-start.1 = ((bf16[8,64,384]{2,1,0:T(8,128)(2,1)}), bf16[8,64,384]{2,1,0:T(8,128)(2,1)S(1)}, u32[]{:S(2)}, u32[]{:S(2)}) async-start(bf16[8,64,384]{2,1,0:T(8,128)(2,1)} %get-tuple-element.9), calls=%async_computation.1 | async-start | bytes 786432 | tf_op jit(solution)/shard_map/all_to_all | solution.py:174
  14.1 0.0 copy-done.1
  14.2 0.4 fusion.11
  14.6 0.3 fusion.9
  14.9 0.1 convert_element_type.81
  15.0 0.8 fusion.17
  15.8 10.0 %all-to-all-done.1 = bf16[8,64,384]{2,1,0:T(8,128)(2,1)S(1)} async-done(((bf16[8,64,384]{2,1,0:T(8,128)(2,1)}), bf16[8,64,384]{2,1,0:T(8,128)(2,1)S(1)}, u32[]{:S(2)}, u32[]{:S(2)}) %all-to-all-start.1) | async-done | bytes 393248 | tf_op jit(solution)/shard_map/all_to_all | solution.py:174
  25.8 3.6 %all-to-all-start = ((bf16[8,65,384]{2,1,0:T(8,128)(2,1)}), bf16[8,65,384]{2,1,0:T(8,128)(2,1)S(1)}, u32[]{:S(2)}, u32[]{:S(2)}) async-start(bf16[8,65,384]{2,1,0:T(8,128)(2,1)} %fusion.17), calls=%async_computation | async-start | bytes 884736 | tf_op jit(solution)/shard_map/all_to_all | solution.py:173
  29.5 1.5 collective-permute-start.2
  31.0 11.1 %all-to-all-done = bf16[8,65,384]{2,1,0:T(8,128)(2,1)S(1)} async-done(((bf16[8,65,384]{2,1,0:T(8,128)(2,1)}), bf16[8,65,384]{2,1,0:T(8,128)(2,1)S(1)}, u32[]{:S(2)}, u32[]{:S(2)}) %all-to-all-start) | async-done | bytes 399392 | tf_op jit(solution)/shard_map/all_to_all | solution.py:173
  42.1 1.5 collective-permute-start
  43.6 0.0 collective-permute-done.2
  43.6 0.1 pad_maximum_fusion.3
  43.7 0.1 collective-permute-start.3
  43.8 6.8 %collective-permute-done = bf16[8,1,65,384]{3,2,0,1:T(8,128)(2,1)S(1)} collective-permute-done((bf16[8,1,65,384]{3,2,0,1:T(8,128)(2,1)S(1)}, bf16[8,1,65,384]{3,2,0,1:T(8,128)(2,1)S(1)}, u32[]{:S(2)}, u32[]{:S(2)}) %collective-permute-start) | collective-permute-done | bytes 399392 | tf_op jit(solution)/shard_map/ppermute | solution.py:171
  50.6 0.1 pad_maximum_fusion.2
  50.7 0.1 copy.63
  50.8 0.1 collective-permute-start.1
  50.9 0.0 copy-done.3
  50.9 0.1 broadcast_add_fusion
  51.0 0.0 collective-permute-done.3
  51.0 1.3 pad_maximum_fusion.1.high_picked.high_rows
  52.3 0.8 collective-permute-done.1
  53.2 0.1 copy.66
  53.3 0.2 pad_maximum_fusion.low_picked.low_rows
  53.5 0.0 copy-start
  53.5 0.1 fusion.21
  53.6 0.8 reshape.187.col_keys
  54.4 0.4 copy-done
  54.8 16.2 %shard_map.55 = (bf16[2048,2048]{1,0:T(8,128)(2,1)}, f32[1,2048]{1,0:T(1,128)}) custom-call(f32[1,2048]{1,0:T(1,128)} %reshape.187.col_keys, bf16[8,4,65,384]{3,2,1,0:T(8,128)(2,1)} %copy-done, bf16[8,4,64,384]{3,2,1,0:T(8,128)(2,1)} %pad_maximum_fusion.1.high_picked.high_rows, bf16[8,4,65,384]{3,2,1,0:T(8,128)(2,1)} %copy-done, ...), custom_call_target="tpu_custom_call" | custom-call | flops 6534725632 | bytes 14680064 | tf_op jit(solution)/shard_map/pallas_call | solution.py:71
  71.0 6.9 %all-to-all-start.2 = ((f32[8,1,256]{2,1,0:T(1,128)}), f32[8,1,256]{2,1,0:T(1,128)S(1)}, u32[]{:S(2)}, u32[]{:S(2)}) async-start(f32[8,1,256]{2,1,0:T(1,128)} %bitcast.93), calls=%async_computation.2 | async-start | bytes 16384 | tf_op jit(solution)/shard_map/all_to_all | solution.py:184
  77.9 0.1 iota_add_fusion
  77.9 0.1 add.102
  78.0 6.4 %all-to-all-done.2 = f32[8,1,256]{2,1,0:T(1,128)S(1)} async-done(((f32[8,1,256]{2,1,0:T(1,128)}), f32[8,1,256]{2,1,0:T(1,128)S(1)}, u32[]{:S(2)}, u32[]{:S(2)}) %all-to-all-start.2) | async-done | bytes 8224 | tf_op jit(solution)/shard_map/all_to_all | solution.py:184
  84.4 0.7 select_reduce_fusion
  85.1 0.0 copy-done.2
  85.1 1.3 convolution_convert_fusion.1
  86.4 0.1 copy.76
  86.5 10.6 %all_to_all.35 = bf16[8,1,256,64]{2,3,1,0:T(8,128)(2,1)S(1)} all-to-all(bf16[8,1,256,64]{2,3,1,0:T(8,128)(2,1)S(1)} %copy.68), channel_id=1, replica_groups=mesh['img'=8,'sub'=4] {'img'}, dimensions={0} | all-to-all | bytes 524288 | tf_op jit(solution)/shard_map/all_to_all | solution.py:193
  97.2 0.1 copy.69
  97.3 0.1 reshape.188
  97.4 6.0 %convolution_bitcast_fusion.1 = f32[8,1,256,64]{2,3,1,0:T(8,128)S(1)} fusion(bf16[8,256,2048]{2,1,0:T(8,128)(2,1)} %bitcast.58, bf16[2048,64,1]{0,1,2:T(8,128)(2,1)S(1)} %reshape.188), kind=kOutput, calls=%fused_computation.18 | convolution fusion | flops 536870912 | bytes 9175040 | tf_op jit(solution)/shard_map/ajk,akc->ajc/dot_general | solution.py:194
  103.5 17.1 %all_to_all.36 = f32[8,1,256,64]{2,3,1,0:T(8,128)S(1)} all-to-all(f32[8,1,256,64]{2,3,1,0:T(8,128)S(1)} %convolution_bitcast_fusion.1), channel_id=1, replica_groups=mesh['img'=8,'sub'=4] {'img'}, dimensions={0} | all-to-all | bytes 1048576 | tf_op jit(solution)/shard_map/all_to_all | solution.py:197
  120.6 1.7 %fusion.6 = bf16[512,64]{0,1:T(8,128)(2,1)S(1)} fusion(f32[2048,64]{0,1:T(8,128)S(1)} %bitcast.73, bf16[512,64]{0,1:T(8,128)(2,1)S(1)} %copy-done.2, f32[512]{0:T(512)S(1)} %get-tuple-element.16, f32[512]{0:T(512)S(1)} %get-tuple-element.15, s32[512]{0:T(512)S(1)} %bitcast.90, s32[512]{0:T(512)S(1)} %bitcast.82, s32[2048]{0:T(1024)S(1)} %add.102), kind=kOutput, calls=%fused_computation.24 | convolution fusion | flops 808648704 | bytes 671744 | tf_op jit(solution)/shard_map/kg,kc->gc/dot_general | solution.py:133
  122.3 1.3 convolution_convert_fusion
  123.6 0.1 copy.78
  123.7 12.0 %all_to_all.37 = bf16[8,1,256,64]{2,3,1,0:T(8,128)(2,1)S(1)} all-to-all(bf16[8,1,256,64]{2,3,1,0:T(8,128)(2,1)S(1)} %copy.72), channel_id=1, replica_groups=mesh['img'=8,'sub'=4] {'img'}, dimensions={0} | all-to-all | bytes 524288 | tf_op jit(solution)/shard_map/all_to_all | solution.py:193
  135.7 0.1 copy.73
  135.8 0.1 reshape.189
  136.0 6.0 %convolution_bitcast_fusion = f32[8,1,256,64]{2,3,1,0:T(8,128)S(1)} fusion(bf16[8,256,2048]{2,1,0:T(8,128)(2,1)} %bitcast.59, bf16[2048,64,1]{0,1,2:T(8,128)(2,1)S(1)} %reshape.189), kind=kOutput, calls=%fused_computation.17 | convolution fusion | flops 536870912 | bytes 9175040 | tf_op jit(solution)/shard_map/ajk,akc->ajc/dot_general | solution.py:194
  142.0 17.3 %all_to_all.38 = f32[8,1,256,64]{2,3,1,0:T(8,128)S(1)} all-to-all(f32[8,1,256,64]{2,3,1,0:T(8,128)S(1)} %convolution_bitcast_fusion), channel_id=1, replica_groups=mesh['img'=8,'sub'=4] {'img'}, dimensions={0} | all-to-all | bytes 1048576 | tf_op jit(solution)/shard_map/all_to_all | solution.py:197
  159.3 2.4 %fusion.7 = bf16[512,64]{0,1:T(8,128)(2,1)} fusion(f32[2048,64]{0,1:T(8,128)S(1)} %bitcast.72, bf16[512,64]{0,1:T(8,128)(2,1)S(1)} %copy-done.2, f32[512]{0:T(512)S(1)} %get-tuple-element.15, s32[512]{0:T(512)S(1)} %bitcast.92, s32[512]{0:T(512)S(1)} %bitcast.84, s32[2048]{0:T(1024)S(1)} %add.102), kind=kOutput, calls=%fused_computation.25 | convolution fusion | flops 808615936 | bytes 669696 | tf_op jit(solution)/shard_map/kg,kc->gc/dot_general | solution.py:133
  (15 shorter events, 0.2 us)
Async XLA Ops:
  0.0 14.1 %copy-start.1 = (s32[512,2]{0,1:T(2,128)S(1)}, s32[512,2]{0,1:T(2,128)}, u32[]{:S(2)}) copy-start(s32[512,2]{0,1:T(2,128)} %param.8) | copy-start | bytes 12292
  6.0 44.9 %copy-start.3 = (s32[4]{0:T(128)S(1)}, s32[4]{0:T(128)}, u32[]{:S(2)}) copy-start(s32[4]{0:T(128)} %constant.11.clone) | copy-start | bytes 52
  6.9 19.0 %all-to-all-start.1 = ((bf16[8,64,384]{2,1,0:T(8,128)(2,1)}), bf16[8,64,384]{2,1,0:T(8,128)(2,1)S(1)}, u32[]{:S(2)}, u32[]{:S(2)}) async-start(bf16[8,64,384]{2,1,0:T(8,128)(2,1)} %get-tuple-element.9), calls=%async_computation.1 | async-start | bytes 786432 | tf_op jit(solution)/shard_map/all_to_all | solution.py:174
  25.8 16.3 %all-to-all-start = ((bf16[8,65,384]{2,1,0:T(8,128)(2,1)}), bf16[8,65,384]{2,1,0:T(8,128)(2,1)S(1)}, u32[]{:S(2)}, u32[]{:S(2)}) async-start(bf16[8,65,384]{2,1,0:T(8,128)(2,1)} %fusion.17), calls=%async_computation | async-start | bytes 884736 | tf_op jit(solution)/shard_map/all_to_all | solution.py:173
  29.5 14.1 %collective-permute-start.2 = (bf16[8,1,64,384]{3,2,1,0:T(8,128)(2,1)S(1)}, bf16[8,1,64,384]{3,2,1,0:T(8,128)(2,1)S(1)}, u32[]{:S(2)}, u32[]{:S(2)}) collective-permute-start(bf16[8,1,64,384]{3,2,1,0:T(8,128)(2,1)S(1)} %bitcast.63), channel_id=1, source_target_pairs={{0,2},{1,3},{2,0},{3,1},{4,6},{5,7},{6,4},{7,5},{8,10},{9,11},{10,... | collective-permute-start | bytes 1179656 | tf_op jit(solution)/shard_map/ppermute | solution.py:171
  42.1 8.5 %collective-permute-start = (bf16[8,1,65,384]{3,2,0,1:T(8,128)(2,1)S(1)}, bf16[8,1,65,384]{3,2,0,1:T(8,128)(2,1)S(1)}, u32[]{:S(2)}, u32[]{:S(2)}) collective-permute-start(bf16[8,1,65,384]{3,2,0,1:T(8,128)(2,1)S(1)} %bitcast.60), channel_id=1, source_target_pairs={{0,2},{1,3},{2,0},{3,1},{4,6},{5,7},{6,4},{7,5},{8,10},{9,11},{10,... | collective-permute-start | bytes 1198088 | tf_op jit(solution)/shard_map/ppermute | solution.py:171
  43.7 7.3 %collective-permute-start.3 = (bf16[8,2,64,384]{3,2,1,0:T(8,128)(2,1)S(1)}, bf16[8,2,64,384]{3,2,1,0:T(8,128)(2,1)S(1)}, u32[]{:S(2)}, u32[]{:S(2)}) collective-permute-start(bf16[8,2,64,384]{3,2,1,0:T(8,128)(2,1)S(1)} %pad_maximum_fusion.3), channel_id=1, source_target_pairs={{0,1},{1,0},{2,3},{3,2},{4,5},{5,4},{6,7},{7,6},{8,9},{9,8},{10,11... | collective-permute-start | bytes 2359304 | tf_op jit(solution)/shard_map/ppermute | solution.py:171
  50.8 2.4 %collective-permute-start.1 = (bf16[8,2,65,384]{3,0,2,1:T(8,128)(2,1)S(1)}, bf16[8,2,65,384]{3,0,2,1:T(8,128)(2,1)S(1)}, u32[]{:S(2)}, u32[]{:S(2)}) collective-permute-start(bf16[8,2,65,384]{3,0,2,1:T(8,128)(2,1)S(1)} %copy.63), channel_id=1, source_target_pairs={{0,1},{1,0},{2,3},{3,2},{4,5},{5,4},{6,7},{7,6},{8,9},{9,8},{10,11... | collective-permute-start | bytes 2396168 | tf_op jit(solution)/shard_map/ppermute | solution.py:171
  53.5 1.3 copy-start
  54.8 30.3 %copy-start.2 = (bf16[512,64]{0,1:T(8,128)(2,1)S(1)}, bf16[512,64]{0,1:T(8,128)(2,1)}, u32[]{:S(2)}) copy-start(bf16[512,64]{0,1:T(8,128)(2,1)} %param.6) | copy-start | bytes 196612
  71.0 13.4 %all-to-all-start.2 = ((f32[8,1,256]{2,1,0:T(1,128)}), f32[8,1,256]{2,1,0:T(1,128)S(1)}, u32[]{:S(2)}, u32[]{:S(2)}) async-start(f32[8,1,256]{2,1,0:T(1,128)} %bitcast.93), calls=%async_computation.2 | async-start | bytes 16384 | tf_op jit(solution)/shard_map/all_to_all | solution.py:184

commit v12 on v11

--- a/solution.py
+++ b/solution.py
@@ -15,21 +15,24 @@
     return moved.reshape((moved.shape[0], moved.shape[1] * moved.shape[2]) + moved.shape[3:])
 
 
-def affinity_kernel(col_keys, low_picked, high_picked, low_rows, high_rows, weights, row_sums):
+def affinity_kernel(col_keys, low_rows, high_rows, weights, row_sums, joined):
     block_rows = weights.shape[0]
     slot_count = weights.shape[1]
-
-    def flat(ref):
-        value = ref[...]
-        return value.reshape(-1, value.shape[-1])
-
+    half = joined.shape[1] - high_rows.shape[-1]
+
+    @pl.when(pl.program_id(0) == 0)
+    def _():
+        low = low_rows[...]
+        high = high_rows[...]
+        joined[:, :half] = low.reshape(slot_count, low.shape[-1])[:, :half]
+        joined[:, half:] = high.reshape(slot_count, high.shape[-1])
+
+    start = pl.multiple_of(pl.program_id(0) * block_rows, block_rows)
     contract = (((1,), (1,)), ((), ()))
     gram = lax.dot_general(
-        flat(low_picked), flat(low_rows), contract, preferred_element_type=jnp.float32
-    ) + lax.dot_general(
-        flat(high_picked), flat(high_rows), contract, preferred_element_type=jnp.float32
-    )
-    start = pl.multiple_of(pl.program_id(0) * block_rows, block_rows)
+        joined[pl.ds(start, block_rows), :], joined[...], contract,
+        preferred_element_type=jnp.float32,
+    )
     own_keys = col_keys[:, pl.ds(start, block_rows)]
     diagonal = (
         lax.broadcasted_iota(jnp.int32, (block_rows, block_rows), 0)
@@ -48,30 +51,21 @@
 def fused_affinity(low, high, keys, part):
     sources, quarters = high.shape[0], high.shape[1]
     slot_count = sources * quarters * part
-    block_rows = quarters * part
-    aligned = part % 16 == 0 and block_rows % 128 == 0
-    if aligned:
-        def spec(array, count):
-            shape = (count, quarters, part, array.shape[3])
-            return pl.BlockSpec(shape, (lambda i: (i, 0, 0, 0)) if count == 1 else (lambda i: (0, 0, 0, 0)))
-        operands = (low, high, low, high)
-        in_specs = [spec(low, 1), spec(high, 1), spec(low, sources), spec(high, sources)]
+    half = low.shape[3]
+    width = half + high.shape[3]
+    if part % 16 == 0:
+        low_spec = pl.BlockSpec((sources, quarters, part, half), lambda i: (0, 0, 0, 0))
+        high_spec = pl.BlockSpec(high.shape, lambda i: (0, 0, 0, 0))
     else:
-        low = low[:, :, :part, :].reshape(slot_count, -1)
-        high = high.reshape(slot_count, -1)
-        block_rows = min(256, slot_count)
-        operands = (low, high, low, high)
-        in_specs = [
-            pl.BlockSpec((block_rows, low.shape[1]), lambda i: (i, 0)),
-            pl.BlockSpec((block_rows, high.shape[1]), lambda i: (i, 0)),
-            pl.BlockSpec((slot_count, low.shape[1]), lambda i: (0, 0)),
-            pl.BlockSpec((slot_count, high.shape[1]), lambda i: (0, 0)),
-        ]
-    width = low.shape[-1] + high.shape[-1]
+        low = low[:, :, :part, :].reshape(slot_count, half)
+        high = high.reshape(slot_count, width - half)
+        low_spec = pl.BlockSpec(low.shape, lambda i: (0, 0))
+        high_spec = pl.BlockSpec(high.shape, lambda i: (0, 0))
+    block_rows = min(512, slot_count)
     return pl.pallas_call(
         affinity_kernel,
         grid=(slot_count // block_rows,),
-        in_specs=[pl.BlockSpec((1, slot_count), lambda i: (0, 0))] + in_specs,
+        in_specs=[pl.BlockSpec((1, slot_count), lambda i: (0, 0)), low_spec, high_spec],
         out_specs=[
             pl.BlockSpec((block_rows, slot_count), lambda i: (i, 0)),
             pl.BlockSpec((1, block_rows), lambda i: (0, i)),
@@ -80,13 +74,14 @@
             jax.ShapeDtypeStruct((slot_count, slot_count), jnp.bfloat16),
             jax.ShapeDtypeStruct((1, slot_count), jnp.float32),
         ],
+        scratch_shapes=[pltpu.VMEM((slot_count, width), jnp.bfloat16)],
         compiler_params=pltpu.CompilerParams(dimension_semantics=("arbitrary",)),
         cost_estimate=pl.CostEstimate(
             flops=2 * slot_count * slot_count * width + 22 * slot_count * slot_count,
             transcendentals=0,
-            bytes_accessed=2 * slot_count * width * 2 + 2 * slot_count * slot_count,
+            bytes_accessed=slot_count * width * 2 + 2 * slot_count * slot_count,
         ),
-    )(keys.reshape(1, slot_count), *operands)
+    )(keys.reshape(1, slot_count), low, high)
 
 
 def on_device(embeddings, labels, image_lists, rank_keys):

time: 162 us -> 160 us (0.988)
  Pallas kernels: 16.2 us -> 13.6 us
    pallas_call x1, Pallas kernels: 16.2 us -> 13.6 us  [fused_affinity(): pl.pallas_call(affinity_kernel, grid=(slot_count // block_rows,), in_spec...]
where the time goes in v12:
time: 160 us; the launch traced here: 159 us
  blocking collectives  56.9 us (36%)
  waiting for transfers between devices  35.2 us (22%)
  starting transfers between devices  20.9 us (13%)
  matrix products  20.6 us (13%)
  Pallas kernels  13.6 us (8%)
  other arithmetic  6.94 us (4%)
  local copies, waits for them, and re-layouts  4.68 us (3%)
    all_to_all x2, blocking collectives, on_device(): lax.all_to_all(bucket_major(product), 'img', split_axis=0, concat_axis=0,...  34.3 us
    all_to_all x2, blocking collectives, on_device(): lax.all_to_all(to_bucket(scaled), 'img', split_axis=0, concat_axis=0, til...  22.6 us
    pallas_call x1, Pallas kernels, fused_affinity(): pl.pallas_call(affinity_kernel, grid=(slot_count // block_rows,), in_spec...  13.6 us
    dot_general x2, matrix products, on_device(): jnp.einsum('ajk,akc->ajc', weights, list_major(arrived), preferred_elemen...  12.1 us
    all_to_all x1, waiting for transfers between devices, on_device(): lax.all_to_all(low_payload, 'img', split_axis=0, concat_axis=0, tiled=True)  11.1 us
    all_to_all x1, waiting for transfers between devices, on_device(): lax.all_to_all(high_payload, 'img', split_axis=0, concat_axis=0, tiled=True)  10 us
    ppermute x4, waiting for transfers between devices, exchange_stage(): return jnp.concatenate([got, lax.ppermute(got, 'sub', pairs)], axis=1)  7.65 us
    all_to_all x1, starting transfers between devices, on_device(): lax.all_to_all(high_payload, 'img', split_axis=0, concat_axis=0, tiled=True)  7.28 us
  transfers between devices with their start and end apart: 7, of which 5 were waited for; matrix products, arithmetic and copies ran while one was open for 2% of the time, Pallas kernels for 0%

profile of v12, /device:TPU:0, one launch (start us, length us, event | category | flops | bytes accessed | tf_op | source)
XLA Modules:
  0.0 159.2 jit_solution(9103292786276940499)
XLA Ops:
  0.0 0.8 copy.57
  0.8 0.2 eq.32
  1.0 0.5 convert_reduce_fusion
  1.5 0.2 reduce_sum.39
  1.8 0.1 copy.58
  1.9 0.7 multiply_add_fusion
  2.6 0.1 iota_add_fusion.1
  2.7 0.1 add.108
  2.7 1.4 fusion.1
  4.1 1.9 %convolution_convert_fusion.2 = bf16[512,768]{1,0:T(8,128)(2,1)S(1)} fusion(bf16[512,768]{1,0:T(8,128)(2,1)} %param.5, f32[512]{0:T(512)S(1)} %add_rsqrt_fusion, s32[512]{0:T(512)S(1)} %bitcast.85, s32[512]{0:T(512)S(1)} %bitcast.77, s32[512]{0:T(512)S(1)} %add.108), kind=kOutput, calls=%fused_computation.13 | convolution fusion | flops 405012480 | bytes 1581056 | tf_op jit(solution)/shard_map/dot_general | solution.py:152
  6.0 0.0 copy-start.3
  6.0 0.8 fusion.22
  6.9 7.3 %all-to-all-start.1 = ((bf16[8,64,384]{2,1,0:T(8,128)(2,1)}), bf16[8,64,384]{2,1,0:T(8,128)(2,1)S(1)}, u32[]{:S(2)}, u32[]{:S(2)}) async-start(bf16[8,64,384]{2,1,0:T(8,128)(2,1)} %get-tuple-element.9), calls=%async_computation.1 | async-start | bytes 786432 | tf_op jit(solution)/shard_map/all_to_all | solution.py:169
  14.1 0.0 copy-done.1
  14.2 0.4 fusion.11
  14.6 0.3 fusion.9
  14.9 0.1 convert_element_type.81
  15.0 0.8 fusion.17
  15.8 10.0 %all-to-all-done.1 = bf16[8,64,384]{2,1,0:T(8,128)(2,1)S(1)} async-done(((bf16[8,64,384]{2,1,0:T(8,128)(2,1)}), bf16[8,64,384]{2,1,0:T(8,128)(2,1)S(1)}, u32[]{:S(2)}, u32[]{:S(2)}) %all-to-all-start.1) | async-done | bytes 393248 | tf_op jit(solution)/shard_map/all_to_all | solution.py:169
  25.8 3.6 %all-to-all-start = ((bf16[8,65,384]{2,1,0:T(8,128)(2,1)}), bf16[8,65,384]{2,1,0:T(8,128)(2,1)S(1)}, u32[]{:S(2)}, u32[]{:S(2)}) async-start(bf16[8,65,384]{2,1,0:T(8,128)(2,1)} %fusion.17), calls=%async_computation | async-start | bytes 884736 | tf_op jit(solution)/shard_map/all_to_all | solution.py:168
  29.5 1.5 collective-permute-start.2
  31.0 11.1 %all-to-all-done = bf16[8,65,384]{2,1,0:T(8,128)(2,1)S(1)} async-done(((bf16[8,65,384]{2,1,0:T(8,128)(2,1)}), bf16[8,65,384]{2,1,0:T(8,128)(2,1)S(1)}, u32[]{:S(2)}, u32[]{:S(2)}) %all-to-all-start) | async-done | bytes 399392 | tf_op jit(solution)/shard_map/all_to_all | solution.py:168
  42.1 1.5 collective-permute-start
  43.6 0.0 collective-permute-done.2
  43.6 0.1 pad_maximum_fusion.3
  43.7 0.1 collective-permute-start.3
  43.8 6.8 %collective-permute-done = bf16[8,1,65,384]{3,2,0,1:T(8,128)(2,1)S(1)} collective-permute-done((bf16[8,1,65,384]{3,2,0,1:T(8,128)(2,1)S(1)}, bf16[8,1,65,384]{3,2,0,1:T(8,128)(2,1)S(1)}, u32[]{:S(2)}, u32[]{:S(2)}) %collective-permute-start) | collective-permute-done | bytes 399392 | tf_op jit(solution)/shard_map/ppermute | solution.py:166
  50.6 0.1 pad_maximum_fusion.2
  50.7 0.1 copy.60
  50.8 0.1 collective-permute-start.1
  50.9 0.0 copy-done.3
  50.9 0.1 broadcast_add_fusion
  51.0 0.0 collective-permute-done.3
  51.0 1.3 pad_maximum_fusion.1.high_rows
  52.3 0.8 collective-permute-done.1
  53.2 0.1 copy.63
  53.3 0.2 pad_maximum_fusion.low_rows
  53.5 0.0 copy-start
  53.5 0.1 fusion.21
  53.6 0.8 reshape.187.col_keys
  54.4 0.4 copy-done
  54.8 13.6 %shard_map.55 = (bf16[2048,2048]{1,0:T(8,128)(2,1)}, f32[1,2048]{1,0:T(1,128)}) custom-call(f32[1,2048]{1,0:T(1,128)} %reshape.187.col_keys, bf16[8,4,65,384]{3,2,1,0:T(8,128)(2,1)} %copy-done, bf16[8,4,64,384]{3,2,1,0:T(8,128)(2,1)} %pad_maximum_fusion.1.high_rows), custom_call_target="tpu_custom_call" | custom-call | flops 6534725632 | bytes 11534336 | tf_op jit(solution)/shard_map/pallas_call | solution.py:65
  68.4 6.9 %all-to-all-start.2 = ((f32[8,1,256]{2,1,0:T(1,128)}), f32[8,1,256]{2,1,0:T(1,128)S(1)}, u32[]{:S(2)}, u32[]{:S(2)}) async-start(f32[8,1,256]{2,1,0:T(1,128)} %bitcast.93), calls=%async_computation.2 | async-start | bytes 16384 | tf_op jit(solution)/shard_map/all_to_all | solution.py:179
  75.3 0.1 iota_add_fusion
  75.4 0.1 add.102
  75.5 6.4 %all-to-all-done.2 = f32[8,1,256]{2,1,0:T(1,128)S(1)} async-done(((f32[8,1,256]{2,1,0:T(1,128)}), f32[8,1,256]{2,1,0:T(1,128)S(1)}, u32[]{:S(2)}, u32[]{:S(2)}) %all-to-all-start.2) | async-done | bytes 8224 | tf_op jit(solution)/shard_map/all_to_all | solution.py:179
  81.8 0.7 select_reduce_fusion
  82.5 0.0 copy-done.2
  82.6 1.3 convolution_convert_fusion.1
  83.8 0.1 copy.73
  84.0 10.6 %all_to_all.35 = bf16[8,1,256,64]{2,3,1,0:T(8,128)(2,1)S(1)} all-to-all(bf16[8,1,256,64]{2,3,1,0:T(8,128)(2,1)S(1)} %copy.65), channel_id=1, replica_groups=mesh['img'=8,'sub'=4] {'img'}, dimensions={0} | all-to-all | bytes 524288 | tf_op jit(solution)/shard_map/all_to_all | solution.py:188
  94.6 0.1 copy.66
  94.7 0.1 reshape.188
  94.9 6.0 %convolution_bitcast_fusion.1 = f32[8,1,256,64]{2,3,1,0:T(8,128)S(1)} fusion(bf16[8,256,2048]{2,1,0:T(8,128)(2,1)} %bitcast.58, bf16[2048,64,1]{0,1,2:T(8,128)(2,1)S(1)} %reshape.188), kind=kOutput, calls=%fused_computation.18 | convolution fusion | flops 536870912 | bytes 9175040 | tf_op jit(solution)/shard_map/ajk,akc->ajc/dot_general | solution.py:189
  100.9 17.1 %all_to_all.36 = f32[8,1,256,64]{2,3,1,0:T(8,128)S(1)} all-to-all(f32[8,1,256,64]{2,3,1,0:T(8,128)S(1)} %convolution_bitcast_fusion.1), channel_id=1, replica_groups=mesh['img'=8,'sub'=4] {'img'}, dimensions={0} | all-to-all | bytes 1048576 | tf_op jit(solution)/shard_map/all_to_all | solution.py:192
  118.0 1.7 %fusion.6 = bf16[512,64]{0,1:T(8,128)(2,1)S(1)} fusion(f32[2048,64]{0,1:T(8,128)S(1)} %bitcast.73, bf16[512,64]{0,1:T(8,128)(2,1)S(1)} %copy-done.2, f32[512]{0:T(512)S(1)} %get-tuple-element.16, f32[512]{0:T(512)S(1)} %get-tuple-element.15, s32[512]{0:T(512)S(1)} %bitcast.90, s32[512]{0:T(512)S(1)} %bitcast.82, s32[2048]{0:T(1024)S(1)} %add.102), kind=kOutput, calls=%fused_computation.24 | convolution fusion | flops 808648704 | bytes 671744 | tf_op jit(solution)/shard_map/kg,kc->gc/dot_general | solution.py:128
  119.8 1.3 convolution_convert_fusion
  121.0 0.1 copy.75
  121.2 12.0 %all_to_all.37 = bf16[8,1,256,64]{2,3,1,0:T(8,128)(2,1)S(1)} all-to-all(bf16[8,1,256,64]{2,3,1,0:T(8,128)(2,1)S(1)} %copy.69), channel_id=1, replica_groups=mesh['img'=8,'sub'=4] {'img'}, dimensions={0} | all-to-all | bytes 524288 | tf_op jit(solution)/shard_map/all_to_all | solution.py:188
  133.1 0.1 copy.70
  133.3 0.1 reshape.189
  133.4 6.0 %convolution_bitcast_fusion = f32[8,1,256,64]{2,3,1,0:T(8,128)S(1)} fusion(bf16[8,256,2048]{2,1,0:T(8,128)(2,1)} %bitcast.59, bf16[2048,64,1]{0,1,2:T(8,128)(2,1)S(1)} %reshape.189), kind=kOutput, calls=%fused_computation.17 | convolution fusion | flops 536870912 | bytes 9175040 | tf_op jit(solution)/shard_map/ajk,akc->ajc/dot_general | solution.py:189
  139.4 17.3 %all_to_all.38 = f32[8,1,256,64]{2,3,1,0:T(8,128)S(1)} all-to-all(f32[8,1,256,64]{2,3,1,0:T(8,128)S(1)} %convolution_bitcast_fusion), channel_id=1, replica_groups=mesh['img'=8,'sub'=4] {'img'}, dimensions={0} | all-to-all | bytes 1048576 | tf_op jit(solution)/shard_map/all_to_all | solution.py:192
  156.8 2.4 %fusion.7 = bf16[512,64]{0,1:T(8,128)(2,1)} fusion(f32[2048,64]{0,1:T(8,128)S(1)} %bitcast.72, bf16[512,64]{0,1:T(8,128)(2,1)S(1)} %copy-done.2, f32[512]{0:T(512)S(1)} %get-tuple-element.15, s32[512]{0:T(512)S(1)} %bitcast.92, s32[512]{0:T(512)S(1)} %bitcast.84, s32[2048]{0:T(1024)S(1)} %add.102), kind=kOutput, calls=%fused_computation.25 | convolution fusion | flops 808615936 | bytes 669696 | tf_op jit(solution)/shard_map/kg,kc->gc/dot_general | solution.py:128
  (15 shorter events, 0.2 us)
Async XLA Ops:
  0.0 14.1 %copy-start.1 = (s32[512,2]{0,1:T(2,128)S(1)}, s32[512,2]{0,1:T(2,128)}, u32[]{:S(2)}) copy-start(s32[512,2]{0,1:T(2,128)} %param.8) | copy-start | bytes 12292
  6.0 44.9 %copy-start.3 = (s32[4]{0:T(128)S(1)}, s32[4]{0:T(128)}, u32[]{:S(2)}) copy-start(s32[4]{0:T(128)} %constant.11.clone) | copy-start | bytes 52
  6.9 19.0 %all-to-all-start.1 = ((bf16[8,64,384]{2,1,0:T(8,128)(2,1)}), bf16[8,64,384]{2,1,0:T(8,128)(2,1)S(1)}, u32[]{:S(2)}, u32[]{:S(2)}) async-start(bf16[8,64,384]{2,1,0:T(8,128)(2,1)} %get-tuple-element.9), calls=%async_computation.1 | async-start | bytes 786432 | tf_op jit(solution)/shard_map/all_to_all | solution.py:169
  25.8 16.3 %all-to-all-start = ((bf16[8,65,384]{2,1,0:T(8,128)(2,1)}), bf16[8,65,384]{2,1,0:T(8,128)(2,1)S(1)}, u32[]{:S(2)}, u32[]{:S(2)}) async-start(bf16[8,65,384]{2,1,0:T(8,128)(2,1)} %fusion.17), calls=%async_computation | async-start | bytes 884736 | tf_op jit(solution)/shard_map/all_to_all | solution.py:168
  29.5 14.1 %collective-permute-start.2 = (bf16[8,1,64,384]{3,2,1,0:T(8,128)(2,1)S(1)}, bf16[8,1,64,384]{3,2,1,0:T(8,128)(2,1)S(1)}, u32[]{:S(2)}, u32[]{:S(2)}) collective-permute-start(bf16[8,1,64,384]{3,2,1,0:T(8,128)(2,1)S(1)} %bitcast.63), channel_id=1, source_target_pairs={{0,2},{1,3},{2,0},{3,1},{4,6},{5,7},{6,4},{7,5},{8,10},{9,11},{10,... | collective-permute-start | bytes 1179656 | tf_op jit(solution)/shard_map/ppermute | solution.py:166
  42.1 8.5 %collective-permute-start = (bf16[8,1,65,384]{3,2,0,1:T(8,128)(2,1)S(1)}, bf16[8,1,65,384]{3,2,0,1:T(8,128)(2,1)S(1)}, u32[]{:S(2)}, u32[]{:S(2)}) collective-permute-start(bf16[8,1,65,384]{3,2,0,1:T(8,128)(2,1)S(1)} %bitcast.60), channel_id=1, source_target_pairs={{0,2},{1,3},{2,0},{3,1},{4,6},{5,7},{6,4},{7,5},{8,10},{9,11},{10,... | collective-permute-start | bytes 1198088 | tf_op jit(solution)/shard_map/ppermute | solution.py:166
  43.7 7.3 %collective-permute-start.3 = (bf16[8,2,64,384]{3,2,1,0:T(8,128)(2,1)S(1)}, bf16[8,2,64,384]{3,2,1,0:T(8,128)(2,1)S(1)}, u32[]{:S(2)}, u32[]{:S(2)}) collective-permute-start(bf16[8,2,64,384]{3,2,1,0:T(8,128)(2,1)S(1)} %pad_maximum_fusion.3), channel_id=1, source_target_pairs={{0,1},{1,0},{2,3},{3,2},{4,5},{5,4},{6,7},{7,6},{8,9},{9,8},{10,11... | collective-permute-start | bytes 2359304 | tf_op jit(solution)/shard_map/ppermute | solution.py:166
  50.8 2.4 %collective-permute-start.1 = (bf16[8,2,65,384]{3,0,2,1:T(8,128)(2,1)S(1)}, bf16[8,2,65,384]{3,0,2,1:T(8,128)(2,1)S(1)}, u32[]{:S(2)}, u32[]{:S(2)}) collective-permute-start(bf16[8,2,65,384]{3,0,2,1:T(8,128)(2,1)S(1)} %copy.60), channel_id=1, source_target_pairs={{0,1},{1,0},{2,3},{3,2},{4,5},{5,4},{6,7},{7,6},{8,9},{9,8},{10,11... | collective-permute-start | bytes 2396168 | tf_op jit(solution)/shard_map/ppermute | solution.py:166
  53.5 1.3 copy-start
  54.8 27.8 %copy-start.2 = (bf16[512,64]{0,1:T(8,128)(2,1)S(1)}, bf16[512,64]{0,1:T(8,128)(2,1)}, u32[]{:S(2)}) copy-start(bf16[512,64]{0,1:T(8,128)(2,1)} %param.6) | copy-start | bytes 196612
  68.4 13.4 %all-to-all-start.2 = ((f32[8,1,256]{2,1,0:T(1,128)}), f32[8,1,256]{2,1,0:T(1,128)S(1)}, u32[]{:S(2)}, u32[]{:S(2)}) async-start(f32[8,1,256]{2,1,0:T(1,128)} %bitcast.93), calls=%async_computation.2 | async-start | bytes 16384 | tf_op jit(solution)/shard_map/all_to_all | solution.py:179

commit v13 on v12

--- a/solution.py
+++ b/solution.py
@@ -150,7 +150,7 @@
     mine_keys = jnp.where(jnp.any(mine_hit, axis=1), key_sum, -4096.0).astype(jnp.bfloat16)
     width = unit.shape[1]
     quarter = jnp.dot(mine_hit.astype(jnp.bfloat16), unit, preferred_element_type=jnp.float32)
-    half = width // 2
+    half = max(128, width // 3 // 128 * 128)
     quarter = quarter.astype(jnp.bfloat16).reshape(img_count, part, width)
     low_payload = jnp.concatenate(
         [

time: 160 us -> 159 us (level)
  blocking collectives: 56.9 us -> 70.6 us
  waiting for transfers between devices: 35.2 us -> 27.8 us
  starting transfers between devices: 20.9 us -> 14.1 us
    all_to_all x0 -> x1, blocking collectives: none -> 13.7 us  [on_device(): lax.all_to_all(low_payload, 'img', split_axis=0, concat_axis=0, tiled=True)]
    all_to_all x1 -> x0, waiting for transfers between devices: 11.1 us -> none  [on_device(): lax.all_to_all(low_payload, 'img', split_axis=0, concat_axis=0, tiled=True)]
    all_to_all x1 -> x0, starting transfers between devices: 3.63 us -> none  [on_device(): lax.all_to_all(low_payload, 'img', split_axis=0, concat_axis=0, tiled=True)]
    all_to_all x1, waiting for transfers between devices: 10 us -> 13.6 us  [on_device(): lax.all_to_all(high_payload, 'img', split_axis=0, concat_axis=0, tiled=True)]
    all_to_all x1, starting transfers between devices: 6.89 us -> 4.64 us  [on_device(): lax.all_to_all(bucket_major(row_sums), 'img', split_axis=0, concat_axis=0...]
  transfers between devices with their start and end apart: 7 -> 6, of which waited for: 5 -> 4; matrix products, arithmetic and copies ran while one was open for 2% -> 2% of each run, Pallas kernels for 0% -> 0%
where the time goes in v13:
time: 159 us
  blocking collectives  70.6 us (44%)
  waiting for transfers between devices  27.8 us (17%)
  matrix products  20.6 us (13%)
  starting transfers between devices  14.1 us (9%)
  Pallas kernels  13.6 us (9%)
  other arithmetic  7.46 us (5%)
  local copies, waits for them, and re-layouts  4.33 us (3%)
    all_to_all x2, blocking collectives, on_device(): lax.all_to_all(bucket_major(product), 'img', split_axis=0, concat_axis=0,...  34.3 us
    all_to_all x2, blocking collectives, on_device(): lax.all_to_all(to_bucket(scaled), 'img', split_axis=0, concat_axis=0, til...  22.6 us
    all_to_all x1, blocking collectives, on_device(): lax.all_to_all(low_payload, 'img', split_axis=0, concat_axis=0, tiled=True)  13.7 us
    pallas_call x1, Pallas kernels, fused_affinity(): pl.pallas_call(affinity_kernel, grid=(slot_count // block_rows,), in_spec...  13.6 us
    all_to_all x1, waiting for transfers between devices, on_device(): lax.all_to_all(high_payload, 'img', split_axis=0, concat_axis=0, tiled=True)  13.6 us
    dot_general x2, matrix products, on_device(): jnp.einsum('ajk,akc->ajc', weights, list_major(arrived), preferred_elemen...  12.1 us
    ppermute x4, waiting for transfers between devices, exchange_stage(): return jnp.concatenate([got, lax.ppermute(got, 'sub', pairs)], axis=1)  7.81 us
    all_to_all x1, starting transfers between devices, on_device(): lax.all_to_all(high_payload, 'img', split_axis=0, concat_axis=0, tiled=True)  7.28 us
  transfers between devices with their start and end apart: 6, of which 4 were waited for; matrix products, arithmetic and copies ran while one was open for 2% of the time, Pallas kernels for 0%

profile of v13, /device:TPU:0, one launch (start us, length us, event | category | flops | bytes accessed | tf_op | source)
XLA Modules:
  0.0 158.7 jit_solution(7784668537698121426)
XLA Ops:
  0.0 0.0 copy-start.1
  0.0 0.8 copy.57
  0.8 0.2 eq.32
  1.0 0.5 convert_reduce_fusion
  1.5 0.2 reduce_sum.39
  1.8 0.1 copy.58
  1.9 0.7 multiply_add_fusion
  2.6 0.1 iota_add_fusion.1
  2.7 0.1 add.108
  2.7 1.4 fusion.1
  4.1 1.9 %convolution_convert_fusion.2 = bf16[512,768]{1,0:T(8,128)(2,1)S(1)} fusion(bf16[512,768]{1,0:T(8,128)(2,1)} %param.5, f32[512]{0:T(512)S(1)} %add_rsqrt_fusion, s32[512]{0:T(512)S(1)} %bitcast.86, s32[512]{0:T(512)S(1)} %bitcast.78, s32[512]{0:T(512)S(1)} %add.108), kind=kOutput, calls=%fused_computation.12 | convolution fusion | flops 405012480 | bytes 1581056 | tf_op jit(solution)/shard_map/dot_general | solution.py:152
  6.0 0.0 copy-start.3
  6.0 0.8 slice.36
  6.9 7.3 %all-to-all-start.1 = ((bf16[8,64,512]{2,1,0:T(8,128)(2,1)}), bf16[8,64,512]{2,1,0:T(8,128)(2,1)S(1)}, u32[]{:S(2)}, u32[]{:S(2)}) async-start(bf16[8,64,512]{2,1,0:T(8,128)(2,1)} %slice.36), calls=%async_computation.1 | async-start | bytes 1048576 | tf_op jit(solution)/shard_map/all_to_all | solution.py:169
  14.2 0.0 copy-done.1
  14.2 0.4 fusion.10
  14.6 0.3 fusion.9
  14.9 0.1 convert_element_type.81
  15.0 13.6 %all-to-all-done.1 = bf16[8,64,512]{2,1,0:T(8,128)(2,1)S(1)} async-done(((bf16[8,64,512]{2,1,0:T(8,128)(2,1)}), bf16[8,64,512]{2,1,0:T(8,128)(2,1)S(1)}, u32[]{:S(2)}, u32[]{:S(2)}) %all-to-all-start.1) | async-done | bytes 524320 | tf_op jit(solution)/shard_map/all_to_all | solution.py:169
  28.6 1.5 collective-permute-start.2
  30.1 13.7 %all_to_all.35 = bf16[8,65,256]{2,1,0:T(8,128)(2,1)S(1)} all-to-all(bf16[8,65,256]{2,1,0:T(8,128)(2,1)S(1)} %fusion.17), channel_id=1, replica_groups=mesh['img'=8,'sub'=4] {'img'}, dimensions={0} | all-to-all | bytes 532480 | tf_op jit(solution)/shard_map/all_to_all | solution.py:168
  43.8 0.5 collective-permute-start
  44.4 0.0 collective-permute-done.2
  44.4 0.1 pad_maximum_fusion.2
  44.5 0.1 collective-permute-start.3
  44.5 6.0 %collective-permute-done = bf16[8,1,65,256]{3,2,0,1:T(8,128)(2,1)S(1)} collective-permute-done((bf16[8,1,65,256]{3,2,0,1:T(8,128)(2,1)S(1)}, bf16[8,1,65,256]{3,2,0,1:T(8,128)(2,1)S(1)}, u32[]{:S(2)}, u32[]{:S(2)}) %collective-permute-start) | collective-permute-done | bytes 266272 | tf_op jit(solution)/shard_map/ppermute | solution.py:166
  50.5 0.1 pad_maximum_fusion.3
  50.6 0.1 copy.60
  50.7 0.1 collective-permute-start.1
  50.8 0.0 copy-done.3
  50.8 0.1 broadcast_add_fusion
  50.9 1.8 %collective-permute-done.1 = bf16[8,2,65,256]{3,0,2,1:T(8,128)(2,1)S(1)} collective-permute-done((bf16[8,2,65,256]{3,0,2,1:T(8,128)(2,1)S(1)}, bf16[8,2,65,256]{3,0,2,1:T(8,128)(2,1)S(1)}, u32[]{:S(2)}, u32[]{:S(2)}) %collective-permute-start.1) | collective-permute-done | bytes 532512 | tf_op jit(solution)/shard_map/ppermute | solution.py:166
  52.7 0.1 copy.63
  52.8 0.1 pad_maximum_fusion.1.low_rows
  52.9 0.0 copy-start
  53.0 0.1 fusion.21
  53.0 0.8 reshape.187.col_keys
  53.8 0.0 collective-permute-done.3
  53.9 2.8 %pad_maximum_fusion.high_rows = bf16[8,4,64,512]{3,2,1,0:T(8,128)(2,1)} fusion(bf16[8,2,64,512]{3,2,1,0:T(8,128)(2,1)} %collective-permute-done.3, bf16[8,1,64,512]{3,2,1,0:T(8,128)(2,1)S(1)} %collective-permute-done.2, bf16[8,1,64,512]{3,2,1,0:T(8,128)(2,1)S(1)} %bitcast.62), kind=kLoop, calls=%fused_computation.7 | loop fusion | flops 2097152 | bytes 4194304 | tf_op jit(solution)/shard_map/concatenate | solution.py:166
  56.7 0.0 copy-done
  56.7 0.0 copy-start.2
  56.7 13.6 %shard_map.55 = (bf16[2048,2048]{1,0:T(8,128)(2,1)}, f32[1,2048]{1,0:T(1,128)}) custom-call(f32[1,2048]{1,0:T(1,128)} %reshape.187.col_keys, bf16[8,4,65,256]{3,2,1,0:T(8,128)(2,1)} %copy-done, bf16[8,4,64,512]{3,2,1,0:T(8,128)(2,1)} %pad_maximum_fusion.high_rows), custom_call_target="tpu_custom_call" | custom-call | flops 6534725632 | bytes 11534336 | tf_op jit(solution)/shard_map/pallas_call | solution.py:65
  70.3 4.6 %all-to-all-start.2 = ((f32[8,1,256]{2,1,0:T(1,128)}), f32[8,1,256]{2,1,0:T(1,128)S(1)}, u32[]{:S(2)}, u32[]{:S(2)}) async-start(f32[8,1,256]{2,1,0:T(1,128)} %bitcast.94), calls=%async_computation.2 | async-start | bytes 16384 | tf_op jit(solution)/shard_map/all_to_all | solution.py:179
  74.9 0.1 iota_add_fusion
  75.0 0.1 add.102
  75.1 6.4 %all-to-all-done.2 = f32[8,1,256]{2,1,0:T(1,128)S(1)} async-done(((f32[8,1,256]{2,1,0:T(1,128)}), f32[8,1,256]{2,1,0:T(1,128)S(1)}, u32[]{:S(2)}, u32[]{:S(2)}) %all-to-all-start.2) | async-done | bytes 8224 | tf_op jit(solution)/shard_map/all_to_all | solution.py:179
  81.4 0.7 select_reduce_fusion
  82.2 0.0 copy-done.2
  82.2 1.3 convolution_convert_fusion.1
  83.5 0.1 copy.73
  83.6 10.6 %all_to_all.36 = bf16[8,1,256,64]{2,3,1,0:T(8,128)(2,1)S(1)} all-to-all(bf16[8,1,256,64]{2,3,1,0:T(8,128)(2,1)S(1)} %copy.65), channel_id=1, replica_groups=mesh['img'=8,'sub'=4] {'img'}, dimensions={0} | all-to-all | bytes 524288 | tf_op jit(solution)/shard_map/all_to_all | solution.py:188
  94.2 0.1 copy.66
  94.4 0.1 reshape.188
  94.5 6.0 %convolution_bitcast_fusion.1 = f32[8,1,256,64]{2,3,1,0:T(8,128)S(1)} fusion(bf16[8,256,2048]{2,1,0:T(8,128)(2,1)} %bitcast.58, bf16[2048,64,1]{0,1,2:T(8,128)(2,1)S(1)} %reshape.188), kind=kOutput, calls=%fused_computation.17 | convolution fusion | flops 536870912 | bytes 9175040 | tf_op jit(solution)/shard_map/ajk,akc->ajc/dot_general | solution.py:189
  100.5 17.0 %all_to_all.37 = f32[8,1,256,64]{2,3,1,0:T(8,128)S(1)} all-to-all(f32[8,1,256,64]{2,3,1,0:T(8,128)S(1)} %convolution_bitcast_fusion.1), channel_id=1, replica_groups=mesh['img'=8,'sub'=4] {'img'}, dimensions={0} | all-to-all | bytes 1048576 | tf_op jit(solution)/shard_map/all_to_all | solution.py:192
  117.6 1.7 %fusion.6 = bf16[512,64]{0,1:T(8,128)(2,1)S(1)} fusion(f32[2048,64]{0,1:T(8,128)S(1)} %bitcast.74, bf16[512,64]{0,1:T(8,128)(2,1)S(1)} %copy-done.2, f32[512]{0:T(512)S(1)} %get-tuple-element.14, f32[512]{0:T(512)S(1)} %get-tuple-element.13, s32[512]{0:T(512)S(1)} %bitcast.91, s32[512]{0:T(512)S(1)} %bitcast.83, s32[2048]{0:T(1024)S(1)} %add.102), kind=kOutput, calls=%fused_computation.24 | convolution fusion | flops 808648704 | bytes 671744 | tf_op jit(solution)/shard_map/kg,kc->gc/dot_general | solution.py:128
  119.4 1.3 convolution_convert_fusion
  120.6 0.1 copy.75
  120.7 12.0 %all_to_all.38 = bf16[8,1,256,64]{2,3,1,0:T(8,128)(2,1)S(1)} all-to-all(bf16[8,1,256,64]{2,3,1,0:T(8,128)(2,1)S(1)} %copy.69), channel_id=1, replica_groups=mesh['img'=8,'sub'=4] {'img'}, dimensions={0} | all-to-all | bytes 524288 | tf_op jit(solution)/shard_map/all_to_all | solution.py:188
  132.7 0.1 copy.70
  132.9 0.1 reshape.189
  133.0 6.0 %convolution_bitcast_fusion = f32[8,1,256,64]{2,3,1,0:T(8,128)S(1)} fusion(bf16[8,256,2048]{2,1,0:T(8,128)(2,1)} %bitcast.59, bf16[2048,64,1]{0,1,2:T(8,128)(2,1)S(1)} %reshape.189), kind=kOutput, calls=%fused_computation.16 | convolution fusion | flops 536870912 | bytes 9175040 | tf_op jit(solution)/shard_map/ajk,akc->ajc/dot_general | solution.py:189
  139.0 17.3 %all_to_all.39 = f32[8,1,256,64]{2,3,1,0:T(8,128)S(1)} all-to-all(f32[8,1,256,64]{2,3,1,0:T(8,128)S(1)} %convolution_bitcast_fusion), channel_id=1, replica_groups=mesh['img'=8,'sub'=4] {'img'}, dimensions={0} | all-to-all | bytes 1048576 | tf_op jit(solution)/shard_map/all_to_all | solution.py:192
  156.4 2.4 %fusion.7 = bf16[512,64]{0,1:T(8,128)(2,1)} fusion(f32[2048,64]{0,1:T(8,128)S(1)} %bitcast.73, bf16[512,64]{0,1:T(8,128)(2,1)S(1)} %copy-done.2, f32[512]{0:T(512)S(1)} %get-tuple-element.13, s32[512]{0:T(512)S(1)} %bitcast.93, s32[512]{0:T(512)S(1)} %bitcast.85, s32[2048]{0:T(1024)S(1)} %add.102), kind=kOutput, calls=%fused_computation.25 | convolution fusion | flops 808615936 | bytes 669696 | tf_op jit(solution)/shard_map/kg,kc->gc/dot_general | solution.py:128
  (15 shorter events, 0.3 us)
Async XLA Ops:
  0.0 14.2 %copy-start.1 = (s32[512,2]{0,1:T(2,128)S(1)}, s32[512,2]{0,1:T(2,128)}, u32[]{:S(2)}) copy-start(s32[512,2]{0,1:T(2,128)} %param.8) | copy-start | bytes 12292
  6.0 44.8 %copy-start.3 = (s32[4]{0:T(128)S(1)}, s32[4]{0:T(128)}, u32[]{:S(2)}) copy-start(s32[4]{0:T(128)} %constant.11.clone) | copy-start | bytes 52
  6.9 21.8 %all-to-all-start.1 = ((bf16[8,64,512]{2,1,0:T(8,128)(2,1)}), bf16[8,64,512]{2,1,0:T(8,128)(2,1)S(1)}, u32[]{:S(2)}, u32[]{:S(2)}) async-start(bf16[8,64,512]{2,1,0:T(8,128)(2,1)} %slice.36), calls=%async_computation.1 | async-start | bytes 1048576 | tf_op jit(solution)/shard_map/all_to_all | solution.py:169
  28.6 15.7 %collective-permute-start.2 = (bf16[8,1,64,512]{3,2,1,0:T(8,128)(2,1)S(1)}, bf16[8,1,64,512]{3,2,1,0:T(8,128)(2,1)S(1)}, u32[]{:S(2)}, u32[]{:S(2)}) collective-permute-start(bf16[8,1,64,512]{3,2,1,0:T(8,128)(2,1)S(1)} %bitcast.60), channel_id=1, source_target_pairs={{0,2},{1,3},{2,0},{3,1},{4,6},{5,7},{6,4},{7,5},{8,10},{9,11},{10,... | collective-permute-start | bytes 1572872 | tf_op jit(solution)/shard_map/ppermute | solution.py:166
  43.8 6.7 %collective-permute-start = (bf16[8,1,65,256]{3,2,0,1:T(8,128)(2,1)S(1)}, bf16[8,1,65,256]{3,2,0,1:T(8,128)(2,1)S(1)}, u32[]{:S(2)}, u32[]{:S(2)}) collective-permute-start(bf16[8,1,65,256]{3,2,0,1:T(8,128)(2,1)S(1)} %bitcast.63), channel_id=1, source_target_pairs={{0,2},{1,3},{2,0},{3,1},{4,6},{5,7},{6,4},{7,5},{8,10},{9,11},{10,... | collective-permute-start | bytes 798728 | tf_op jit(solution)/shard_map/ppermute | solution.py:166
  44.5 9.4 %collective-permute-start.3 = (bf16[8,2,64,512]{3,2,1,0:T(8,128)(2,1)S(1)}, bf16[8,2,64,512]{3,2,1,0:T(8,128)(2,1)}, u32[]{:S(2)}, u32[]{:S(2)}) collective-permute-start(bf16[8,2,64,512]{3,2,1,0:T(8,128)(2,1)S(1)} %pad_maximum_fusion.2), channel_id=1, source_target_pairs={{0,1},{1,0},{2,3},{3,2},{4,5},{5,4},{6,7},{7,6},{8,9},{9,8},{10,11... | collective-permute-start | bytes 3145736 | tf_op jit(solution)/shard_map/ppermute | solution.py:166
  50.7 2.0 %collective-permute-start.1 = (bf16[8,2,65,256]{3,0,2,1:T(8,128)(2,1)S(1)}, bf16[8,2,65,256]{3,0,2,1:T(8,128)(2,1)S(1)}, u32[]{:S(2)}, u32[]{:S(2)}) collective-permute-start(bf16[8,2,65,256]{3,0,2,1:T(8,128)(2,1)S(1)} %copy.60), channel_id=1, source_target_pairs={{0,1},{1,0},{2,3},{3,2},{4,5},{5,4},{6,7},{7,6},{8,9},{9,8},{10,11... | collective-permute-start | bytes 1597448 | tf_op jit(solution)/shard_map/ppermute | solution.py:166
  52.9 3.7 %copy-start = (bf16[8,4,65,256]{3,2,1,0:T(8,128)(2,1)}, bf16[8,4,65,256]{3,2,1,0:T(8,128)(2,1)S(1)}, u32[]{:S(2)}) copy-start(bf16[8,4,65,256]{3,2,1,0:T(8,128)(2,1)S(1)} %pad_maximum_fusion.1.low_rows) | copy-start | bytes 3194884
  56.7 25.5 %copy-start.2 = (bf16[512,64]{0,1:T(8,128)(2,1)S(1)}, bf16[512,64]{0,1:T(8,128)(2,1)}, u32[]{:S(2)}) copy-start(bf16[512,64]{0,1:T(8,128)(2,1)} %param.6) | copy-start | bytes 196612
  70.3 11.2 %all-to-all-start.2 = ((f32[8,1,256]{2,1,0:T(1,128)}), f32[8,1,256]{2,1,0:T(1,128)S(1)}, u32[]{:S(2)}, u32[]{:S(2)}) async-start(f32[8,1,256]{2,1,0:T(1,128)} %bitcast.94), calls=%async_computation.2 | async-start | bytes 16384 | tf_op jit(solution)/shard_map/all_to_all | solution.py:179

commit v14 on v13

--- a/solution.py
+++ b/solution.py
@@ -127,7 +127,7 @@
         flat = returned.reshape(slot_total, -1)
         return jnp.einsum(
             "kg,kc->gc", pick.astype(jnp.float32), flat,
-            precision=lax.Precision.HIGHEST, preferred_element_type=jnp.float32,
+            precision=lax.Precision.HIGH, preferred_element_type=jnp.float32,
         )
 
     values = embeddings.astype(jnp.float32)

time: 159 us -> 159 us (level)
  no operation moved by 1% of the time
where the time goes in v14:
time: 159 us; the launch traced here: 158 us
  blocking collectives  70.6 us (44%)
  waiting for transfers between devices  27.8 us (17%)
  matrix products  19.8 us (12%)
  starting transfers between devices  14.1 us (9%)
  Pallas kernels  13.6 us (9%)
  other arithmetic  7.46 us (5%)
  local copies, waits for them, and re-layouts  4.33 us (3%)
    all_to_all x2, blocking collectives, on_device(): lax.all_to_all(bucket_major(product), 'img', split_axis=0, concat_axis=0,...  34.3 us
    all_to_all x2, blocking collectives, on_device(): lax.all_to_all(to_bucket(scaled), 'img', split_axis=0, concat_axis=0, til...  22.6 us
    all_to_all x1, blocking collectives, on_device(): lax.all_to_all(low_payload, 'img', split_axis=0, concat_axis=0, tiled=True)  13.7 us
    pallas_call x1, Pallas kernels, fused_affinity(): pl.pallas_call(affinity_kernel, grid=(slot_count // block_rows,), in_spec...  13.6 us
    all_to_all x1, waiting for transfers between devices, on_device(): lax.all_to_all(high_payload, 'img', split_axis=0, concat_axis=0, tiled=True)  13.6 us
    dot_general x2, matrix products, on_device(): jnp.einsum('ajk,akc->ajc', weights, list_major(arrived), preferred_elemen...  12.1 us
    ppermute x4, waiting for transfers between devices, exchange_stage(): return jnp.concatenate([got, lax.ppermute(got, 'sub', pairs)], axis=1)  7.81 us
    all_to_all x1, starting transfers between devices, on_device(): lax.all_to_all(high_payload, 'img', split_axis=0, concat_axis=0, tiled=True)  7.28 us
  transfers between devices with their start and end apart: 6, of which 4 were waited for; matrix products, arithmetic and copies ran while one was open for 2% of the time, Pallas kernels for 0%

profile of v14, /device:TPU:0, one launch (start us, length us, event | category | flops | bytes accessed | tf_op | source)
XLA Modules:
  0.0 157.9 jit_solution(3264670572761075103)
XLA Ops:
  0.0 0.0 copy-start.1
  0.0 0.8 copy.57
  0.8 0.2 eq.32
  1.0 0.5 convert_reduce_fusion
  1.5 0.2 reduce_sum.39
  1.8 0.1 copy.58
  1.9 0.7 multiply_add_fusion
  2.6 0.1 iota_add_fusion.1
  2.7 0.1 add.108
  2.7 1.4 fusion.1
  4.1 1.9 %convolution_convert_fusion.2 = bf16[512,768]{1,0:T(8,128)(2,1)S(1)} fusion(bf16[512,768]{1,0:T(8,128)(2,1)} %param.5, f32[512]{0:T(512)S(1)} %add_rsqrt_fusion, s32[512]{0:T(512)S(1)} %bitcast.86, s32[512]{0:T(512)S(1)} %bitcast.78, s32[512]{0:T(512)S(1)} %add.108), kind=kOutput, calls=%fused_computation.12 | convolution fusion | flops 405012480 | bytes 1581056 | tf_op jit(solution)/shard_map/dot_general | solution.py:152
  6.0 0.0 copy-start.3
  6.0 0.8 slice.36
  6.9 7.3 %all-to-all-start.1 = ((bf16[8,64,512]{2,1,0:T(8,128)(2,1)}), bf16[8,64,512]{2,1,0:T(8,128)(2,1)S(1)}, u32[]{:S(2)}, u32[]{:S(2)}) async-start(bf16[8,64,512]{2,1,0:T(8,128)(2,1)} %slice.36), calls=%async_computation.1 | async-start | bytes 1048576 | tf_op jit(solution)/shard_map/all_to_all | solution.py:169
  14.2 0.0 copy-done.1
  14.2 0.4 fusion.10
  14.6 0.3 fusion.9
  14.9 0.1 convert_element_type.81
  15.0 13.6 %all-to-all-done.1 = bf16[8,64,512]{2,1,0:T(8,128)(2,1)S(1)} async-done(((bf16[8,64,512]{2,1,0:T(8,128)(2,1)}), bf16[8,64,512]{2,1,0:T(8,128)(2,1)S(1)}, u32[]{:S(2)}, u32[]{:S(2)}) %all-to-all-start.1) | async-done | bytes 524320 | tf_op jit(solution)/shard_map/all_to_all | solution.py:169
  28.6 1.5 collective-permute-start.2
  30.1 13.7 %all_to_all.35 = bf16[8,65,256]{2,1,0:T(8,128)(2,1)S(1)} all-to-all(bf16[8,65,256]{2,1,0:T(8,128)(2,1)S(1)} %fusion.17), channel_id=1, replica_groups=mesh['img'=8,'sub'=4] {'img'}, dimensions={0} | all-to-all | bytes 532480 | tf_op jit(solution)/shard_map/all_to_all | solution.py:168
  43.8 0.5 collective-permute-start
  44.4 0.0 collective-permute-done.2
  44.4 0.1 pad_maximum_fusion.2
  44.5 0.1 collective-permute-start.3
  44.5 6.0 %collective-permute-done = bf16[8,1,65,256]{3,2,0,1:T(8,128)(2,1)S(1)} collective-permute-done((bf16[8,1,65,256]{3,2,0,1:T(8,128)(2,1)S(1)}, bf16[8,1,65,256]{3,2,0,1:T(8,128)(2,1)S(1)}, u32[]{:S(2)}, u32[]{:S(2)}) %collective-permute-start) | collective-permute-done | bytes 266272 | tf_op jit(solution)/shard_map/ppermute | solution.py:166
  50.5 0.1 pad_maximum_fusion.3
  50.6 0.1 copy.60
  50.7 0.1 collective-permute-start.1
  50.8 0.0 copy-done.3
  50.8 0.1 broadcast_add_fusion
  50.9 1.8 %collective-permute-done.1 = bf16[8,2,65,256]{3,0,2,1:T(8,128)(2,1)S(1)} collective-permute-done((bf16[8,2,65,256]{3,0,2,1:T(8,128)(2,1)S(1)}, bf16[8,2,65,256]{3,0,2,1:T(8,128)(2,1)S(1)}, u32[]{:S(2)}, u32[]{:S(2)}) %collective-permute-start.1) | collective-permute-done | bytes 532512 | tf_op jit(solution)/shard_map/ppermute | solution.py:166
  52.7 0.1 copy.63
  52.8 0.1 pad_maximum_fusion.1.low_rows
  52.9 0.0 copy-start
  53.0 0.1 fusion.21
  53.0 0.8 reshape.187.col_keys
  53.8 0.0 collective-permute-done.3
  53.9 2.8 %pad_maximum_fusion.high_rows = bf16[8,4,64,512]{3,2,1,0:T(8,128)(2,1)} fusion(bf16[8,2,64,512]{3,2,1,0:T(8,128)(2,1)} %collective-permute-done.3, bf16[8,1,64,512]{3,2,1,0:T(8,128)(2,1)S(1)} %collective-permute-done.2, bf16[8,1,64,512]{3,2,1,0:T(8,128)(2,1)S(1)} %bitcast.62), kind=kLoop, calls=%fused_computation.7 | loop fusion | flops 2097152 | bytes 4194304 | tf_op jit(solution)/shard_map/concatenate | solution.py:166
  56.7 0.0 copy-done
  56.7 0.0 copy-start.2
  56.7 13.6 %shard_map.55 = (bf16[2048,2048]{1,0:T(8,128)(2,1)}, f32[1,2048]{1,0:T(1,128)}) custom-call(f32[1,2048]{1,0:T(1,128)} %reshape.187.col_keys, bf16[8,4,65,256]{3,2,1,0:T(8,128)(2,1)} %copy-done, bf16[8,4,64,512]{3,2,1,0:T(8,128)(2,1)} %pad_maximum_fusion.high_rows), custom_call_target="tpu_custom_call" | custom-call | flops 6534725632 | bytes 11534336 | tf_op jit(solution)/shard_map/pallas_call | solution.py:65
  70.3 4.6 %all-to-all-start.2 = ((f32[8,1,256]{2,1,0:T(1,128)}), f32[8,1,256]{2,1,0:T(1,128)S(1)}, u32[]{:S(2)}, u32[]{:S(2)}) async-start(f32[8,1,256]{2,1,0:T(1,128)} %bitcast.94), calls=%async_computation.2 | async-start | bytes 16384 | tf_op jit(solution)/shard_map/all_to_all | solution.py:179
  74.9 0.1 iota_add_fusion
  75.0 0.1 add.102
  75.1 6.4 %all-to-all-done.2 = f32[8,1,256]{2,1,0:T(1,128)S(1)} async-done(((f32[8,1,256]{2,1,0:T(1,128)}), f32[8,1,256]{2,1,0:T(1,128)S(1)}, u32[]{:S(2)}, u32[]{:S(2)}) %all-to-all-start.2) | async-done | bytes 8224 | tf_op jit(solution)/shard_map/all_to_all | solution.py:179
  81.4 0.7 select_reduce_fusion
  82.2 0.0 copy-done.2
  82.2 1.3 convolution_convert_fusion.1
  83.5 0.1 copy.73
  83.6 10.6 %all_to_all.36 = bf16[8,1,256,64]{2,3,1,0:T(8,128)(2,1)S(1)} all-to-all(bf16[8,1,256,64]{2,3,1,0:T(8,128)(2,1)S(1)} %copy.65), channel_id=1, replica_groups=mesh['img'=8,'sub'=4] {'img'}, dimensions={0} | all-to-all | bytes 524288 | tf_op jit(solution)/shard_map/all_to_all | solution.py:188
  94.2 0.1 copy.66
  94.4 0.1 reshape.188
  94.5 6.0 %convolution_bitcast_fusion.1 = f32[8,1,256,64]{2,3,1,0:T(8,128)S(1)} fusion(bf16[8,256,2048]{2,1,0:T(8,128)(2,1)} %bitcast.58, bf16[2048,64,1]{0,1,2:T(8,128)(2,1)S(1)} %reshape.188), kind=kOutput, calls=%fused_computation.17 | convolution fusion | flops 536870912 | bytes 9175040 | tf_op jit(solution)/shard_map/ajk,akc->ajc/dot_general | solution.py:189
  100.5 17.0 %all_to_all.37 = f32[8,1,256,64]{2,3,1,0:T(8,128)S(1)} all-to-all(f32[8,1,256,64]{2,3,1,0:T(8,128)S(1)} %convolution_bitcast_fusion.1), channel_id=1, replica_groups=mesh['img'=8,'sub'=4] {'img'}, dimensions={0} | all-to-all | bytes 1048576 | tf_op jit(solution)/shard_map/all_to_all | solution.py:192
  117.6 1.3 fusion.6
  118.9 1.3 convolution_convert_fusion
  120.2 0.1 copy.75
  120.3 12.0 %all_to_all.38 = bf16[8,1,256,64]{2,3,1,0:T(8,128)(2,1)S(1)} all-to-all(bf16[8,1,256,64]{2,3,1,0:T(8,128)(2,1)S(1)} %copy.69), channel_id=1, replica_groups=mesh['img'=8,'sub'=4] {'img'}, dimensions={0} | all-to-all | bytes 524288 | tf_op jit(solution)/shard_map/all_to_all | solution.py:188
  132.3 0.1 copy.70
  132.4 0.1 reshape.189
  132.6 6.0 %convolution_bitcast_fusion = f32[8,1,256,64]{2,3,1,0:T(8,128)S(1)} fusion(bf16[8,256,2048]{2,1,0:T(8,128)(2,1)} %bitcast.59, bf16[2048,64,1]{0,1,2:T(8,128)(2,1)S(1)} %reshape.189), kind=kOutput, calls=%fused_computation.16 | convolution fusion | flops 536870912 | bytes 9175040 | tf_op jit(solution)/shard_map/ajk,akc->ajc/dot_general | solution.py:189
  138.6 17.3 %all_to_all.39 = f32[8,1,256,64]{2,3,1,0:T(8,128)S(1)} all-to-all(f32[8,1,256,64]{2,3,1,0:T(8,128)S(1)} %convolution_bitcast_fusion), channel_id=1, replica_groups=mesh['img'=8,'sub'=4] {'img'}, dimensions={0} | all-to-all | bytes 1048576 | tf_op jit(solution)/shard_map/all_to_all | solution.py:192
  155.9 2.0 %fusion.7 = bf16[512,64]{0,1:T(8,128)(2,1)} fusion(f32[2048,64]{0,1:T(8,128)S(1)} %bitcast.73, bf16[512,64]{0,1:T(8,128)(2,1)S(1)} %copy-done.2, f32[512]{0:T(512)S(1)} %get-tuple-element.13, s32[512]{0:T(512)S(1)} %bitcast.93, s32[512]{0:T(512)S(1)} %bitcast.85, s32[2048]{0:T(1024)S(1)} %add.102), kind=kOutput, calls=%fused_computation.25 | convolution fusion | flops 405962752 | bytes 669696 | tf_op jit(solution)/shard_map/kg,kc->gc/dot_general | solution.py:128
  (15 shorter events, 0.3 us)
Async XLA Ops:
  0.0 14.2 %copy-start.1 = (s32[512,2]{0,1:T(2,128)S(1)}, s32[512,2]{0,1:T(2,128)}, u32[]{:S(2)}) copy-start(s32[512,2]{0,1:T(2,128)} %param.8) | copy-start | bytes 12292
  6.0 44.8 %copy-start.3 = (s32[4]{0:T(128)S(1)}, s32[4]{0:T(128)}, u32[]{:S(2)}) copy-start(s32[4]{0:T(128)} %constant.11.clone) | copy-start | bytes 52
  6.9 21.8 %all-to-all-start.1 = ((bf16[8,64,512]{2,1,0:T(8,128)(2,1)}), bf16[8,64,512]{2,1,0:T(8,128)(2,1)S(1)}, u32[]{:S(2)}, u32[]{:S(2)}) async-start(bf16[8,64,512]{2,1,0:T(8,128)(2,1)} %slice.36), calls=%async_computation.1 | async-start | bytes 1048576 | tf_op jit(solution)/shard_map/all_to_all | solution.py:169
  28.6 15.7 %collective-permute-start.2 = (bf16[8,1,64,512]{3,2,1,0:T(8,128)(2,1)S(1)}, bf16[8,1,64,512]{3,2,1,0:T(8,128)(2,1)S(1)}, u32[]{:S(2)}, u32[]{:S(2)}) collective-permute-start(bf16[8,1,64,512]{3,2,1,0:T(8,128)(2,1)S(1)} %bitcast.60), channel_id=1, source_target_pairs={{0,2},{1,3},{2,0},{3,1},{4,6},{5,7},{6,4},{7,5},{8,10},{9,11},{10,... | collective-permute-start | bytes 1572872 | tf_op jit(solution)/shard_map/ppermute | solution.py:166
  43.8 6.7 %collective-permute-start = (bf16[8,1,65,256]{3,2,0,1:T(8,128)(2,1)S(1)}, bf16[8,1,65,256]{3,2,0,1:T(8,128)(2,1)S(1)}, u32[]{:S(2)}, u32[]{:S(2)}) collective-permute-start(bf16[8,1,65,256]{3,2,0,1:T(8,128)(2,1)S(1)} %bitcast.63), channel_id=1, source_target_pairs={{0,2},{1,3},{2,0},{3,1},{4,6},{5,7},{6,4},{7,5},{8,10},{9,11},{10,... | collective-permute-start | bytes 798728 | tf_op jit(solution)/shard_map/ppermute | solution.py:166
  44.5 9.4 %collective-permute-start.3 = (bf16[8,2,64,512]{3,2,1,0:T(8,128)(2,1)S(1)}, bf16[8,2,64,512]{3,2,1,0:T(8,128)(2,1)}, u32[]{:S(2)}, u32[]{:S(2)}) collective-permute-start(bf16[8,2,64,512]{3,2,1,0:T(8,128)(2,1)S(1)} %pad_maximum_fusion.2), channel_id=1, source_target_pairs={{0,1},{1,0},{2,3},{3,2},{4,5},{5,4},{6,7},{7,6},{8,9},{9,8},{10,11... | collective-permute-start | bytes 3145736 | tf_op jit(solution)/shard_map/ppermute | solution.py:166
  50.7 2.0 %collective-permute-start.1 = (bf16[8,2,65,256]{3,0,2,1:T(8,128)(2,1)S(1)}, bf16[8,2,65,256]{3,0,2,1:T(8,128)(2,1)S(1)}, u32[]{:S(2)}, u32[]{:S(2)}) collective-permute-start(bf16[8,2,65,256]{3,0,2,1:T(8,128)(2,1)S(1)} %copy.60), channel_id=1, source_target_pairs={{0,1},{1,0},{2,3},{3,2},{4,5},{5,4},{6,7},{7,6},{8,9},{9,8},{10,11... | collective-permute-start | bytes 1597448 | tf_op jit(solution)/shard_map/ppermute | solution.py:166
  52.9 3.7 %copy-start = (bf16[8,4,65,256]{3,2,1,0:T(8,128)(2,1)}, bf16[8,4,65,256]{3,2,1,0:T(8,128)(2,1)S(1)}, u32[]{:S(2)}) copy-start(bf16[8,4,65,256]{3,2,1,0:T(8,128)(2,1)S(1)} %pad_maximum_fusion.1.low_rows) | copy-start | bytes 3194884
  56.7 25.5 %copy-start.2 = (bf16[512,64]{0,1:T(8,128)(2,1)S(1)}, bf16[512,64]{0,1:T(8,128)(2,1)}, u32[]{:S(2)}) copy-start(bf16[512,64]{0,1:T(8,128)(2,1)} %param.6) | copy-start | bytes 196612
  70.3 11.2 %all-to-all-start.2 = ((f32[8,1,256]{2,1,0:T(1,128)}), f32[8,1,256]{2,1,0:T(1,128)S(1)}, u32[]{:S(2)}, u32[]{:S(2)}) async-start(f32[8,1,256]{2,1,0:T(1,128)} %bitcast.94), calls=%async_computation.2 | async-start | bytes 16384 | tf_op jit(solution)/shard_map/all_to_all | solution.py:179

commit v15 on v14

--- a/solution.py
+++ b/solution.py
@@ -1,3 +1,5 @@
+import functools
+
 import jax
 import jax.numpy as jnp
 from jax import lax
@@ -84,6 +86,86 @@
     )(keys.reshape(1, slot_count), low, high)
 
 
+def pieces_kernel(low_count, high_count, col_keys, *refs):
+    low_refs = refs[:low_count]
+    high_refs = refs[low_count:low_count + high_count]
+    weights, row_sums, joined = refs[low_count + high_count:]
+    block_rows = weights.shape[0]
+    slot_count = weights.shape[1]
+    quarters, part, width = joined.shape[1], joined.shape[2], joined.shape[3]
+    half = low_refs[0].shape[-1]
+
+    @pl.when(pl.program_id(0) == 0)
+    def _():
+        for group, lo, hi in ((low_refs, 0, half), (high_refs, half, width)):
+            at = 0
+            for ref in group:
+                count = ref.shape[1]
+                joined[:, at:at + count, :, lo:hi] = ref[...]
+                at += count
+
+    per_block = block_rows // (quarters * part)
+    first = pl.multiple_of(pl.program_id(0) * per_block, per_block)
+    start = pl.multiple_of(pl.program_id(0) * block_rows, block_rows)
+    contract = (((1,), (1,)), ((), ()))
+    gram = lax.dot_general(
+        joined[pl.ds(first, per_block)].reshape(block_rows, width),
+        joined[...].reshape(slot_count, width), contract,
+        preferred_element_type=jnp.float32,
+    )
+    own_keys = col_keys[:, pl.ds(start, block_rows)]
+    diagonal = (
+        lax.broadcasted_iota(jnp.int32, (block_rows, block_rows), 0)
+        == lax.broadcasted_iota(jnp.int32, (block_rows, block_rows), 1)
+    )
+    row_keys = jnp.sum(jnp.where(diagonal, own_keys, 0.0), axis=1, keepdims=True)
+    keep = jnp.abs(row_keys - col_keys[...]) <= BAND
+    positive = jnp.maximum(gram, 0.0)
+    cubed = jnp.where(keep, positive * positive * positive, 0.0).astype(jnp.bfloat16)
+    weights[...] = cubed
+    ones = jnp.ones((8, slot_count), jnp.bfloat16)
+    summed = lax.dot_general(ones, cubed, contract, preferred_element_type=jnp.float32)
+    row_sums[...] = summed[0:1, :]
+
+
+def pieces_affinity(low_pieces, high_pieces, keys, part):
+    sources = low_pieces[0].shape[0]
+    quarters = sum(piece.shape[1] for piece in low_pieces)
+    half = low_pieces[0].shape[3]
+    width = half + high_pieces[0].shape[3]
+    if part % 16 != 0 or (2 * quarters * part) % 128 != 0:
+        low = jnp.concatenate([piece[:, :, :part] for piece in low_pieces], axis=1)
+        high = jnp.concatenate([piece[:, :, :part] for piece in high_pieces], axis=1)
+        return fused_affinity(low, high, keys, part)
+    slot_count = sources * quarters * part
+    block_rows = min(512, slot_count)
+    pieces = list(low_pieces) + list(high_pieces)
+    specs = [
+        pl.BlockSpec((sources, piece.shape[1], part, piece.shape[3]), lambda i: (0, 0, 0, 0))
+        for piece in pieces
+    ]
+    return pl.pallas_call(
+        functools.partial(pieces_kernel, len(low_pieces), len(high_pieces)),
+        grid=(slot_count // block_rows,),
+        in_specs=[pl.BlockSpec((1, slot_count), lambda i: (0, 0))] + specs,
+        out_specs=[
+            pl.BlockSpec((block_rows, slot_count), lambda i: (i, 0)),
+            pl.BlockSpec((1, block_rows), lambda i: (0, i)),
+        ],
+        out_shape=[
+            jax.ShapeDtypeStruct((slot_count, slot_count), jnp.bfloat16),
+            jax.ShapeDtypeStruct((1, slot_count), jnp.float32),
+        ],
+        scratch_shapes=[pltpu.VMEM((sources, quarters, part, width), jnp.bfloat16)],
+        compiler_params=pltpu.CompilerParams(dimension_semantics=("arbitrary",)),
+        cost_estimate=pl.CostEstimate(
+            flops=2 * slot_count * slot_count * width + 22 * slot_count * slot_count,
+            transcendentals=0,
+            bytes_accessed=slot_count * width * 2 + 2 * slot_count * slot_count,
+        ),
+    )(keys.reshape(1, slot_count), *pieces)
+
+
 def on_device(embeddings, labels, image_lists, rank_keys):
     img_count = lax.axis_size("img")
     sub_count = lax.axis_size("sub")
@@ -168,13 +250,18 @@
     low_got = lax.all_to_all(low_payload, "img", split_axis=0, concat_axis=0, tiled=True)[:, None]
     high_got = lax.all_to_all(high_payload, "img", split_axis=0, concat_axis=0, tiled=True)[:, None]
     bit = sub_count // 2
-    while bit >= 1:
+    while bit > 1:
         low_got = exchange_stage(low_got, bit)
         high_got = exchange_stage(high_got, bit)
         bit //= 2
+    last = [(t, t ^ bit) for t in range(sub_count)] if bit == 1 else None
+    low_pieces = [low_got] + ([lax.ppermute(low_got, "sub", last)] if last else [])
+    high_pieces = [high_got] + ([lax.ppermute(high_got, "sub", last)] if last else [])
     slot_count = slot_total
-    key_rows = low_got[:, :, part, :part].reshape(slot_count).astype(jnp.float32)
-    weight_mat, row_sums = fused_affinity(low_got, high_got, key_rows, part)
+    key_rows = jnp.concatenate(
+        [piece[:, :, part, :part] for piece in low_pieces], axis=1
+    ).reshape(slot_count).astype(jnp.float32)
+    weight_mat, row_sums = pieces_affinity(low_pieces, high_pieces, key_rows, part)
     weights = weight_mat.reshape(1, slot_count, slot_count)
     degree_slots = lax.all_to_all(
         bucket_major(row_sums), "img", split_axis=0, concat_axis=0, tiled=True

time: 159 us -> 157 us (0.987)
  other arithmetic: 7.46 us -> 4.49 us
  local copies, waits for them, and re-layouts: 4.33 us -> 6.86 us
    concatenate x4 -> x3, other arithmetic: 3.09 us -> 0.17 us  [exchange_stage(): return jnp.concatenate([got, lax.ppermute(got, 'sub', pairs)], axis=1)]
    ppermute x4 -> x2, waiting for transfers between devices: 7.81 us -> 5.99 us  [exchange_stage(): return jnp.concatenate([got, lax.ppermute(got, 'sub', pairs)], axis=1)]
where the time goes in v15:
time: 157 us; the launch traced here: 156 us
  blocking collectives  70.6 us (45%)
  waiting for transfers between devices  26.9 us (17%)
  matrix products  19.8 us (13%)
  starting transfers between devices  14.1 us (9%)
  Pallas kernels  13.5 us (9%)
  local copies, waits for them, and re-layouts  6.86 us (4%)
  other arithmetic  4.49 us (3%)
    all_to_all x2, blocking collectives, on_device(): lax.all_to_all(bucket_major(product), 'img', split_axis=0, concat_axis=0,...  34.3 us
    all_to_all x2, blocking collectives, on_device(): lax.all_to_all(to_bucket(scaled), 'img', split_axis=0, concat_axis=0, til...  22.6 us
    all_to_all x1, blocking collectives, on_device(): lax.all_to_all(low_payload, 'img', split_axis=0, concat_axis=0, tiled=True)  13.7 us
    all_to_all x1, waiting for transfers between devices, on_device(): lax.all_to_all(high_payload, 'img', split_axis=0, concat_axis=0, tiled=True)  13.6 us
    pallas_call x1, Pallas kernels, pieces_affinity(): pl.pallas_call(functools.partial(pieces_kernel, len(low_pieces), len(high...  13.5 us
    dot_general x2, matrix products, on_device(): jnp.einsum('ajk,akc->ajc', weights, list_major(arrived), preferred_elemen...  12.1 us
    all_to_all x1, starting transfers between devices, on_device(): lax.all_to_all(high_payload, 'img', split_axis=0, concat_axis=0, tiled=True)  7.28 us
    all_to_all x1, waiting for transfers between devices, on_device(): lax.all_to_all(bucket_major(row_sums), 'img', split_axis=0, concat_axis=0...  6.36 us
  transfers between devices with their start and end apart: 6, of which 4 were waited for; matrix products, arithmetic and copies ran while one was open for 2% of the time, Pallas kernels for 0%

profile of v15, /device:TPU:0, one launch (start us, length us, event | category | flops | bytes accessed | tf_op | source)
XLA Modules:
  0.0 156.5 jit_solution(1114837503839331328)
XLA Ops:
  0.0 0.0 copy-start.1
  0.0 0.8 copy.61
  0.8 0.2 eq.32
  1.0 0.5 convert_reduce_fusion
  1.5 0.2 reduce_sum.39
  1.8 0.1 copy.62
  1.9 0.7 multiply_add_fusion
  2.6 0.1 iota_add_fusion.1
  2.7 0.1 add.108
  2.7 1.4 fusion.1
  4.1 1.9 %convolution_convert_fusion.2 = bf16[512,768]{1,0:T(8,128)(2,1)S(1)} fusion(bf16[512,768]{1,0:T(8,128)(2,1)} %param.5, f32[512]{0:T(512)S(1)} %add_rsqrt_fusion, s32[512]{0:T(512)S(1)} %bitcast.86, s32[512]{0:T(512)S(1)} %bitcast.78, s32[512]{0:T(512)S(1)} %add.108), kind=kOutput, calls=%fused_computation.11 | convolution fusion | flops 405012480 | bytes 1581056 | tf_op jit(solution)/shard_map/dot_general | solution.py:234
  6.0 0.0 copy-start.4
  6.0 0.8 slice.42
  6.9 7.3 %all-to-all-start.1 = ((bf16[8,64,512]{2,1,0:T(8,128)(2,1)}), bf16[8,64,512]{2,1,0:T(8,128)(2,1)S(1)}, u32[]{:S(2)}, u32[]{:S(2)}) async-start(bf16[8,64,512]{2,1,0:T(8,128)(2,1)} %slice.42), calls=%async_computation.1 | async-start | bytes 1048576 | tf_op jit(solution)/shard_map/all_to_all | solution.py:251
  14.2 0.0 copy-done.1
  14.2 0.4 fusion.10
  14.6 0.3 fusion.9
  14.9 0.1 convert_element_type.81
  15.0 13.6 %all-to-all-done.1 = bf16[8,64,512]{2,1,0:T(8,128)(2,1)S(1)} async-done(((bf16[8,64,512]{2,1,0:T(8,128)(2,1)}), bf16[8,64,512]{2,1,0:T(8,128)(2,1)S(1)}, u32[]{:S(2)}, u32[]{:S(2)}) %all-to-all-start.1) | async-done | bytes 524320 | tf_op jit(solution)/shard_map/all_to_all | solution.py:251
  28.6 1.5 collective-permute-start.2
  30.1 13.7 %all_to_all.35 = bf16[8,65,256]{2,1,0:T(8,128)(2,1)S(1)} all-to-all(bf16[8,65,256]{2,1,0:T(8,128)(2,1)S(1)} %fusion.17), channel_id=1, replica_groups=mesh['img'=8,'sub'=4] {'img'}, dimensions={0} | all-to-all | bytes 532480 | tf_op jit(solution)/shard_map/all_to_all | solution.py:250
  43.8 0.5 collective-permute-start
  44.4 0.0 collective-permute-done.2
  44.4 0.1 pad_maximum_fusion.refs_2_
  44.5 0.0 copy-start
  44.5 0.1 collective-permute-start.3
  44.6 6.0 %collective-permute-done = bf16[8,1,65,256]{3,2,0,1:T(8,128)(2,1)S(1)} collective-permute-done((bf16[8,1,65,256]{3,2,0,1:T(8,128)(2,1)S(1)}, bf16[8,1,65,256]{3,2,0,1:T(8,128)(2,1)S(1)}, u32[]{:S(2)}, u32[]{:S(2)}) %collective-permute-start) | collective-permute-done | bytes 266272 | tf_op jit(solution)/shard_map/ppermute | solution.py:248
  50.5 0.1 pad_maximum_fusion.1
  50.6 0.1 copy.64
  50.7 0.1 collective-permute-start.1
  50.8 0.0 copy-done.4
  50.8 0.1 broadcast_add_fusion
  50.9 0.9 copy.66.refs_0_
  51.8 0.9 collective-permute-done.1
  52.7 0.7 reshape.188.col_keys
  53.4 0.9 copy.67.refs_1_
  54.3 0.0 copy-start.3
  54.4 0.0 collective-permute-done.3.refs_3_
  54.4 0.0 copy-done
  54.4 0.0 copy-start.2
  54.4 1.0 copy-done.2
  55.3 13.5 %shard_map.55 = (bf16[2048,2048]{1,0:T(8,128)(2,1)}, f32[1,2048]{1,0:T(1,128)}) custom-call(f32[1,2048]{1,0:T(1,128)} %reshape.188.col_keys, bf16[8,2,65,256]{3,2,1,0:T(8,128)(2,1)} %copy.66.refs_0_, bf16[8,2,65,256]{3,2,1,0:T(8,128)(2,1)} %copy.67.refs_1_, bf16[8,2,64,512]{3,2,1,0:T(8,128)(2,1)} %copy-done, bf16[8,2,64,512]{3,2,1,0:T(8,128)(2,1)} %copy-done.2), custom_call_target="tpu_custom_call" | custom-call | flops 6534725632 | bytes 11534336 | tf_op jit(solution)/shard_map/pallas_call | solution.py:147
  68.8 4.6 %all-to-all-start.2 = ((f32[8,1,256]{2,1,0:T(1,128)}), f32[8,1,256]{2,1,0:T(1,128)S(1)}, u32[]{:S(2)}, u32[]{:S(2)}) async-start(f32[8,1,256]{2,1,0:T(1,128)} %bitcast.95), calls=%async_computation.2 | async-start | bytes 16384 | tf_op jit(solution)/shard_map/all_to_all | solution.py:266
  73.5 0.1 iota_add_fusion
  73.5 0.1 add.102
  73.6 6.4 %all-to-all-done.2 = f32[8,1,256]{2,1,0:T(1,128)S(1)} async-done(((f32[8,1,256]{2,1,0:T(1,128)}), f32[8,1,256]{2,1,0:T(1,128)S(1)}, u32[]{:S(2)}, u32[]{:S(2)}) %all-to-all-start.2) | async-done | bytes 8224 | tf_op jit(solution)/shard_map/all_to_all | solution.py:266
  80.0 0.7 select_reduce_fusion
  80.7 0.0 copy-done.3
  80.7 1.3 convolution_convert_fusion.1
  82.0 0.1 copy.78
  82.1 10.6 %all_to_all.36 = bf16[8,1,256,64]{2,3,1,0:T(8,128)(2,1)S(1)} all-to-all(bf16[8,1,256,64]{2,3,1,0:T(8,128)(2,1)S(1)} %copy.69), channel_id=1, replica_groups=mesh['img'=8,'sub'=4] {'img'}, dimensions={0} | all-to-all | bytes 524288 | tf_op jit(solution)/shard_map/all_to_all | solution.py:275
  92.8 0.1 copy.70
  92.9 0.1 reshape.189
  93.0 6.0 %convolution_bitcast_fusion.1 = f32[8,1,256,64]{2,3,1,0:T(8,128)S(1)} fusion(bf16[8,256,2048]{2,1,0:T(8,128)(2,1)} %bitcast.60, bf16[2048,64,1]{0,1,2:T(8,128)(2,1)S(1)} %reshape.189), kind=kOutput, calls=%fused_computation.16 | convolution fusion | flops 536870912 | bytes 9175040 | tf_op jit(solution)/shard_map/ajk,akc->ajc/dot_general | solution.py:276
  99.1 17.0 %all_to_all.37 = f32[8,1,256,64]{2,3,1,0:T(8,128)S(1)} all-to-all(f32[8,1,256,64]{2,3,1,0:T(8,128)S(1)} %convolution_bitcast_fusion.1), channel_id=1, replica_groups=mesh['img'=8,'sub'=4] {'img'}, dimensions={0} | all-to-all | bytes 1048576 | tf_op jit(solution)/shard_map/all_to_all | solution.py:279
  116.1 1.3 fusion.6
  117.5 1.3 convolution_convert_fusion
  118.8 0.1 copy.80
  118.9 12.0 %all_to_all.38 = bf16[8,1,256,64]{2,3,1,0:T(8,128)(2,1)S(1)} all-to-all(bf16[8,1,256,64]{2,3,1,0:T(8,128)(2,1)S(1)} %copy.73), channel_id=1, replica_groups=mesh['img'=8,'sub'=4] {'img'}, dimensions={0} | all-to-all | bytes 524288 | tf_op jit(solution)/shard_map/all_to_all | solution.py:275
  130.8 0.1 copy.74
  131.0 0.1 reshape.190
  131.1 6.0 %convolution_bitcast_fusion = f32[8,1,256,64]{2,3,1,0:T(8,128)S(1)} fusion(bf16[8,256,2048]{2,1,0:T(8,128)(2,1)} %bitcast.61, bf16[2048,64,1]{0,1,2:T(8,128)(2,1)S(1)} %reshape.190), kind=kOutput, calls=%fused_computation.15 | convolution fusion | flops 536870912 | bytes 9175040 | tf_op jit(solution)/shard_map/ajk,akc->ajc/dot_general | solution.py:276
  137.2 17.3 %all_to_all.39 = f32[8,1,256,64]{2,3,1,0:T(8,128)S(1)} all-to-all(f32[8,1,256,64]{2,3,1,0:T(8,128)S(1)} %convolution_bitcast_fusion), channel_id=1, replica_groups=mesh['img'=8,'sub'=4] {'img'}, dimensions={0} | all-to-all | bytes 1048576 | tf_op jit(solution)/shard_map/all_to_all | solution.py:279
  154.5 2.0 %fusion.7 = bf16[512,64]{0,1:T(8,128)(2,1)} fusion(f32[2048,64]{0,1:T(8,128)S(1)} %bitcast.73, bf16[512,64]{0,1:T(8,128)(2,1)S(1)} %copy-done.3, f32[512]{0:T(512)S(1)} %get-tuple-element.13, s32[512]{0:T(512)S(1)} %bitcast.93, s32[512]{0:T(512)S(1)} %bitcast.85, s32[2048]{0:T(1024)S(1)} %add.102), kind=kOutput, calls=%fused_computation.23 | convolution fusion | flops 405962752 | bytes 669696 | tf_op jit(solution)/shard_map/kg,kc->gc/dot_general | solution.py:210
  (20 shorter events, 0.3 us)
Async XLA Ops:
  0.0 14.2 %copy-start.1 = (s32[512,2]{0,1:T(2,128)S(1)}, s32[512,2]{0,1:T(2,128)}, u32[]{:S(2)}) copy-start(s32[512,2]{0,1:T(2,128)} %param.8) | copy-start | bytes 12292
  6.0 44.8 %copy-start.4 = (s32[4]{0:T(128)S(1)}, s32[4]{0:T(128)}, u32[]{:S(2)}) copy-start(s32[4]{0:T(128)} %constant.11.clone) | copy-start | bytes 52
  6.9 21.8 %all-to-all-start.1 = ((bf16[8,64,512]{2,1,0:T(8,128)(2,1)}), bf16[8,64,512]{2,1,0:T(8,128)(2,1)S(1)}, u32[]{:S(2)}, u32[]{:S(2)}) async-start(bf16[8,64,512]{2,1,0:T(8,128)(2,1)} %slice.42), calls=%async_computation.1 | async-start | bytes 1048576 | tf_op jit(solution)/shard_map/all_to_all | solution.py:251
  28.6 15.7 %collective-permute-start.2 = (bf16[8,1,64,512]{3,2,1,0:T(8,128)(2,1)S(1)}, bf16[8,1,64,512]{3,2,1,0:T(8,128)(2,1)S(1)}, u32[]{:S(2)}, u32[]{:S(2)}) collective-permute-start(bf16[8,1,64,512]{3,2,1,0:T(8,128)(2,1)S(1)} %bitcast.67), channel_id=1, source_target_pairs={{0,2},{1,3},{2,0},{3,1},{4,6},{5,7},{6,4},{7,5},{8,10},{9,11},{10,... | collective-permute-start | bytes 1572872 | tf_op jit(solution)/shard_map/ppermute | solution.py:248
  43.8 6.7 %collective-permute-start = (bf16[8,1,65,256]{3,2,0,1:T(8,128)(2,1)S(1)}, bf16[8,1,65,256]{3,2,0,1:T(8,128)(2,1)S(1)}, u32[]{:S(2)}, u32[]{:S(2)}) collective-permute-start(bf16[8,1,65,256]{3,2,0,1:T(8,128)(2,1)S(1)} %bitcast.62), channel_id=1, source_target_pairs={{0,2},{1,3},{2,0},{3,1},{4,6},{5,7},{6,4},{7,5},{8,10},{9,11},{10,... | collective-permute-start | bytes 798728 | tf_op jit(solution)/shard_map/ppermute | solution.py:248
  44.5 9.9 %copy-start = (bf16[8,2,64,512]{3,2,1,0:T(8,128)(2,1)}, bf16[8,2,64,512]{3,2,1,0:T(8,128)(2,1)S(1)}, u32[]{:S(2)}) copy-start(bf16[8,2,64,512]{3,2,1,0:T(8,128)(2,1)S(1)} %pad_maximum_fusion.refs_2_) | copy-start | bytes 3145732
  44.5 9.9 %collective-permute-start.3 = (bf16[8,2,64,512]{3,2,1,0:T(8,128)(2,1)S(1)}, bf16[8,2,64,512]{3,2,1,0:T(8,128)(2,1)S(1)}, u32[]{:S(2)}, u32[]{:S(2)}) collective-permute-start(bf16[8,2,64,512]{3,2,1,0:T(8,128)(2,1)S(1)} %pad_maximum_fusion.refs_2_), channel_id=1, source_target_pairs={{0,1},{1,0},{2,3},{3,2},{4,5},{5,4},{6,7},{7,6},{8,9},{9,8},{10,11... | collective-permute-start | bytes 3145736 | tf_op jit(solution)/shard_map/ppermute | solution.py:259
  50.7 2.0 %collective-permute-start.1 = (bf16[8,2,65,256]{3,0,2,1:T(8,128)(2,1)S(1)}, bf16[8,2,65,256]{3,0,2,1:T(8,128)(2,1)S(1)}, u32[]{:S(2)}, u32[]{:S(2)}) collective-permute-start(bf16[8,2,65,256]{3,0,2,1:T(8,128)(2,1)S(1)} %copy.64), channel_id=1, source_target_pairs={{0,1},{1,0},{2,3},{3,2},{4,5},{5,4},{6,7},{7,6},{8,9},{9,8},{10,11... | collective-permute-start | bytes 1597448 | tf_op jit(solution)/shard_map/ppermute | solution.py:258
  54.3 26.4 %copy-start.3 = (bf16[512,64]{0,1:T(8,128)(2,1)S(1)}, bf16[512,64]{0,1:T(8,128)(2,1)}, u32[]{:S(2)}) copy-start(bf16[512,64]{0,1:T(8,128)(2,1)} %param.6) | copy-start | bytes 196612
  54.4 1.0 copy-start.2
  68.8 11.2 %all-to-all-start.2 = ((f32[8,1,256]{2,1,0:T(1,128)}), f32[8,1,256]{2,1,0:T(1,128)S(1)}, u32[]{:S(2)}, u32[]{:S(2)}) async-start(f32[8,1,256]{2,1,0:T(1,128)} %bitcast.95), calls=%async_computation.2 | async-start | bytes 16384 | tf_op jit(solution)/shard_map/all_to_all | solution.py:266

commit v16 on v15

--- a/solution.py
+++ b/solution.py
@@ -100,9 +100,9 @@
         for group, lo, hi in ((low_refs, 0, half), (high_refs, half, width)):
             at = 0
             for ref in group:
-                count = ref.shape[1]
-                joined[:, at:at + count, :, lo:hi] = ref[...]
-                at += count
+                for m in range(ref.shape[0]):
+                    joined[:, at, :, lo:hi] = ref[m]
+                    at += 1
 
     per_block = block_rows // (quarters * part)
     first = pl.multiple_of(pl.program_id(0) * per_block, per_block)
@@ -129,19 +129,20 @@
 
 
 def pieces_affinity(low_pieces, high_pieces, keys, part):
-    sources = low_pieces[0].shape[0]
-    quarters = sum(piece.shape[1] for piece in low_pieces)
+    sources = low_pieces[0].shape[1]
+    quarters = sum(piece.shape[0] for piece in low_pieces)
     half = low_pieces[0].shape[3]
     width = half + high_pieces[0].shape[3]
     if part % 16 != 0 or (2 * quarters * part) % 128 != 0:
-        low = jnp.concatenate([piece[:, :, :part] for piece in low_pieces], axis=1)
-        high = jnp.concatenate([piece[:, :, :part] for piece in high_pieces], axis=1)
-        return fused_affinity(low, high, keys, part)
+        def source_major(group):
+            stacked = jnp.concatenate([piece[:, :, :part] for piece in group], axis=0)
+            return jnp.moveaxis(stacked, 0, 1)
+        return fused_affinity(source_major(low_pieces), source_major(high_pieces), keys, part)
     slot_count = sources * quarters * part
     block_rows = min(512, slot_count)
     pieces = list(low_pieces) + list(high_pieces)
     specs = [
-        pl.BlockSpec((sources, piece.shape[1], part, piece.shape[3]), lambda i: (0, 0, 0, 0))
+        pl.BlockSpec((piece.shape[0], sources, part, piece.shape[3]), lambda i: (0, 0, 0, 0))
         for piece in pieces
     ]
     return pl.pallas_call(
@@ -245,10 +246,10 @@
 
     def exchange_stage(got, bit):
         pairs = [(t, t ^ bit) for t in range(sub_count)]
-        return jnp.concatenate([got, lax.ppermute(got, "sub", pairs)], axis=1)
-
-    low_got = lax.all_to_all(low_payload, "img", split_axis=0, concat_axis=0, tiled=True)[:, None]
-    high_got = lax.all_to_all(high_payload, "img", split_axis=0, concat_axis=0, tiled=True)[:, None]
+        return jnp.concatenate([got, lax.ppermute(got, "sub", pairs)], axis=0)
+
+    low_got = lax.all_to_all(low_payload, "img", split_axis=0, concat_axis=0, tiled=True)[None]
+    high_got = lax.all_to_all(high_payload, "img", split_axis=0, concat_axis=0, tiled=True)[None]
     bit = sub_count // 2
     while bit > 1:
         low_got = exchange_stage(low_got, bit)
@@ -258,8 +259,8 @@
     low_pieces = [low_got] + ([lax.ppermute(low_got, "sub", last)] if last else [])
     high_pieces = [high_got] + ([lax.ppermute(high_got, "sub", last)] if last else [])
     slot_count = slot_total
-    key_rows = jnp.concatenate(
-        [piece[:, :, part, :part] for piece in low_pieces], axis=1
+    key_rows = jnp.moveaxis(
+        jnp.concatenate([piece[:, :, part, :part] for piece in low_pieces], axis=0), 0, 1
     ).reshape(slot_count).astype(jnp.float32)
     weight_mat, row_sums = pieces_affinity(low_pieces, high_pieces, key_rows, part)
     weights = weight_mat.reshape(1, slot_count, slot_count)

time: 157 us -> 156 us (level)
  local copies, waits for them, and re-layouts: 6.86 us -> 5.02 us
where the time goes in v16:
time: 156 us
  blocking collectives  70.6 us (45%)
  waiting for transfers between devices  27.7 us (18%)
  matrix products  19.8 us (13%)
  starting transfers between devices  14.1 us (9%)
  Pallas kernels  13.6 us (9%)
  local copies, waits for them, and re-layouts  5.02 us (3%)
  other arithmetic  4.48 us (3%)
    all_to_all x2, blocking collectives, on_device(): lax.all_to_all(bucket_major(product), 'img', split_axis=0, concat_axis=0,...  34.3 us
    all_to_all x2, blocking collectives, on_device(): lax.all_to_all(to_bucket(scaled), 'img', split_axis=0, concat_axis=0, til...  22.6 us
    all_to_all x1, blocking collectives, on_device(): lax.all_to_all(low_payload, 'img', split_axis=0, concat_axis=0, tiled=True)  13.7 us
    all_to_all x1, waiting for transfers between devices, on_device(): lax.all_to_all(high_payload, 'img', split_axis=0, concat_axis=0, tiled=True)  13.6 us
    pallas_call x1, Pallas kernels, pieces_affinity(): pl.pallas_call(functools.partial(pieces_kernel, len(low_pieces), len(high...  13.6 us
    dot_general x2, matrix products, on_device(): jnp.einsum('ajk,akc->ajc', weights, list_major(arrived), preferred_elemen...  12.1 us
    all_to_all x1, starting transfers between devices, on_device(): lax.all_to_all(high_payload, 'img', split_axis=0, concat_axis=0, tiled=True)  7.28 us
    all_to_all x1, waiting for transfers between devices, on_device(): lax.all_to_all(bucket_major(row_sums), 'img', split_axis=0, concat_axis=0...  6.36 us
  transfers between devices with their start and end apart: 6, of which 4 were waited for; matrix products, arithmetic and copies ran while one was open for 2% of the time, Pallas kernels for 0%

profile of v16, /device:TPU:0, one launch (start us, length us, event | category | flops | bytes accessed | tf_op | source)
XLA Modules:
  0.0 155.6 jit_solution(10635868676873436021)
XLA Ops:
  0.0 0.0 copy-start.2
  0.0 0.8 copy.55
  0.8 0.2 eq.32
  1.0 0.5 convert_reduce_fusion
  1.5 0.2 reduce_sum.39
  1.8 0.1 copy.56
  1.9 0.7 multiply_add_fusion
  2.6 0.1 iota_add_fusion.1
  2.7 0.1 add.108
  2.7 1.4 fusion.1
  4.1 1.9 %convolution_convert_fusion.2 = bf16[512,768]{1,0:T(8,128)(2,1)S(1)} fusion(bf16[512,768]{1,0:T(8,128)(2,1)} %param.5, f32[512]{0:T(512)S(1)} %add_rsqrt_fusion, s32[512]{0:T(512)S(1)} %bitcast.90, s32[512]{0:T(512)S(1)} %bitcast.82, s32[512]{0:T(512)S(1)} %add.108), kind=kOutput, calls=%fused_computation.11 | convolution fusion | flops 405012480 | bytes 1581056 | tf_op jit(solution)/shard_map/dot_general | solution.py:235
  6.0 0.0 copy-start.4
  6.0 0.8 slice.42
  6.9 7.3 %all-to-all-start.1 = ((bf16[8,64,512]{2,1,0:T(8,128)(2,1)}), bf16[8,64,512]{2,1,0:T(8,128)(2,1)S(1)}, u32[]{:S(2)}, u32[]{:S(2)}) async-start(bf16[8,64,512]{2,1,0:T(8,128)(2,1)} %slice.42), calls=%async_computation.1 | async-start | bytes 1048576 | tf_op jit(solution)/shard_map/all_to_all | solution.py:252
  14.2 0.0 copy-done.2
  14.2 0.4 fusion.10
  14.6 0.3 fusion.9
  14.9 0.1 convert_element_type.86
  15.0 13.6 %all-to-all-done.1 = bf16[8,64,512]{2,1,0:T(8,128)(2,1)S(1)} async-done(((bf16[8,64,512]{2,1,0:T(8,128)(2,1)}), bf16[8,64,512]{2,1,0:T(8,128)(2,1)S(1)}, u32[]{:S(2)}, u32[]{:S(2)}) %all-to-all-start.1) | async-done | bytes 524320 | tf_op jit(solution)/shard_map/all_to_all | solution.py:252
  28.6 1.5 collective-permute-start.2
  30.1 13.7 %all_to_all.35 = bf16[8,65,256]{2,1,0:T(8,128)(2,1)S(1)} all-to-all(bf16[8,65,256]{2,1,0:T(8,128)(2,1)S(1)} %fusion.17), channel_id=1, replica_groups=mesh['img'=8,'sub'=4] {'img'}, dimensions={0} | all-to-all | bytes 532480 | tf_op jit(solution)/shard_map/all_to_all | solution.py:251
  43.8 0.5 collective-permute-start
  44.4 0.0 collective-permute-done.2
  44.4 0.1 pad_maximum_fusion.refs_2_
  44.5 0.0 copy-start.1
  44.5 0.1 collective-permute-start.3
  44.6 6.0 %collective-permute-done = bf16[1,8,65,256]{3,2,1,0:T(8,128)(2,1)S(1)} collective-permute-done((bf16[1,8,65,256]{3,2,1,0:T(8,128)(2,1)S(1)}, bf16[1,8,65,256]{3,2,1,0:T(8,128)(2,1)S(1)}, u32[]{:S(2)}, u32[]{:S(2)}) %collective-permute-start) | collective-permute-done | bytes 266272 | tf_op jit(solution)/shard_map/ppermute | solution.py:249
  50.5 0.1 pad_maximum_fusion.1.refs_0_
  50.6 0.0 copy-start
  50.6 0.1 copy.58
  50.7 0.1 collective-permute-start.1
  50.8 0.0 copy-done.4
  50.8 0.1 broadcast_add_fusion
  50.9 1.8 %collective-permute-done.1 = bf16[2,8,65,256]{3,1,2,0:T(8,128)(2,1)S(1)} collective-permute-done((bf16[2,8,65,256]{3,1,2,0:T(8,128)(2,1)S(1)}, bf16[2,8,65,256]{3,1,2,0:T(8,128)(2,1)S(1)}, u32[]{:S(2)}, u32[]{:S(2)}) %collective-permute-start.1) | collective-permute-done | bytes 532512 | tf_op jit(solution)/shard_map/ppermute | solution.py:259
  52.7 0.7 reshape.188.col_keys
  53.4 0.9 copy.61.refs_1_
  54.4 0.0 copy-start.3
  54.4 0.0 collective-permute-done.3.refs_3_
  54.4 0.0 copy-done.1
  54.4 0.0 copy-done
  54.4 13.6 %shard_map.55 = (bf16[2048,2048]{1,0:T(8,128)(2,1)}, f32[1,2048]{1,0:T(1,128)}) custom-call(f32[1,2048]{1,0:T(1,128)} %reshape.188.col_keys, bf16[2,8,65,256]{3,2,1,0:T(8,128)(2,1)} %copy-done, bf16[2,8,65,256]{3,2,1,0:T(8,128)(2,1)} %copy.61.refs_1_, bf16[2,8,64,512]{3,2,1,0:T(8,128)(2,1)} %copy-done.1, bf16[2,8,64,512]{3,2,1,0:T(8,128)(2,1)} %collective-permute-done.3.refs_3_), custom_call_target="tpu_custom_call" | custom-call | flops 6534725632 | bytes 11534336 | tf_op jit(solution)/shard_map/pallas_call | solution.py:148
  67.9 4.6 %all-to-all-start.2 = ((f32[8,1,256]{2,1,0:T(1,128)}), f32[8,1,256]{2,1,0:T(1,128)S(1)}, u32[]{:S(2)}, u32[]{:S(2)}) async-start(f32[8,1,256]{2,1,0:T(1,128)} %bitcast.99), calls=%async_computation.2 | async-start | bytes 16384 | tf_op jit(solution)/shard_map/all_to_all | solution.py:267
  72.6 0.1 iota_add_fusion
  72.7 0.1 add.102
  72.7 6.4 %all-to-all-done.2 = f32[8,1,256]{2,1,0:T(1,128)S(1)} async-done(((f32[8,1,256]{2,1,0:T(1,128)}), f32[8,1,256]{2,1,0:T(1,128)S(1)}, u32[]{:S(2)}, u32[]{:S(2)}) %all-to-all-start.2) | async-done | bytes 8224 | tf_op jit(solution)/shard_map/all_to_all | solution.py:267
  79.1 0.7 select_reduce_fusion
  79.8 0.0 copy-done.3
  79.8 1.3 convolution_convert_fusion.1
  81.1 0.1 copy.73
  81.2 10.6 %all_to_all.36 = bf16[8,1,256,64]{2,3,1,0:T(8,128)(2,1)S(1)} all-to-all(bf16[8,1,256,64]{2,3,1,0:T(8,128)(2,1)S(1)} %copy.63), channel_id=1, replica_groups=mesh['img'=8,'sub'=4] {'img'}, dimensions={0} | all-to-all | bytes 524288 | tf_op jit(solution)/shard_map/all_to_all | solution.py:276
  91.9 0.1 copy.64
  92.0 0.1 reshape.189
  92.2 6.0 %convolution_bitcast_fusion.1 = f32[8,1,256,64]{2,3,1,0:T(8,128)S(1)} fusion(bf16[8,256,2048]{2,1,0:T(8,128)(2,1)} %bitcast.64, bf16[2048,64,1]{0,1,2:T(8,128)(2,1)S(1)} %reshape.189), kind=kOutput, calls=%fused_computation.16 | convolution fusion | flops 536870912 | bytes 9175040 | tf_op jit(solution)/shard_map/ajk,akc->ajc/dot_general | solution.py:277
  98.2 17.0 %all_to_all.37 = f32[8,1,256,64]{2,3,1,0:T(8,128)S(1)} all-to-all(f32[8,1,256,64]{2,3,1,0:T(8,128)S(1)} %convolution_bitcast_fusion.1), channel_id=1, replica_groups=mesh['img'=8,'sub'=4] {'img'}, dimensions={0} | all-to-all | bytes 1048576 | tf_op jit(solution)/shard_map/all_to_all | solution.py:280
  115.3 1.3 fusion.6
  116.6 1.3 convolution_convert_fusion
  117.9 0.1 copy.75
  118.0 12.0 %all_to_all.38 = bf16[8,1,256,64]{2,3,1,0:T(8,128)(2,1)S(1)} all-to-all(bf16[8,1,256,64]{2,3,1,0:T(8,128)(2,1)S(1)} %copy.67), channel_id=1, replica_groups=mesh['img'=8,'sub'=4] {'img'}, dimensions={0} | all-to-all | bytes 524288 | tf_op jit(solution)/shard_map/all_to_all | solution.py:276
  130.0 0.1 copy.68
  130.1 0.1 reshape.190
  130.2 6.0 %convolution_bitcast_fusion = f32[8,1,256,64]{2,3,1,0:T(8,128)S(1)} fusion(bf16[8,256,2048]{2,1,0:T(8,128)(2,1)} %bitcast.65, bf16[2048,64,1]{0,1,2:T(8,128)(2,1)S(1)} %reshape.190), kind=kOutput, calls=%fused_computation.15 | convolution fusion | flops 536870912 | bytes 9175040 | tf_op jit(solution)/shard_map/ajk,akc->ajc/dot_general | solution.py:277
  136.3 17.3 %all_to_all.39 = f32[8,1,256,64]{2,3,1,0:T(8,128)S(1)} all-to-all(f32[8,1,256,64]{2,3,1,0:T(8,128)S(1)} %convolution_bitcast_fusion), channel_id=1, replica_groups=mesh['img'=8,'sub'=4] {'img'}, dimensions={0} | all-to-all | bytes 1048576 | tf_op jit(solution)/shard_map/all_to_all | solution.py:280
  153.6 2.0 %fusion.7 = bf16[512,64]{0,1:T(8,128)(2,1)} fusion(f32[2048,64]{0,1:T(8,128)S(1)} %bitcast.77, bf16[512,64]{0,1:T(8,128)(2,1)S(1)} %copy-done.3, f32[512]{0:T(512)S(1)} %get-tuple-element.13, s32[512]{0:T(512)S(1)} %bitcast.97, s32[512]{0:T(512)S(1)} %bitcast.89, s32[2048]{0:T(1024)S(1)} %add.102), kind=kOutput, calls=%fused_computation.23 | convolution fusion | flops 405962752 | bytes 669696 | tf_op jit(solution)/shard_map/kg,kc->gc/dot_general | solution.py:211
  (20 shorter events, 0.3 us)
Async XLA Ops:
  0.0 14.2 %copy-start.2 = (s32[512,2]{0,1:T(2,128)S(1)}, s32[512,2]{0,1:T(2,128)}, u32[]{:S(2)}) copy-start(s32[512,2]{0,1:T(2,128)} %param.8) | copy-start | bytes 12292
  6.0 44.8 %copy-start.4 = (s32[4]{0:T(128)S(1)}, s32[4]{0:T(128)}, u32[]{:S(2)}) copy-start(s32[4]{0:T(128)} %constant.11.clone) | copy-start | bytes 52
  6.9 21.8 %all-to-all-start.1 = ((bf16[8,64,512]{2,1,0:T(8,128)(2,1)}), bf16[8,64,512]{2,1,0:T(8,128)(2,1)S(1)}, u32[]{:S(2)}, u32[]{:S(2)}) async-start(bf16[8,64,512]{2,1,0:T(8,128)(2,1)} %slice.42), calls=%async_computation.1 | async-start | bytes 1048576 | tf_op jit(solution)/shard_map/all_to_all | solution.py:252
  28.6 15.7 %collective-permute-start.2 = (bf16[1,8,64,512]{3,2,1,0:T(8,128)(2,1)S(1)}, bf16[1,8,64,512]{3,2,1,0:T(8,128)(2,1)S(1)}, u32[]{:S(2)}, u32[]{:S(2)}) collective-permute-start(bf16[1,8,64,512]{3,2,1,0:T(8,128)(2,1)S(1)} %bitcast.71), channel_id=1, source_target_pairs={{0,2},{1,3},{2,0},{3,1},{4,6},{5,7},{6,4},{7,5},{8,10},{9,11},{10,... | collective-permute-start | bytes 1572872 | tf_op jit(solution)/shard_map/ppermute | solution.py:249
  43.8 6.7 %collective-permute-start = (bf16[1,8,65,256]{3,2,1,0:T(8,128)(2,1)S(1)}, bf16[1,8,65,256]{3,2,1,0:T(8,128)(2,1)S(1)}, u32[]{:S(2)}, u32[]{:S(2)}) collective-permute-start(bf16[1,8,65,256]{3,2,1,0:T(8,128)(2,1)S(1)} %bitcast.66), channel_id=1, source_target_pairs={{0,2},{1,3},{2,0},{3,1},{4,6},{5,7},{6,4},{7,5},{8,10},{9,11},{10,... | collective-permute-start | bytes 798728 | tf_op jit(solution)/shard_map/ppermute | solution.py:249
  44.5 9.9 %copy-start.1 = (bf16[2,8,64,512]{3,2,1,0:T(8,128)(2,1)}, bf16[2,8,64,512]{3,2,1,0:T(8,128)(2,1)S(1)}, u32[]{:S(2)}) copy-start(bf16[2,8,64,512]{3,2,1,0:T(8,128)(2,1)S(1)} %pad_maximum_fusion.refs_2_) | copy-start | bytes 3145732
  44.5 9.9 %collective-permute-start.3 = (bf16[2,8,64,512]{3,2,1,0:T(8,128)(2,1)S(1)}, bf16[2,8,64,512]{3,2,1,0:T(8,128)(2,1)}, u32[]{:S(2)}, u32[]{:S(2)}) collective-permute-start(bf16[2,8,64,512]{3,2,1,0:T(8,128)(2,1)S(1)} %pad_maximum_fusion.refs_2_), channel_id=1, source_target_pairs={{0,1},{1,0},{2,3},{3,2},{4,5},{5,4},{6,7},{7,6},{8,9},{9,8},{10,11... | collective-permute-start | bytes 3145736 | tf_op jit(solution)/shard_map/ppermute | solution.py:260
  50.6 3.8 %copy-start = (bf16[2,8,65,256]{3,2,1,0:T(8,128)(2,1)}, bf16[2,8,65,256]{3,2,1,0:T(8,128)(2,1)S(1)}, u32[]{:S(2)}) copy-start(bf16[2,8,65,256]{3,2,1,0:T(8,128)(2,1)S(1)} %pad_maximum_fusion.1.refs_0_) | copy-start | bytes 1597444
  50.7 2.0 %collective-permute-start.1 = (bf16[2,8,65,256]{3,1,2,0:T(8,128)(2,1)S(1)}, bf16[2,8,65,256]{3,1,2,0:T(8,128)(2,1)S(1)}, u32[]{:S(2)}, u32[]{:S(2)}) collective-permute-start(bf16[2,8,65,256]{3,1,2,0:T(8,128)(2,1)S(1)} %copy.58), channel_id=1, source_target_pairs={{0,1},{1,0},{2,3},{3,2},{4,5},{5,4},{6,7},{7,6},{8,9},{9,8},{10,11... | collective-permute-start | bytes 1597448 | tf_op jit(solution)/shard_map/ppermute | solution.py:259
  54.4 25.5 %copy-start.3 = (bf16[512,64]{0,1:T(8,128)(2,1)S(1)}, bf16[512,64]{0,1:T(8,128)(2,1)}, u32[]{:S(2)}) copy-start(bf16[512,64]{0,1:T(8,128)(2,1)} %param.6) | copy-start | bytes 196612
  67.9 11.2 %all-to-all-start.2 = ((f32[8,1,256]{2,1,0:T(1,128)}), f32[8,1,256]{2,1,0:T(1,128)S(1)}, u32[]{:S(2)}, u32[]{:S(2)}) async-start(f32[8,1,256]{2,1,0:T(1,128)} %bitcast.99), calls=%async_computation.2 | async-start | bytes 16384 | tf_op jit(solution)/shard_map/all_to_all | solution.py:267

commit v17 on v16

--- a/solution.py
+++ b/solution.py
@@ -232,17 +232,21 @@
     )
     mine_keys = jnp.where(jnp.any(mine_hit, axis=1), key_sum, -4096.0).astype(jnp.bfloat16)
     width = unit.shape[1]
-    quarter = jnp.dot(mine_hit.astype(jnp.bfloat16), unit, preferred_element_type=jnp.float32)
     half = max(128, width // 3 // 128 * 128)
-    quarter = quarter.astype(jnp.bfloat16).reshape(img_count, part, width)
+    mine_pick = mine_hit.astype(jnp.bfloat16)
+
+    def quarter_rows(columns):
+        picked = jnp.dot(mine_pick, columns, preferred_element_type=jnp.float32)
+        return picked.astype(jnp.bfloat16).reshape(img_count, part, columns.shape[1])
+
     low_payload = jnp.concatenate(
         [
-            quarter[:, :, :half],
+            quarter_rows(unit[:, :half]),
             jnp.pad(mine_keys.reshape(img_count, 1, part), ((0, 0), (0, 0), (0, half - part))),
         ],
         axis=1,
     )
-    high_payload = quarter[:, :, half:]
+    high_payload = quarter_rows(unit[:, half:])
 
     def exchange_stage(got, bit):
         pairs = [(t, t ^ bit) for t in range(sub_count)]

time: 156 us -> 156 us (level)
  no operation moved by 1% of the time
where the time goes in v17:
time: 156 us
  blocking collectives  70.6 us (45%)
  waiting for transfers between devices  27.4 us (18%)
  matrix products  19.6 us (13%)
  starting transfers between devices  14.2 us (9%)
  Pallas kernels  13.6 us (9%)
  other arithmetic  5.81 us (4%)
  local copies, waits for them, and re-layouts  4.16 us (3%)
    all_to_all x2, blocking collectives, on_device(): lax.all_to_all(bucket_major(product), 'img', split_axis=0, concat_axis=0,...  34.3 us
    all_to_all x2, blocking collectives, on_device(): lax.all_to_all(to_bucket(scaled), 'img', split_axis=0, concat_axis=0, til...  22.6 us
    all_to_all x1, blocking collectives, on_device(): lax.all_to_all(low_payload, 'img', split_axis=0, concat_axis=0, tiled=True)  13.7 us
    pallas_call x1, Pallas kernels, pieces_affinity(): pl.pallas_call(functools.partial(pieces_kernel, len(low_pieces), len(high...  13.6 us
    all_to_all x1, waiting for transfers between devices, on_device(): lax.all_to_all(high_payload, 'img', split_axis=0, concat_axis=0, tiled=True)  13.2 us
    dot_general x2, matrix products, on_device(): jnp.einsum('ajk,akc->ajc', weights, list_major(arrived), preferred_elemen...  12.1 us
    all_to_all x1, starting transfers between devices, on_device(): lax.all_to_all(high_payload, 'img', split_axis=0, concat_axis=0, tiled=True)  7.41 us
    all_to_all x1, waiting for transfers between devices, on_device(): lax.all_to_all(bucket_major(row_sums), 'img', split_axis=0, concat_axis=0...  6.36 us
  transfers between devices with their start and end apart: 6, of which 4 were waited for; matrix products, arithmetic and copies ran while one was open for 2% of the time, Pallas kernels for 0%

profile of v17, /device:TPU:0, one launch (start us, length us, event | category | flops | bytes accessed | tf_op | source)
XLA Modules:
  0.0 155.6 jit_solution(6264895009954839532)
XLA Ops:
  0.0 0.0 copy-start.2
  0.0 0.8 copy.55
  0.8 0.2 eq.32
  1.0 0.5 convert_reduce_fusion
  1.5 0.2 reduce_sum.39
  1.8 0.1 copy.56
  1.9 0.7 multiply_add_fusion
  2.6 0.1 iota_add_fusion.1
  2.7 0.1 add.108
  2.7 1.4 fusion.1
  4.1 1.3 fusion.2
  5.5 1.3 convolution_convert_fusion.2
  6.7 0.0 copy-start.4
  6.7 7.4 %all-to-all-start.1 = ((bf16[8,64,512]{2,1,0:T(8,128)(2,1)}), bf16[8,64,512]{2,1,0:T(8,128)(2,1)S(1)}, u32[]{:S(2)}, u32[]{:S(2)}) async-start(bf16[8,64,512]{2,1,0:T(8,128)(2,1)} %bitcast.8), calls=%async_computation.1 | async-start | bytes 1048576 | tf_op jit(solution)/shard_map/all_to_all | solution.py:256
  14.2 0.4 fusion.10
  14.5 0.0 copy-done.2
  14.6 0.3 fusion.9
  14.9 0.1 convert_element_type.90
  15.0 0.4 convolution_convert_fusion.3
  15.4 13.2 %all-to-all-done.1 = bf16[8,64,512]{2,1,0:T(8,128)(2,1)S(1)} async-done(((bf16[8,64,512]{2,1,0:T(8,128)(2,1)}), bf16[8,64,512]{2,1,0:T(8,128)(2,1)S(1)}, u32[]{:S(2)}, u32[]{:S(2)}) %all-to-all-start.1) | async-done | bytes 524320 | tf_op jit(solution)/shard_map/all_to_all | solution.py:256
  28.6 1.5 collective-permute-start.2
  30.2 13.7 %all_to_all.35 = bf16[8,65,256]{2,1,0:T(8,128)(2,1)S(1)} all-to-all(bf16[8,65,256]{2,1,0:T(8,128)(2,1)S(1)} %fusion.19), channel_id=1, replica_groups=mesh['img'=8,'sub'=4] {'img'}, dimensions={0} | all-to-all | bytes 532480 | tf_op jit(solution)/shard_map/all_to_all | solution.py:255
  43.8 0.5 collective-permute-start
  44.4 0.0 collective-permute-done.2
  44.4 0.1 pad_maximum_fusion.refs_2_
  44.5 0.0 copy-start.1
  44.5 0.1 collective-permute-start.3
  44.6 6.0 %collective-permute-done = bf16[1,8,65,256]{3,2,1,0:T(8,128)(2,1)S(1)} collective-permute-done((bf16[1,8,65,256]{3,2,1,0:T(8,128)(2,1)S(1)}, bf16[1,8,65,256]{3,2,1,0:T(8,128)(2,1)S(1)}, u32[]{:S(2)}, u32[]{:S(2)}) %collective-permute-start) | collective-permute-done | bytes 266272 | tf_op jit(solution)/shard_map/ppermute | solution.py:253
  50.6 0.1 pad_maximum_fusion.1.refs_0_
  50.6 0.0 copy-start
  50.6 0.1 copy.58
  50.7 0.1 collective-permute-start.1
  50.8 0.0 copy-done.4
  50.8 0.1 broadcast_add_fusion
  50.9 1.8 %collective-permute-done.1 = bf16[2,8,65,256]{3,1,2,0:T(8,128)(2,1)S(1)} collective-permute-done((bf16[2,8,65,256]{3,1,2,0:T(8,128)(2,1)S(1)}, bf16[2,8,65,256]{3,1,2,0:T(8,128)(2,1)S(1)}, u32[]{:S(2)}, u32[]{:S(2)}) %collective-permute-start.1) | collective-permute-done | bytes 532512 | tf_op jit(solution)/shard_map/ppermute | solution.py:263
  52.7 0.7 reshape.192.col_keys
  53.4 0.9 copy.61.refs_1_
  54.4 0.0 copy-start.3
  54.4 0.0 collective-permute-done.3.refs_3_
  54.4 0.0 copy-done.1
  54.4 0.0 copy-done
  54.4 13.6 %shard_map.55 = (bf16[2048,2048]{1,0:T(8,128)(2,1)}, f32[1,2048]{1,0:T(1,128)}) custom-call(f32[1,2048]{1,0:T(1,128)} %reshape.192.col_keys, bf16[2,8,65,256]{3,2,1,0:T(8,128)(2,1)} %copy-done, bf16[2,8,65,256]{3,2,1,0:T(8,128)(2,1)} %copy.61.refs_1_, bf16[2,8,64,512]{3,2,1,0:T(8,128)(2,1)} %copy-done.1, bf16[2,8,64,512]{3,2,1,0:T(8,128)(2,1)} %collective-permute-done.3.refs_3_), custom_call_target="tpu_custom_call" | custom-call | flops 6534725632 | bytes 11534336 | tf_op jit(solution)/shard_map/pallas_call | solution.py:148
  67.9 4.6 %all-to-all-start.2 = ((f32[8,1,256]{2,1,0:T(1,128)}), f32[8,1,256]{2,1,0:T(1,128)S(1)}, u32[]{:S(2)}, u32[]{:S(2)}) async-start(f32[8,1,256]{2,1,0:T(1,128)} %bitcast.101), calls=%async_computation.2 | async-start | bytes 16384 | tf_op jit(solution)/shard_map/all_to_all | solution.py:271
  72.6 0.1 iota_add_fusion
  72.7 0.1 add.102
  72.8 6.4 %all-to-all-done.2 = f32[8,1,256]{2,1,0:T(1,128)S(1)} async-done(((f32[8,1,256]{2,1,0:T(1,128)}), f32[8,1,256]{2,1,0:T(1,128)S(1)}, u32[]{:S(2)}, u32[]{:S(2)}) %all-to-all-start.2) | async-done | bytes 8224 | tf_op jit(solution)/shard_map/all_to_all | solution.py:271
  79.1 0.7 select_reduce_fusion
  79.8 0.0 copy-done.3
  79.8 1.3 convolution_convert_fusion.1
  81.1 0.1 copy.73
  81.2 10.6 %all_to_all.36 = bf16[8,1,256,64]{2,3,1,0:T(8,128)(2,1)S(1)} all-to-all(bf16[8,1,256,64]{2,3,1,0:T(8,128)(2,1)S(1)} %copy.63), channel_id=1, replica_groups=mesh['img'=8,'sub'=4] {'img'}, dimensions={0} | all-to-all | bytes 524288 | tf_op jit(solution)/shard_map/all_to_all | solution.py:280
  91.9 0.1 copy.64
  92.0 0.1 reshape.193
  92.2 6.0 %convolution_bitcast_fusion.1 = f32[8,1,256,64]{2,3,1,0:T(8,128)S(1)} fusion(bf16[8,256,2048]{2,1,0:T(8,128)(2,1)} %bitcast.65, bf16[2048,64,1]{0,1,2:T(8,128)(2,1)S(1)} %reshape.193), kind=kOutput, calls=%fused_computation.16 | convolution fusion | flops 536870912 | bytes 9175040 | tf_op jit(solution)/shard_map/ajk,akc->ajc/dot_general | solution.py:281
  98.2 17.0 %all_to_all.37 = f32[8,1,256,64]{2,3,1,0:T(8,128)S(1)} all-to-all(f32[8,1,256,64]{2,3,1,0:T(8,128)S(1)} %convolution_bitcast_fusion.1), channel_id=1, replica_groups=mesh['img'=8,'sub'=4] {'img'}, dimensions={0} | all-to-all | bytes 1048576 | tf_op jit(solution)/shard_map/all_to_all | solution.py:284
  115.3 1.3 fusion.6
  116.6 1.3 convolution_convert_fusion
  117.9 0.1 copy.75
  118.0 12.0 %all_to_all.38 = bf16[8,1,256,64]{2,3,1,0:T(8,128)(2,1)S(1)} all-to-all(bf16[8,1,256,64]{2,3,1,0:T(8,128)(2,1)S(1)} %copy.67), channel_id=1, replica_groups=mesh['img'=8,'sub'=4] {'img'}, dimensions={0} | all-to-all | bytes 524288 | tf_op jit(solution)/shard_map/all_to_all | solution.py:280
  130.0 0.1 copy.68
  130.1 0.1 reshape.194
  130.3 6.0 %convolution_bitcast_fusion = f32[8,1,256,64]{2,3,1,0:T(8,128)S(1)} fusion(bf16[8,256,2048]{2,1,0:T(8,128)(2,1)} %bitcast.66, bf16[2048,64,1]{0,1,2:T(8,128)(2,1)S(1)} %reshape.194), kind=kOutput, calls=%fused_computation.15 | convolution fusion | flops 536870912 | bytes 9175040 | tf_op jit(solution)/shard_map/ajk,akc->ajc/dot_general | solution.py:281
  136.3 17.3 %all_to_all.39 = f32[8,1,256,64]{2,3,1,0:T(8,128)S(1)} all-to-all(f32[8,1,256,64]{2,3,1,0:T(8,128)S(1)} %convolution_bitcast_fusion), channel_id=1, replica_groups=mesh['img'=8,'sub'=4] {'img'}, dimensions={0} | all-to-all | bytes 1048576 | tf_op jit(solution)/shard_map/all_to_all | solution.py:284
  153.6 2.0 %fusion.7 = bf16[512,64]{0,1:T(8,128)(2,1)} fusion(f32[2048,64]{0,1:T(8,128)S(1)} %bitcast.76, bf16[512,64]{0,1:T(8,128)(2,1)S(1)} %copy-done.3, f32[512]{0:T(512)S(1)} %get-tuple-element.13, s32[512]{0:T(512)S(1)} %bitcast.99, s32[512]{0:T(512)S(1)} %bitcast.90, s32[2048]{0:T(1024)S(1)} %add.102), kind=kOutput, calls=%fused_computation.24 | convolution fusion | flops 405962752 | bytes 669696 | tf_op jit(solution)/shard_map/kg,kc->gc/dot_general | solution.py:211
  (19 shorter events, 0.3 us)
Async XLA Ops:
  0.0 14.5 %copy-start.2 = (s32[512,2]{0,1:T(2,128)S(1)}, s32[512,2]{0,1:T(2,128)}, u32[]{:S(2)}) copy-start(s32[512,2]{0,1:T(2,128)} %param.8) | copy-start | bytes 12292
  6.7 44.1 %copy-start.4 = (s32[4]{0:T(128)S(1)}, s32[4]{0:T(128)}, u32[]{:S(2)}) copy-start(s32[4]{0:T(128)} %constant.11.clone) | copy-start | bytes 52
  6.7 21.9 %all-to-all-start.1 = ((bf16[8,64,512]{2,1,0:T(8,128)(2,1)}), bf16[8,64,512]{2,1,0:T(8,128)(2,1)S(1)}, u32[]{:S(2)}, u32[]{:S(2)}) async-start(bf16[8,64,512]{2,1,0:T(8,128)(2,1)} %bitcast.8), calls=%async_computation.1 | async-start | bytes 1048576 | tf_op jit(solution)/shard_map/all_to_all | solution.py:256
  28.6 15.7 %collective-permute-start.2 = (bf16[1,8,64,512]{3,2,1,0:T(8,128)(2,1)S(1)}, bf16[1,8,64,512]{3,2,1,0:T(8,128)(2,1)S(1)}, u32[]{:S(2)}, u32[]{:S(2)}) collective-permute-start(bf16[1,8,64,512]{3,2,1,0:T(8,128)(2,1)S(1)} %bitcast.72), channel_id=1, source_target_pairs={{0,2},{1,3},{2,0},{3,1},{4,6},{5,7},{6,4},{7,5},{8,10},{9,11},{10,... | collective-permute-start | bytes 1572872 | tf_op jit(solution)/shard_map/ppermute | solution.py:253
  43.8 6.7 %collective-permute-start = (bf16[1,8,65,256]{3,2,1,0:T(8,128)(2,1)S(1)}, bf16[1,8,65,256]{3,2,1,0:T(8,128)(2,1)S(1)}, u32[]{:S(2)}, u32[]{:S(2)}) collective-permute-start(bf16[1,8,65,256]{3,2,1,0:T(8,128)(2,1)S(1)} %bitcast.67), channel_id=1, source_target_pairs={{0,2},{1,3},{2,0},{3,1},{4,6},{5,7},{6,4},{7,5},{8,10},{9,11},{10,... | collective-permute-start | bytes 798728 | tf_op jit(solution)/shard_map/ppermute | solution.py:253
  44.5 9.9 %copy-start.1 = (bf16[2,8,64,512]{3,2,1,0:T(8,128)(2,1)}, bf16[2,8,64,512]{3,2,1,0:T(8,128)(2,1)S(1)}, u32[]{:S(2)}) copy-start(bf16[2,8,64,512]{3,2,1,0:T(8,128)(2,1)S(1)} %pad_maximum_fusion.refs_2_) | copy-start | bytes 3145732
  44.5 9.9 %collective-permute-start.3 = (bf16[2,8,64,512]{3,2,1,0:T(8,128)(2,1)S(1)}, bf16[2,8,64,512]{3,2,1,0:T(8,128)(2,1)}, u32[]{:S(2)}, u32[]{:S(2)}) collective-permute-start(bf16[2,8,64,512]{3,2,1,0:T(8,128)(2,1)S(1)} %pad_maximum_fusion.refs_2_), channel_id=1, source_target_pairs={{0,1},{1,0},{2,3},{3,2},{4,5},{5,4},{6,7},{7,6},{8,9},{9,8},{10,11... | collective-permute-start | bytes 3145736 | tf_op jit(solution)/shard_map/ppermute | solution.py:264
  50.6 3.8 %copy-start = (bf16[2,8,65,256]{3,2,1,0:T(8,128)(2,1)}, bf16[2,8,65,256]{3,2,1,0:T(8,128)(2,1)S(1)}, u32[]{:S(2)}) copy-start(bf16[2,8,65,256]{3,2,1,0:T(8,128)(2,1)S(1)} %pad_maximum_fusion.1.refs_0_) | copy-start | bytes 1597444
  50.7 2.0 %collective-permute-start.1 = (bf16[2,8,65,256]{3,1,2,0:T(8,128)(2,1)S(1)}, bf16[2,8,65,256]{3,1,2,0:T(8,128)(2,1)S(1)}, u32[]{:S(2)}, u32[]{:S(2)}) collective-permute-start(bf16[2,8,65,256]{3,1,2,0:T(8,128)(2,1)S(1)} %copy.58), channel_id=1, source_target_pairs={{0,1},{1,0},{2,3},{3,2},{4,5},{5,4},{6,7},{7,6},{8,9},{9,8},{10,11... | collective-permute-start | bytes 1597448 | tf_op jit(solution)/shard_map/ppermute | solution.py:263
  54.4 25.5 %copy-start.3 = (bf16[512,64]{0,1:T(8,128)(2,1)S(1)}, bf16[512,64]{0,1:T(8,128)(2,1)}, u32[]{:S(2)}) copy-start(bf16[512,64]{0,1:T(8,128)(2,1)} %param.6) | copy-start | bytes 196612
  67.9 11.2 %all-to-all-start.2 = ((f32[8,1,256]{2,1,0:T(1,128)}), f32[8,1,256]{2,1,0:T(1,128)S(1)}, u32[]{:S(2)}, u32[]{:S(2)}) async-start(f32[8,1,256]{2,1,0:T(1,128)} %bitcast.101), calls=%async_computation.2 | async-start | bytes 16384 | tf_op jit(solution)/shard_map/all_to_all | solution.py:271

commit v18 on v16

--- a/solution.py
+++ b/solution.py
@@ -86,10 +86,10 @@
     )(keys.reshape(1, slot_count), low, high)
 
 
-def pieces_kernel(low_count, high_count, col_keys, *refs):
+def pieces_kernel(low_count, high_count, *refs):
     low_refs = refs[:low_count]
     high_refs = refs[low_count:low_count + high_count]
-    weights, row_sums, joined = refs[low_count + high_count:]
+    weights, row_sums, joined, col_keys = refs[low_count + high_count:]
     block_rows = weights.shape[0]
     slot_count = weights.shape[1]
     quarters, part, width = joined.shape[1], joined.shape[2], joined.shape[3]
@@ -101,8 +101,11 @@
             at = 0
             for ref in group:
                 for m in range(ref.shape[0]):
-                    joined[:, at, :, lo:hi] = ref[m]
+                    joined[:, at, :, lo:hi] = ref[m, :, :part, :]
                     at += 1
+        key_parts = [ref[m, :, part, :part] for ref in low_refs for m in range(ref.shape[0])]
+        key_grid = jnp.concatenate(key_parts, axis=1).astype(jnp.float32)
+        col_keys[...] = key_grid.reshape(1, slot_count)
 
     per_block = block_rows // (quarters * part)
     first = pl.multiple_of(pl.program_id(0) * per_block, per_block)
@@ -141,14 +144,11 @@
     slot_count = sources * quarters * part
     block_rows = min(512, slot_count)
     pieces = list(low_pieces) + list(high_pieces)
-    specs = [
-        pl.BlockSpec((piece.shape[0], sources, part, piece.shape[3]), lambda i: (0, 0, 0, 0))
-        for piece in pieces
-    ]
+    specs = [pl.BlockSpec(piece.shape, lambda i: (0, 0, 0, 0)) for piece in pieces]
     return pl.pallas_call(
         functools.partial(pieces_kernel, len(low_pieces), len(high_pieces)),
         grid=(slot_count // block_rows,),
-        in_specs=[pl.BlockSpec((1, slot_count), lambda i: (0, 0))] + specs,
+        in_specs=specs,
         out_specs=[
             pl.BlockSpec((block_rows, slot_count), lambda i: (i, 0)),
             pl.BlockSpec((1, block_rows), lambda i: (0, i)),
@@ -157,14 +157,17 @@
             jax.ShapeDtypeStruct((slot_count, slot_count), jnp.bfloat16),
             jax.ShapeDtypeStruct((1, slot_count), jnp.float32),
         ],
-        scratch_shapes=[pltpu.VMEM((sources, quarters, part, width), jnp.bfloat16)],
+        scratch_shapes=[
+            pltpu.VMEM((sources, quarters, part, width), jnp.bfloat16),
+            pltpu.VMEM((1, slot_count), jnp.float32),
+        ],
         compiler_params=pltpu.CompilerParams(dimension_semantics=("arbitrary",)),
         cost_estimate=pl.CostEstimate(
             flops=2 * slot_count * slot_count * width + 22 * slot_count * slot_count,
             transcendentals=0,
             bytes_accessed=slot_count * width * 2 + 2 * slot_count * slot_count,
         ),
-    )(keys.reshape(1, slot_count), *pieces)
+    )(*pieces)
 
 
 def on_device(embeddings, labels, image_lists, rank_keys):

time: 156 us -> 159 us (1.019)
  blocking collectives: 70.6 us -> 56.9 us
  waiting for transfers between devices: 27.7 us -> 37.4 us
  starting transfers between devices: 14.1 us -> 18.3 us
    all_to_all x1 -> x0, blocking collectives: 13.7 us -> none  [on_device(): lax.all_to_all(low_payload, 'img', split_axis=0, concat_axis=0, tiled=True)]
    ppermute x2, waiting for transfers between devices: 5.99 us -> 12.6 us  [exchange_stage(): return jnp.concatenate([got, lax.ppermute(got, 'sub', pairs)], axis=0)]
    all_to_all x0 -> x1, starting transfers between devices: none -> 3.64 us  [on_device(): lax.all_to_all(low_payload, 'img', split_axis=0, concat_axis=0, tiled=True)]
    all_to_all x0 -> x1, waiting for transfers between devices: none -> 2.96 us  [on_device(): lax.all_to_all(low_payload, 'img', split_axis=0, concat_axis=0, tiled=True)]
  transfers between devices with their start and end apart: 6 -> 7, of which waited for: 4 -> 6; matrix products, arithmetic and copies ran while one was open for 2% -> 2% of each run, Pallas kernels for 0% -> 0%
where the time goes in v18:
time: 159 us; the launch traced here: 158 us
  blocking collectives  56.9 us (36%)
  waiting for transfers between devices  37.4 us (24%)
  matrix products  19.8 us (12%)
  starting transfers between devices  18.3 us (12%)
  Pallas kernels  14.8 us (9%)
  local copies, waits for them, and re-layouts  5.27 us (3%)
  other arithmetic  5.17 us (3%)
    all_to_all x2, blocking collectives, on_device(): lax.all_to_all(bucket_major(product), 'img', split_axis=0, concat_axis=0,...  34.3 us
    all_to_all x2, blocking collectives, on_device(): lax.all_to_all(to_bucket(scaled), 'img', split_axis=0, concat_axis=0, til...  22.6 us
    pallas_call x1, Pallas kernels, pieces_affinity(): pl.pallas_call(functools.partial(pieces_kernel, len(low_pieces), len(high...  14.8 us
    all_to_all x1, waiting for transfers between devices, on_device(): lax.all_to_all(high_payload, 'img', split_axis=0, concat_axis=0, tiled=True)  13.7 us
    ppermute x2, waiting for transfers between devices, exchange_stage(): return jnp.concatenate([got, lax.ppermute(got, 'sub', pairs)], axis=0)  12.6 us
    dot_general x2, matrix products, on_device(): jnp.einsum('ajk,akc->ajc', weights, list_major(arrived), preferred_elemen...  12.1 us
    all_to_all x1, starting transfers between devices, on_device(): lax.all_to_all(high_payload, 'img', split_axis=0, concat_axis=0, tiled=True)  7.28 us
    all_to_all x1, waiting for transfers between devices, on_device(): lax.all_to_all(bucket_major(row_sums), 'img', split_axis=0, concat_axis=0...  6.36 us
  transfers between devices with their start and end apart: 7, of which 6 were waited for; matrix products, arithmetic and copies ran while one was open for 2% of the time, Pallas kernels for 0%

profile of v18, /device:TPU:0, one launch (start us, length us, event | category | flops | bytes accessed | tf_op | source)
XLA Modules:
  0.0 157.9 jit_solution(9149216172688579995)
XLA Ops:
  0.0 0.8 copy.48
  0.8 0.2 eq.32
  1.0 0.5 convert_reduce_fusion
  1.5 0.2 reduce_sum.39
  1.8 0.1 copy.49
  1.9 0.7 multiply_add_fusion
  2.6 0.1 iota_add_fusion.1
  2.7 0.1 add.108
  2.7 1.4 fusion.1
  4.1 1.9 %convolution_convert_fusion.2 = bf16[512,768]{1,0:T(8,128)(2,1)S(1)} fusion(bf16[512,768]{1,0:T(8,128)(2,1)} %param.5, f32[512]{0:T(512)S(1)} %add_rsqrt_fusion, s32[512]{0:T(512)S(1)} %bitcast.80, s32[512]{0:T(512)S(1)} %bitcast.72, s32[512]{0:T(512)S(1)} %add.108), kind=kOutput, calls=%fused_computation.11 | convolution fusion | flops 405012480 | bytes 1581056 | tf_op jit(solution)/shard_map/dot_general | solution.py:238
  6.0 0.0 copy-start.5
  6.0 0.8 slice.31
  6.9 7.3 %all-to-all-start.1 = ((bf16[8,64,512]{2,1,0:T(8,128)(2,1)}), bf16[8,64,512]{2,1,0:T(8,128)(2,1)S(1)}, u32[]{:S(2)}, u32[]{:S(2)}) async-start(bf16[8,64,512]{2,1,0:T(8,128)(2,1)} %slice.31), calls=%async_computation.1 | async-start | bytes 1048576 | tf_op jit(solution)/shard_map/all_to_all | solution.py:255
  14.2 0.0 copy-done.2
  14.2 0.4 fusion.10
  14.6 0.3 fusion.9
  14.9 13.7 %all-to-all-done.1 = bf16[8,64,512]{2,1,0:T(8,128)(2,1)S(1)} async-done(((bf16[8,64,512]{2,1,0:T(8,128)(2,1)}), bf16[8,64,512]{2,1,0:T(8,128)(2,1)S(1)}, u32[]{:S(2)}, u32[]{:S(2)}) %all-to-all-start.1) | async-done | bytes 524320 | tf_op jit(solution)/shard_map/all_to_all | solution.py:255
  28.6 1.5 collective-permute-start.2
  30.1 0.1 convert_element_type.65
  30.2 0.7 fusion.17
  30.9 3.6 %all-to-all-start = ((bf16[8,65,256]{2,1,0:T(8,128)(2,1)}), bf16[8,65,256]{2,1,0:T(8,128)(2,1)S(1)}, u32[]{:S(2)}, u32[]{:S(2)}) async-start(bf16[8,65,256]{2,1,0:T(8,128)(2,1)} %fusion.17), calls=%async_computation | async-start | bytes 589824 | tf_op jit(solution)/shard_map/all_to_all | solution.py:254
  34.6 6.4 %collective-permute-done.2 = bf16[1,8,64,512]{3,2,1,0:T(8,128)(2,1)S(1)} collective-permute-done((bf16[1,8,64,512]{3,2,1,0:T(8,128)(2,1)S(1)}, bf16[1,8,64,512]{3,2,1,0:T(8,128)(2,1)S(1)}, u32[]{:S(2)}, u32[]{:S(2)}) %collective-permute-start.2) | collective-permute-done | bytes 524320 | tf_op jit(solution)/shard_map/ppermute | solution.py:252
  40.9 0.1 pad_maximum_fusion.refs_2_
  41.0 0.0 copy-start.1
  41.1 0.1 collective-permute-start.3
  41.1 3.0 %all-to-all-done = bf16[8,65,256]{2,1,0:T(8,128)(2,1)S(1)} async-done(((bf16[8,65,256]{2,1,0:T(8,128)(2,1)}), bf16[8,65,256]{2,1,0:T(8,128)(2,1)S(1)}, u32[]{:S(2)}, u32[]{:S(2)}) %all-to-all-start) | async-done | bytes 266272 | tf_op jit(solution)/shard_map/all_to_all | solution.py:254
  44.1 0.5 collective-permute-start
  44.6 6.2 %collective-permute-done = bf16[1,8,65,256]{3,2,1,0:T(8,128)(2,1)S(1)} collective-permute-done((bf16[1,8,65,256]{3,2,1,0:T(8,128)(2,1)S(1)}, bf16[1,8,65,256]{3,2,1,0:T(8,128)(2,1)S(1)}, u32[]{:S(2)}, u32[]{:S(2)}) %collective-permute-start) | collective-permute-done | bytes 266272 | tf_op jit(solution)/shard_map/ppermute | solution.py:252
  50.8 0.1 pad_maximum_fusion.1.refs_0_
  50.9 0.0 copy-start
  50.9 0.1 copy.51
  51.0 0.1 collective-permute-start.1
  51.1 0.0 copy-done.5
  51.1 0.1 broadcast_add_fusion
  51.2 1.8 %collective-permute-done.1 = bf16[2,8,65,256]{3,1,2,0:T(8,128)(2,1)S(1)} collective-permute-done((bf16[2,8,65,256]{3,1,2,0:T(8,128)(2,1)S(1)}, bf16[2,8,65,256]{3,1,2,0:T(8,128)(2,1)S(1)}, u32[]{:S(2)}, u32[]{:S(2)}) %collective-permute-start.1) | collective-permute-done | bytes 532512 | tf_op jit(solution)/shard_map/ppermute | solution.py:262
  53.0 0.9 copy.52.refs_1_
  53.9 0.0 collective-permute-done.3.refs_3_
  53.9 0.0 copy-done.1
  53.9 0.0 copy-done
  53.9 0.0 copy-start.3
  53.9 1.0 copy-done.3
  54.9 14.8 %shard_map.55 = (bf16[2048,2048]{1,0:T(8,128)(2,1)}, f32[1,2048]{1,0:T(1,128)}) custom-call(bf16[2,8,65,256]{3,2,1,0:T(8,128)(2,1)} %copy-done, bf16[2,8,65,256]{3,2,1,0:T(8,128)(2,1)} %copy.52.refs_1_, bf16[2,8,64,512]{3,2,1,0:T(8,128)(2,1)} %copy-done.1, bf16[2,8,64,512]{3,2,1,0:T(8,128)(2,1)} %copy-done.3), custom_call_target="tpu_custom_call" | custom-call | flops 6534725632 | bytes 11534336 | tf_op jit(solution)/shard_map/pallas_call | solution.py:148
  69.7 5.2 %all-to-all-start.2 = ((f32[8,1,256]{2,1,0:T(1,128)}), f32[8,1,256]{2,1,0:T(1,128)S(1)}, u32[]{:S(2)}, u32[]{:S(2)}) async-start(f32[8,1,256]{2,1,0:T(1,128)} %bitcast.88), calls=%async_computation.2 | async-start | bytes 16384 | tf_op jit(solution)/shard_map/all_to_all | solution.py:270
  74.9 0.1 iota_add_fusion
  75.0 0.1 add.102
  75.1 6.4 %all-to-all-done.2 = f32[8,1,256]{2,1,0:T(1,128)S(1)} async-done(((f32[8,1,256]{2,1,0:T(1,128)}), f32[8,1,256]{2,1,0:T(1,128)S(1)}, u32[]{:S(2)}, u32[]{:S(2)}) %all-to-all-start.2) | async-done | bytes 8224 | tf_op jit(solution)/shard_map/all_to_all | solution.py:270
  81.4 0.7 select_reduce_fusion
  82.1 0.0 copy-done.4
  82.2 1.3 convolution_convert_fusion.1
  83.4 0.1 copy.62
  83.5 10.6 %all_to_all.35 = bf16[8,1,256,64]{2,3,1,0:T(8,128)(2,1)S(1)} all-to-all(bf16[8,1,256,64]{2,3,1,0:T(8,128)(2,1)S(1)} %copy.54), channel_id=1, replica_groups=mesh['img'=8,'sub'=4] {'img'}, dimensions={0} | all-to-all | bytes 524288 | tf_op jit(solution)/shard_map/all_to_all | solution.py:279
  94.2 0.1 copy.55
  94.3 0.1 reshape.174
  94.5 6.0 %convolution_bitcast_fusion.1 = f32[8,1,256,64]{2,3,1,0:T(8,128)S(1)} fusion(bf16[8,256,2048]{2,1,0:T(8,128)(2,1)} %bitcast.55, bf16[2048,64,1]{0,1,2:T(8,128)(2,1)S(1)} %reshape.174), kind=kOutput, calls=%fused_computation.16 | convolution fusion | flops 536870912 | bytes 9175040 | tf_op jit(solution)/shard_map/ajk,akc->ajc/dot_general | solution.py:280
  100.5 17.0 %all_to_all.36 = f32[8,1,256,64]{2,3,1,0:T(8,128)S(1)} all-to-all(f32[8,1,256,64]{2,3,1,0:T(8,128)S(1)} %convolution_bitcast_fusion.1), channel_id=1, replica_groups=mesh['img'=8,'sub'=4] {'img'}, dimensions={0} | all-to-all | bytes 1048576 | tf_op jit(solution)/shard_map/all_to_all | solution.py:283
  117.6 1.3 fusion.6
  118.9 1.3 convolution_convert_fusion
  120.2 0.1 copy.64
  120.3 12.0 %all_to_all.37 = bf16[8,1,256,64]{2,3,1,0:T(8,128)(2,1)S(1)} all-to-all(bf16[8,1,256,64]{2,3,1,0:T(8,128)(2,1)S(1)} %copy.58), channel_id=1, replica_groups=mesh['img'=8,'sub'=4] {'img'}, dimensions={0} | all-to-all | bytes 524288 | tf_op jit(solution)/shard_map/all_to_all | solution.py:279
  132.3 0.1 copy.59
  132.4 0.1 reshape.175
  132.6 6.0 %convolution_bitcast_fusion = f32[8,1,256,64]{2,3,1,0:T(8,128)S(1)} fusion(bf16[8,256,2048]{2,1,0:T(8,128)(2,1)} %bitcast.56, bf16[2048,64,1]{0,1,2:T(8,128)(2,1)S(1)} %reshape.175), kind=kOutput, calls=%fused_computation.15 | convolution fusion | flops 536870912 | bytes 9175040 | tf_op jit(solution)/shard_map/ajk,akc->ajc/dot_general | solution.py:280
  138.6 17.3 %all_to_all.38 = f32[8,1,256,64]{2,3,1,0:T(8,128)S(1)} all-to-all(f32[8,1,256,64]{2,3,1,0:T(8,128)S(1)} %convolution_bitcast_fusion), channel_id=1, replica_groups=mesh['img'=8,'sub'=4] {'img'}, dimensions={0} | all-to-all | bytes 1048576 | tf_op jit(solution)/shard_map/all_to_all | solution.py:283
  155.9 2.0 %fusion.7 = bf16[512,64]{0,1:T(8,128)(2,1)} fusion(f32[2048,64]{0,1:T(8,128)S(1)} %bitcast.67, bf16[512,64]{0,1:T(8,128)(2,1)S(1)} %copy-done.4, f32[512]{0:T(512)S(1)} %get-tuple-element.13, s32[512]{0:T(512)S(1)} %bitcast.87, s32[512]{0:T(512)S(1)} %bitcast.79, s32[2048]{0:T(1024)S(1)} %add.102), kind=kOutput, calls=%fused_computation.23 | convolution fusion | flops 405962752 | bytes 669696 | tf_op jit(solution)/shard_map/kg,kc->gc/dot_general | solution.py:214
  (16 shorter events, 0.3 us)
Async XLA Ops:
  0.0 14.2 %copy-start.2 = (s32[512,2]{0,1:T(2,128)S(1)}, s32[512,2]{0,1:T(2,128)}, u32[]{:S(2)}) copy-start(s32[512,2]{0,1:T(2,128)} %param.8) | copy-start | bytes 12292
  6.0 45.1 %copy-start.5 = (s32[4]{0:T(128)S(1)}, s32[4]{0:T(128)}, u32[]{:S(2)}) copy-start(s32[4]{0:T(128)} %constant.11.clone) | copy-start | bytes 52
  6.9 21.8 %all-to-all-start.1 = ((bf16[8,64,512]{2,1,0:T(8,128)(2,1)}), bf16[8,64,512]{2,1,0:T(8,128)(2,1)S(1)}, u32[]{:S(2)}, u32[]{:S(2)}) async-start(bf16[8,64,512]{2,1,0:T(8,128)(2,1)} %slice.31), calls=%async_computation.1 | async-start | bytes 1048576 | tf_op jit(solution)/shard_map/all_to_all | solution.py:255
  28.6 12.3 %collective-permute-start.2 = (bf16[1,8,64,512]{3,2,1,0:T(8,128)(2,1)S(1)}, bf16[1,8,64,512]{3,2,1,0:T(8,128)(2,1)S(1)}, u32[]{:S(2)}, u32[]{:S(2)}) collective-permute-start(bf16[1,8,64,512]{3,2,1,0:T(8,128)(2,1)S(1)} %bitcast.59), channel_id=1, source_target_pairs={{0,2},{1,3},{2,0},{3,1},{4,6},{5,7},{6,4},{7,5},{8,10},{9,11},{10,... | collective-permute-start | bytes 1572872 | tf_op jit(solution)/shard_map/ppermute | solution.py:252
  30.9 13.2 %all-to-all-start = ((bf16[8,65,256]{2,1,0:T(8,128)(2,1)}), bf16[8,65,256]{2,1,0:T(8,128)(2,1)S(1)}, u32[]{:S(2)}, u32[]{:S(2)}) async-start(bf16[8,65,256]{2,1,0:T(8,128)(2,1)} %fusion.17), calls=%async_computation | async-start | bytes 589824 | tf_op jit(solution)/shard_map/all_to_all | solution.py:254
  41.0 12.9 %copy-start.1 = (bf16[2,8,64,512]{3,2,1,0:T(8,128)(2,1)}, bf16[2,8,64,512]{3,2,1,0:T(8,128)(2,1)S(1)}, u32[]{:S(2)}) copy-start(bf16[2,8,64,512]{3,2,1,0:T(8,128)(2,1)S(1)} %pad_maximum_fusion.refs_2_) | copy-start | bytes 3145732
  41.1 12.9 %collective-permute-start.3 = (bf16[2,8,64,512]{3,2,1,0:T(8,128)(2,1)S(1)}, bf16[2,8,64,512]{3,2,1,0:T(8,128)(2,1)S(1)}, u32[]{:S(2)}, u32[]{:S(2)}) collective-permute-start(bf16[2,8,64,512]{3,2,1,0:T(8,128)(2,1)S(1)} %pad_maximum_fusion.refs_2_), channel_id=1, source_target_pairs={{0,1},{1,0},{2,3},{3,2},{4,5},{5,4},{6,7},{7,6},{8,9},{9,8},{10,11... | collective-permute-start | bytes 3145736 | tf_op jit(solution)/shard_map/ppermute | solution.py:263
  44.1 6.7 %collective-permute-start = (bf16[1,8,65,256]{3,2,1,0:T(8,128)(2,1)S(1)}, bf16[1,8,65,256]{3,2,1,0:T(8,128)(2,1)S(1)}, u32[]{:S(2)}, u32[]{:S(2)}) collective-permute-start(bf16[1,8,65,256]{3,2,1,0:T(8,128)(2,1)S(1)} %bitcast.61), channel_id=1, source_target_pairs={{0,2},{1,3},{2,0},{3,1},{4,6},{5,7},{6,4},{7,5},{8,10},{9,11},{10,... | collective-permute-start | bytes 798728 | tf_op jit(solution)/shard_map/ppermute | solution.py:252
  50.9 3.0 %copy-start = (bf16[2,8,65,256]{3,2,1,0:T(8,128)(2,1)}, bf16[2,8,65,256]{3,2,1,0:T(8,128)(2,1)S(1)}, u32[]{:S(2)}) copy-start(bf16[2,8,65,256]{3,2,1,0:T(8,128)(2,1)S(1)} %pad_maximum_fusion.1.refs_0_) | copy-start | bytes 1597444
  51.0 2.0 %collective-permute-start.1 = (bf16[2,8,65,256]{3,1,2,0:T(8,128)(2,1)S(1)}, bf16[2,8,65,256]{3,1,2,0:T(8,128)(2,1)S(1)}, u32[]{:S(2)}, u32[]{:S(2)}) collective-permute-start(bf16[2,8,65,256]{3,1,2,0:T(8,128)(2,1)S(1)} %copy.51), channel_id=1, source_target_pairs={{0,1},{1,0},{2,3},{3,2},{4,5},{5,4},{6,7},{7,6},{8,9},{9,8},{10,11... | collective-permute-start | bytes 1597448 | tf_op jit(solution)/shard_map/ppermute | solution.py:262
  53.9 28.2 %copy-start.4 = (bf16[512,64]{0,1:T(8,128)(2,1)S(1)}, bf16[512,64]{0,1:T(8,128)(2,1)}, u32[]{:S(2)}) copy-start(bf16[512,64]{0,1:T(8,128)(2,1)} %param.6) | copy-start | bytes 196612
  53.9 1.0 copy-start.3
  69.7 11.7 %all-to-all-start.2 = ((f32[8,1,256]{2,1,0:T(1,128)}), f32[8,1,256]{2,1,0:T(1,128)S(1)}, u32[]{:S(2)}, u32[]{:S(2)}) async-start(f32[8,1,256]{2,1,0:T(1,128)} %bitcast.88), calls=%async_computation.2 | async-start | bytes 16384 | tf_op jit(solution)/shard_map/all_to_all | solution.py:270

commit v19 on v16

--- a/solution.py
+++ b/solution.py
@@ -196,7 +196,7 @@
     hit_a = slot_of_pair[None, :, 0] == slot_ids
     hit_b = slot_of_pair[None, :, 1] == slot_ids
     hit = hit_a | hit_b
-    pick = hit.astype(jnp.bfloat16)
+    pick = lax.optimization_barrier(hit.astype(jnp.bfloat16))
 
     def to_bucket(rows):
         picked = jnp.dot(pick, rows, preferred_element_type=jnp.float32).astype(rows.dtype)
@@ -267,7 +267,7 @@
     degree_slots = lax.all_to_all(
         bucket_major(row_sums), "img", split_axis=0, concat_axis=0, tiled=True
     )
-    degree = jnp.sum(jnp.where(hit, degree_slots.reshape(slot_total, 1), 0.0), axis=0)
+    degree = jnp.sum(jnp.where(pick > 0, degree_slots.reshape(slot_total, 1), 0.0), axis=0)
     inv = lax.rsqrt(degree)
     starting = labels.astype(jnp.float32)
     current = starting

time: 156 us -> 157 us (level)
  blocking collectives: 70.6 us -> 56.9 us
  waiting for transfers between devices: 27.7 us -> 37 us
  starting transfers between devices: 14.1 us -> 19.8 us
  matrix products: 19.8 us -> 17.8 us
    all_to_all x1 -> x0, blocking collectives: 13.7 us -> none  [on_device(): lax.all_to_all(low_payload, 'img', split_axis=0, concat_axis=0, tiled=True)]
    all_to_all x0 -> x1, waiting for transfers between devices: none -> 8.26 us  [on_device(): lax.all_to_all(low_payload, 'img', split_axis=0, concat_axis=0, tiled=True)]
    all_to_all x0 -> x1, starting transfers between devices: none -> 3.64 us  [on_device(): lax.all_to_all(low_payload, 'img', split_axis=0, concat_axis=0, tiled=True)]
    ppermute x2, waiting for transfers between devices: 5.99 us -> 8.43 us  [exchange_stage(): return jnp.concatenate([got, lax.ppermute(got, 'sub', pairs)], axis=0)]
  transfers between devices with their start and end apart: 6 -> 7, of which waited for: 4 -> 6; matrix products, arithmetic and copies ran while one was open for 2% -> 3% of each run, Pallas kernels for 0% -> 0%
where the time goes in v19:
time: 157 us; the launch traced here: 156 us
  blocking collectives  56.9 us (36%)
  waiting for transfers between devices  37 us (24%)
  starting transfers between devices  19.8 us (13%)
  matrix products  17.8 us (11%)
  Pallas kernels  13.4 us (9%)
  other arithmetic  5.88 us (4%)
  local copies, waits for them, and re-layouts  5.01 us (3%)
    all_to_all x2, blocking collectives, on_device(): lax.all_to_all(bucket_major(product), 'img', split_axis=0, concat_axis=0,...  34.3 us
    all_to_all x2, blocking collectives, on_device(): lax.all_to_all(to_bucket(scaled), 'img', split_axis=0, concat_axis=0, til...  22.6 us
    pallas_call x1, Pallas kernels, pieces_affinity(): pl.pallas_call(functools.partial(pieces_kernel, len(low_pieces), len(high...  13.4 us
    all_to_all x1, waiting for transfers between devices, on_device(): lax.all_to_all(high_payload, 'img', split_axis=0, concat_axis=0, tiled=True)  12.8 us
    dot_general x2, matrix products, on_device(): jnp.einsum('ajk,akc->ajc', weights, list_major(arrived), preferred_elemen...  12.1 us
    ppermute x2, waiting for transfers between devices, exchange_stage(): return jnp.concatenate([got, lax.ppermute(got, 'sub', pairs)], axis=0)  8.43 us
    all_to_all x1, waiting for transfers between devices, on_device(): lax.all_to_all(low_payload, 'img', split_axis=0, concat_axis=0, tiled=True)  8.26 us
    all_to_all x1, starting transfers between devices, on_device(): lax.all_to_all(high_payload, 'img', split_axis=0, concat_axis=0, tiled=True)  7.28 us
  transfers between devices with their start and end apart: 7, of which 6 were waited for; matrix products, arithmetic and copies ran while one was open for 3% of the time, Pallas kernels for 0%

profile of v19, /device:TPU:0, one launch (start us, length us, event | category | flops | bytes accessed | tf_op | source)
XLA Modules:
  0.0 155.9 jit_solution(4768392919910137528)
XLA Ops:
  0.0 0.8 copy.55
  0.8 0.2 eq.32
  1.0 0.5 convert_reduce_fusion
  1.5 0.2 reduce_sum.39
  1.7 0.1 copy.56
  1.9 0.7 multiply_add_fusion
  2.6 0.1 iota_add_fusion.1
  2.6 0.1 add.108
  2.7 1.4 fusion.1
  4.1 0.0 copy-start.3
  4.1 1.9 %convolution_convert_fusion.2 = bf16[512,768]{1,0:T(8,128)(2,1)S(1)} fusion(bf16[512,768]{1,0:T(8,128)(2,1)} %param.5, f32[512]{0:T(512)S(1)} %add_rsqrt_fusion, s32[512]{0:T(512)S(1)} %bitcast.90, s32[512]{0:T(512)S(1)} %bitcast.86, s32[512]{0:T(512)S(1)} %add.108), kind=kOutput, calls=%fused_computation.11 | convolution fusion | flops 405012480 | bytes 1581056 | tf_op jit(solution)/shard_map/dot_general | solution.py:235
  6.0 0.0 copy-start.4
  6.0 0.8 slice.42
  6.9 7.3 %all-to-all-start.1 = ((bf16[8,64,512]{2,1,0:T(8,128)(2,1)}), bf16[8,64,512]{2,1,0:T(8,128)(2,1)S(1)}, u32[]{:S(2)}, u32[]{:S(2)}) async-start(bf16[8,64,512]{2,1,0:T(8,128)(2,1)} %slice.42), calls=%async_computation.1 | async-start | bytes 1048576 | tf_op jit(solution)/shard_map/all_to_all | solution.py:252
  14.2 0.0 copy-done.3
  14.2 0.4 fusion.10
  14.6 0.3 fusion.9
  14.9 0.1 convert_element_type.89
  15.0 0.8 fusion.17
  15.8 12.8 %all-to-all-done.1 = bf16[8,64,512]{2,1,0:T(8,128)(2,1)S(1)} async-done(((bf16[8,64,512]{2,1,0:T(8,128)(2,1)}), bf16[8,64,512]{2,1,0:T(8,128)(2,1)S(1)}, u32[]{:S(2)}, u32[]{:S(2)}) %all-to-all-start.1) | async-done | bytes 524320 | tf_op jit(solution)/shard_map/all_to_all | solution.py:252
  28.6 3.6 %all-to-all-start = ((bf16[8,65,256]{2,1,0:T(8,128)(2,1)}), bf16[8,65,256]{2,1,0:T(8,128)(2,1)S(1)}, u32[]{:S(2)}, u32[]{:S(2)}) async-start(bf16[8,65,256]{2,1,0:T(8,128)(2,1)} %fusion.17), calls=%async_computation | async-start | bytes 589824 | tf_op jit(solution)/shard_map/all_to_all | solution.py:251
  32.3 1.5 collective-permute-start.2
  33.7 8.3 %all-to-all-done = bf16[8,65,256]{2,1,0:T(8,128)(2,1)S(1)} async-done(((bf16[8,65,256]{2,1,0:T(8,128)(2,1)}), bf16[8,65,256]{2,1,0:T(8,128)(2,1)S(1)}, u32[]{:S(2)}, u32[]{:S(2)}) %all-to-all-start) | async-done | bytes 266272 | tf_op jit(solution)/shard_map/all_to_all | solution.py:251
  42.0 1.5 collective-permute-start
  43.5 0.0 copy-done.4
  43.5 3.6 %collective-permute-done.2 = bf16[1,8,64,512]{3,2,1,0:T(8,128)(2,1)S(1)} collective-permute-done((bf16[1,8,64,512]{3,2,1,0:T(8,128)(2,1)S(1)}, bf16[1,8,64,512]{3,2,1,0:T(8,128)(2,1)S(1)}, u32[]{:S(2)}, u32[]{:S(2)}) %collective-permute-start.2) | collective-permute-done | bytes 524320 | tf_op jit(solution)/shard_map/ppermute | solution.py:249
  47.1 0.1 pad_maximum_fusion.refs_2_
  47.2 0.0 copy-start.1
  47.2 0.1 collective-permute-start.3
  47.3 4.9 %collective-permute-done = bf16[1,8,65,256]{3,2,1,0:T(8,128)(2,1)S(1)} collective-permute-done((bf16[1,8,65,256]{3,2,1,0:T(8,128)(2,1)S(1)}, bf16[1,8,65,256]{3,2,1,0:T(8,128)(2,1)S(1)}, u32[]{:S(2)}, u32[]{:S(2)}) %collective-permute-start) | collective-permute-done | bytes 266272 | tf_op jit(solution)/shard_map/ppermute | solution.py:249
  52.1 0.1 pad_maximum_fusion.1.refs_0_
  52.2 0.0 copy-start
  52.2 0.1 copy.58
  52.3 0.1 collective-permute-start.1
  52.4 0.1 broadcast_add_fusion
  52.5 0.1 iota_add_fusion
  52.6 0.1 add.102
  52.7 1.6 %collective-permute-done.1 = bf16[2,8,65,256]{3,1,2,0:T(8,128)(2,1)S(1)} collective-permute-done((bf16[2,8,65,256]{3,1,2,0:T(8,128)(2,1)S(1)}, bf16[2,8,65,256]{3,1,2,0:T(8,128)(2,1)S(1)}, u32[]{:S(2)}, u32[]{:S(2)}) %collective-permute-start.1) | collective-permute-done | bytes 532512 | tf_op jit(solution)/shard_map/ppermute | solution.py:259
  54.3 0.7 reshape.188.col_keys
  55.0 0.9 copy.61.refs_1_
  56.0 0.0 collective-permute-done.3.refs_3_
  56.0 0.0 copy-done.1
  56.0 13.4 %shard_map.55 = (bf16[2048,2048]{1,0:T(8,128)(2,1)}, f32[1,2048]{1,0:T(1,128)}) custom-call(f32[1,2048]{1,0:T(1,128)} %reshape.188.col_keys, bf16[2,8,65,256]{3,2,1,0:T(8,128)(2,1)} %copy-done, bf16[2,8,65,256]{3,2,1,0:T(8,128)(2,1)} %copy.61.refs_1_, bf16[2,8,64,512]{3,2,1,0:T(8,128)(2,1)} %copy-done.1, bf16[2,8,64,512]{3,2,1,0:T(8,128)(2,1)} %collective-permute-done.3.refs_3_), custom_call_target="tpu_custom_call" | custom-call | flops 6534725632 | bytes 11534336 | tf_op jit(solution)/shard_map/pallas_call | solution.py:148
  69.3 5.7 %all-to-all-start.2 = ((f32[8,1,256]{2,1,0:T(1,128)}), f32[8,1,256]{2,1,0:T(1,128)S(1)}, u32[]{:S(2)}, u32[]{:S(2)}) async-start(f32[8,1,256]{2,1,0:T(1,128)} %bitcast.95), calls=%async_computation.2 | async-start | bytes 16384 | tf_op jit(solution)/shard_map/all_to_all | solution.py:267
  75.0 0.7 or_convert_fusion
  75.8 5.8 %all-to-all-done.2 = f32[8,1,256]{2,1,0:T(1,128)S(1)} async-done(((f32[8,1,256]{2,1,0:T(1,128)}), f32[8,1,256]{2,1,0:T(1,128)S(1)}, u32[]{:S(2)}, u32[]{:S(2)}) %all-to-all-start.2) | async-done | bytes 8224 | tf_op jit(solution)/shard_map/all_to_all | solution.py:267
  81.6 0.6 select_reduce_fusion
  82.2 0.0 copy-done.2
  82.2 0.8 convolution_convert_fusion.1
  83.0 0.1 copy.73
  83.1 10.6 %all_to_all.35 = bf16[8,1,256,64]{2,3,1,0:T(8,128)(2,1)S(1)} all-to-all(bf16[8,1,256,64]{2,3,1,0:T(8,128)(2,1)S(1)} %copy.63), channel_id=1, replica_groups=mesh['img'=8,'sub'=4] {'img'}, dimensions={0} | all-to-all | bytes 524288 | tf_op jit(solution)/shard_map/all_to_all | solution.py:276
  93.7 0.1 copy.64
  93.9 0.1 reshape.189
  94.0 6.0 %convolution_bitcast_fusion.1 = f32[8,1,256,64]{2,3,1,0:T(8,128)S(1)} fusion(bf16[8,256,2048]{2,1,0:T(8,128)(2,1)} %bitcast.68, bf16[2048,64,1]{0,1,2:T(8,128)(2,1)S(1)} %reshape.189), kind=kOutput, calls=%fused_computation.16 | convolution fusion | flops 536870912 | bytes 9175040 | tf_op jit(solution)/shard_map/ajk,akc->ajc/dot_general | solution.py:277
  100.1 17.0 %all_to_all.36 = f32[8,1,256,64]{2,3,1,0:T(8,128)S(1)} all-to-all(f32[8,1,256,64]{2,3,1,0:T(8,128)S(1)} %convolution_bitcast_fusion.1), channel_id=1, replica_groups=mesh['img'=8,'sub'=4] {'img'}, dimensions={0} | all-to-all | bytes 1048576 | tf_op jit(solution)/shard_map/all_to_all | solution.py:280
  117.1 0.8 fusion.6
  118.0 0.8 convolution_convert_fusion
  118.7 0.1 copy.75
  118.8 12.0 %all_to_all.37 = bf16[8,1,256,64]{2,3,1,0:T(8,128)(2,1)S(1)} all-to-all(bf16[8,1,256,64]{2,3,1,0:T(8,128)(2,1)S(1)} %copy.67), channel_id=1, replica_groups=mesh['img'=8,'sub'=4] {'img'}, dimensions={0} | all-to-all | bytes 524288 | tf_op jit(solution)/shard_map/all_to_all | solution.py:276
  130.8 0.1 copy.68
  130.9 0.1 reshape.190
  131.1 6.0 %convolution_bitcast_fusion = f32[8,1,256,64]{2,3,1,0:T(8,128)S(1)} fusion(bf16[8,256,2048]{2,1,0:T(8,128)(2,1)} %bitcast.69, bf16[2048,64,1]{0,1,2:T(8,128)(2,1)S(1)} %reshape.190), kind=kOutput, calls=%fused_computation.15 | convolution fusion | flops 536870912 | bytes 9175040 | tf_op jit(solution)/shard_map/ajk,akc->ajc/dot_general | solution.py:277
  137.1 17.3 %all_to_all.38 = f32[8,1,256,64]{2,3,1,0:T(8,128)S(1)} all-to-all(f32[8,1,256,64]{2,3,1,0:T(8,128)S(1)} %convolution_bitcast_fusion), channel_id=1, replica_groups=mesh['img'=8,'sub'=4] {'img'}, dimensions={0} | all-to-all | bytes 1048576 | tf_op jit(solution)/shard_map/all_to_all | solution.py:280
  154.4 1.5 fusion.7
  (21 shorter events, 0.3 us)
Async XLA Ops:
  4.1 10.1 %copy-start.3 = (s32[512,2]{0,1:T(2,128)S(1)}, s32[512,2]{0,1:T(2,128)}, u32[]{:S(2)}) copy-start(s32[512,2]{0,1:T(2,128)} %param.8) | copy-start | bytes 12292
  6.0 37.5 %copy-start.4 = (s32[4]{0:T(128)S(1)}, s32[4]{0:T(128)}, u32[]{:S(2)}) copy-start(s32[4]{0:T(128)} %constant.10.clone) | copy-start | bytes 52
  6.9 21.8 %all-to-all-start.1 = ((bf16[8,64,512]{2,1,0:T(8,128)(2,1)}), bf16[8,64,512]{2,1,0:T(8,128)(2,1)S(1)}, u32[]{:S(2)}, u32[]{:S(2)}) async-start(bf16[8,64,512]{2,1,0:T(8,128)(2,1)} %slice.42), calls=%async_computation.1 | async-start | bytes 1048576 | tf_op jit(solution)/shard_map/all_to_all | solution.py:252
  28.6 13.4 %all-to-all-start = ((bf16[8,65,256]{2,1,0:T(8,128)(2,1)}), bf16[8,65,256]{2,1,0:T(8,128)(2,1)S(1)}, u32[]{:S(2)}, u32[]{:S(2)}) async-start(bf16[8,65,256]{2,1,0:T(8,128)(2,1)} %fusion.17), calls=%async_computation | async-start | bytes 589824 | tf_op jit(solution)/shard_map/all_to_all | solution.py:251
  32.3 14.8 %collective-permute-start.2 = (bf16[1,8,64,512]{3,2,1,0:T(8,128)(2,1)S(1)}, bf16[1,8,64,512]{3,2,1,0:T(8,128)(2,1)S(1)}, u32[]{:S(2)}, u32[]{:S(2)}) collective-permute-start(bf16[1,8,64,512]{3,2,1,0:T(8,128)(2,1)S(1)} %bitcast.75), channel_id=1, source_target_pairs={{0,2},{1,3},{2,0},{3,1},{4,6},{5,7},{6,4},{7,5},{8,10},{9,11},{10,... | collective-permute-start | bytes 1572872 | tf_op jit(solution)/shard_map/ppermute | solution.py:249
  42.0 10.1 %collective-permute-start = (bf16[1,8,65,256]{3,2,1,0:T(8,128)(2,1)S(1)}, bf16[1,8,65,256]{3,2,1,0:T(8,128)(2,1)S(1)}, u32[]{:S(2)}, u32[]{:S(2)}) collective-permute-start(bf16[1,8,65,256]{3,2,1,0:T(8,128)(2,1)S(1)} %bitcast.70), channel_id=1, source_target_pairs={{0,2},{1,3},{2,0},{3,1},{4,6},{5,7},{6,4},{7,5},{8,10},{9,11},{10,... | collective-permute-start | bytes 798728 | tf_op jit(solution)/shard_map/ppermute | solution.py:249
  47.2 8.8 %copy-start.1 = (bf16[2,8,64,512]{3,2,1,0:T(8,128)(2,1)}, bf16[2,8,64,512]{3,2,1,0:T(8,128)(2,1)S(1)}, u32[]{:S(2)}) copy-start(bf16[2,8,64,512]{3,2,1,0:T(8,128)(2,1)S(1)} %pad_maximum_fusion.refs_2_) | copy-start | bytes 3145732
  47.2 8.8 %collective-permute-start.3 = (bf16[2,8,64,512]{3,2,1,0:T(8,128)(2,1)S(1)}, bf16[2,8,64,512]{3,2,1,0:T(8,128)(2,1)}, u32[]{:S(2)}, u32[]{:S(2)}) collective-permute-start(bf16[2,8,64,512]{3,2,1,0:T(8,128)(2,1)S(1)} %pad_maximum_fusion.refs_2_), channel_id=1, source_target_pairs={{0,1},{1,0},{2,3},{3,2},{4,5},{5,4},{6,7},{7,6},{8,9},{9,8},{10,11... | collective-permute-start | bytes 3145736 | tf_op jit(solution)/shard_map/ppermute | solution.py:260
  52.2 3.8 %copy-start = (bf16[2,8,65,256]{3,2,1,0:T(8,128)(2,1)}, bf16[2,8,65,256]{3,2,1,0:T(8,128)(2,1)S(1)}, u32[]{:S(2)}) copy-start(bf16[2,8,65,256]{3,2,1,0:T(8,128)(2,1)S(1)} %pad_maximum_fusion.1.refs_0_) | copy-start | bytes 1597444
  52.3 2.0 %collective-permute-start.1 = (bf16[2,8,65,256]{3,1,2,0:T(8,128)(2,1)S(1)}, bf16[2,8,65,256]{3,1,2,0:T(8,128)(2,1)S(1)}, u32[]{:S(2)}, u32[]{:S(2)}) collective-permute-start(bf16[2,8,65,256]{3,1,2,0:T(8,128)(2,1)S(1)} %copy.58), channel_id=1, source_target_pairs={{0,1},{1,0},{2,3},{3,2},{4,5},{5,4},{6,7},{7,6},{8,9},{9,8},{10,11... | collective-permute-start | bytes 1597448 | tf_op jit(solution)/shard_map/ppermute | solution.py:259
  69.3 12.2 %all-to-all-start.2 = ((f32[8,1,256]{2,1,0:T(1,128)}), f32[8,1,256]{2,1,0:T(1,128)S(1)}, u32[]{:S(2)}, u32[]{:S(2)}) async-start(f32[8,1,256]{2,1,0:T(1,128)} %bitcast.95), calls=%async_computation.2 | async-start | bytes 16384 | tf_op jit(solution)/shard_map/all_to_all | solution.py:267
  75.0 7.2 %copy-start.2 = (bf16[512,64]{0,1:T(8,128)(2,1)S(1)}, bf16[512,64]{0,1:T(8,128)(2,1)}, u32[]{:S(2)}) copy-start(bf16[512,64]{0,1:T(8,128)(2,1)} %param.6) | copy-start | bytes 196612

commit v20 on v19

--- a/solution.py
+++ b/solution.py
@@ -196,7 +196,7 @@
     hit_a = slot_of_pair[None, :, 0] == slot_ids
     hit_b = slot_of_pair[None, :, 1] == slot_ids
     hit = hit_a | hit_b
-    pick = lax.optimization_barrier(hit.astype(jnp.bfloat16))
+    pick = hit.astype(jnp.bfloat16)
 
     def to_bucket(rows):
         picked = jnp.dot(pick, rows, preferred_element_type=jnp.float32).astype(rows.dtype)
@@ -250,6 +250,7 @@
 
     low_got = lax.all_to_all(low_payload, "img", split_axis=0, concat_axis=0, tiled=True)[None]
     high_got = lax.all_to_all(high_payload, "img", split_axis=0, concat_axis=0, tiled=True)[None]
+    high_got, pick = lax.optimization_barrier((high_got, pick))
     bit = sub_count // 2
     while bit > 1:
         low_got = exchange_stage(low_got, bit)

time: 157 us -> 158 us (level)
  blocking collectives: 56.9 us -> 69.3 us
  waiting for transfers between devices: 37 us -> 29.7 us
  starting transfers between devices: 19.8 us -> 14 us
  local copies, waits for them, and re-layouts: 5.01 us -> 6.67 us
    all_to_all x0 -> x1, blocking collectives: none -> 12.4 us  [on_device(): lax.all_to_all(bucket_major(row_sums), 'img', split_axis=0, concat_axis=0...]
    all_to_all x1 -> x0, waiting for transfers between devices: 5.79 us -> none  [on_device(): lax.all_to_all(bucket_major(row_sums), 'img', split_axis=0, concat_axis=0...]
    all_to_all x1 -> x0, starting transfers between devices: 5.72 us -> none  [on_device(): lax.all_to_all(bucket_major(row_sums), 'img', split_axis=0, concat_axis=0...]
  transfers between devices with their start and end apart: 7 -> 6, of which waited for: 6 -> 5; matrix products, arithmetic and copies ran while one was open for 3% -> 4% of each run, Pallas kernels for 0% -> 0%
where the time goes in v20:
time: 158 us; the launch traced here: 157 us
  blocking collectives  69.3 us (44%)
  waiting for transfers between devices  29.7 us (19%)
  matrix products  17.8 us (11%)
  starting transfers between devices  14 us (9%)
  Pallas kernels  13.3 us (8%)
  local copies, waits for them, and re-layouts  6.67 us (4%)
  other arithmetic  5.74 us (4%)
    all_to_all x2, blocking collectives, on_device(): lax.all_to_all(bucket_major(product), 'img', split_axis=0, concat_axis=0,...  34.3 us
    all_to_all x2, blocking collectives, on_device(): lax.all_to_all(to_bucket(scaled), 'img', split_axis=0, concat_axis=0, til...  22.6 us
    pallas_call x1, Pallas kernels, pieces_affinity(): pl.pallas_call(functools.partial(pieces_kernel, len(low_pieces), len(high...  13.3 us
    all_to_all x1, waiting for transfers between devices, on_device(): lax.all_to_all(high_payload, 'img', split_axis=0, concat_axis=0, tiled=True)  12.6 us
    all_to_all x1, blocking collectives, on_device(): lax.all_to_all(bucket_major(row_sums), 'img', split_axis=0, concat_axis=0...  12.4 us
    dot_general x2, matrix products, on_device(): jnp.einsum('ajk,akc->ajc', weights, list_major(arrived), preferred_elemen...  12.1 us
    ppermute x2, waiting for transfers between devices, exchange_stage(): return jnp.concatenate([got, lax.ppermute(got, 'sub', pairs)], axis=0)  7.73 us
    all_to_all x1, waiting for transfers between devices, on_device(): lax.all_to_all(low_payload, 'img', split_axis=0, concat_axis=0, tiled=True)  7.49 us
  transfers between devices with their start and end apart: 6, of which 5 were waited for; matrix products, arithmetic and copies ran while one was open for 4% of the time, Pallas kernels for 0%

profile of v20, /device:TPU:0, one launch (start us, length us, event | category | flops | bytes accessed | tf_op | source)
XLA Modules:
  0.0 156.8 jit_solution(2644756640899998131)
XLA Ops:
  0.0 1.4 fusion.1
  1.4 0.1 iota_add_fusion.1
  1.4 0.1 add.101
  1.5 0.8 copy.55
  2.4 0.2 eq.32
  2.5 0.5 convert_reduce_fusion
  3.1 0.2 reduce_sum.39
  3.3 0.1 copy.56
  3.4 0.7 multiply_add_fusion
  4.1 0.0 copy-start.3
  4.1 0.0 copy-start.2
  4.1 1.9 %convolution_convert_fusion.2 = bf16[512,768]{1,0:T(8,128)(2,1)S(1)} fusion(bf16[512,768]{1,0:T(8,128)(2,1)} %param.5, f32[512]{0:T(512)S(1)} %add_rsqrt_fusion, s32[512]{0:T(512)S(1)} %bitcast.90, s32[512]{0:T(512)S(1)} %bitcast.86, s32[512]{0:T(512)S(1)} %add.101), kind=kOutput, calls=%fused_computation.11 | convolution fusion | flops 405012480 | bytes 1581056 | tf_op jit(solution)/shard_map/dot_general | solution.py:235
  6.0 0.8 slice.36
  6.8 7.3 %all-to-all-start = ((bf16[8,64,512]{2,1,0:T(8,128)(2,1)}), bf16[8,64,512]{2,1,0:T(8,128)(2,1)S(1)}, u32[]{:S(2)}, u32[]{:S(2)}) async-start(bf16[8,64,512]{2,1,0:T(8,128)(2,1)} %slice.36), calls=%async_computation | async-start | bytes 1048576 | tf_op jit(solution)/shard_map/all_to_all | solution.py:252
  14.1 0.0 copy-done.3
  14.1 0.1 broadcast_add_fusion
  14.2 0.1 iota_add_fusion
  14.3 0.0 copy-done.2
  14.3 0.1 add.110
  14.4 0.4 fusion.10
  14.8 0.3 fusion.9
  15.2 0.1 convert_element_type.89
  15.3 0.7 fusion.17
  16.0 12.6 %all-to-all-done = bf16[8,64,512]{2,1,0:T(8,128)(2,1)S(1)} async-done(((bf16[8,64,512]{2,1,0:T(8,128)(2,1)}), bf16[8,64,512]{2,1,0:T(8,128)(2,1)S(1)}, u32[]{:S(2)}, u32[]{:S(2)}) %all-to-all-start) | async-done | bytes 524320 | tf_op jit(solution)/shard_map/all_to_all | solution.py:252
  28.6 3.6 %all-to-all-start.1 = ((bf16[8,65,256]{2,1,0:T(8,128)(2,1)}), bf16[8,65,256]{2,1,0:T(8,128)(2,1)S(1)}, u32[]{:S(2)}, u32[]{:S(2)}) async-start(bf16[8,65,256]{2,1,0:T(8,128)(2,1)} %fusion.17), calls=%async_computation.1 | async-start | bytes 589824 | tf_op jit(solution)/shard_map/all_to_all | solution.py:251
  32.2 0.7 or_convert_fusion
  32.9 1.6 collective-permute-start.2
  34.5 7.5 %all-to-all-done.1 = bf16[8,65,256]{2,1,0:T(8,128)(2,1)S(1)} async-done(((bf16[8,65,256]{2,1,0:T(8,128)(2,1)}), bf16[8,65,256]{2,1,0:T(8,128)(2,1)S(1)}, u32[]{:S(2)}, u32[]{:S(2)}) %all-to-all-start.1) | async-done | bytes 266272 | tf_op jit(solution)/shard_map/all_to_all | solution.py:251
  42.0 1.5 collective-permute-start
  43.5 0.8 constant_dynamic-update-slice_fusion.1
  44.3 3.5 %collective-permute-done.2 = bf16[1,8,64,512]{3,2,1,0:T(8,128)(2,1)S(1)} collective-permute-done((bf16[1,8,64,512]{3,2,1,0:T(8,128)(2,1)S(1)}, bf16[1,8,64,512]{3,2,1,0:T(8,128)(2,1)S(1)}, u32[]{:S(2)}, u32[]{:S(2)}) %collective-permute-start.2) | collective-permute-done | bytes 524320 | tf_op jit(solution)/shard_map/ppermute | solution.py:249
  47.8 0.8 constant_dynamic-update-slice_fusion.refs_2_
  48.7 0.0 collective-permute-start.3
  48.7 4.2 %collective-permute-done = bf16[1,8,65,256]{3,2,1,0:T(8,128)(2,1)S(1)} collective-permute-done((bf16[1,8,65,256]{3,2,1,0:T(8,128)(2,1)S(1)}, bf16[1,8,65,256]{3,2,1,0:T(8,128)(2,1)S(1)}, u32[]{:S(2)}, u32[]{:S(2)}) %collective-permute-start) | collective-permute-done | bytes 266272 | tf_op jit(solution)/shard_map/ppermute | solution.py:249
  52.9 0.1 pad_maximum_fusion.refs_0_
  53.0 0.0 copy-start
  53.0 0.1 copy.58
  53.1 0.1 collective-permute-start.1
  53.2 1.9 %collective-permute-done.1 = bf16[2,8,65,256]{3,1,2,0:T(8,128)(2,1)S(1)} collective-permute-done((bf16[2,8,65,256]{3,1,2,0:T(8,128)(2,1)S(1)}, bf16[2,8,65,256]{3,1,2,0:T(8,128)(2,1)S(1)}, u32[]{:S(2)}, u32[]{:S(2)}) %collective-permute-start.1) | collective-permute-done | bytes 532512 | tf_op jit(solution)/shard_map/ppermute | solution.py:260
  55.1 0.7 reshape.188.col_keys
  55.8 0.9 copy.61.refs_1_
  56.7 0.0 collective-permute-done.3.refs_3_
  56.7 0.0 copy-done
  56.7 13.3 %shard_map.55 = (bf16[2048,2048]{1,0:T(8,128)(2,1)}, f32[1,2048]{1,0:T(1,128)}) custom-call(f32[1,2048]{1,0:T(1,128)} %reshape.188.col_keys, bf16[2,8,65,256]{3,2,1,0:T(8,128)(2,1)} %copy-done, bf16[2,8,65,256]{3,2,1,0:T(8,128)(2,1)} %copy.61.refs_1_, bf16[2,8,64,512]{3,2,1,0:T(8,128)(2,1)} %constant_dynamic-update-slice_fusion.refs_2_, ...), custom_call_target="tpu_custom_call" | custom-call | flops 6534725632 | bytes 11534336 | tf_op jit(solution)/shard_map/pallas_call | solution.py:148
  70.1 0.0 copy-start.1
  70.1 12.4 %all_to_all.35 = f32[8,1,256]{2,1,0:T(1,128)S(1)} all-to-all(f32[8,1,256]{2,1,0:T(1,128)} %bitcast.95), channel_id=1, replica_groups=mesh['img'=8,'sub'=4] {'img'}, dimensions={0} | all-to-all | bytes 16384 | tf_op jit(solution)/shard_map/all_to_all | solution.py:268
  82.4 0.6 select_reduce_fusion
  83.1 0.0 copy-done.1
  83.1 0.8 convolution_convert_fusion.1
  83.8 0.1 copy.73
  84.0 10.6 %all_to_all.36 = bf16[8,1,256,64]{2,3,1,0:T(8,128)(2,1)S(1)} all-to-all(bf16[8,1,256,64]{2,3,1,0:T(8,128)(2,1)S(1)} %copy.63), channel_id=1, replica_groups=mesh['img'=8,'sub'=4] {'img'}, dimensions={0} | all-to-all | bytes 524288 | tf_op jit(solution)/shard_map/all_to_all | solution.py:277
  94.6 0.1 copy.64
  94.8 0.1 reshape.189
  94.9 6.0 %convolution_bitcast_fusion.1 = f32[8,1,256,64]{2,3,1,0:T(8,128)S(1)} fusion(bf16[8,256,2048]{2,1,0:T(8,128)(2,1)} %bitcast.68, bf16[2048,64,1]{0,1,2:T(8,128)(2,1)S(1)} %reshape.189), kind=kOutput, calls=%fused_computation.16 | convolution fusion | flops 536870912 | bytes 9175040 | tf_op jit(solution)/shard_map/ajk,akc->ajc/dot_general | solution.py:278
  100.9 17.1 %all_to_all.37 = f32[8,1,256,64]{2,3,1,0:T(8,128)S(1)} all-to-all(f32[8,1,256,64]{2,3,1,0:T(8,128)S(1)} %convolution_bitcast_fusion.1), channel_id=1, replica_groups=mesh['img'=8,'sub'=4] {'img'}, dimensions={0} | all-to-all | bytes 1048576 | tf_op jit(solution)/shard_map/all_to_all | solution.py:281
  118.0 0.8 fusion.6
  118.9 0.8 convolution_convert_fusion
  119.6 0.1 copy.75
  119.7 12.0 %all_to_all.38 = bf16[8,1,256,64]{2,3,1,0:T(8,128)(2,1)S(1)} all-to-all(bf16[8,1,256,64]{2,3,1,0:T(8,128)(2,1)S(1)} %copy.67), channel_id=1, replica_groups=mesh['img'=8,'sub'=4] {'img'}, dimensions={0} | all-to-all | bytes 524288 | tf_op jit(solution)/shard_map/all_to_all | solution.py:277
  131.7 0.1 copy.68
  131.9 0.1 reshape.190
  132.0 6.0 %convolution_bitcast_fusion = f32[8,1,256,64]{2,3,1,0:T(8,128)S(1)} fusion(bf16[8,256,2048]{2,1,0:T(8,128)(2,1)} %bitcast.69, bf16[2048,64,1]{0,1,2:T(8,128)(2,1)S(1)} %reshape.190), kind=kOutput, calls=%fused_computation.15 | convolution fusion | flops 536870912 | bytes 9175040 | tf_op jit(solution)/shard_map/ajk,akc->ajc/dot_general | solution.py:278
  138.0 17.3 %all_to_all.39 = f32[8,1,256,64]{2,3,1,0:T(8,128)S(1)} all-to-all(f32[8,1,256,64]{2,3,1,0:T(8,128)S(1)} %convolution_bitcast_fusion), channel_id=1, replica_groups=mesh['img'=8,'sub'=4] {'img'}, dimensions={0} | all-to-all | bytes 1048576 | tf_op jit(solution)/shard_map/all_to_all | solution.py:281
  155.4 1.5 fusion.7
  (19 shorter events, 0.3 us)
Async XLA Ops:
  4.1 10.0 %copy-start.3 = (s32[4]{0:T(128)S(1)}, s32[4]{0:T(128)}, u32[]{:S(2)}) copy-start(s32[4]{0:T(128)} %constant.10.clone) | copy-start | bytes 52
  4.1 10.2 %copy-start.2 = (s32[512,2]{0,1:T(2,128)S(1)}, s32[512,2]{0,1:T(2,128)}, u32[]{:S(2)}) copy-start(s32[512,2]{0,1:T(2,128)} %param.8) | copy-start | bytes 12292
  6.8 21.8 %all-to-all-start = ((bf16[8,64,512]{2,1,0:T(8,128)(2,1)}), bf16[8,64,512]{2,1,0:T(8,128)(2,1)S(1)}, u32[]{:S(2)}, u32[]{:S(2)}) async-start(bf16[8,64,512]{2,1,0:T(8,128)(2,1)} %slice.36), calls=%async_computation | async-start | bytes 1048576 | tf_op jit(solution)/shard_map/all_to_all | solution.py:252
  28.6 13.4 %all-to-all-start.1 = ((bf16[8,65,256]{2,1,0:T(8,128)(2,1)}), bf16[8,65,256]{2,1,0:T(8,128)(2,1)S(1)}, u32[]{:S(2)}, u32[]{:S(2)}) async-start(bf16[8,65,256]{2,1,0:T(8,128)(2,1)} %fusion.17), calls=%async_computation.1 | async-start | bytes 589824 | tf_op jit(solution)/shard_map/all_to_all | solution.py:251
  32.9 14.9 %collective-permute-start.2 = (bf16[1,8,64,512]{3,2,1,0:T(8,128)(2,1)S(1)}, bf16[1,8,64,512]{3,2,1,0:T(8,128)(2,1)S(1)}, u32[]{:S(2)}, u32[]{:S(2)}) collective-permute-start(bf16[1,8,64,512]{3,2,1,0:T(8,128)(2,1)S(1)} %bitcast.73), channel_id=1, source_target_pairs={{0,2},{1,3},{2,0},{3,1},{4,6},{5,7},{6,4},{7,5},{8,10},{9,11},{10,... | collective-permute-start | bytes 1572872 | tf_op jit(solution)/shard_map/ppermute | solution.py:249
  42.0 10.9 %collective-permute-start = (bf16[1,8,65,256]{3,2,1,0:T(8,128)(2,1)S(1)}, bf16[1,8,65,256]{3,2,1,0:T(8,128)(2,1)S(1)}, u32[]{:S(2)}, u32[]{:S(2)}) collective-permute-start(bf16[1,8,65,256]{3,2,1,0:T(8,128)(2,1)S(1)} %bitcast.70), channel_id=1, source_target_pairs={{0,2},{1,3},{2,0},{3,1},{4,6},{5,7},{6,4},{7,5},{8,10},{9,11},{10,... | collective-permute-start | bytes 798728 | tf_op jit(solution)/shard_map/ppermute | solution.py:249
  48.7 8.0 %collective-permute-start.3 = (bf16[2,8,64,512]{3,2,1,0:T(8,128)(2,1)}, bf16[2,8,64,512]{3,2,1,0:T(8,128)(2,1)}, u32[]{:S(2)}, u32[]{:S(2)}) collective-permute-start(bf16[2,8,64,512]{3,2,1,0:T(8,128)(2,1)} %constant_dynamic-update-slice_fusion.refs_2_), channel_id=1, source_target_pairs={{0,1},{1,0},{2,3},{3,2},{4,5},{5,4},{6,7},{7,6},{8,9},{9,8},{10,11... | collective-permute-start | bytes 3145736 | tf_op jit(solution)/shard_map/ppermute | solution.py:261
  53.0 3.8 %copy-start = (bf16[2,8,65,256]{3,2,1,0:T(8,128)(2,1)}, bf16[2,8,65,256]{3,2,1,0:T(8,128)(2,1)S(1)}, u32[]{:S(2)}) copy-start(bf16[2,8,65,256]{3,2,1,0:T(8,128)(2,1)S(1)} %pad_maximum_fusion.refs_0_) | copy-start | bytes 1597444
  53.1 2.0 %collective-permute-start.1 = (bf16[2,8,65,256]{3,1,2,0:T(8,128)(2,1)S(1)}, bf16[2,8,65,256]{3,1,2,0:T(8,128)(2,1)S(1)}, u32[]{:S(2)}, u32[]{:S(2)}) collective-permute-start(bf16[2,8,65,256]{3,1,2,0:T(8,128)(2,1)S(1)} %copy.58), channel_id=1, source_target_pairs={{0,1},{1,0},{2,3},{3,2},{4,5},{5,4},{6,7},{7,6},{8,9},{9,8},{10,11... | collective-permute-start | bytes 1597448 | tf_op jit(solution)/shard_map/ppermute | solution.py:260
  70.1 13.0 %copy-start.1 = (bf16[512,64]{0,1:T(8,128)(2,1)S(1)}, bf16[512,64]{0,1:T(8,128)(2,1)}, u32[]{:S(2)}) copy-start(bf16[512,64]{0,1:T(8,128)(2,1)} %param.6) | copy-start | bytes 196612

commit v21 on v20

--- a/solution.py
+++ b/solution.py
@@ -250,7 +250,6 @@
 
     low_got = lax.all_to_all(low_payload, "img", split_axis=0, concat_axis=0, tiled=True)[None]
     high_got = lax.all_to_all(high_payload, "img", split_axis=0, concat_axis=0, tiled=True)[None]
-    high_got, pick = lax.optimization_barrier((high_got, pick))
     bit = sub_count // 2
     while bit > 1:
         low_got = exchange_stage(low_got, bit)
@@ -259,6 +258,7 @@
     last = [(t, t ^ bit) for t in range(sub_count)] if bit == 1 else None
     low_pieces = [low_got] + ([lax.ppermute(low_got, "sub", last)] if last else [])
     high_pieces = [high_got] + ([lax.ppermute(high_got, "sub", last)] if last else [])
+    low_pieces[-1], pick = lax.optimization_barrier((low_pieces[-1], pick))
     slot_count = slot_total
     key_rows = jnp.moveaxis(
         jnp.concatenate([piece[:, :, part, :part] for piece in low_pieces], axis=0), 0, 1

time: 158 us -> 157 us (level)
  local copies, waits for them, and re-layouts: 6.67 us -> 4.99 us
where the time goes in v21:
time: 157 us; the launch traced here: 156 us
  blocking collectives  69.2 us (44%)
  waiting for transfers between devices  29.5 us (19%)
  matrix products  17.8 us (11%)
  starting transfers between devices  14 us (9%)
  Pallas kernels  13.3 us (8%)
  other arithmetic  6.9 us (4%)
  local copies, waits for them, and re-layouts  4.99 us (3%)
    all_to_all x2, blocking collectives, on_device(): lax.all_to_all(bucket_major(product), 'img', split_axis=0, concat_axis=0,...  34.2 us
    all_to_all x2, blocking collectives, on_device(): lax.all_to_all(to_bucket(scaled), 'img', split_axis=0, concat_axis=0, til...  22.6 us
    pallas_call x1, Pallas kernels, pieces_affinity(): pl.pallas_call(functools.partial(pieces_kernel, len(low_pieces), len(high...  13.3 us
    all_to_all x1, waiting for transfers between devices, on_device(): lax.all_to_all(high_payload, 'img', split_axis=0, concat_axis=0, tiled=True)  12.9 us
    all_to_all x1, blocking collectives, on_device(): lax.all_to_all(bucket_major(row_sums), 'img', split_axis=0, concat_axis=0...  12.4 us
    dot_general x2, matrix products, on_device(): jnp.einsum('ajk,akc->ajc', weights, list_major(arrived), preferred_elemen...  12.1 us
    all_to_all x1, waiting for transfers between devices, on_device(): lax.all_to_all(low_payload, 'img', split_axis=0, concat_axis=0, tiled=True)  8.1 us
    ppermute x2, waiting for transfers between devices, exchange_stage(): return jnp.concatenate([got, lax.ppermute(got, 'sub', pairs)], axis=0)  7.43 us
  transfers between devices with their start and end apart: 6, of which 5 were waited for; matrix products, arithmetic and copies ran while one was open for 4% of the time, Pallas kernels for 0%

profile of v21, /device:TPU:0, one launch (start us, length us, event | category | flops | bytes accessed | tf_op | source)
XLA Modules:
  0.0 156.0 jit_solution(14875436034810901928)
XLA Ops:
  0.0 1.4 fusion.1
  1.4 0.1 iota_add_fusion.1
  1.4 0.1 add.101
  1.5 0.8 copy.56
  2.4 0.2 eq.32
  2.5 0.5 convert_reduce_fusion
  3.1 0.2 reduce_sum.39
  3.3 0.1 copy.57
  3.4 0.7 multiply_add_fusion
  4.1 0.0 copy-start.2
  4.1 1.9 %convolution_convert_fusion.2 = bf16[512,768]{1,0:T(8,128)(2,1)S(1)} fusion(bf16[512,768]{1,0:T(8,128)(2,1)} %param.5, f32[512]{0:T(512)S(1)} %add_rsqrt_fusion, s32[512]{0:T(512)S(1)} %bitcast.88, s32[512]{0:T(512)S(1)} %bitcast.84, s32[512]{0:T(512)S(1)} %add.101), kind=kOutput, calls=%fused_computation.11 | convolution fusion | flops 405012480 | bytes 1581056 | tf_op jit(solution)/shard_map/dot_general | solution.py:235
  6.0 0.0 copy-start.3
  6.0 0.8 slice.42
  6.8 7.3 %all-to-all-start.1 = ((bf16[8,64,512]{2,1,0:T(8,128)(2,1)}), bf16[8,64,512]{2,1,0:T(8,128)(2,1)S(1)}, u32[]{:S(2)}, u32[]{:S(2)}) async-start(bf16[8,64,512]{2,1,0:T(8,128)(2,1)} %slice.42), calls=%async_computation.1 | async-start | bytes 1048576 | tf_op jit(solution)/shard_map/all_to_all | solution.py:252
  14.1 0.0 copy-done.2
  14.2 0.4 fusion.10
  14.6 0.3 fusion.9
  14.9 0.1 convert_element_type.89
  15.0 0.7 fusion.17
  15.7 12.9 %all-to-all-done.1 = bf16[8,64,512]{2,1,0:T(8,128)(2,1)S(1)} async-done(((bf16[8,64,512]{2,1,0:T(8,128)(2,1)}), bf16[8,64,512]{2,1,0:T(8,128)(2,1)S(1)}, u32[]{:S(2)}, u32[]{:S(2)}) %all-to-all-start.1) | async-done | bytes 524320 | tf_op jit(solution)/shard_map/all_to_all | solution.py:252
  28.6 3.6 %all-to-all-start = ((bf16[8,65,256]{2,1,0:T(8,128)(2,1)}), bf16[8,65,256]{2,1,0:T(8,128)(2,1)S(1)}, u32[]{:S(2)}, u32[]{:S(2)}) async-start(bf16[8,65,256]{2,1,0:T(8,128)(2,1)} %fusion.17), calls=%async_computation | async-start | bytes 589824 | tf_op jit(solution)/shard_map/all_to_all | solution.py:251
  32.2 0.0 copy-done.3
  32.3 1.6 collective-permute-start.2
  33.8 0.1 broadcast_add_fusion
  33.9 8.1 %all-to-all-done = bf16[8,65,256]{2,1,0:T(8,128)(2,1)S(1)} async-done(((bf16[8,65,256]{2,1,0:T(8,128)(2,1)}), bf16[8,65,256]{2,1,0:T(8,128)(2,1)S(1)}, u32[]{:S(2)}, u32[]{:S(2)}) %all-to-all-start) | async-done | bytes 266272 | tf_op jit(solution)/shard_map/all_to_all | solution.py:251
  42.0 1.5 collective-permute-start
  43.5 0.1 iota_add_fusion
  43.6 0.1 add.111
  43.6 3.5 %collective-permute-done.2 = bf16[1,8,64,512]{3,2,1,0:T(8,128)(2,1)S(1)} collective-permute-done((bf16[1,8,64,512]{3,2,1,0:T(8,128)(2,1)S(1)}, bf16[1,8,64,512]{3,2,1,0:T(8,128)(2,1)S(1)}, u32[]{:S(2)}, u32[]{:S(2)}) %collective-permute-start.2) | collective-permute-done | bytes 524320 | tf_op jit(solution)/shard_map/ppermute | solution.py:249
  47.1 1.1 pad_maximum_fusion.refs_2_
  48.3 0.0 collective-permute-start.3
  48.3 3.9 %collective-permute-done = bf16[1,8,65,256]{3,2,1,0:T(8,128)(2,1)S(1)} collective-permute-done((bf16[1,8,65,256]{3,2,1,0:T(8,128)(2,1)S(1)}, bf16[1,8,65,256]{3,2,1,0:T(8,128)(2,1)S(1)}, u32[]{:S(2)}, u32[]{:S(2)}) %collective-permute-start) | collective-permute-done | bytes 266272 | tf_op jit(solution)/shard_map/ppermute | solution.py:249
  52.2 0.1 pad_maximum_fusion.1.refs_0_
  52.3 0.0 copy-start
  52.3 0.1 copy.59
  52.4 0.1 collective-permute-start.1
  52.5 0.7 or_convert_fusion
  53.2 1.1 collective-permute-done.1
  54.4 0.9 copy.62.refs_1_
  55.3 0.0 copy-done
  55.3 0.7 reshape.188.col_keys
  56.0 0.0 collective-permute-done.3.refs_3_
  56.0 13.3 %shard_map.55 = (bf16[2048,2048]{1,0:T(8,128)(2,1)}, f32[1,2048]{1,0:T(1,128)}) custom-call(f32[1,2048]{1,0:T(1,128)} %reshape.188.col_keys, bf16[2,8,65,256]{3,2,1,0:T(8,128)(2,1)} %copy-done, bf16[2,8,65,256]{3,2,1,0:T(8,128)(2,1)} %copy.62.refs_1_, bf16[2,8,64,512]{3,2,1,0:T(8,128)(2,1)} %pad_maximum_fusion.refs_2_, ...), custom_call_target="tpu_custom_call" | custom-call | flops 6534725632 | bytes 11534336 | tf_op jit(solution)/shard_map/pallas_call | solution.py:148
  69.3 0.0 copy-start.1
  69.3 12.4 %all_to_all.35 = f32[8,1,256]{2,1,0:T(1,128)S(1)} all-to-all(f32[8,1,256]{2,1,0:T(1,128)} %bitcast.93), channel_id=1, replica_groups=mesh['img'=8,'sub'=4] {'img'}, dimensions={0} | all-to-all | bytes 16384 | tf_op jit(solution)/shard_map/all_to_all | solution.py:268
  81.7 0.6 select_reduce_fusion
  82.4 0.0 copy-done.1
  82.4 0.8 convolution_convert_fusion.1
  83.1 0.1 copy.73
  83.3 10.6 %all_to_all.36 = bf16[8,1,256,64]{2,3,1,0:T(8,128)(2,1)S(1)} all-to-all(bf16[8,1,256,64]{2,3,1,0:T(8,128)(2,1)S(1)} %copy.64), channel_id=1, replica_groups=mesh['img'=8,'sub'=4] {'img'}, dimensions={0} | all-to-all | bytes 524288 | tf_op jit(solution)/shard_map/all_to_all | solution.py:277
  93.9 0.1 copy.65
  94.0 0.1 reshape.189
  94.2 6.0 %convolution_bitcast_fusion.1 = f32[8,1,256,64]{2,3,1,0:T(8,128)S(1)} fusion(bf16[8,256,2048]{2,1,0:T(8,128)(2,1)} %bitcast.66, bf16[2048,64,1]{0,1,2:T(8,128)(2,1)S(1)} %reshape.189), kind=kOutput, calls=%fused_computation.16 | convolution fusion | flops 536870912 | bytes 9175040 | tf_op jit(solution)/shard_map/ajk,akc->ajc/dot_general | solution.py:278
  100.2 17.0 %all_to_all.37 = f32[8,1,256,64]{2,3,1,0:T(8,128)S(1)} all-to-all(f32[8,1,256,64]{2,3,1,0:T(8,128)S(1)} %convolution_bitcast_fusion.1), channel_id=1, replica_groups=mesh['img'=8,'sub'=4] {'img'}, dimensions={0} | all-to-all | bytes 1048576 | tf_op jit(solution)/shard_map/all_to_all | solution.py:281
  117.2 0.8 fusion.6
  118.1 0.8 convolution_convert_fusion
  118.8 0.1 copy.75
  118.9 12.0 %all_to_all.38 = bf16[8,1,256,64]{2,3,1,0:T(8,128)(2,1)S(1)} all-to-all(bf16[8,1,256,64]{2,3,1,0:T(8,128)(2,1)S(1)} %copy.68), channel_id=1, replica_groups=mesh['img'=8,'sub'=4] {'img'}, dimensions={0} | all-to-all | bytes 524288 | tf_op jit(solution)/shard_map/all_to_all | solution.py:277
  130.9 0.1 copy.69
  131.0 0.1 reshape.190
  131.2 6.0 %convolution_bitcast_fusion = f32[8,1,256,64]{2,3,1,0:T(8,128)S(1)} fusion(bf16[8,256,2048]{2,1,0:T(8,128)(2,1)} %bitcast.67, bf16[2048,64,1]{0,1,2:T(8,128)(2,1)S(1)} %reshape.190), kind=kOutput, calls=%fused_computation.15 | convolution fusion | flops 536870912 | bytes 9175040 | tf_op jit(solution)/shard_map/ajk,akc->ajc/dot_general | solution.py:278
  137.2 17.3 %all_to_all.39 = f32[8,1,256,64]{2,3,1,0:T(8,128)S(1)} all-to-all(f32[8,1,256,64]{2,3,1,0:T(8,128)S(1)} %convolution_bitcast_fusion), channel_id=1, replica_groups=mesh['img'=8,'sub'=4] {'img'}, dimensions={0} | all-to-all | bytes 1048576 | tf_op jit(solution)/shard_map/all_to_all | solution.py:281
  154.5 1.5 fusion.7
  (19 shorter events, 0.3 us)
Async XLA Ops:
  4.1 10.0 %copy-start.2 = (s32[512,2]{0,1:T(2,128)S(1)}, s32[512,2]{0,1:T(2,128)}, u32[]{:S(2)}) copy-start(s32[512,2]{0,1:T(2,128)} %param.8) | copy-start | bytes 12292
  6.0 26.2 %copy-start.3 = (s32[4]{0:T(128)S(1)}, s32[4]{0:T(128)}, u32[]{:S(2)}) copy-start(s32[4]{0:T(128)} %constant.10.clone) | copy-start | bytes 52
  6.8 21.8 %all-to-all-start.1 = ((bf16[8,64,512]{2,1,0:T(8,128)(2,1)}), bf16[8,64,512]{2,1,0:T(8,128)(2,1)S(1)}, u32[]{:S(2)}, u32[]{:S(2)}) async-start(bf16[8,64,512]{2,1,0:T(8,128)(2,1)} %slice.42), calls=%async_computation.1 | async-start | bytes 1048576 | tf_op jit(solution)/shard_map/all_to_all | solution.py:252
  28.6 13.4 %all-to-all-start = ((bf16[8,65,256]{2,1,0:T(8,128)(2,1)}), bf16[8,65,256]{2,1,0:T(8,128)(2,1)S(1)}, u32[]{:S(2)}, u32[]{:S(2)}) async-start(bf16[8,65,256]{2,1,0:T(8,128)(2,1)} %fusion.17), calls=%async_computation | async-start | bytes 589824 | tf_op jit(solution)/shard_map/all_to_all | solution.py:251
  32.3 14.9 %collective-permute-start.2 = (bf16[1,8,64,512]{3,2,1,0:T(8,128)(2,1)S(1)}, bf16[1,8,64,512]{3,2,1,0:T(8,128)(2,1)S(1)}, u32[]{:S(2)}, u32[]{:S(2)}) collective-permute-start(bf16[1,8,64,512]{3,2,1,0:T(8,128)(2,1)S(1)} %bitcast.73), channel_id=1, source_target_pairs={{0,2},{1,3},{2,0},{3,1},{4,6},{5,7},{6,4},{7,5},{8,10},{9,11},{10,... | collective-permute-start | bytes 1572872 | tf_op jit(solution)/shard_map/ppermute | solution.py:249
  42.0 10.2 %collective-permute-start = (bf16[1,8,65,256]{3,2,1,0:T(8,128)(2,1)S(1)}, bf16[1,8,65,256]{3,2,1,0:T(8,128)(2,1)S(1)}, u32[]{:S(2)}, u32[]{:S(2)}) collective-permute-start(bf16[1,8,65,256]{3,2,1,0:T(8,128)(2,1)S(1)} %bitcast.68), channel_id=1, source_target_pairs={{0,2},{1,3},{2,0},{3,1},{4,6},{5,7},{6,4},{7,5},{8,10},{9,11},{10,... | collective-permute-start | bytes 798728 | tf_op jit(solution)/shard_map/ppermute | solution.py:249
  48.3 7.7 %collective-permute-start.3 = (bf16[2,8,64,512]{3,2,1,0:T(8,128)(2,1)}, bf16[2,8,64,512]{3,2,1,0:T(8,128)(2,1)}, u32[]{:S(2)}, u32[]{:S(2)}) collective-permute-start(bf16[2,8,64,512]{3,2,1,0:T(8,128)(2,1)} %pad_maximum_fusion.refs_2_), channel_id=1, source_target_pairs={{0,1},{1,0},{2,3},{3,2},{4,5},{5,4},{6,7},{7,6},{8,9},{9,8},{10,11... | collective-permute-start | bytes 3145736 | tf_op jit(solution)/shard_map/ppermute | solution.py:260
  52.3 3.0 %copy-start = (bf16[2,8,65,256]{3,2,1,0:T(8,128)(2,1)}, bf16[2,8,65,256]{3,2,1,0:T(8,128)(2,1)S(1)}, u32[]{:S(2)}) copy-start(bf16[2,8,65,256]{3,2,1,0:T(8,128)(2,1)S(1)} %pad_maximum_fusion.1.refs_0_) | copy-start | bytes 1597444
  52.4 2.0 %collective-permute-start.1 = (bf16[2,8,65,256]{3,1,2,0:T(8,128)(2,1)S(1)}, bf16[2,8,65,256]{3,1,2,0:T(8,128)(2,1)S(1)}, u32[]{:S(2)}, u32[]{:S(2)}) collective-permute-start(bf16[2,8,65,256]{3,1,2,0:T(8,128)(2,1)S(1)} %copy.59), channel_id=1, source_target_pairs={{0,1},{1,0},{2,3},{3,2},{4,5},{5,4},{6,7},{7,6},{8,9},{9,8},{10,11... | collective-permute-start | bytes 1597448 | tf_op jit(solution)/shard_map/ppermute | solution.py:259
  69.3 13.0 %copy-start.1 = (bf16[512,64]{0,1:T(8,128)(2,1)S(1)}, bf16[512,64]{0,1:T(8,128)(2,1)}, u32[]{:S(2)}) copy-start(bf16[512,64]{0,1:T(8,128)(2,1)} %param.6) | copy-start | bytes 196612

commit v22 on v16

--- a/solution.py
+++ b/solution.py
@@ -233,7 +233,7 @@
     mine_keys = jnp.where(jnp.any(mine_hit, axis=1), key_sum, -4096.0).astype(jnp.bfloat16)
     width = unit.shape[1]
     quarter = jnp.dot(mine_hit.astype(jnp.bfloat16), unit, preferred_element_type=jnp.float32)
-    half = max(128, width // 3 // 128 * 128)
+    half = max(128, width // 6 // 128 * 128)
     quarter = quarter.astype(jnp.bfloat16).reshape(img_count, part, width)
     low_payload = jnp.concatenate(
         [

time: 156 us -> 168 us (1.077)
  blocking collectives: 70.6 us -> 94.5 us
  starting transfers between devices: 14.1 us -> 6.39 us
  waiting for transfers between devices: 27.7 us -> 24 us
    all_to_all x0 -> x1, blocking collectives: none -> 24.8 us  [on_device(): lax.all_to_all(high_payload, 'img', split_axis=0, concat_axis=0, tiled=True)]
    all_to_all x1 -> x0, waiting for transfers between devices: 13.6 us -> none  [on_device(): lax.all_to_all(high_payload, 'img', split_axis=0, concat_axis=0, tiled=True)]
    ppermute x2, waiting for transfers between devices: 5.99 us -> 16.3 us  [exchange_stage(): return jnp.concatenate([got, lax.ppermute(got, 'sub', pairs)], axis=0)]
    all_to_all x1 -> x0, starting transfers between devices: 7.28 us -> none  [on_device(): lax.all_to_all(high_payload, 'img', split_axis=0, concat_axis=0, tiled=True)]
  transfers between devices with their start and end apart: 6 -> 5, of which waited for: 4 -> 4; matrix products, arithmetic and copies ran while one was open for 2% -> 1% of each run, Pallas kernels for 0% -> 0%
where the time goes in v22:
time: 168 us; the launch traced here: 167 us
  blocking collectives  94.5 us (56%)
  waiting for transfers between devices  24 us (14%)
  matrix products  19.8 us (12%)
  Pallas kernels  13.6 us (8%)
  starting transfers between devices  6.39 us (4%)
  other arithmetic  4.48 us (3%)
  local copies, waits for them, and re-layouts  4.31 us (3%)
    all_to_all x2, blocking collectives, on_device(): lax.all_to_all(bucket_major(product), 'img', split_axis=0, concat_axis=0,...  34.5 us
    all_to_all x1, blocking collectives, on_device(): lax.all_to_all(high_payload, 'img', split_axis=0, concat_axis=0, tiled=True)  24.8 us
    all_to_all x2, blocking collectives, on_device(): lax.all_to_all(to_bucket(scaled), 'img', split_axis=0, concat_axis=0, til...  22.9 us
    ppermute x2, waiting for transfers between devices, exchange_stage(): return jnp.concatenate([got, lax.ppermute(got, 'sub', pairs)], axis=0)  16.3 us
    pallas_call x1, Pallas kernels, pieces_affinity(): pl.pallas_call(functools.partial(pieces_kernel, len(low_pieces), len(high...  13.6 us
    all_to_all x1, blocking collectives, on_device(): lax.all_to_all(low_payload, 'img', split_axis=0, concat_axis=0, tiled=True)  12.3 us
    dot_general x2, matrix products, on_device(): jnp.einsum('ajk,akc->ajc', weights, list_major(arrived), preferred_elemen...  12.1 us
    all_to_all x1, waiting for transfers between devices, on_device(): lax.all_to_all(bucket_major(row_sums), 'img', split_axis=0, concat_axis=0...  6.29 us
  transfers between devices with their start and end apart: 5, of which 4 were waited for; matrix products, arithmetic and copies ran while one was open for 1% of the time, Pallas kernels for 0%

profile of v22, /device:TPU:0, one launch (start us, length us, event | category | flops | bytes accessed | tf_op | source)
XLA Modules:
  0.0 167.5 jit_solution(3261861016330516848)
XLA Ops:
  0.0 0.0 copy-start.2
  0.0 0.8 copy.49
  0.8 0.2 eq.32
  1.0 0.5 convert_reduce_fusion
  1.5 0.2 reduce_sum.39
  1.8 0.1 copy.50
  1.9 0.7 multiply_add_fusion
  2.6 0.1 iota_add_fusion.1
  2.7 0.1 add.108
  2.7 1.4 fusion.1
  4.1 0.0 copy-start.6
  4.1 1.9 %convolution_convert_fusion.2 = bf16[512,768]{1,0:T(8,128)(2,1)S(1)} fusion(bf16[512,768]{1,0:T(8,128)(2,1)} %param.5, f32[512]{0:T(512)S(1)} %add_rsqrt_fusion, s32[512]{0:T(512)S(1)} %bitcast.89, s32[512]{0:T(512)S(1)} %bitcast.81, s32[512]{0:T(512)S(1)} %add.108), kind=kOutput, calls=%fused_computation.11 | convolution fusion | flops 405012480 | bytes 1581056 | tf_op jit(solution)/shard_map/dot_general | solution.py:235
  6.0 0.1 slice.42
  6.1 24.8 %all_to_all.35 = bf16[8,64,640]{2,1,0:T(8,128)(2,1)S(1)} all-to-all(bf16[8,64,640]{2,1,0:T(8,128)(2,1)S(1)} %slice.42), channel_id=1, replica_groups=mesh['img'=8,'sub'=4] {'img'}, dimensions={0} | all-to-all | bytes 1310720 | tf_op jit(solution)/shard_map/all_to_all | solution.py:252
  30.9 1.5 collective-permute-start.2
  32.4 0.0 copy-done.2
  32.4 0.4 fusion.10
  32.8 0.3 fusion.9
  33.1 12.6 %collective-permute-done.2 = bf16[1,8,64,640]{3,2,1,0:T(8,128)(2,1)S(1)} collective-permute-done((bf16[1,8,64,640]{3,2,1,0:T(8,128)(2,1)S(1)}, bf16[1,8,64,640]{3,2,1,0:T(8,128)(2,1)S(1)}, u32[]{:S(2)}, u32[]{:S(2)}) %collective-permute-start.2) | collective-permute-done | bytes 655392 | tf_op jit(solution)/shard_map/ppermute | solution.py:249
  45.8 0.1 pad_maximum_fusion.refs_2_
  45.9 0.0 copy-start
  45.9 0.1 collective-permute-start.3
  46.0 0.1 convert_element_type.86
  46.1 12.3 %all_to_all.36 = bf16[8,65,128]{2,1,0:T(8,128)(2,1)S(1)} all-to-all(bf16[8,65,128]{2,1,0:T(8,128)(2,1)S(1)} %fusion.17), channel_id=1, replica_groups=mesh['img'=8,'sub'=4] {'img'}, dimensions={0} | all-to-all | bytes 266240 | tf_op jit(solution)/shard_map/all_to_all | solution.py:251
  58.4 1.5 collective-permute-start
  59.9 0.0 copy-done.6
  60.0 3.6 %collective-permute-done = bf16[1,8,65,128]{3,2,1,0:T(8,128)(2,1)S(1)} collective-permute-done((bf16[1,8,65,128]{3,2,1,0:T(8,128)(2,1)S(1)}, bf16[1,8,65,128]{3,2,1,0:T(8,128)(2,1)S(1)}, u32[]{:S(2)}, u32[]{:S(2)}) %collective-permute-start) | collective-permute-done | bytes 133152 | tf_op jit(solution)/shard_map/ppermute | solution.py:249
  63.6 0.0 copy-start.1
  63.6 0.1 collective-permute-start.1
  63.7 0.1 broadcast_add_fusion
  63.8 1.5 collective-permute-done.1.refs_1_
  65.3 0.0 copy-start.3
  65.3 0.7 reshape.188.col_keys
  66.0 0.0 copy-start.5
  66.0 0.0 collective-permute-done.3.refs_3_
  66.0 0.0 copy-done
  66.0 0.0 copy-done.1
  66.0 0.0 copy-done.3
  66.0 0.0 copy-start.4
  66.1 1.1 copy-done.4
  67.1 13.6 %shard_map.55 = (bf16[2048,2048]{1,0:T(8,128)(2,1)}, f32[1,2048]{1,0:T(1,128)}) custom-call(f32[1,2048]{1,0:T(1,128)} %reshape.188.col_keys, bf16[2,8,65,128]{3,2,1,0:T(8,128)(2,1)} %copy-done.1, bf16[2,8,65,128]{3,2,1,0:T(8,128)(2,1)} %copy-done.3, bf16[2,8,64,640]{3,2,1,0:T(8,128)(2,1)} %copy-done, bf16[2,8,64,640]{3,2,1,0:T(8,128)(2,1)} %copy-done.4), custom_call_target="tpu_custom_call" | custom-call | flops 6534725632 | bytes 11534336 | tf_op jit(solution)/shard_map/pallas_call | solution.py:148
  80.8 3.3 %all-to-all-start.2 = ((f32[8,1,256]{2,1,0:T(1,128)}), f32[8,1,256]{2,1,0:T(1,128)S(1)}, u32[]{:S(2)}, u32[]{:S(2)}) async-start(f32[8,1,256]{2,1,0:T(1,128)} %bitcast.99), calls=%async_computation.2 | async-start | bytes 16384 | tf_op jit(solution)/shard_map/all_to_all | solution.py:267
  84.1 0.1 iota_add_fusion
  84.1 0.1 add.102
  84.2 6.3 %all-to-all-done.2 = f32[8,1,256]{2,1,0:T(1,128)S(1)} async-done(((f32[8,1,256]{2,1,0:T(1,128)}), f32[8,1,256]{2,1,0:T(1,128)S(1)}, u32[]{:S(2)}, u32[]{:S(2)}) %all-to-all-start.2) | async-done | bytes 8224 | tf_op jit(solution)/shard_map/all_to_all | solution.py:267
  90.5 0.7 select_reduce_fusion
  91.2 0.0 copy-done.5
  91.2 1.3 convolution_convert_fusion.1
  92.5 0.1 copy.64
  92.6 10.9 %all_to_all.37 = bf16[8,1,256,64]{2,3,1,0:T(8,128)(2,1)S(1)} all-to-all(bf16[8,1,256,64]{2,3,1,0:T(8,128)(2,1)S(1)} %copy.54), channel_id=1, replica_groups=mesh['img'=8,'sub'=4] {'img'}, dimensions={0} | all-to-all | bytes 524288 | tf_op jit(solution)/shard_map/all_to_all | solution.py:276
  103.6 0.1 copy.55
  103.7 0.1 reshape.189
  103.8 6.0 %convolution_bitcast_fusion.1 = f32[8,1,256,64]{2,3,1,0:T(8,128)S(1)} fusion(bf16[8,256,2048]{2,1,0:T(8,128)(2,1)} %bitcast.63, bf16[2048,64,1]{0,1,2:T(8,128)(2,1)S(1)} %reshape.189), kind=kOutput, calls=%fused_computation.17 | convolution fusion | flops 536870912 | bytes 9175040 | tf_op jit(solution)/shard_map/ajk,akc->ajc/dot_general | solution.py:277
  109.9 17.2 %all_to_all.38 = f32[8,1,256,64]{2,3,1,0:T(8,128)S(1)} all-to-all(f32[8,1,256,64]{2,3,1,0:T(8,128)S(1)} %convolution_bitcast_fusion.1), channel_id=1, replica_groups=mesh['img'=8,'sub'=4] {'img'}, dimensions={0} | all-to-all | bytes 1048576 | tf_op jit(solution)/shard_map/all_to_all | solution.py:280
  127.1 1.3 fusion.6
  128.5 1.3 convolution_convert_fusion
  129.8 0.1 copy.66
  129.9 12.0 %all_to_all.39 = bf16[8,1,256,64]{2,3,1,0:T(8,128)(2,1)S(1)} all-to-all(bf16[8,1,256,64]{2,3,1,0:T(8,128)(2,1)S(1)} %copy.58), channel_id=1, replica_groups=mesh['img'=8,'sub'=4] {'img'}, dimensions={0} | all-to-all | bytes 524288 | tf_op jit(solution)/shard_map/all_to_all | solution.py:276
  141.8 0.1 copy.59
  142.0 0.1 reshape.190
  142.1 6.0 %convolution_bitcast_fusion = f32[8,1,256,64]{2,3,1,0:T(8,128)S(1)} fusion(bf16[8,256,2048]{2,1,0:T(8,128)(2,1)} %bitcast.64, bf16[2048,64,1]{0,1,2:T(8,128)(2,1)S(1)} %reshape.190), kind=kOutput, calls=%fused_computation.16 | convolution fusion | flops 536870912 | bytes 9175040 | tf_op jit(solution)/shard_map/ajk,akc->ajc/dot_general | solution.py:277
  148.2 17.3 %all_to_all.40 = f32[8,1,256,64]{2,3,1,0:T(8,128)S(1)} all-to-all(f32[8,1,256,64]{2,3,1,0:T(8,128)S(1)} %convolution_bitcast_fusion), channel_id=1, replica_groups=mesh['img'=8,'sub'=4] {'img'}, dimensions={0} | all-to-all | bytes 1048576 | tf_op jit(solution)/shard_map/all_to_all | solution.py:280
  165.5 2.0 %fusion.7 = bf16[512,64]{0,1:T(8,128)(2,1)} fusion(f32[2048,64]{0,1:T(8,128)S(1)} %bitcast.76, bf16[512,64]{0,1:T(8,128)(2,1)S(1)} %copy-done.5, f32[512]{0:T(512)S(1)} %get-tuple-element.13, s32[512]{0:T(512)S(1)} %bitcast.96, s32[512]{0:T(512)S(1)} %bitcast.88, s32[2048]{0:T(1024)S(1)} %add.102), kind=kOutput, calls=%fused_computation.24 | convolution fusion | flops 405962752 | bytes 669696 | tf_op jit(solution)/shard_map/kg,kc->gc/dot_general | solution.py:211
  (22 shorter events, 0.3 us)
Async XLA Ops:
  0.0 32.4 %copy-start.2 = (s32[512,2]{0,1:T(2,128)S(1)}, s32[512,2]{0,1:T(2,128)}, u32[]{:S(2)}) copy-start(s32[512,2]{0,1:T(2,128)} %param.8) | copy-start | bytes 12292
  4.1 55.8 %copy-start.6 = (s32[4]{0:T(128)S(1)}, s32[4]{0:T(128)}, u32[]{:S(2)}) copy-start(s32[4]{0:T(128)} %constant.11.clone) | copy-start | bytes 52
  30.9 14.9 %collective-permute-start.2 = (bf16[1,8,64,640]{3,2,1,0:T(8,128)(2,1)S(1)}, bf16[1,8,64,640]{3,2,1,0:T(8,128)(2,1)S(1)}, u32[]{:S(2)}, u32[]{:S(2)}) collective-permute-start(bf16[1,8,64,640]{3,2,1,0:T(8,128)(2,1)S(1)} %bitcast.65), channel_id=1, source_target_pairs={{0,2},{1,3},{2,0},{3,1},{4,6},{5,7},{6,4},{7,5},{8,10},{9,11},{10,... | collective-permute-start | bytes 1966088 | tf_op jit(solution)/shard_map/ppermute | solution.py:249
  45.9 20.1 %copy-start = (bf16[2,8,64,640]{3,2,1,0:T(8,128)(2,1)}, bf16[2,8,64,640]{3,2,1,0:T(8,128)(2,1)S(1)}, u32[]{:S(2)}) copy-start(bf16[2,8,64,640]{3,2,1,0:T(8,128)(2,1)S(1)} %pad_maximum_fusion.refs_2_) | copy-start | bytes 3932164
  45.9 20.1 %collective-permute-start.3 = (bf16[2,8,64,640]{3,2,1,0:T(8,128)(2,1)S(1)}, bf16[2,8,64,640]{3,2,1,0:T(8,128)(2,1)S(1)}, u32[]{:S(2)}, u32[]{:S(2)}) collective-permute-start(bf16[2,8,64,640]{3,2,1,0:T(8,128)(2,1)S(1)} %pad_maximum_fusion.refs_2_), channel_id=1, source_target_pairs={{0,1},{1,0},{2,3},{3,2},{4,5},{5,4},{6,7},{7,6},{8,9},{9,8},{10,11... | collective-permute-start | bytes 3932168 | tf_op jit(solution)/shard_map/ppermute | solution.py:260
  58.4 5.1 %collective-permute-start = (bf16[1,8,65,128]{3,2,1,0:T(8,128)(2,1)S(1)}, bf16[1,8,65,128]{3,2,1,0:T(8,128)(2,1)S(1)}, u32[]{:S(2)}, u32[]{:S(2)}) collective-permute-start(bf16[1,8,65,128]{3,2,1,0:T(8,128)(2,1)S(1)} %bitcast.69), channel_id=1, source_target_pairs={{0,2},{1,3},{2,0},{3,1},{4,6},{5,7},{6,4},{7,5},{8,10},{9,11},{10,... | collective-permute-start | bytes 399368 | tf_op jit(solution)/shard_map/ppermute | solution.py:249
  63.6 2.4 %copy-start.1 = (bf16[2,8,65,128]{3,2,1,0:T(8,128)(2,1)}, bf16[2,8,65,128]{3,2,1,0:T(8,128)(2,1)S(1)}, u32[]{:S(2)}) copy-start(bf16[2,8,65,128]{3,2,1,0:T(8,128)(2,1)S(1)} %pad_maximum_fusion.1.refs_0_) | copy-start | bytes 798724
  63.6 1.6 collective-permute-start.1
  65.3 0.8 copy-start.3
  66.0 25.2 %copy-start.5 = (bf16[512,64]{0,1:T(8,128)(2,1)S(1)}, bf16[512,64]{0,1:T(8,128)(2,1)}, u32[]{:S(2)}) copy-start(bf16[512,64]{0,1:T(8,128)(2,1)} %param.6) | copy-start | bytes 196612
  66.0 1.1 copy-start.4
  80.8 9.7 %all-to-all-start.2 = ((f32[8,1,256]{2,1,0:T(1,128)}), f32[8,1,256]{2,1,0:T(1,128)S(1)}, u32[]{:S(2)}, u32[]{:S(2)}) async-start(f32[8,1,256]{2,1,0:T(1,128)} %bitcast.99), calls=%async_computation.2 | async-start | bytes 16384 | tf_op jit(solution)/shard_map/all_to_all | solution.py:267

commit v23 on v22

--- a/solution.py
+++ b/solution.py
@@ -233,7 +233,7 @@
     mine_keys = jnp.where(jnp.any(mine_hit, axis=1), key_sum, -4096.0).astype(jnp.bfloat16)
     width = unit.shape[1]
     quarter = jnp.dot(mine_hit.astype(jnp.bfloat16), unit, preferred_element_type=jnp.float32)
-    half = max(128, width // 6 // 128 * 128)
+    half = max(128, width // 2 // 128 * 128)
     quarter = quarter.astype(jnp.bfloat16).reshape(img_count, part, width)
     low_payload = jnp.concatenate(
         [

time: 168 us -> 159 us (0.946)
  blocking collectives: 94.5 us -> 76.9 us
  starting transfers between devices: 6.39 us -> 12.3 us
  local copies, waits for them, and re-layouts: 4.31 us -> 6.03 us
    all_to_all x1 -> x0, blocking collectives: 24.8 us -> none  [on_device(): lax.all_to_all(high_payload, 'img', split_axis=0, concat_axis=0, tiled=True)]
    all_to_all x0 -> x1, waiting for transfers between devices: none -> 9.89 us  [on_device(): lax.all_to_all(high_payload, 'img', split_axis=0, concat_axis=0, tiled=True)]
    ppermute x2, waiting for transfers between devices: 16.3 us -> 6.53 us  [exchange_stage(): return jnp.concatenate([got, lax.ppermute(got, 'sub', pairs)], axis=0)]
    all_to_all x1, blocking collectives: 12.3 us -> 20 us  [on_device(): lax.all_to_all(low_payload, 'img', split_axis=0, concat_axis=0, tiled=True)]
    all_to_all x0 -> x1, starting transfers between devices: none -> 3.45 us  [on_device(): lax.all_to_all(high_payload, 'img', split_axis=0, concat_axis=0, tiled=True)]
    all_to_all x1, starting transfers between devices: 3.27 us -> 5.72 us  [on_device(): lax.all_to_all(bucket_major(row_sums), 'img', split_axis=0, concat_axis=0...]
  transfers between devices with their start and end apart: 5 -> 6, of which waited for: 4 -> 4; matrix products, arithmetic and copies ran while one was open for 1% -> 2% of each run, Pallas kernels for 0% -> 0%
where the time goes in v23:
time: 159 us; the launch traced here: 158 us
  blocking collectives  76.9 us (48%)
  waiting for transfers between devices  23.4 us (15%)
  matrix products  19.8 us (12%)
  Pallas kernels  13.6 us (9%)
  starting transfers between devices  12.3 us (8%)
  other arithmetic  6.15 us (4%)
  local copies, waits for them, and re-layouts  6.03 us (4%)
    all_to_all x2, blocking collectives, on_device(): lax.all_to_all(bucket_major(product), 'img', split_axis=0, concat_axis=0,...  34.3 us
    all_to_all x2, blocking collectives, on_device(): lax.all_to_all(to_bucket(scaled), 'img', split_axis=0, concat_axis=0, til...  22.6 us
    all_to_all x1, blocking collectives, on_device(): lax.all_to_all(low_payload, 'img', split_axis=0, concat_axis=0, tiled=True)  20 us
    pallas_call x1, Pallas kernels, pieces_affinity(): pl.pallas_call(functools.partial(pieces_kernel, len(low_pieces), len(high...  13.6 us
    dot_general x2, matrix products, on_device(): jnp.einsum('ajk,akc->ajc', weights, list_major(arrived), preferred_elemen...  12.1 us
    all_to_all x1, waiting for transfers between devices, on_device(): lax.all_to_all(high_payload, 'img', split_axis=0, concat_axis=0, tiled=True)  9.89 us
    ppermute x2, waiting for transfers between devices, exchange_stage(): return jnp.concatenate([got, lax.ppermute(got, 'sub', pairs)], axis=0)  6.53 us
    all_to_all x1, waiting for transfers between devices, on_device(): lax.all_to_all(bucket_major(row_sums), 'img', split_axis=0, concat_axis=0...  6.36 us
  transfers between devices with their start and end apart: 6, of which 4 were waited for; matrix products, arithmetic and copies ran while one was open for 2% of the time, Pallas kernels for 0%

profile of v23, /device:TPU:0, one launch (start us, length us, event | category | flops | bytes accessed | tf_op | source)
XLA Modules:
  0.0 158.4 jit_solution(14193467169904350947)
XLA Ops:
  0.0 0.8 copy.55
  0.8 0.2 eq.32
  1.0 0.5 convert_reduce_fusion
  1.5 0.2 reduce_sum.39
  1.7 0.1 copy.56
  1.9 0.7 multiply_add_fusion
  2.6 0.1 iota_add_fusion.1
  2.7 0.1 add.108
  2.7 0.7 convert_element_type.72
  3.4 0.4 fusion.11
  3.8 0.3 fusion.9
  4.2 0.1 convert_element_type.86
  4.3 1.4 fusion.1
  5.6 1.9 %convolution_convert_fusion.2 = bf16[512,768]{1,0:T(8,128)(2,1)S(1)} fusion(bf16[512,768]{1,0:T(8,128)(2,1)} %param.5, f32[512]{0:T(512)S(1)} %add_rsqrt_fusion, s32[512]{0:T(512)S(1)} %bitcast.91, s32[512]{0:T(512)S(1)} %bitcast.83, s32[512]{0:T(512)S(1)} %add.108), kind=kOutput, calls=%fused_computation.11 | convolution fusion | flops 405012480 | bytes 1581056 | tf_op jit(solution)/shard_map/dot_general | solution.py:235
  7.5 0.0 copy-start.3
  7.5 0.9 fusion.22
  8.5 20.0 %all_to_all.35 = bf16[8,65,384]{2,1,0:T(8,128)(2,1)S(1)} all-to-all(bf16[8,65,384]{2,1,0:T(8,128)(2,1)S(1)} %fusion.17), channel_id=1, replica_groups=mesh['img'=8,'sub'=4] {'img'}, dimensions={0} | all-to-all | bytes 798720 | tf_op jit(solution)/shard_map/all_to_all | solution.py:251
  28.5 3.5 %all-to-all-start.1 = ((bf16[8,64,384]{2,1,0:T(8,128)(2,1)}), bf16[8,64,384]{2,1,0:T(8,128)(2,1)S(1)}, u32[]{:S(2)}, u32[]{:S(2)}) async-start(bf16[8,64,384]{2,1,0:T(8,128)(2,1)} %get-tuple-element.9), calls=%async_computation.1 | async-start | bytes 786432 | tf_op jit(solution)/shard_map/all_to_all | solution.py:252
  32.0 1.6 collective-permute-start
  33.5 9.9 %all-to-all-done.1 = bf16[8,64,384]{2,1,0:T(8,128)(2,1)S(1)} async-done(((bf16[8,64,384]{2,1,0:T(8,128)(2,1)}), bf16[8,64,384]{2,1,0:T(8,128)(2,1)S(1)}, u32[]{:S(2)}, u32[]{:S(2)}) %all-to-all-start.1) | async-done | bytes 393248 | tf_op jit(solution)/shard_map/all_to_all | solution.py:252
  43.4 1.5 collective-permute-start.2
  44.9 0.0 collective-permute-done
  44.9 0.1 pad_maximum_fusion.refs_0_
  45.0 0.0 copy-start
  45.0 0.1 copy.58
  45.1 0.1 collective-permute-start.1
  45.2 6.5 %collective-permute-done.2 = bf16[1,8,64,384]{3,2,1,0:T(8,128)(2,1)S(1)} collective-permute-done((bf16[1,8,64,384]{3,2,1,0:T(8,128)(2,1)S(1)}, bf16[1,8,64,384]{3,2,1,0:T(8,128)(2,1)S(1)}, u32[]{:S(2)}, u32[]{:S(2)}) %collective-permute-start.2) | collective-permute-done | bytes 393248 | tf_op jit(solution)/shard_map/ppermute | solution.py:249
  51.7 1.0 pad_maximum_fusion.1.refs_2_
  52.7 0.0 collective-permute-start.3
  52.7 0.0 copy-done.3
  52.7 0.1 broadcast_add_fusion
  52.9 0.0 collective-permute-done.1
  52.9 0.7 reshape.188.col_keys
  53.6 1.0 copy.61.refs_1_
  54.6 0.0 copy-start.2
  54.6 0.6 collective-permute-done.3.refs_3_
  55.2 0.0 copy-done
  55.2 0.0 copy-start.1
  55.2 0.9 copy-done.1
  56.1 13.6 %shard_map.55 = (bf16[2048,2048]{1,0:T(8,128)(2,1)}, f32[1,2048]{1,0:T(1,128)}) custom-call(f32[1,2048]{1,0:T(1,128)} %reshape.188.col_keys, bf16[2,8,65,384]{3,2,1,0:T(8,128)(2,1)} %copy-done, bf16[2,8,65,384]{3,2,1,0:T(8,128)(2,1)} %copy.61.refs_1_, bf16[2,8,64,384]{3,2,1,0:T(8,128)(2,1)} %pad_maximum_fusion.1.refs_2_, bf16[2,8,64,384]{3,2,1,0:T(8,128)(2,1)} %copy-done.1), custom_call_target="tpu_custom_call" | custom-call | flops 6534725632 | bytes 11534336 | tf_op jit(solution)/shard_map/pallas_call | solution.py:148
  69.7 5.7 %all-to-all-start.2 = ((f32[8,1,256]{2,1,0:T(1,128)}), f32[8,1,256]{2,1,0:T(1,128)S(1)}, u32[]{:S(2)}, u32[]{:S(2)}) async-start(f32[8,1,256]{2,1,0:T(1,128)} %bitcast.98), calls=%async_computation.2 | async-start | bytes 16384 | tf_op jit(solution)/shard_map/all_to_all | solution.py:267
  75.4 0.1 iota_add_fusion
  75.5 0.1 add.102
  75.6 6.4 %all-to-all-done.2 = f32[8,1,256]{2,1,0:T(1,128)S(1)} async-done(((f32[8,1,256]{2,1,0:T(1,128)}), f32[8,1,256]{2,1,0:T(1,128)S(1)}, u32[]{:S(2)}, u32[]{:S(2)}) %all-to-all-start.2) | async-done | bytes 8224 | tf_op jit(solution)/shard_map/all_to_all | solution.py:267
  81.9 0.7 select_reduce_fusion
  82.7 0.0 copy-done.2
  82.7 1.3 convolution_convert_fusion.1
  83.9 0.1 copy.73
  84.1 10.6 %all_to_all.36 = bf16[8,1,256,64]{2,3,1,0:T(8,128)(2,1)S(1)} all-to-all(bf16[8,1,256,64]{2,3,1,0:T(8,128)(2,1)S(1)} %copy.63), channel_id=1, replica_groups=mesh['img'=8,'sub'=4] {'img'}, dimensions={0} | all-to-all | bytes 524288 | tf_op jit(solution)/shard_map/all_to_all | solution.py:276
  94.7 0.1 copy.64
  94.9 0.1 reshape.189
  95.0 6.0 %convolution_bitcast_fusion.1 = f32[8,1,256,64]{2,3,1,0:T(8,128)S(1)} fusion(bf16[8,256,2048]{2,1,0:T(8,128)(2,1)} %bitcast.64, bf16[2048,64,1]{0,1,2:T(8,128)(2,1)S(1)} %reshape.189), kind=kOutput, calls=%fused_computation.16 | convolution fusion | flops 536870912 | bytes 9175040 | tf_op jit(solution)/shard_map/ajk,akc->ajc/dot_general | solution.py:277
  101.0 17.0 %all_to_all.37 = f32[8,1,256,64]{2,3,1,0:T(8,128)S(1)} all-to-all(f32[8,1,256,64]{2,3,1,0:T(8,128)S(1)} %convolution_bitcast_fusion.1), channel_id=1, replica_groups=mesh['img'=8,'sub'=4] {'img'}, dimensions={0} | all-to-all | bytes 1048576 | tf_op jit(solution)/shard_map/all_to_all | solution.py:280
  118.1 1.3 fusion.6
  119.5 1.3 convolution_convert_fusion
  120.7 0.1 copy.75
  120.8 12.0 %all_to_all.38 = bf16[8,1,256,64]{2,3,1,0:T(8,128)(2,1)S(1)} all-to-all(bf16[8,1,256,64]{2,3,1,0:T(8,128)(2,1)S(1)} %copy.67), channel_id=1, replica_groups=mesh['img'=8,'sub'=4] {'img'}, dimensions={0} | all-to-all | bytes 524288 | tf_op jit(solution)/shard_map/all_to_all | solution.py:276
  132.8 0.1 copy.68
  133.0 0.1 reshape.190
  133.1 6.0 %convolution_bitcast_fusion = f32[8,1,256,64]{2,3,1,0:T(8,128)S(1)} fusion(bf16[8,256,2048]{2,1,0:T(8,128)(2,1)} %bitcast.65, bf16[2048,64,1]{0,1,2:T(8,128)(2,1)S(1)} %reshape.190), kind=kOutput, calls=%fused_computation.15 | convolution fusion | flops 536870912 | bytes 9175040 | tf_op jit(solution)/shard_map/ajk,akc->ajc/dot_general | solution.py:277
  139.1 17.3 %all_to_all.39 = f32[8,1,256,64]{2,3,1,0:T(8,128)S(1)} all-to-all(f32[8,1,256,64]{2,3,1,0:T(8,128)S(1)} %convolution_bitcast_fusion), channel_id=1, replica_groups=mesh['img'=8,'sub'=4] {'img'}, dimensions={0} | all-to-all | bytes 1048576 | tf_op jit(solution)/shard_map/all_to_all | solution.py:280
  156.5 2.0 %fusion.7 = bf16[512,64]{0,1:T(8,128)(2,1)} fusion(f32[2048,64]{0,1:T(8,128)S(1)} %bitcast.76, bf16[512,64]{0,1:T(8,128)(2,1)S(1)} %copy-done.2, f32[512]{0:T(512)S(1)} %get-tuple-element.15, s32[512]{0:T(512)S(1)} %bitcast.96, s32[512]{0:T(512)S(1)} %bitcast.88, s32[2048]{0:T(1024)S(1)} %add.102), kind=kOutput, calls=%fused_computation.23 | convolution fusion | flops 405962752 | bytes 669696 | tf_op jit(solution)/shard_map/kg,kc->gc/dot_general | solution.py:211
  (18 shorter events, 0.3 us)
Async XLA Ops:
  7.5 45.2 %copy-start.3 = (s32[4]{0:T(128)S(1)}, s32[4]{0:T(128)}, u32[]{:S(2)}) copy-start(s32[4]{0:T(128)} %constant.11.clone) | copy-start | bytes 52
  28.5 14.9 %all-to-all-start.1 = ((bf16[8,64,384]{2,1,0:T(8,128)(2,1)}), bf16[8,64,384]{2,1,0:T(8,128)(2,1)S(1)}, u32[]{:S(2)}, u32[]{:S(2)}) async-start(bf16[8,64,384]{2,1,0:T(8,128)(2,1)} %get-tuple-element.9), calls=%async_computation.1 | async-start | bytes 786432 | tf_op jit(solution)/shard_map/all_to_all | solution.py:252
  32.0 12.9 %collective-permute-start = (bf16[1,8,65,384]{3,2,1,0:T(8,128)(2,1)S(1)}, bf16[1,8,65,384]{3,2,1,0:T(8,128)(2,1)S(1)}, u32[]{:S(2)}, u32[]{:S(2)}) collective-permute-start(bf16[1,8,65,384]{3,2,1,0:T(8,128)(2,1)S(1)} %bitcast.66), channel_id=1, source_target_pairs={{0,2},{1,3},{2,0},{3,1},{4,6},{5,7},{6,4},{7,5},{8,10},{9,11},{10,... | collective-permute-start | bytes 1198088 | tf_op jit(solution)/shard_map/ppermute | solution.py:249
  43.4 8.3 %collective-permute-start.2 = (bf16[1,8,64,384]{3,2,1,0:T(8,128)(2,1)S(1)}, bf16[1,8,64,384]{3,2,1,0:T(8,128)(2,1)S(1)}, u32[]{:S(2)}, u32[]{:S(2)}) collective-permute-start(bf16[1,8,64,384]{3,2,1,0:T(8,128)(2,1)S(1)} %bitcast.71), channel_id=1, source_target_pairs={{0,2},{1,3},{2,0},{3,1},{4,6},{5,7},{6,4},{7,5},{8,10},{9,11},{10,... | collective-permute-start | bytes 1179656 | tf_op jit(solution)/shard_map/ppermute | solution.py:249
  45.0 10.2 %copy-start = (bf16[2,8,65,384]{3,2,1,0:T(8,128)(2,1)}, bf16[2,8,65,384]{3,2,1,0:T(8,128)(2,1)S(1)}, u32[]{:S(2)}) copy-start(bf16[2,8,65,384]{3,2,1,0:T(8,128)(2,1)S(1)} %pad_maximum_fusion.refs_0_) | copy-start | bytes 2396164
  45.1 7.7 %collective-permute-start.1 = (bf16[2,8,65,384]{3,1,2,0:T(8,128)(2,1)S(1)}, bf16[2,8,65,384]{3,1,2,0:T(8,128)(2,1)S(1)}, u32[]{:S(2)}, u32[]{:S(2)}) collective-permute-start(bf16[2,8,65,384]{3,1,2,0:T(8,128)(2,1)S(1)} %copy.58), channel_id=1, source_target_pairs={{0,1},{1,0},{2,3},{3,2},{4,5},{5,4},{6,7},{7,6},{8,9},{9,8},{10,11... | collective-permute-start | bytes 2396168 | tf_op jit(solution)/shard_map/ppermute | solution.py:259
  52.7 2.5 %collective-permute-start.3 = (bf16[2,8,64,384]{3,2,1,0:T(8,128)(2,1)}, bf16[2,8,64,384]{3,2,1,0:T(8,128)(2,1)S(1)}, u32[]{:S(2)}, u32[]{:S(2)}) collective-permute-start(bf16[2,8,64,384]{3,2,1,0:T(8,128)(2,1)} %pad_maximum_fusion.1.refs_2_), channel_id=1, source_target_pairs={{0,1},{1,0},{2,3},{3,2},{4,5},{5,4},{6,7},{7,6},{8,9},{9,8},{10,11... | collective-permute-start | bytes 2359304 | tf_op jit(solution)/shard_map/ppermute | solution.py:260
  54.6 28.0 %copy-start.2 = (bf16[512,64]{0,1:T(8,128)(2,1)S(1)}, bf16[512,64]{0,1:T(8,128)(2,1)}, u32[]{:S(2)}) copy-start(bf16[512,64]{0,1:T(8,128)(2,1)} %param.6) | copy-start | bytes 196612
  55.2 0.9 copy-start.1
  69.7 12.2 %all-to-all-start.2 = ((f32[8,1,256]{2,1,0:T(1,128)}), f32[8,1,256]{2,1,0:T(1,128)S(1)}, u32[]{:S(2)}, u32[]{:S(2)}) async-start(f32[8,1,256]{2,1,0:T(1,128)} %bitcast.98), calls=%async_computation.2 | async-start | bytes 16384 | tf_op jit(solution)/shard_map/all_to_all | solution.py:267

commit v24 on v16

--- a/solution.py
+++ b/solution.py
@@ -139,7 +139,7 @@
             return jnp.moveaxis(stacked, 0, 1)
         return fused_affinity(source_major(low_pieces), source_major(high_pieces), keys, part)
     slot_count = sources * quarters * part
-    block_rows = min(512, slot_count)
+    block_rows = min(1024, slot_count)
     pieces = list(low_pieces) + list(high_pieces)
     specs = [
         pl.BlockSpec((piece.shape[0], sources, part, piece.shape[3]), lambda i: (0, 0, 0, 0))

time: 156 us -> 157 us (level)
  no operation moved by 1% of the time
where the time goes in v24:
time: 157 us; the launch traced here: 156 us
  blocking collectives  70.6 us (45%)
  waiting for transfers between devices  27.7 us (18%)
  matrix products  19.8 us (13%)
  starting transfers between devices  14.1 us (9%)
  Pallas kernels  14 us (9%)
  local copies, waits for them, and re-layouts  5.02 us (3%)
  other arithmetic  4.48 us (3%)
    all_to_all x2, blocking collectives, on_device(): lax.all_to_all(bucket_major(product), 'img', split_axis=0, concat_axis=0,...  34.3 us
    all_to_all x2, blocking collectives, on_device(): lax.all_to_all(to_bucket(scaled), 'img', split_axis=0, concat_axis=0, til...  22.6 us
    pallas_call x1, Pallas kernels, pieces_affinity(): pl.pallas_call(functools.partial(pieces_kernel, len(low_pieces), len(high...  14 us
    all_to_all x1, blocking collectives, on_device(): lax.all_to_all(low_payload, 'img', split_axis=0, concat_axis=0, tiled=True)  13.7 us
    all_to_all x1, waiting for transfers between devices, on_device(): lax.all_to_all(high_payload, 'img', split_axis=0, concat_axis=0, tiled=True)  13.6 us
    dot_general x2, matrix products, on_device(): jnp.einsum('ajk,akc->ajc', weights, list_major(arrived), preferred_elemen...  12.1 us
    all_to_all x1, starting transfers between devices, on_device(): lax.all_to_all(high_payload, 'img', split_axis=0, concat_axis=0, tiled=True)  7.28 us
    all_to_all x1, waiting for transfers between devices, on_device(): lax.all_to_all(bucket_major(row_sums), 'img', split_axis=0, concat_axis=0...  6.36 us
  transfers between devices with their start and end apart: 6, of which 4 were waited for; matrix products, arithmetic and copies ran while one was open for 2% of the time, Pallas kernels for 0%

profile of v24, /device:TPU:0, one launch (start us, length us, event | category | flops | bytes accessed | tf_op | source)
XLA Modules:
  0.0 156.0 jit_solution(6697906343834965206)
XLA Ops:
  0.0 0.0 copy-start.2
  0.0 0.8 copy.55
  0.8 0.2 eq.32
  1.0 0.5 convert_reduce_fusion
  1.5 0.2 reduce_sum.39
  1.8 0.1 copy.56
  1.9 0.7 multiply_add_fusion
  2.6 0.1 iota_add_fusion.1
  2.7 0.1 add.108
  2.7 1.4 fusion.1
  4.1 1.9 %convolution_convert_fusion.2 = bf16[512,768]{1,0:T(8,128)(2,1)S(1)} fusion(bf16[512,768]{1,0:T(8,128)(2,1)} %param.5, f32[512]{0:T(512)S(1)} %add_rsqrt_fusion, s32[512]{0:T(512)S(1)} %bitcast.90, s32[512]{0:T(512)S(1)} %bitcast.82, s32[512]{0:T(512)S(1)} %add.108), kind=kOutput, calls=%fused_computation.11 | convolution fusion | flops 405012480 | bytes 1581056 | tf_op jit(solution)/shard_map/dot_general | solution.py:235
  6.0 0.0 copy-start.4
  6.0 0.8 slice.42
  6.9 7.3 %all-to-all-start.1 = ((bf16[8,64,512]{2,1,0:T(8,128)(2,1)}), bf16[8,64,512]{2,1,0:T(8,128)(2,1)S(1)}, u32[]{:S(2)}, u32[]{:S(2)}) async-start(bf16[8,64,512]{2,1,0:T(8,128)(2,1)} %slice.42), calls=%async_computation.1 | async-start | bytes 1048576 | tf_op jit(solution)/shard_map/all_to_all | solution.py:252
  14.2 0.0 copy-done.2
  14.2 0.4 fusion.10
  14.6 0.3 fusion.9
  14.9 0.1 convert_element_type.86
  15.0 13.6 %all-to-all-done.1 = bf16[8,64,512]{2,1,0:T(8,128)(2,1)S(1)} async-done(((bf16[8,64,512]{2,1,0:T(8,128)(2,1)}), bf16[8,64,512]{2,1,0:T(8,128)(2,1)S(1)}, u32[]{:S(2)}, u32[]{:S(2)}) %all-to-all-start.1) | async-done | bytes 524320 | tf_op jit(solution)/shard_map/all_to_all | solution.py:252
  28.6 1.5 collective-permute-start.2
  30.1 13.7 %all_to_all.35 = bf16[8,65,256]{2,1,0:T(8,128)(2,1)S(1)} all-to-all(bf16[8,65,256]{2,1,0:T(8,128)(2,1)S(1)} %fusion.17), channel_id=1, replica_groups=mesh['img'=8,'sub'=4] {'img'}, dimensions={0} | all-to-all | bytes 532480 | tf_op jit(solution)/shard_map/all_to_all | solution.py:251
  43.8 0.5 collective-permute-start
  44.4 0.0 collective-permute-done.2
  44.4 0.1 pad_maximum_fusion.refs_2_
  44.5 0.0 copy-start.1
  44.5 0.1 collective-permute-start.3
  44.6 6.0 %collective-permute-done = bf16[1,8,65,256]{3,2,1,0:T(8,128)(2,1)S(1)} collective-permute-done((bf16[1,8,65,256]{3,2,1,0:T(8,128)(2,1)S(1)}, bf16[1,8,65,256]{3,2,1,0:T(8,128)(2,1)S(1)}, u32[]{:S(2)}, u32[]{:S(2)}) %collective-permute-start) | collective-permute-done | bytes 266272 | tf_op jit(solution)/shard_map/ppermute | solution.py:249
  50.5 0.1 pad_maximum_fusion.1.refs_0_
  50.6 0.0 copy-start
  50.6 0.1 copy.58
  50.7 0.1 collective-permute-start.1
  50.8 0.0 copy-done.4
  50.8 0.1 broadcast_add_fusion
  50.9 1.8 %collective-permute-done.1 = bf16[2,8,65,256]{3,1,2,0:T(8,128)(2,1)S(1)} collective-permute-done((bf16[2,8,65,256]{3,1,2,0:T(8,128)(2,1)S(1)}, bf16[2,8,65,256]{3,1,2,0:T(8,128)(2,1)S(1)}, u32[]{:S(2)}, u32[]{:S(2)}) %collective-permute-start.1) | collective-permute-done | bytes 532512 | tf_op jit(solution)/shard_map/ppermute | solution.py:259
  52.7 0.7 reshape.188.col_keys
  53.4 0.9 copy.61.refs_1_
  54.4 0.0 copy-start.3
  54.4 0.0 collective-permute-done.3.refs_3_
  54.4 0.0 copy-done.1
  54.4 0.0 copy-done
  54.4 14.0 %shard_map.55 = (bf16[2048,2048]{1,0:T(8,128)(2,1)}, f32[1,2048]{1,0:T(1,128)}) custom-call(f32[1,2048]{1,0:T(1,128)} %reshape.188.col_keys, bf16[2,8,65,256]{3,2,1,0:T(8,128)(2,1)} %copy-done, bf16[2,8,65,256]{3,2,1,0:T(8,128)(2,1)} %copy.61.refs_1_, bf16[2,8,64,512]{3,2,1,0:T(8,128)(2,1)} %copy-done.1, bf16[2,8,64,512]{3,2,1,0:T(8,128)(2,1)} %collective-permute-done.3.refs_3_), custom_call_target="tpu_custom_call" | custom-call | flops 6534725632 | bytes 11534336 | tf_op jit(solution)/shard_map/pallas_call | solution.py:148
  68.4 4.7 %all-to-all-start.2 = ((f32[8,1,256]{2,1,0:T(1,128)}), f32[8,1,256]{2,1,0:T(1,128)S(1)}, u32[]{:S(2)}, u32[]{:S(2)}) async-start(f32[8,1,256]{2,1,0:T(1,128)} %bitcast.99), calls=%async_computation.2 | async-start | bytes 16384 | tf_op jit(solution)/shard_map/all_to_all | solution.py:267
  73.0 0.1 iota_add_fusion
  73.1 0.1 add.102
  73.2 6.4 %all-to-all-done.2 = f32[8,1,256]{2,1,0:T(1,128)S(1)} async-done(((f32[8,1,256]{2,1,0:T(1,128)}), f32[8,1,256]{2,1,0:T(1,128)S(1)}, u32[]{:S(2)}, u32[]{:S(2)}) %all-to-all-start.2) | async-done | bytes 8224 | tf_op jit(solution)/shard_map/all_to_all | solution.py:267
  79.5 0.7 select_reduce_fusion
  80.3 0.0 copy-done.3
  80.3 1.3 convolution_convert_fusion.1
  81.5 0.1 copy.73
  81.7 10.6 %all_to_all.36 = bf16[8,1,256,64]{2,3,1,0:T(8,128)(2,1)S(1)} all-to-all(bf16[8,1,256,64]{2,3,1,0:T(8,128)(2,1)S(1)} %copy.63), channel_id=1, replica_groups=mesh['img'=8,'sub'=4] {'img'}, dimensions={0} | all-to-all | bytes 524288 | tf_op jit(solution)/shard_map/all_to_all | solution.py:276
  92.3 0.1 copy.64
  92.5 0.1 reshape.189
  92.6 6.0 %convolution_bitcast_fusion.1 = f32[8,1,256,64]{2,3,1,0:T(8,128)S(1)} fusion(bf16[8,256,2048]{2,1,0:T(8,128)(2,1)} %bitcast.64, bf16[2048,64,1]{0,1,2:T(8,128)(2,1)S(1)} %reshape.189), kind=kOutput, calls=%fused_computation.16 | convolution fusion | flops 536870912 | bytes 9175040 | tf_op jit(solution)/shard_map/ajk,akc->ajc/dot_general | solution.py:277
  98.6 17.0 %all_to_all.37 = f32[8,1,256,64]{2,3,1,0:T(8,128)S(1)} all-to-all(f32[8,1,256,64]{2,3,1,0:T(8,128)S(1)} %convolution_bitcast_fusion.1), channel_id=1, replica_groups=mesh['img'=8,'sub'=4] {'img'}, dimensions={0} | all-to-all | bytes 1048576 | tf_op jit(solution)/shard_map/all_to_all | solution.py:280
  115.7 1.3 fusion.6
  117.0 1.3 convolution_convert_fusion
  118.3 0.1 copy.75
  118.4 12.0 %all_to_all.38 = bf16[8,1,256,64]{2,3,1,0:T(8,128)(2,1)S(1)} all-to-all(bf16[8,1,256,64]{2,3,1,0:T(8,128)(2,1)S(1)} %copy.67), channel_id=1, replica_groups=mesh['img'=8,'sub'=4] {'img'}, dimensions={0} | all-to-all | bytes 524288 | tf_op jit(solution)/shard_map/all_to_all | solution.py:276
  130.4 0.1 copy.68
  130.5 0.1 reshape.190
  130.7 6.0 %convolution_bitcast_fusion = f32[8,1,256,64]{2,3,1,0:T(8,128)S(1)} fusion(bf16[8,256,2048]{2,1,0:T(8,128)(2,1)} %bitcast.65, bf16[2048,64,1]{0,1,2:T(8,128)(2,1)S(1)} %reshape.190), kind=kOutput, calls=%fused_computation.15 | convolution fusion | flops 536870912 | bytes 9175040 | tf_op jit(solution)/shard_map/ajk,akc->ajc/dot_general | solution.py:277
  136.7 17.3 %all_to_all.39 = f32[8,1,256,64]{2,3,1,0:T(8,128)S(1)} all-to-all(f32[8,1,256,64]{2,3,1,0:T(8,128)S(1)} %convolution_bitcast_fusion), channel_id=1, replica_groups=mesh['img'=8,'sub'=4] {'img'}, dimensions={0} | all-to-all | bytes 1048576 | tf_op jit(solution)/shard_map/all_to_all | solution.py:280
  154.0 2.0 %fusion.7 = bf16[512,64]{0,1:T(8,128)(2,1)} fusion(f32[2048,64]{0,1:T(8,128)S(1)} %bitcast.77, bf16[512,64]{0,1:T(8,128)(2,1)S(1)} %copy-done.3, f32[512]{0:T(512)S(1)} %get-tuple-element.13, s32[512]{0:T(512)S(1)} %bitcast.97, s32[512]{0:T(512)S(1)} %bitcast.89, s32[2048]{0:T(1024)S(1)} %add.102), kind=kOutput, calls=%fused_computation.23 | convolution fusion | flops 405962752 | bytes 669696 | tf_op jit(solution)/shard_map/kg,kc->gc/dot_general | solution.py:211
  (20 shorter events, 0.3 us)
Async XLA Ops:
  0.0 14.2 %copy-start.2 = (s32[512,2]{0,1:T(2,128)S(1)}, s32[512,2]{0,1:T(2,128)}, u32[]{:S(2)}) copy-start(s32[512,2]{0,1:T(2,128)} %param.8) | copy-start | bytes 12292
  6.0 44.8 %copy-start.4 = (s32[4]{0:T(128)S(1)}, s32[4]{0:T(128)}, u32[]{:S(2)}) copy-start(s32[4]{0:T(128)} %constant.11.clone) | copy-start | bytes 52
  6.9 21.8 %all-to-all-start.1 = ((bf16[8,64,512]{2,1,0:T(8,128)(2,1)}), bf16[8,64,512]{2,1,0:T(8,128)(2,1)S(1)}, u32[]{:S(2)}, u32[]{:S(2)}) async-start(bf16[8,64,512]{2,1,0:T(8,128)(2,1)} %slice.42), calls=%async_computation.1 | async-start | bytes 1048576 | tf_op jit(solution)/shard_map/all_to_all | solution.py:252
  28.6 15.7 %collective-permute-start.2 = (bf16[1,8,64,512]{3,2,1,0:T(8,128)(2,1)S(1)}, bf16[1,8,64,512]{3,2,1,0:T(8,128)(2,1)S(1)}, u32[]{:S(2)}, u32[]{:S(2)}) collective-permute-start(bf16[1,8,64,512]{3,2,1,0:T(8,128)(2,1)S(1)} %bitcast.71), channel_id=1, source_target_pairs={{0,2},{1,3},{2,0},{3,1},{4,6},{5,7},{6,4},{7,5},{8,10},{9,11},{10,... | collective-permute-start | bytes 1572872 | tf_op jit(solution)/shard_map/ppermute | solution.py:249
  43.8 6.7 %collective-permute-start = (bf16[1,8,65,256]{3,2,1,0:T(8,128)(2,1)S(1)}, bf16[1,8,65,256]{3,2,1,0:T(8,128)(2,1)S(1)}, u32[]{:S(2)}, u32[]{:S(2)}) collective-permute-start(bf16[1,8,65,256]{3,2,1,0:T(8,128)(2,1)S(1)} %bitcast.66), channel_id=1, source_target_pairs={{0,2},{1,3},{2,0},{3,1},{4,6},{5,7},{6,4},{7,5},{8,10},{9,11},{10,... | collective-permute-start | bytes 798728 | tf_op jit(solution)/shard_map/ppermute | solution.py:249
  44.5 9.9 %copy-start.1 = (bf16[2,8,64,512]{3,2,1,0:T(8,128)(2,1)}, bf16[2,8,64,512]{3,2,1,0:T(8,128)(2,1)S(1)}, u32[]{:S(2)}) copy-start(bf16[2,8,64,512]{3,2,1,0:T(8,128)(2,1)S(1)} %pad_maximum_fusion.refs_2_) | copy-start | bytes 3145732
  44.5 9.9 %collective-permute-start.3 = (bf16[2,8,64,512]{3,2,1,0:T(8,128)(2,1)S(1)}, bf16[2,8,64,512]{3,2,1,0:T(8,128)(2,1)}, u32[]{:S(2)}, u32[]{:S(2)}) collective-permute-start(bf16[2,8,64,512]{3,2,1,0:T(8,128)(2,1)S(1)} %pad_maximum_fusion.refs_2_), channel_id=1, source_target_pairs={{0,1},{1,0},{2,3},{3,2},{4,5},{5,4},{6,7},{7,6},{8,9},{9,8},{10,11... | collective-permute-start | bytes 3145736 | tf_op jit(solution)/shard_map/ppermute | solution.py:260
  50.6 3.8 %copy-start = (bf16[2,8,65,256]{3,2,1,0:T(8,128)(2,1)}, bf16[2,8,65,256]{3,2,1,0:T(8,128)(2,1)S(1)}, u32[]{:S(2)}) copy-start(bf16[2,8,65,256]{3,2,1,0:T(8,128)(2,1)S(1)} %pad_maximum_fusion.1.refs_0_) | copy-start | bytes 1597444
  50.7 2.0 %collective-permute-start.1 = (bf16[2,8,65,256]{3,1,2,0:T(8,128)(2,1)S(1)}, bf16[2,8,65,256]{3,1,2,0:T(8,128)(2,1)S(1)}, u32[]{:S(2)}, u32[]{:S(2)}) collective-permute-start(bf16[2,8,65,256]{3,1,2,0:T(8,128)(2,1)S(1)} %copy.58), channel_id=1, source_target_pairs={{0,1},{1,0},{2,3},{3,2},{4,5},{5,4},{6,7},{7,6},{8,9},{9,8},{10,11... | collective-permute-start | bytes 1597448 | tf_op jit(solution)/shard_map/ppermute | solution.py:259
  54.4 25.9 %copy-start.3 = (bf16[512,64]{0,1:T(8,128)(2,1)S(1)}, bf16[512,64]{0,1:T(8,128)(2,1)}, u32[]{:S(2)}) copy-start(bf16[512,64]{0,1:T(8,128)(2,1)} %param.6) | copy-start | bytes 196612
  68.4 11.2 %all-to-all-start.2 = ((f32[8,1,256]{2,1,0:T(1,128)}), f32[8,1,256]{2,1,0:T(1,128)S(1)}, u32[]{:S(2)}, u32[]{:S(2)}) async-start(f32[8,1,256]{2,1,0:T(1,128)} %bitcast.99), calls=%async_computation.2 | async-start | bytes 16384 | tf_op jit(solution)/shard_map/all_to_all | solution.py:267
